TPU v7x, 256 devices: a whole 4x4x8 slice. The times are simulated.
256 devices in a mesh: row: 4 (over z_lo), col: 64 (over y, x, z_hi, core).
Axes of the slice: x: 4, y: 4, z: 8 (z_hi: 2, z_lo: 4; z = z_hi * 4 + z_lo), core: 2. Of those that a mesh axis runs over, the one named last changes fastest.
Arguments:
- iterate: float32 [256, 131072], P('row', 'col'), may hold values from -6 to 6
- residual: float32 [256, 131072], P('row', 'col'), may hold values from -24 to 24
- direction: float32 [256, 131072], P('row', 'col'), may hold values from -24 to 24
- window_weight: float32 [16, 8192], P('row', 'col'), may hold values from 0.2 to 5
- freq_weight: float32 [32, 32], replicated, may hold values from 0.2 to 5
Outputs:
- new_iterate: float32 [256, 131072], P('row', 'col')
- new_residual: float32 [256, 131072], P('row', 'col')
- new_direction: float32 [256, 131072], P('row', 'col')
All inputs are finite; a program needn't handle non-finite values.
Results may differ from a plain program's by a relative error of at most 0.0003.
Values sent between devices are 32-bit elements; how exact they have to be, the bound alone decides.
No kernel may reach another device: no remote copies, remote signals or barrier semaphores. Data moves between devices by JAX's collectives and lax.ppermute only.
A program may use at most 64 MiB of HBM per device.

v0:
```python
import jax
import jax.numpy as jnp
from jax import lax
from jax.sharding import Mesh
from jax.sharding import PartitionSpec as P

COL = ("col_0", "col_1", "col_2", "col_3")
ROW_COL = ("row", "col_0", "col_1", "col_2", "col_3")


precise = lax.Precision.HIGHEST
damping = 0.5


def passed_along(value, axis, steps):
    count = lax.axis_size(axis)
    leading, last = (max(0, -steps), min(count, count - steps))
    return lax.ppermute(value, axis, [(source, source + steps) for source in range(leading, last)])


def over_axes(x, axes):
    for axis in axes:
        x = lax.psum(x, axis)
    return x


def tables():
    positions = jnp.arange(32, dtype=jnp.float32)
    window = jnp.exp(-0.5 * ((positions - 15.5) / 8.0) ** 2)
    phases = 2.0 * jnp.pi * jnp.outer(positions, positions) / 32.0
    cos_part = jnp.cos(phases) * window[None, :] / jnp.sqrt(32.0)
    sin_part = -jnp.sin(phases) * window[None, :] / jnp.sqrt(32.0)
    column_table = jnp.concatenate([cos_part.T, sin_part.T], axis=1)
    cos_split = cos_part.reshape(32, 2, 16)
    sin_split = sin_part.reshape(32, 2, 16)
    upper = jnp.stack([cos_split, -sin_split], axis=-1)
    lower = jnp.stack([sin_split, cos_split], axis=-1)
    row_table = jnp.concatenate([upper, lower], axis=0).reshape(64, 64)
    return (column_table, row_table)


def analyze(region, column_table, row_table):
    win_rows = region.shape[0] // 16 - 1
    win_cols = region.shape[1] // 16 - 1
    blocks = region.reshape(win_rows + 1, 16, win_cols + 1, 16)
    section_one = jnp.einsum(
        "akbl,lp->akpb", blocks[:, :, :win_cols], column_table[:16], precision=precise
    )
    section_one = section_one + jnp.einsum(
        "akbl,lp->akpb", blocks[:, :, 1:], column_table[16:], precision=precise
    )
    section_one = section_one.reshape(win_rows + 1, 16, 2, 32, win_cols)
    paired = jnp.stack([section_one[:-1], section_one[1:]], axis=1).reshape(
        win_rows, 64, 32, win_cols
    )
    return jnp.einsum("tm,amvb->atvb", row_table, paired, precision=precise)


def weigh(coefficients, window_weight, freq_weight):
    doubled = jnp.concatenate([freq_weight, freq_weight], axis=0)
    return coefficients * doubled[None, :, :, None] * window_weight[:, None, None, :]


def synthesize(coefficients, column_table, row_table):
    win_rows = coefficients.shape[0]
    win_cols = coefficients.shape[3]
    spread = jnp.einsum("tm,atvb->amvb", row_table, coefficients, precision=precise)
    spread = spread.reshape(win_rows, 2, 16, 64, win_cols)
    stacked = jnp.pad(spread[:, 0], ((0, 1), (0, 0), (0, 0), (0, 0))) + jnp.pad(
        spread[:, 1], ((1, 0), (0, 0), (0, 0), (0, 0))
    )
    lower_piece = jnp.einsum("akpb,lp->akbl", stacked, column_table[:16], precision=precise)
    upper_piece = jnp.einsum("akpb,lp->akbl", stacked, column_table[16:], precision=precise)
    blocks = jnp.pad(lower_piece, ((0, 0), (0, 0), (0, 1), (0, 0))) + jnp.pad(
        upper_piece, ((0, 0), (0, 0), (1, 0), (0, 0))
    )
    return blocks.reshape(16 * (win_rows + 1), 16 * (win_cols + 1))


def per_device(iterate, residual, direction, window_weight, freq_weight):
    column_table, row_table = tables()
    height, breadth = direction.shape
    beside = passed_along(direction[:, :16], COL, -1)
    widened = jnp.concatenate([direction, beside], axis=1)
    below = passed_along(widened[:16], "row", -1)
    region = jnp.concatenate([widened, below], axis=0)
    coefficients = weigh(analyze(region, column_table, row_table), window_weight, freq_weight)
    spread = synthesize(coefficients, column_table, row_table)
    arrived_rows = passed_along(spread[height:], "row", 1)
    upper_rows = jnp.concatenate([spread[:16] + arrived_rows, spread[16:height]], axis=0)
    arrived_cols = passed_along(upper_rows[:, breadth:], COL, 1)
    synthesized = jnp.concatenate(
        [upper_rows[:, :16] + arrived_cols, upper_rows[:, 16:breadth]], axis=1
    )
    applied = synthesized + damping * direction
    norm_now, curvature, cross_term, image_norm = (
        over_axes(jnp.sum(residual * residual), ROW_COL),
        over_axes(jnp.sum(direction * applied), ROW_COL),
        over_axes(jnp.sum(residual * applied), ROW_COL),
        over_axes(jnp.sum(applied * applied), ROW_COL),
    )
    step_length = norm_now / curvature
    new_iterate = iterate + step_length * direction
    new_residual = residual - step_length * applied
    norm_next = norm_now - 2.0 * step_length * cross_term + step_length * step_length * image_norm
    new_direction = new_residual + norm_next / norm_now * direction
    return (new_iterate, new_residual, new_direction)


def solution(mesh):
    finer = Mesh(
        mesh.devices.reshape(mesh.shape["row"], 4, 4, 2, 2),
        ("row", "col_0", "col_1", "col_2", "col_3"),
    )
    return jax.shard_map(
        per_device,
        mesh=finer,
        in_specs=(P("row", COL), P("row", COL), P("row", COL), P("row", COL), P()),
        out_specs=(P("row", COL), P("row", COL), P("row", COL)),
        check_vma=False,
    )
```

profile of v0, /device:TPU:1, one launch (start us, length us, event | category | flops | bytes accessed | tf_op | source)
XLA Modules:
  0.0 132.1 jit_solution(15178026938067578234)
XLA Ops:
  1.4 5.1 %collective-permute-start = (f32[64,16]{1,0:T(8,128)S(1)}, f32[64,16]{1,0:T(8,128)S(1)}, u32[]{:S(2)}, u32[]{:S(2)}) collective-permute-start(f32[64,16]{1,0:T(8,128)S(1)} %slice.62), channel_id=1, source_target_pairs={{1,0},{2,1},{3,2},{4,3},{5,4},{6,5},{7,6},{8,7},{9,8},{10,9},{11,1... | collective-permute-start | bytes 12296 | tf_op jit(solution)/shard_map/ppermute | solution.py:18
  8.7 4.5 %collective-permute-done = f32[64,16]{1,0:T(8,128)S(1)} collective-permute-done((f32[64,16]{1,0:T(8,128)S(1)}, f32[64,16]{1,0:T(8,128)S(1)}, u32[]{:S(2)}, u32[]{:S(2)}) %collective-permute-start) | collective-permute-done | bytes 4128 | tf_op jit(solution)/shard_map/ppermute | solution.py:18
  13.2 1.3 collective-permute-start.1
  14.7 4.3 %collective-permute-done.1 = f32[16,2064]{1,0:T(8,128)S(1)} collective-permute-done((f32[16,2064]{1,0:T(8,128)S(1)}, f32[16,2064]{1,0:T(8,128)S(1)}, u32[]{:S(2)}, u32[]{:S(2)}) %collective-permute-start.1) | collective-permute-done | bytes 132128 | tf_op jit(solution)/shard_map/ppermute | solution.py:18
  19.0 3.2 %reshape.132 = f32[5,16,129,16]{3,2,1,0:T(8,128)} reshape(f32[80,2064]{1,0:T(8,128)S(1)} %pad_maximum_fusion) | data formatting | bytes 1320960 | tf_op jit(solution)/shard_map/reshape | solution.py:45
  22.3 8.1 %fusion = f32[64,5,16,128]{3,0,2,1:T(8,128)S(1)} fusion(f32[16,64,1,1]{1,0,3,2:T(8,128)S(1)} %fusion.25, f32[5,16,129,16]{3,2,1,0:T(8,128)} %reshape.132), kind=kOutput, calls=%fused_computation | convolution fusion | flops 125829120 | bytes 7868416 | tf_op jit(solution)/shard_map/akbl,lp->akpb/dot_general | solution.py:49
  30.4 5.8 %add_bitcast_fusion = f32[5,16,64,128]{3,2,1,0:T(8,128)S(1)} fusion(f32[64,5,16,128]{3,0,2,1:T(8,128)S(1)} %fusion, f32[5,16,129,16]{3,2,1,0:T(8,128)S(1)} %copy-done, f32[32,32]{1,0:T(8,128)S(1)} %get-tuple-element.40, f32[32,32]{1,0:T(8,128)S(1)} %get-tuple-element.41), kind=kOutput, calls=%fused_computation.12 | convolution fusion | flops 126485504 | bytes 10518528 | tf_op jit(solution)/shard_map/akbl,lp->akpb/dot_general | solution.py:46
  36.8 1.2 copy.29
  39.3 4.2 %fusion.4 = f32[4,32,128,64,1,1]{2,3,5,4,1,0:T(8,128)S(1)} fusion(f32[4,1,16,2,32,128]{5,2,3,1,4,0:T(8,128)S(1)} %copy.30, f32[4,1,16,2,32,128]{5,2,3,1,4,0:T(8,128)S(1)} %copy.29, f32[64,2,16,2]{0,2,3,1:T(8,128)S(1)} %maximum_maximum_fusion), kind=kOutput, calls=%fused_computation.4 | convolution fusion | flops 806354944 | bytes 8404992 | tf_op jit(solution)/shard_map/tm,amvb->atvb/dot_general | solution.py:56
  43.5 4.4 %fusion.11 = f32[4,64,32,128]{3,1,2,0:T(8,128)S(1)} fusion(f32[64,64,1,1]{0,1,3,2:T(8,128)S(1)} %bitcast.50, f32[4,32,128,64,1,1]{2,3,5,4,1,0:T(8,128)S(1)} %fusion.4, f32[4,128]{1,0:T(4,128)S(1)} %copy-done.4, f32[64,32]{0,1:T(8,128)S(1)} %copy.31), kind=kOutput, calls=%fused_computation.13 | convolution fusion | flops 807403520 | bytes 8415232 | tf_op jit(solution)/shard_map/tm,atvb->amvb/dot_general | solution.py:67
  47.9 2.4 %copy.33 = f32[4,64,32,128]{3,2,1,0:T(8,128)S(1)} copy(f32[4,64,32,128]{3,1,2,0:T(8,128)S(1)} %fusion.11) | data formatting | bytes 8388608 | tf_op jit(solution)/shard_map/tm,atvb->amvb/transpose | solution.py:67
  50.9 1.5 %fusion.19 = f32[5,16,128,16]{2,3,1,0:T(8,128)S(1)} fusion(f32[4,16,64,128]{3,2,1,0:T(8,128)S(1)} %get-tuple-element.31, f32[4,16,64,128]{3,2,1,0:T(8,128)S(1)} %get-tuple-element.30, f32[32,32]{1,0:T(8,128)S(1)} %get-tuple-element.40, f32[32,32]{1,0:T(8,128)S(1)} %get-tuple-element.41), kind=kOutput, calls=%fused_computation.19 | convolution fusion | flops 126485504 | bytes 4857856 | tf_op jit(solution)/shard_map/akpb,lp->akbl/dot_general | solution.py:72
  52.4 1.5 %fusion.18 = f32[5,16,128,16]{2,3,1,0:T(8,128)S(1)} fusion(f32[16,64,1,1]{1,0,3,2:T(8,128)S(1)} %fusion.25, f32[4,16,64,128]{3,2,1,0:T(8,128)S(1)} %get-tuple-element.31, f32[4,16,64,128]{3,2,1,0:T(8,128)S(1)} %get-tuple-element.30), kind=kOutput, calls=%fused_computation.18 | convolution fusion | flops 126484480 | bytes 4853760 | tf_op jit(solution)/shard_map/akpb,lp->akbl/dot_general | solution.py:73
  55.5 3.4 %collective-permute-start.2 = (f32[16,2064]{1,0:T(8,128)}, f32[16,2064]{1,0:T(8,128)}, u32[]{:S(2)}, u32[]{:S(2)}) collective-permute-start(f32[16,2064]{1,0:T(8,128)} %slice.74), channel_id=1, source_target_pairs={{0,64},{64,128},{128,192},{1,65},{65,129},{129,193},{2,66},{66,130... | collective-permute-start | bytes 396296 | tf_op jit(solution)/shard_map/ppermute | solution.py:18
  60.7 2.1 %copy.37 = f32[3,16,129,16]{3,2,1,0:T(8,128)S(1)} copy(f32[3,16,129,16]{2,3,1,0:T(8,128)} %pad_add_fusion.3) | data formatting | bytes 792576 | tf_op jit(solution)/shard_map/slice | solution.py:90
  62.8 1.6 %slice.76 = f32[48,2064]{1,0:T(8,128)} reshape(f32[3,16,129,16]{3,2,1,0:T(8,128)S(1)} %copy.37) | data formatting | bytes 792576 | tf_op jit(solution)/shard_map/slice | solution.py:90
  66.2 3.8 %collective-permute-start.3 = (f32[64,16]{1,0:T(8,128)S(1)}, f32[64,16]{1,0:T(8,128)S(1)}, u32[]{:S(2)}, u32[]{:S(2)}) collective-permute-start(f32[64,16]{1,0:T(8,128)S(1)} %pad_maximum_fusion.1), channel_id=1, source_target_pairs={{0,1},{1,2},{2,3},{3,4},{4,5},{5,6},{6,7},{7,8},{8,9},{9,10},{10,1... | collective-permute-start | bytes 12296 | tf_op jit(solution)/shard_map/ppermute | solution.py:18
  71.8 2.1 %multiply_reduce_fusion = (f32[]{:T(128)}, f32[]{:T(128)}, f32[]{:T(128)}, f32[]{:T(128)}, f32[64,2048]{1,0:T(8,128)S(1)}) fusion(f32[64,2048]{1,0:T(8,128)} %param.6, f32[64,2048]{1,0:T(8,128)} %param.7, f32[48,2064]{1,0:T(8,128)} %slice.76, f32[16,2064]{1,0:T(8,128)S(1)} %add.98, f32[64,16]{1,0:T(8,128)S(1)} %maximum_add_fusion), kind=kLoop, calls=%fused_computation.27 | loop fusion | flops 1966076 | bytes 2105360 | tf_op jit(solution)/shard_map/reduce_sum | solution.py:100
  73.9 7.4 %all-reduce.6 = (f32[]{:T(128)}, f32[]{:T(128)}, f32[]{:T(128)}, f32[]{:T(128)}) all-reduce(f32[]{:T(128)} %get-tuple-element.5, f32[]{:T(128)} %get-tuple-element.6, f32[]{:T(128)} %get-tuple-element.4, f32[]{:T(128)} %get-tuple-element.3), channel_id=1, replica_groups=mesh['row'=4,'col_0'=4,'col_1'=4,'col_2'=2,'col_3'=2] {'row'}, use_global_device_ids=true, to_apply=%region_1.2 | all-reduce | flops 4 | bytes 32 | tf_op jit(solution)/shard_map/psum | solution.py:23
  81.3 11.2 %all-reduce.5 = (f32[]{:T(128)}, f32[]{:T(128)}, f32[]{:T(128)}, f32[]{:T(128)}) all-reduce(f32[]{:T(128)} %get-tuple-element.15, f32[]{:T(128)} %get-tuple-element.16, f32[]{:T(128)} %get-tuple-element.17, f32[]{:T(128)} %get-tuple-element.18), channel_id=1, replica_groups=mesh['row'=4,'col_0'=4,'col_1'=4,'col_2'=2,'col_3'=2] {'col_0'}, use_global_device_ids=true, to_apply=%region_2.3 | all-reduce | flops 4 | bytes 32 | tf_op jit(solution)/shard_map/psum | solution.py:23
  92.6 8.9 %all-reduce.4 = (f32[]{:T(128)}, f32[]{:T(128)}, f32[]{:T(128)}, f32[]{:T(128)}) all-reduce(f32[]{:T(128)} %get-tuple-element.11, f32[]{:T(128)} %get-tuple-element.12, f32[]{:T(128)} %get-tuple-element.13, f32[]{:T(128)} %get-tuple-element.14), channel_id=1, replica_groups=mesh['row'=4,'col_0'=4,'col_1'=4,'col_2'=2,'col_3'=2] {'col_1'}, use_global_device_ids=true, to_apply=%region_3.4 | all-reduce | flops 4 | bytes 32 | tf_op jit(solution)/shard_map/psum | solution.py:23
  101.5 8.3 %all-reduce.8 = (f32[]{:T(128)}, f32[]{:T(128)}, f32[]{:T(128)}, f32[]{:T(128)}) all-reduce(f32[]{:T(128)} %get-tuple-element.7, f32[]{:T(128)} %get-tuple-element.8, f32[]{:T(128)} %get-tuple-element.9, f32[]{:T(128)} %get-tuple-element.10), channel_id=1, replica_groups=mesh['row'=4,'col_0'=4,'col_1'=4,'col_2'=2,'col_3'=2] {'col_2'}, use_global_device_ids=true, to_apply=%region_4.5 | all-reduce | flops 4 | bytes 32 | tf_op jit(solution)/shard_map/psum | solution.py:23
  109.8 17.1 %all-reduce.7 = (f32[]{:T(128)}, f32[]{:T(128)}, f32[]{:T(128)}, f32[]{:T(128)}) all-reduce(f32[]{:T(128)} %get-tuple-element.23, f32[]{:T(128)} %get-tuple-element.24, f32[]{:T(128)} %get-tuple-element.25, f32[]{:T(128)} %get-tuple-element.26), channel_id=1, replica_groups=mesh['row'=4,'col_0'=4,'col_1'=4,'col_2'=2,'col_3'=2] {'col_3'}, use_global_device_ids=true, to_apply=%region_5.6 | all-reduce | flops 4 | bytes 32 | tf_op jit(solution)/shard_map/psum | solution.py:23
  130.9 1.2 multiply_add_fusion
  (38 shorter events, 12.6 us)
Async XLA Ops:
  1.4 11.8 %collective-permute-start = (f32[64,16]{1,0:T(8,128)S(1)}, f32[64,16]{1,0:T(8,128)S(1)}, u32[]{:S(2)}, u32[]{:S(2)}) collective-permute-start(f32[64,16]{1,0:T(8,128)S(1)} %slice.62), channel_id=1, source_target_pairs={{1,0},{2,1},{3,2},{4,3},{5,4},{6,5},{7,6},{8,7},{9,8},{10,9},{11,1... | collective-permute-start | bytes 12296 | tf_op jit(solution)/shard_map/ppermute | solution.py:18
  13.2 5.8 %collective-permute-start.1 = (f32[16,2064]{1,0:T(8,128)S(1)}, f32[16,2064]{1,0:T(8,128)S(1)}, u32[]{:S(2)}, u32[]{:S(2)}) collective-permute-start(f32[16,2064]{1,0:T(8,128)S(1)} %slice.82), channel_id=1, source_target_pairs={{64,0},{128,64},{192,128},{65,1},{129,65},{193,129},{66,2},{130,66... | collective-permute-start | bytes 396296 | tf_op jit(solution)/shard_map/ppermute | solution.py:18
  22.3 8.1 %copy-start = (f32[5,16,129,16]{3,2,1,0:T(8,128)S(1)}, f32[5,16,129,16]{3,2,1,0:T(8,128)}, u32[]{:S(2)}) copy-start(f32[5,16,129,16]{3,2,1,0:T(8,128)} %reshape.132) | copy-start | bytes 1981444
  39.3 4.2 %copy-start.4 = (f32[4,128]{1,0:T(4,128)S(1)}, f32[4,128]{1,0:T(4,128)}, u32[]{:S(2)}) copy-start(f32[4,128]{1,0:T(4,128)} %param.8) | copy-start | bytes 6148
  55.5 8.9 %collective-permute-start.2 = (f32[16,2064]{1,0:T(8,128)}, f32[16,2064]{1,0:T(8,128)}, u32[]{:S(2)}, u32[]{:S(2)}) collective-permute-start(f32[16,2064]{1,0:T(8,128)} %slice.74), channel_id=1, source_target_pairs={{0,64},{64,128},{128,192},{1,65},{65,129},{129,193},{2,66},{66,130... | collective-permute-start | bytes 396296 | tf_op jit(solution)/shard_map/ppermute | solution.py:18
  64.4 66.4 %copy-start.1 = (f32[64,2048]{1,0:T(8,128)S(1)}, f32[64,2048]{1,0:T(8,128)}, u32[]{:S(2)}) copy-start(f32[64,2048]{1,0:T(8,128)} %param.7) | copy-start | bytes 1572868
  64.4 66.4 %copy-start.2 = (f32[64,2048]{1,0:T(8,128)S(1)}, f32[64,2048]{1,0:T(8,128)}, u32[]{:S(2)}) copy-start(f32[64,2048]{1,0:T(8,128)} %param.6) | copy-start | bytes 1572868
  64.4 66.5 %copy-start.3 = (f32[64,2048]{1,0:T(8,128)S(1)}, f32[64,2048]{1,0:T(8,128)}, u32[]{:S(2)}) copy-start(f32[64,2048]{1,0:T(8,128)} %param.5) | copy-start | bytes 1572868
  66.2 4.8 %collective-permute-start.3 = (f32[64,16]{1,0:T(8,128)S(1)}, f32[64,16]{1,0:T(8,128)S(1)}, u32[]{:S(2)}, u32[]{:S(2)}) collective-permute-start(f32[64,16]{1,0:T(8,128)S(1)} %pad_maximum_fusion.1), channel_id=1, source_target_pairs={{0,1},{1,2},{2,3},{3,4},{4,5},{5,6},{6,7},{7,8},{8,9},{9,10},{10,1... | collective-permute-start | bytes 12296 | tf_op jit(solution)/shard_map/ppermute | solution.py:18
where the time goes:
time: 133 us; the launch traced here: 132 us
  blocking collectives  52.9 us (40%)
  matrix products  25.5 us (19%)
  local copies, waits for them, and re-layouts  17 us (13%)
  starting transfers between devices  13.6 us (10%)
  waiting for transfers between devices  9.75 us (7%)
  other arithmetic  8.5 us (6%)
  between operations  4.85 us (4%)
    psum x5, blocking collectives, over_axes(): x = lax.psum(x, axis)  52.9 us
    ppermute x4, starting transfers between devices, passed_along(): lax.ppermute(value, axis, [(source, source + steps) for source in range(l...  13.6 us
    ppermute x4, waiting for transfers between devices, passed_along(): lax.ppermute(value, axis, [(source, source + steps) for source in range(l...  9.75 us
    dot_general x1, matrix products, analyze(): jnp.einsum('akbl,lp->akpb', blocks[:, :, 1:], column_table[16:], precisio...  8.08 us
    dot_general x1, matrix products, analyze(): jnp.einsum('akbl,lp->akpb', blocks[:, :, :win_cols], column_table[:16], p...  5.81 us
    dot_general x1, matrix products, synthesize(): jnp.einsum('tm,atvb->amvb', row_table, coefficients, precision=precise)  4.37 us
    dot_general x1, matrix products, analyze(): return jnp.einsum('tm,amvb->atvb', row_table, paired, precision=precise)  4.16 us
    slice x2, local copies, waits for them, and re-layouts, per_device(): spread[16:height]  3.69 us
  transfers between devices with their start and end apart: 4, of which 3 were waited for; matrix products, arithmetic and copies ran while one was open for 6% of the time, Pallas kernels for 0%

commit v1 on v0

--- a/solution.py
+++ b/solution.py
@@ -5,7 +5,16 @@
 from jax.sharding import PartitionSpec as P
 
 COL = ("col_0", "col_1", "col_2", "col_3")
-ROW_COL = ("row", "col_0", "col_1", "col_2", "col_3")
+DOUBLING = (
+    ("col_3", 1),
+    ("row", 1),
+    ("row", 2),
+    ("col_0", 1),
+    ("col_0", 2),
+    ("col_1", 1),
+    ("col_1", 2),
+    ("col_2", 1),
+)
 
 
 precise = lax.Precision.HIGHEST
@@ -18,9 +27,10 @@
     return lax.ppermute(value, axis, [(source, source + steps) for source in range(leading, last)])
 
 
-def over_axes(x, axes):
-    for axis in axes:
-        x = lax.psum(x, axis)
+def summed_everywhere(x, steps):
+    for axis, mask in steps:
+        count = lax.axis_size(axis)
+        x = x + lax.ppermute(x, axis, [(i, i ^ mask) for i in range(count)])
     return x
 
 
@@ -93,12 +103,18 @@
         [upper_rows[:, :16] + arrived_cols, upper_rows[:, 16:breadth]], axis=1
     )
     applied = synthesized + damping * direction
-    norm_now, curvature, cross_term, image_norm = (
-        over_axes(jnp.sum(residual * residual), ROW_COL),
-        over_axes(jnp.sum(direction * applied), ROW_COL),
-        over_axes(jnp.sum(residual * applied), ROW_COL),
-        over_axes(jnp.sum(applied * applied), ROW_COL),
+    sums = summed_everywhere(
+        jnp.stack(
+            [
+                jnp.sum(residual * residual),
+                jnp.sum(direction * applied),
+                jnp.sum(residual * applied),
+                jnp.sum(applied * applied),
+            ]
+        ),
+        DOUBLING,
     )
+    norm_now, curvature, cross_term, image_norm = sums[0], sums[1], sums[2], sums[3]
     step_length = norm_now / curvature
     new_iterate = iterate + step_length * direction
     new_residual = residual - step_length * applied

time: 133 us -> 132 us (level)
  the two profiles are of different devices: /device:TPU:1 before, /device:TPU:16 now
where the time goes in v1:
time: 132 us; the launch traced here: 131 us
  waiting for transfers between devices  47.4 us (36%)
  matrix products  25.5 us (19%)
  starting transfers between devices  19.4 us (15%)
  local copies, waits for them, and re-layouts  17.6 us (13%)
  other arithmetic  16.4 us (12%)
  between operations  4.79 us (4%)
    ppermute x8, waiting for transfers between devices, summed_everywhere(): x = x + lax.ppermute(x, axis, [(i, i ^ mask) for i in range(count)])  31.7 us
    ppermute x4, starting transfers between devices, passed_along(): lax.ppermute(value, axis, [(source, source + steps) for source in range(l...  17.4 us
    ppermute x4, waiting for transfers between devices, passed_along(): lax.ppermute(value, axis, [(source, source + steps) for source in range(l...  15.6 us
    dot_general x1, matrix products, analyze(): jnp.einsum('akbl,lp->akpb', blocks[:, :, 1:], column_table[16:], precisio...  8.09 us
    dot_general x1, matrix products, analyze(): jnp.einsum('akbl,lp->akpb', blocks[:, :, :win_cols], column_table[:16], p...  5.8 us
    add x8, other arithmetic, summed_everywhere(): x = x + lax.ppermute(x, axis, [(i, i ^ mask) for i in range(count)])  5.26 us
    dot_general x1, matrix products, synthesize(): jnp.einsum('tm,atvb->amvb', row_table, coefficients, precision=precise)  4.37 us
    dot_general x1, matrix products, analyze(): return jnp.einsum('tm,amvb->atvb', row_table, paired, precision=precise)  4.16 us
  transfers between devices with their start and end apart: 12, of which 10 were waited for; matrix products, arithmetic and copies ran while one was open for 6% of the time, Pallas kernels for 0%

profile of v1, /device:TPU:16, one launch (start us, length us, event | category | flops | bytes accessed | tf_op | source)
XLA Modules:
  0.0 131.1 jit_solution(15147711236376388880)
XLA Ops:
  1.4 10.6 %collective-permute-start = (f32[64,16]{1,0:T(8,128)S(1)}, f32[64,16]{1,0:T(8,128)S(1)}, u32[]{:S(2)}, u32[]{:S(2)}) collective-permute-start(f32[64,16]{1,0:T(8,128)S(1)} %slice.74), channel_id=1, source_target_pairs={{1,0},{2,1},{3,2},{4,3},{5,4},{6,5},{7,6},{8,7},{9,8},{10,9},{11,1... | collective-permute-start | bytes 12296 | tf_op jit(solution)/shard_map/ppermute | solution.py:27
  15.7 5.4 %collective-permute-done.1 = f32[16,2064]{1,0:T(8,128)S(1)} collective-permute-done((f32[16,2064]{1,0:T(8,128)S(1)}, f32[16,2064]{1,0:T(8,128)S(1)}, u32[]{:S(2)}, u32[]{:S(2)}) %collective-permute-start.1) | collective-permute-done | bytes 132128 | tf_op jit(solution)/shard_map/ppermute | solution.py:27
  21.2 3.3 %reshape.132 = f32[5,16,129,16]{3,2,1,0:T(8,128)} reshape(f32[80,2064]{1,0:T(8,128)S(1)} %pad_maximum_fusion) | data formatting | bytes 1320960 | tf_op jit(solution)/shard_map/reshape | solution.py:55
  24.5 8.1 %fusion = f32[64,5,16,128]{3,0,2,1:T(8,128)S(1)} fusion(f32[16,64,1,1]{1,0,3,2:T(8,128)S(1)} %fusion.25, f32[5,16,129,16]{3,2,1,0:T(8,128)} %reshape.132), kind=kOutput, calls=%fused_computation | convolution fusion | flops 125829120 | bytes 7868416 | tf_op jit(solution)/shard_map/akbl,lp->akpb/dot_general | solution.py:59
  32.6 5.8 %add_bitcast_fusion = f32[5,16,64,128]{3,2,1,0:T(8,128)S(1)} fusion(f32[64,5,16,128]{3,0,2,1:T(8,128)S(1)} %fusion, f32[5,16,129,16]{3,2,1,0:T(8,128)S(1)} %copy-done, f32[32,32]{1,0:T(8,128)S(1)} %get-tuple-element.24, f32[32,32]{1,0:T(8,128)S(1)} %get-tuple-element.25), kind=kOutput, calls=%fused_computation.12 | convolution fusion | flops 126485504 | bytes 10518528 | tf_op jit(solution)/shard_map/akbl,lp->akpb/dot_general | solution.py:56
  41.5 4.2 %fusion.4 = f32[4,32,128,64,1,1]{2,3,5,4,1,0:T(8,128)S(1)} fusion(f32[4,1,16,2,32,128]{5,2,3,1,4,0:T(8,128)S(1)} %copy.30, f32[4,1,16,2,32,128]{5,2,3,1,4,0:T(8,128)S(1)} %copy.29, f32[64,2,16,2]{0,2,3,1:T(8,128)S(1)} %maximum_maximum_fusion), kind=kOutput, calls=%fused_computation.4 | convolution fusion | flops 806354944 | bytes 8404992 | tf_op jit(solution)/shard_map/tm,amvb->atvb/dot_general | solution.py:66
  45.6 4.4 %fusion.11 = f32[4,64,32,128]{3,1,2,0:T(8,128)S(1)} fusion(f32[64,64,1,1]{0,1,3,2:T(8,128)S(1)} %bitcast.58, f32[4,32,128,64,1,1]{2,3,5,4,1,0:T(8,128)S(1)} %fusion.4, f32[4,128]{1,0:T(4,128)S(1)} %copy-done.4, f32[64,32]{0,1:T(8,128)S(1)} %copy.31), kind=kOutput, calls=%fused_computation.13 | convolution fusion | flops 807403520 | bytes 8415232 | tf_op jit(solution)/shard_map/tm,atvb->amvb/dot_general | solution.py:77
  50.0 2.4 %copy.33 = f32[4,64,32,128]{3,2,1,0:T(8,128)S(1)} copy(f32[4,64,32,128]{3,1,2,0:T(8,128)S(1)} %fusion.11) | data formatting | bytes 8388608 | tf_op jit(solution)/shard_map/tm,atvb->amvb/transpose | solution.py:77
  57.7 3.6 %collective-permute-start.2 = (f32[16,2064]{1,0:T(8,128)}, f32[16,2064]{1,0:T(8,128)}, u32[]{:S(2)}, u32[]{:S(2)}) collective-permute-start(f32[16,2064]{1,0:T(8,128)} %slice.86), channel_id=1, source_target_pairs={{0,64},{64,128},{128,192},{1,65},{65,129},{129,193},{2,66},{66,130... | collective-permute-start | bytes 396296 | tf_op jit(solution)/shard_map/ppermute | solution.py:27
  63.1 2.1 %copy.37 = f32[3,16,129,16]{3,2,1,0:T(8,128)S(1)} copy(f32[3,16,129,16]{2,3,1,0:T(8,128)} %pad_add_fusion.3) | data formatting | bytes 792576 | tf_op jit(solution)/shard_map/slice | solution.py:100
  65.2 1.6 %slice.88 = f32[48,2064]{1,0:T(8,128)} reshape(f32[3,16,129,16]{3,2,1,0:T(8,128)S(1)} %copy.37) | data formatting | bytes 792576 | tf_op jit(solution)/shard_map/slice | solution.py:100
  68.6 1.9 %collective-permute-start.3 = (f32[64,16]{1,0:T(8,128)S(1)}, f32[64,16]{1,0:T(8,128)S(1)}, u32[]{:S(2)}, u32[]{:S(2)}) collective-permute-start(f32[64,16]{1,0:T(8,128)S(1)} %pad_maximum_fusion.1), channel_id=1, source_target_pairs={{0,1},{1,2},{2,3},{3,4},{4,5},{5,6},{6,7},{7,8},{8,9},{9,10},{10,1... | collective-permute-start | bytes 12296 | tf_op jit(solution)/shard_map/ppermute | solution.py:27
  70.5 10.2 %collective-permute-done.3 = f32[64,16]{1,0:T(8,128)S(1)} collective-permute-done((f32[64,16]{1,0:T(8,128)S(1)}, f32[64,16]{1,0:T(8,128)S(1)}, u32[]{:S(2)}, u32[]{:S(2)}) %collective-permute-start.3) | collective-permute-done | bytes 4128 | tf_op jit(solution)/shard_map/ppermute | solution.py:27
  81.5 2.2 %multiply_reduce_fusion.3 = (f32[]{:T(128)}, f32[]{:T(128)}, f32[]{:T(128)}, f32[]{:T(128)}, f32[64,2048]{1,0:T(8,128)S(1)}) fusion(f32[64,2048]{1,0:T(8,128)} %param.6, f32[64,2048]{1,0:T(8,128)} %param.7, f32[48,2064]{1,0:T(8,128)} %slice.88, f32[16,2064]{1,0:T(8,128)S(1)} %add.82, f32[64,16]{1,0:T(8,128)S(1)} %maximum_add_fusion), kind=kLoop, calls=%fused_computation.32 | loop fusion | flops 1966076 | bytes 2105360 | tf_op jit(solution)/shard_map/reduce_sum | solution.py:109
  83.7 2.6 %pad_maximum_fusion.4 = f32[4]{0:T(128)S(1)} fusion(f32[1]{0:T(128)} %bitcast.23, f32[1]{0:T(128)} %bitcast.22, f32[1]{0:T(128)} %bitcast.21, f32[1]{0:T(128)} %bitcast), kind=kLoop, calls=%fused_computation.57 | loop fusion | flops 12 | bytes 32 | tf_op jit(solution)/shard_map/stack | solution.py:107
  87.4 2.6 %fusion.40 = f32[4]{0:T(128)S(1)} fusion(f32[4]{0:T(128)S(1)} %collective-permute-done.4, f32[1]{0:T(128)} %bitcast.23, f32[1]{0:T(128)} %bitcast.22, f32[1]{0:T(128)} %bitcast.21, f32[1]{0:T(128)} %bitcast), kind=kLoop, calls=%fused_computation.66 | loop fusion | flops 16 | bytes 48 | tf_op jit(solution)/shard_map/add | solution.py:33
  90.5 3.2 %collective-permute-done.5 = f32[4]{0:T(128)S(1)} collective-permute-done((f32[4]{0:T(128)S(1)}, f32[4]{0:T(128)S(1)}, u32[]{:S(2)}, u32[]{:S(2)}) %collective-permute-start.5) | collective-permute-done | bytes 48 | tf_op jit(solution)/shard_map/ppermute | solution.py:33
  93.6 2.6 %fusion.41 = f32[4]{0:T(128)S(1)} fusion(f32[4]{0:T(128)S(1)} %collective-permute-done.5, f32[4]{0:T(128)S(1)} %collective-permute-done.4, f32[1]{0:T(128)} %bitcast.23, f32[1]{0:T(128)} %bitcast.22, f32[1]{0:T(128)} %bitcast.21, f32[1]{0:T(128)} %bitcast), kind=kLoop, calls=%fused_computation.67 | loop fusion | flops 20 | bytes 64 | tf_op jit(solution)/shard_map/add | solution.py:33
  96.3 4.4 %collective-permute-done.6 = f32[4]{0:T(128)S(1)} collective-permute-done((f32[4]{0:T(128)S(1)}, f32[4]{0:T(128)S(1)}, u32[]{:S(2)}, u32[]{:S(2)}) %collective-permute-start.6) | collective-permute-done | bytes 48 | tf_op jit(solution)/shard_map/ppermute | solution.py:33
  102.3 2.0 %collective-permute-done.7 = f32[4]{0:T(128)S(1)} collective-permute-done((f32[4]{0:T(128)S(1)}, f32[4]{0:T(128)S(1)}, u32[]{:S(2)}, u32[]{:S(2)}) %collective-permute-start.7) | collective-permute-done | bytes 48 | tf_op jit(solution)/shard_map/ppermute | solution.py:33
  104.3 5.0 %collective-permute-done.8 = f32[4]{0:T(128)S(1)} collective-permute-done((f32[4]{0:T(128)S(1)}, f32[4]{0:T(128)S(1)}, u32[]{:S(2)}, u32[]{:S(2)}) %collective-permute-start.8) | collective-permute-done | bytes 48 | tf_op jit(solution)/shard_map/ppermute | solution.py:33
  109.3 3.5 %collective-permute-done.9 = f32[4]{0:T(128)S(1)} collective-permute-done((f32[4]{0:T(128)S(1)}, f32[4]{0:T(128)S(1)}, u32[]{:S(2)}, u32[]{:S(2)}) %collective-permute-start.9) | collective-permute-done | bytes 48 | tf_op jit(solution)/shard_map/ppermute | solution.py:33
  112.9 5.0 %collective-permute-done.10 = f32[4]{0:T(128)S(1)} collective-permute-done((f32[4]{0:T(128)S(1)}, f32[4]{0:T(128)S(1)}, u32[]{:S(2)}, u32[]{:S(2)}) %collective-permute-start.10) | collective-permute-done | bytes 48 | tf_op jit(solution)/shard_map/ppermute | solution.py:33
  117.9 7.4 %collective-permute-done.11 = f32[4]{0:T(128)S(1)} collective-permute-done((f32[4]{0:T(128)S(1)}, f32[4]{0:T(128)S(1)}, u32[]{:S(2)}, u32[]{:S(2)}) %collective-permute-start.11) | collective-permute-done | bytes 48 | tf_op jit(solution)/shard_map/ppermute | solution.py:33
  (59 shorter events, 22.2 us)
Async XLA Ops:
  1.4 12.8 %collective-permute-start = (f32[64,16]{1,0:T(8,128)S(1)}, f32[64,16]{1,0:T(8,128)S(1)}, u32[]{:S(2)}, u32[]{:S(2)}) collective-permute-start(f32[64,16]{1,0:T(8,128)S(1)} %slice.74), channel_id=1, source_target_pairs={{1,0},{2,1},{3,2},{4,3},{5,4},{6,5},{7,6},{8,7},{9,8},{10,9},{11,1... | collective-permute-start | bytes 12296 | tf_op jit(solution)/shard_map/ppermute | solution.py:27
  14.2 6.9 %collective-permute-start.1 = (f32[16,2064]{1,0:T(8,128)S(1)}, f32[16,2064]{1,0:T(8,128)S(1)}, u32[]{:S(2)}, u32[]{:S(2)}) collective-permute-start(f32[16,2064]{1,0:T(8,128)S(1)} %slice.98), channel_id=1, source_target_pairs={{64,0},{128,64},{192,128},{65,1},{129,65},{193,129},{66,2},{130,66... | collective-permute-start | bytes 396296 | tf_op jit(solution)/shard_map/ppermute | solution.py:27
  24.5 8.1 %copy-start = (f32[5,16,129,16]{3,2,1,0:T(8,128)S(1)}, f32[5,16,129,16]{3,2,1,0:T(8,128)}, u32[]{:S(2)}) copy-start(f32[5,16,129,16]{3,2,1,0:T(8,128)} %reshape.132) | copy-start | bytes 1981444
  41.5 4.2 %copy-start.4 = (f32[4,128]{1,0:T(4,128)S(1)}, f32[4,128]{1,0:T(4,128)}, u32[]{:S(2)}) copy-start(f32[4,128]{1,0:T(4,128)} %param.8) | copy-start | bytes 6148
  57.7 9.2 %collective-permute-start.2 = (f32[16,2064]{1,0:T(8,128)}, f32[16,2064]{1,0:T(8,128)}, u32[]{:S(2)}, u32[]{:S(2)}) collective-permute-start(f32[16,2064]{1,0:T(8,128)} %slice.86), channel_id=1, source_target_pairs={{0,64},{64,128},{128,192},{1,65},{65,129},{129,193},{2,66},{66,130... | collective-permute-start | bytes 396296 | tf_op jit(solution)/shard_map/ppermute | solution.py:27
  66.8 63.0 %copy-start.1 = (f32[64,2048]{1,0:T(8,128)S(1)}, f32[64,2048]{1,0:T(8,128)}, u32[]{:S(2)}) copy-start(f32[64,2048]{1,0:T(8,128)} %param.7) | copy-start | bytes 1572868
  66.8 63.1 %copy-start.2 = (f32[64,2048]{1,0:T(8,128)S(1)}, f32[64,2048]{1,0:T(8,128)}, u32[]{:S(2)}) copy-start(f32[64,2048]{1,0:T(8,128)} %param.6) | copy-start | bytes 1572868
  66.8 63.1 %copy-start.3 = (f32[64,2048]{1,0:T(8,128)S(1)}, f32[64,2048]{1,0:T(8,128)}, u32[]{:S(2)}) copy-start(f32[64,2048]{1,0:T(8,128)} %param.5) | copy-start | bytes 1572868
  68.6 12.1 %collective-permute-start.3 = (f32[64,16]{1,0:T(8,128)S(1)}, f32[64,16]{1,0:T(8,128)S(1)}, u32[]{:S(2)}, u32[]{:S(2)}) collective-permute-start(f32[64,16]{1,0:T(8,128)S(1)} %pad_maximum_fusion.1), channel_id=1, source_target_pairs={{0,1},{1,2},{2,3},{3,4},{4,5},{5,6},{6,7},{7,8},{8,9},{9,10},{10,1... | collective-permute-start | bytes 12296 | tf_op jit(solution)/shard_map/ppermute | solution.py:27
  86.3 1.1 collective-permute-start.4
  90.1 3.6 %collective-permute-start.5 = (f32[4]{0:T(128)S(1)}, f32[4]{0:T(128)S(1)}, u32[]{:S(2)}, u32[]{:S(2)}) collective-permute-start(f32[4]{0:T(128)S(1)} %fusion.40), channel_id=1, source_target_pairs={{0,64},{64,0},{128,192},{192,128},{1,65},{65,1},{129,193},{193,129... | collective-permute-start | bytes 56 | tf_op jit(solution)/shard_map/ppermute | solution.py:33
  96.2 4.5 %collective-permute-start.6 = (f32[4]{0:T(128)S(1)}, f32[4]{0:T(128)S(1)}, u32[]{:S(2)}, u32[]{:S(2)}) collective-permute-start(f32[4]{0:T(128)S(1)} %fusion.41), channel_id=1, source_target_pairs={{0,128},{64,192},{128,0},{192,64},{1,129},{65,193},{129,1},{193,65... | collective-permute-start | bytes 56 | tf_op jit(solution)/shard_map/ppermute | solution.py:33
  100.7 3.5 %collective-permute-start.7 = (f32[4]{0:T(128)S(1)}, f32[4]{0:T(128)S(1)}, u32[]{:S(2)}, u32[]{:S(2)}) collective-permute-start(f32[4]{0:T(128)S(1)} %add.87), channel_id=1, source_target_pairs={{0,16},{16,0},{32,48},{48,32},{1,17},{17,1},{33,49},{49,33},{2,18}... | collective-permute-start | bytes 56 | tf_op jit(solution)/shard_map/ppermute | solution.py:33
  104.3 5.0 %collective-permute-start.8 = (f32[4]{0:T(128)S(1)}, f32[4]{0:T(128)S(1)}, u32[]{:S(2)}, u32[]{:S(2)}) collective-permute-start(f32[4]{0:T(128)S(1)} %add.88), channel_id=1, source_target_pairs={{0,32},{16,48},{32,0},{48,16},{1,33},{17,49},{33,1},{49,17},{2,34}... | collective-permute-start | bytes 56 | tf_op jit(solution)/shard_map/ppermute | solution.py:33
  109.3 3.5 %collective-permute-start.9 = (f32[4]{0:T(128)S(1)}, f32[4]{0:T(128)S(1)}, u32[]{:S(2)}, u32[]{:S(2)}) collective-permute-start(f32[4]{0:T(128)S(1)} %add.89), channel_id=1, source_target_pairs={{0,4},{4,0},{8,12},{12,8},{1,5},{5,1},{9,13},{13,9},{2,6},{6,2},{1... | collective-permute-start | bytes 56 | tf_op jit(solution)/shard_map/ppermute | solution.py:33
  112.8 5.0 %collective-permute-start.10 = (f32[4]{0:T(128)S(1)}, f32[4]{0:T(128)S(1)}, u32[]{:S(2)}, u32[]{:S(2)}) collective-permute-start(f32[4]{0:T(128)S(1)} %add.90), channel_id=1, source_target_pairs={{0,8},{4,12},{8,0},{12,4},{1,9},{5,13},{9,1},{13,5},{2,10},{6,14},... | collective-permute-start | bytes 56 | tf_op jit(solution)/shard_map/ppermute | solution.py:33
  117.9 7.4 %collective-permute-start.11 = (f32[4]{0:T(128)S(1)}, f32[4]{0:T(128)S(1)}, u32[]{:S(2)}, u32[]{:S(2)}) collective-permute-start(f32[4]{0:T(128)S(1)} %add.91), channel_id=1, source_target_pairs={{0,2},{2,0},{1,3},{3,1},{4,6},{6,4},{5,7},{7,5},{8,10},{10,8},{9,1... | collective-permute-start | bytes 56 | tf_op jit(solution)/shard_map/ppermute | solution.py:33

commit v2 on v1

--- a/solution.py
+++ b/solution.py
@@ -25,6 +25,16 @@
     count = lax.axis_size(axis)
     leading, last = (max(0, -steps), min(count, count - steps))
     return lax.ppermute(value, axis, [(source, source + steps) for source in range(leading, last)])
+
+
+def passed_diagonally(value, steps):
+    rows, cols = lax.axis_size("row"), lax.axis_size(COL)
+    pairs = [
+        (r * cols + c, (r + steps) * cols + (c + steps))
+        for r in range(max(0, -steps), min(rows, rows - steps))
+        for c in range(max(0, -steps), min(cols, cols - steps))
+    ]
+    return lax.ppermute(value, ("row",) + COL, pairs)
 
 
 def summed_everywhere(x, steps):
@@ -91,29 +101,34 @@
     column_table, row_table = tables()
     height, breadth = direction.shape
     beside = passed_along(direction[:, :16], COL, -1)
-    widened = jnp.concatenate([direction, beside], axis=1)
-    below = passed_along(widened[:16], "row", -1)
-    region = jnp.concatenate([widened, below], axis=0)
+    below = passed_along(direction[:16], "row", -1)
+    corner = passed_diagonally(direction[:16, :16], -1)
+    region = jnp.concatenate(
+        [
+            jnp.concatenate([direction, beside], axis=1),
+            jnp.concatenate([below, corner], axis=1),
+        ],
+        axis=0,
+    )
     coefficients = weigh(analyze(region, column_table, row_table), window_weight, freq_weight)
     spread = synthesize(coefficients, column_table, row_table)
-    arrived_rows = passed_along(spread[height:], "row", 1)
-    upper_rows = jnp.concatenate([spread[:16] + arrived_rows, spread[16:height]], axis=0)
-    arrived_cols = passed_along(upper_rows[:, breadth:], COL, 1)
-    synthesized = jnp.concatenate(
-        [upper_rows[:, :16] + arrived_cols, upper_rows[:, 16:breadth]], axis=1
+    arrived_rows = passed_along(spread[height:, :breadth], "row", 1)
+    arrived_cols = passed_along(spread[:height, breadth:], COL, 1)
+    arrived_corner = passed_diagonally(spread[height:, breadth:], 1)
+    synthesized = (
+        spread[:height, :breadth]
+        + jnp.pad(arrived_rows, ((0, height - 16), (0, 0)))
+        + jnp.pad(
+            arrived_cols
+            + jnp.pad(arrived_corner, ((0, height - 16), (0, 0))),
+            ((0, 0), (0, breadth - 16)),
+        )
     )
     applied = synthesized + damping * direction
-    sums = summed_everywhere(
-        jnp.stack(
-            [
-                jnp.sum(residual * residual),
-                jnp.sum(direction * applied),
-                jnp.sum(residual * applied),
-                jnp.sum(applied * applied),
-            ]
-        ),
-        DOUBLING,
+    products = jnp.stack(
+        [residual * residual, direction * applied, residual * applied, applied * applied]
     )
+    sums = summed_everywhere(jnp.sum(products, axis=(1, 2)), DOUBLING)
     norm_now, curvature, cross_term, image_norm = sums[0], sums[1], sums[2], sums[3]
     step_length = norm_now / curvature
     new_iterate = iterate + step_length * direction

time: 132 us -> 120 us (0.909)
  waiting for transfers between devices: 47.4 us -> 25 us
  starting transfers between devices: 19.4 us -> 37.9 us
  other arithmetic: 16.4 us -> 4.53 us
  local copies, waits for them, and re-layouts: 17.6 us -> 20.1 us
    ppermute x8, starting transfers between devices: 2.05 us -> 16.5 us  [summed_everywhere(): x = x + lax.ppermute(x, axis, [(i, i ^ mask) for i in range(count)])]
    ppermute x8, waiting for transfers between devices: 31.7 us -> 18.7 us  [summed_everywhere(): x = x + lax.ppermute(x, axis, [(i, i ^ mask) for i in range(count)])]
    ppermute x4, waiting for transfers between devices: 15.6 us -> 3.96 us  [passed_along(): lax.ppermute(value, axis, [(source, source + steps) for source in range(l...]
    add x8, other arithmetic: 5.26 us -> 0.03 us  [summed_everywhere(): x = x + lax.ppermute(x, axis, [(i, i ^ mask) for i in range(count)])]
    slice x7 -> x5, local copies, waits for them, and re-layouts: 5.74 us -> 1.64 us  [the longest x1 0.92 us: per_device(): below = passed_along(direction[:16], 'row', -1)]
    ppermute x0 -> x2, starting transfers between devices: none -> 4.03 us  [passed_diagonally(): return lax.ppermute(value, ('row',) + COL, pairs)]
    add x0 -> x1, local copies, waits for them, and re-layouts: none -> 3.89 us  [synthesize(): jnp.pad(lower_piece, ((0, 0), (0, 0), (0, 1), (0, 0)))]
    reshape x0 -> x1, local copies, waits for them, and re-layouts: none -> 3.88 us  [synthesize(): return blocks.reshape(16 * (win_rows + 1), 16 * (win_cols + 1))]
  transfers between devices with their start and end apart: 12 -> 14, of which waited for: 10 -> 10; matrix products, arithmetic and copies ran while one was open for 6% -> 2% of each run, Pallas kernels for 0% -> 0%
where the time goes in v2:
time: 120 us; the launch traced here: 118 us
  starting transfers between devices  37.9 us (32%)
  matrix products  25.9 us (22%)
  waiting for transfers between devices  25 us (21%)
  local copies, waits for them, and re-layouts  20.1 us (17%)
  between operations  5.02 us (4%)
  other arithmetic  4.53 us (4%)
    ppermute x8, waiting for transfers between devices, summed_everywhere(): x = x + lax.ppermute(x, axis, [(i, i ^ mask) for i in range(count)])  18.7 us
    ppermute x4, starting transfers between devices, passed_along(): lax.ppermute(value, axis, [(source, source + steps) for source in range(l...  17.4 us
    ppermute x8, starting transfers between devices, summed_everywhere(): x = x + lax.ppermute(x, axis, [(i, i ^ mask) for i in range(count)])  16.5 us
    dot_general x1, matrix products, analyze(): jnp.einsum('akbl,lp->akpb', blocks[:, :, 1:], column_table[16:], precisio...  8.11 us
    dot_general x1, matrix products, analyze(): jnp.einsum('akbl,lp->akpb', blocks[:, :, :win_cols], column_table[:16], p...  5.88 us
    dot_general x1, matrix products, synthesize(): jnp.einsum('tm,atvb->amvb', row_table, coefficients, precision=precise)  4.64 us
    dot_general x1, matrix products, analyze(): return jnp.einsum('tm,amvb->atvb', row_table, paired, precision=precise)  4.2 us
    ppermute x2, starting transfers between devices, passed_diagonally(): return lax.ppermute(value, ('row',) + COL, pairs)  4.03 us
  transfers between devices with their start and end apart: 14, of which 10 were waited for; matrix products, arithmetic and copies ran while one was open for 2% of the time, Pallas kernels for 0%

profile of v2, /device:TPU:16, one launch (start us, length us, event | category | flops | bytes accessed | tf_op | source)
XLA Modules:
  0.0 118.5 jit_solution(3305084950814725735)
XLA Ops:
  3.6 10.6 %collective-permute-start = (f32[64,16]{1,0:T(8,128)S(1)}, f32[64,16]{1,0:T(8,128)S(1)}, u32[]{:S(2)}, u32[]{:S(2)}) collective-permute-start(f32[64,16]{1,0:T(8,128)S(1)} %slice.62), channel_id=1, source_target_pairs={{1,0},{2,1},{3,2},{4,3},{5,4},{6,5},{7,6},{8,7},{9,8},{10,9},{11,1... | collective-permute-start | bytes 12296 | tf_op jit(solution)/shard_map/ppermute | solution.py:27
  17.5 2.4 %collective-permute-done.2 = f32[16,16]{1,0:T(8,128)S(1)} collective-permute-done((f32[16,16]{1,0:T(8,128)S(1)}, f32[16,16]{1,0:T(8,128)S(1)}, u32[]{:S(2)}, u32[]{:S(2)}) %collective-permute-start.2) | collective-permute-done | bytes 1056 | tf_op jit(solution)/shard_map/ppermute | solution.py:37
  21.0 3.3 %reshape.131 = f32[5,16,129,16]{3,2,1,0:T(8,128)} reshape(f32[80,2064]{1,0:T(8,128)S(1)} %maximum_maximum_fusion) | data formatting | bytes 1320960 | tf_op jit(solution)/shard_map/reshape | solution.py:65
  24.3 8.1 %fusion = f32[64,5,16,128]{3,0,2,1:T(8,128)S(1)} fusion(f32[16,64,1,1]{1,0,3,2:T(8,128)S(1)} %fusion.25, f32[5,16,129,16]{3,2,1,0:T(8,128)} %reshape.131), kind=kOutput, calls=%fused_computation | convolution fusion | flops 125829120 | bytes 7868416 | tf_op jit(solution)/shard_map/akbl,lp->akpb/dot_general | solution.py:69
  32.4 5.9 %add_bitcast_fusion = f32[5,16,64,128]{3,2,1,0:T(8,128)S(1)} fusion(f32[64,5,16,128]{3,0,2,1:T(8,128)S(1)} %fusion, f32[5,16,129,16]{3,2,1,0:T(8,128)S(1)} %copy-done, f32[32,32]{1,0:T(8,128)S(1)} %get-tuple-element.22, f32[32,32]{1,0:T(8,128)S(1)} %get-tuple-element.23), kind=kOutput, calls=%fused_computation.12 | convolution fusion | flops 126485504 | bytes 10518528 | tf_op jit(solution)/shard_map/akbl,lp->akpb/dot_general | solution.py:66
  41.4 4.2 %fusion.4 = f32[4,32,128,64,1,1]{2,3,5,4,1,0:T(8,128)S(1)} fusion(f32[4,1,16,2,32,128]{5,2,3,1,4,0:T(8,128)S(1)} %copy.26, f32[4,1,16,2,32,128]{5,2,3,1,4,0:T(8,128)S(1)} %copy.25, f32[64,2,16,2]{0,2,3,1:T(8,128)S(1)} %maximum_maximum_fusion.1), kind=kOutput, calls=%fused_computation.4 | convolution fusion | flops 806354944 | bytes 8404992 | tf_op jit(solution)/shard_map/tm,amvb->atvb/dot_general | solution.py:76
  45.6 4.6 %fusion.11 = f32[4,64,32,128]{3,1,2,0:T(8,128)S(1)} fusion(f32[64,64,1,1]{0,1,3,2:T(8,128)S(1)} %bitcast.62, f32[4,32,128,64,1,1]{2,3,5,4,1,0:T(8,128)S(1)} %fusion.4, f32[4,128]{1,0:T(4,128)S(1)} %copy-done.4, f32[64,32]{0,1:T(8,128)S(1)} %copy.27), kind=kOutput, calls=%fused_computation.13 | convolution fusion | flops 807403520 | bytes 8415232 | tf_op jit(solution)/shard_map/tm,atvb->amvb/dot_general | solution.py:87
  50.2 2.4 %copy.29 = f32[4,64,32,128]{3,2,1,0:T(8,128)S(1)} copy(f32[4,64,32,128]{3,1,2,0:T(8,128)S(1)} %fusion.11) | data formatting | bytes 8388608 | tf_op jit(solution)/shard_map/tm,atvb->amvb/transpose | solution.py:87
  56.7 3.9 %copy.31 = f32[5,16,129,16]{3,2,1,0:T(8,128)} copy(f32[5,16,129,16]{2,3,1,0:T(8,128)S(1)} %pad_add_fusion.3) | data formatting | bytes 1320960 | tf_op jit(solution)/shard_map/add | solution.py:94
  60.5 3.9 %reshape.134 = f32[80,2064]{1,0:T(8,128)S(1)} reshape(f32[5,16,129,16]{3,2,1,0:T(8,128)} %copy.31) | data formatting | bytes 1320960 | tf_op jit(solution)/shard_map/reshape | solution.py:97
  64.5 2.1 %collective-permute-start.4 = (f32[64,16]{1,0:T(8,128)S(1)}, f32[64,16]{1,0:T(8,128)S(1)}, u32[]{:S(2)}, u32[]{:S(2)}) collective-permute-start(f32[64,16]{1,0:T(8,128)S(1)} %slice.90), channel_id=1, source_target_pairs={{0,1},{1,2},{2,3},{3,4},{4,5},{5,6},{6,7},{7,8},{8,9},{9,10},{10,1... | collective-permute-start | bytes 12296 | tf_op jit(solution)/shard_map/ppermute | solution.py:27
  66.5 2.7 %collective-permute-start.5 = (f32[16,16]{1,0:T(8,128)S(1)}, f32[16,16]{1,0:T(8,128)S(1)}, u32[]{:S(2)}, u32[]{:S(2)}) collective-permute-start(f32[16,16]{1,0:T(8,128)S(1)} %slice.91), channel_id=1, source_target_pairs={{0,65},{1,66},{2,67},{3,68},{4,69},{5,70},{6,71},{7,72},{8,73},{9,... | collective-permute-start | bytes 3080 | tf_op jit(solution)/shard_map/ppermute | solution.py:37
  69.3 3.5 %collective-permute-start.3 = (f32[16,2048]{1,0:T(8,128)S(1)}, f32[16,2048]{1,0:T(8,128)S(1)}, u32[]{:S(2)}, u32[]{:S(2)}) collective-permute-start(f32[16,2048]{1,0:T(8,128)S(1)} %slice.89), channel_id=1, source_target_pairs={{0,64},{64,128},{128,192},{1,65},{65,129},{129,193},{2,66},{66,130... | collective-permute-start | bytes 393224 | tf_op jit(solution)/shard_map/ppermute | solution.py:27
  72.8 4.0 %collective-permute-done.4 = f32[64,16]{1,0:T(8,128)S(1)} collective-permute-done((f32[64,16]{1,0:T(8,128)S(1)}, f32[64,16]{1,0:T(8,128)S(1)}, u32[]{:S(2)}, u32[]{:S(2)}) %collective-permute-start.4) | collective-permute-done | bytes 4128 | tf_op jit(solution)/shard_map/ppermute | solution.py:27
  78.9 3.0 %collective-permute-start.7 = (f32[4]{0:T(128)S(1)}, f32[4]{0:T(128)S(1)}, u32[]{:S(2)}, u32[]{:S(2)}) collective-permute-start(f32[4]{0:T(128)S(1)} %add.95), channel_id=1, source_target_pairs={{0,64},{64,0},{128,192},{192,128},{1,65},{65,1},{129,193},{193,129... | collective-permute-start | bytes 56 | tf_op jit(solution)/shard_map/ppermute | solution.py:43
  83.4 2.9 %collective-permute-start.8 = (f32[4]{0:T(128)S(1)}, f32[4]{0:T(128)S(1)}, u32[]{:S(2)}, u32[]{:S(2)}) collective-permute-start(f32[4]{0:T(128)S(1)} %add.96), channel_id=1, source_target_pairs={{0,128},{64,192},{128,0},{192,64},{1,129},{65,193},{129,1},{193,65... | collective-permute-start | bytes 56 | tf_op jit(solution)/shard_map/ppermute | solution.py:43
  87.9 1.6 %collective-permute-start.9 = (f32[4]{0:T(128)S(1)}, f32[4]{0:T(128)S(1)}, u32[]{:S(2)}, u32[]{:S(2)}) collective-permute-start(f32[4]{0:T(128)S(1)} %add.97), channel_id=1, source_target_pairs={{0,16},{16,0},{32,48},{48,32},{1,17},{17,1},{33,49},{49,33},{2,18}... | collective-permute-start | bytes 56 | tf_op jit(solution)/shard_map/ppermute | solution.py:43
  89.5 1.9 %collective-permute-done.9 = f32[4]{0:T(128)S(1)} collective-permute-done((f32[4]{0:T(128)S(1)}, f32[4]{0:T(128)S(1)}, u32[]{:S(2)}, u32[]{:S(2)}) %collective-permute-start.9) | collective-permute-done | bytes 48 | tf_op jit(solution)/shard_map/ppermute | solution.py:43
  91.4 5.0 %collective-permute-done.10 = f32[4]{0:T(128)S(1)} collective-permute-done((f32[4]{0:T(128)S(1)}, f32[4]{0:T(128)S(1)}, u32[]{:S(2)}, u32[]{:S(2)}) %collective-permute-start.10) | collective-permute-done | bytes 48 | tf_op jit(solution)/shard_map/ppermute | solution.py:43
  97.1 2.9 %collective-permute-done.11 = f32[4]{0:T(128)S(1)} collective-permute-done((f32[4]{0:T(128)S(1)}, f32[4]{0:T(128)S(1)}, u32[]{:S(2)}, u32[]{:S(2)}) %collective-permute-start.11) | collective-permute-done | bytes 48 | tf_op jit(solution)/shard_map/ppermute | solution.py:43
  100.0 3.5 %collective-permute-start.12 = (f32[4]{0:T(128)S(1)}, f32[4]{0:T(128)S(1)}, u32[]{:S(2)}, u32[]{:S(2)}) collective-permute-start(f32[4]{0:T(128)S(1)} %add.100), channel_id=1, source_target_pairs={{0,8},{4,12},{8,0},{12,4},{1,9},{5,13},{9,1},{13,5},{2,10},{6,14},... | collective-permute-start | bytes 56 | tf_op jit(solution)/shard_map/ppermute | solution.py:43
  103.5 1.6 %collective-permute-done.12 = f32[4]{0:T(128)S(1)} collective-permute-done((f32[4]{0:T(128)S(1)}, f32[4]{0:T(128)S(1)}, u32[]{:S(2)}, u32[]{:S(2)}) %collective-permute-start.12) | collective-permute-done | bytes 48 | tf_op jit(solution)/shard_map/ppermute | solution.py:43
  105.1 4.0 %collective-permute-start.13 = (f32[4]{0:T(128)S(1)}, f32[4]{0:T(128)S(1)}, u32[]{:S(2)}, u32[]{:S(2)}) collective-permute-start(f32[4]{0:T(128)S(1)} %add.101), channel_id=1, source_target_pairs={{0,2},{2,0},{1,3},{3,1},{4,6},{6,4},{5,7},{7,5},{8,10},{10,8},{9,1... | collective-permute-start | bytes 56 | tf_op jit(solution)/shard_map/ppermute | solution.py:43
  109.1 3.4 %collective-permute-done.13 = f32[4]{0:T(128)S(1)} collective-permute-done((f32[4]{0:T(128)S(1)}, f32[4]{0:T(128)S(1)}, u32[]{:S(2)}, u32[]{:S(2)}) %collective-permute-start.13) | collective-permute-done | bytes 48 | tf_op jit(solution)/shard_map/ppermute | solution.py:43
  (59 shorter events, 22.1 us)
Async XLA Ops:
  1.5 18.3 %collective-permute-start.1 = (f32[16,2048]{1,0:T(8,128)S(1)}, f32[16,2048]{1,0:T(8,128)S(1)}, u32[]{:S(2)}, u32[]{:S(2)}) collective-permute-start(f32[16,2048]{1,0:T(8,128)S(1)} %slice.63), channel_id=1, source_target_pairs={{64,0},{128,64},{192,128},{65,1},{129,65},{193,129},{66,2},{130,66... | collective-permute-start | bytes 393224 | tf_op jit(solution)/shard_map/ppermute | solution.py:27
  3.6 16.3 %collective-permute-start = (f32[64,16]{1,0:T(8,128)S(1)}, f32[64,16]{1,0:T(8,128)S(1)}, u32[]{:S(2)}, u32[]{:S(2)}) collective-permute-start(f32[64,16]{1,0:T(8,128)S(1)} %slice.62), channel_id=1, source_target_pairs={{1,0},{2,1},{3,2},{4,3},{5,4},{6,5},{7,6},{8,7},{9,8},{10,9},{11,1... | collective-permute-start | bytes 12296 | tf_op jit(solution)/shard_map/ppermute | solution.py:27
  14.9 5.0 %collective-permute-start.2 = (f32[16,16]{1,0:T(8,128)S(1)}, f32[16,16]{1,0:T(8,128)S(1)}, u32[]{:S(2)}, u32[]{:S(2)}) collective-permute-start(f32[16,16]{1,0:T(8,128)S(1)} %slice.64), channel_id=1, source_target_pairs={{65,0},{66,1},{67,2},{68,3},{69,4},{70,5},{71,6},{72,7},{73,8},{74... | collective-permute-start | bytes 3080 | tf_op jit(solution)/shard_map/ppermute | solution.py:37
  24.3 8.1 %copy-start = (f32[5,16,129,16]{3,2,1,0:T(8,128)S(1)}, f32[5,16,129,16]{3,2,1,0:T(8,128)}, u32[]{:S(2)}) copy-start(f32[5,16,129,16]{3,2,1,0:T(8,128)} %reshape.131) | copy-start | bytes 1981444
  41.4 4.2 %copy-start.4 = (f32[4,128]{1,0:T(4,128)S(1)}, f32[4,128]{1,0:T(4,128)}, u32[]{:S(2)}) copy-start(f32[4,128]{1,0:T(4,128)} %param.8) | copy-start | bytes 6148
  60.5 16.2 %copy-start.1 = (f32[64,2048]{1,0:T(8,128)S(1)}, f32[64,2048]{1,0:T(8,128)}, u32[]{:S(2)}) copy-start(f32[64,2048]{1,0:T(8,128)} %param.7) | copy-start | bytes 1572868
  64.4 12.5 %copy-start.2 = (f32[64,2048]{1,0:T(8,128)S(1)}, f32[64,2048]{1,0:T(8,128)}, u32[]{:S(2)}) copy-start(f32[64,2048]{1,0:T(8,128)} %param.6) | copy-start | bytes 1572868
  64.5 12.3 %collective-permute-start.4 = (f32[64,16]{1,0:T(8,128)S(1)}, f32[64,16]{1,0:T(8,128)S(1)}, u32[]{:S(2)}, u32[]{:S(2)}) collective-permute-start(f32[64,16]{1,0:T(8,128)S(1)} %slice.90), channel_id=1, source_target_pairs={{0,1},{1,2},{2,3},{3,4},{4,5},{5,6},{6,7},{7,8},{8,9},{9,10},{10,1... | collective-permute-start | bytes 12296 | tf_op jit(solution)/shard_map/ppermute | solution.py:27
  66.5 6.3 %collective-permute-start.5 = (f32[16,16]{1,0:T(8,128)S(1)}, f32[16,16]{1,0:T(8,128)S(1)}, u32[]{:S(2)}, u32[]{:S(2)}) collective-permute-start(f32[16,16]{1,0:T(8,128)S(1)} %slice.91), channel_id=1, source_target_pairs={{0,65},{1,66},{2,67},{3,68},{4,69},{5,70},{6,71},{7,72},{8,73},{9,... | collective-permute-start | bytes 3080 | tf_op jit(solution)/shard_map/ppermute | solution.py:37
  69.3 7.4 %collective-permute-start.3 = (f32[16,2048]{1,0:T(8,128)S(1)}, f32[16,2048]{1,0:T(8,128)S(1)}, u32[]{:S(2)}, u32[]{:S(2)}) collective-permute-start(f32[16,2048]{1,0:T(8,128)S(1)} %slice.89), channel_id=1, source_target_pairs={{0,64},{64,128},{128,192},{1,65},{65,129},{129,193},{2,66},{66,130... | collective-permute-start | bytes 393224 | tf_op jit(solution)/shard_map/ppermute | solution.py:27
  76.9 40.3 %copy-start.3 = (f32[64,2048]{1,0:T(8,128)S(1)}, f32[64,2048]{1,0:T(8,128)}, u32[]{:S(2)}) copy-start(f32[64,2048]{1,0:T(8,128)} %param.5) | copy-start | bytes 1572868
  77.3 1.6 %collective-permute-start.6 = (f32[4]{0:T(128)S(1)}, f32[4]{0:T(128)S(1)}, u32[]{:S(2)}, u32[]{:S(2)}) collective-permute-start(f32[4]{0:T(128)S(1)} %maximum_reduce_fusion), channel_id=1, source_target_pairs={{0,1},{1,0},{2,3},{3,2},{4,5},{5,4},{6,7},{7,6},{8,9},{9,8},{10,11... | collective-permute-start | bytes 56 | tf_op jit(solution)/shard_map/ppermute | solution.py:43
  78.9 4.5 %collective-permute-start.7 = (f32[4]{0:T(128)S(1)}, f32[4]{0:T(128)S(1)}, u32[]{:S(2)}, u32[]{:S(2)}) collective-permute-start(f32[4]{0:T(128)S(1)} %add.95), channel_id=1, source_target_pairs={{0,64},{64,0},{128,192},{192,128},{1,65},{65,1},{129,193},{193,129... | collective-permute-start | bytes 56 | tf_op jit(solution)/shard_map/ppermute | solution.py:43
  83.4 4.4 %collective-permute-start.8 = (f32[4]{0:T(128)S(1)}, f32[4]{0:T(128)S(1)}, u32[]{:S(2)}, u32[]{:S(2)}) collective-permute-start(f32[4]{0:T(128)S(1)} %add.96), channel_id=1, source_target_pairs={{0,128},{64,192},{128,0},{192,64},{1,129},{65,193},{129,1},{193,65... | collective-permute-start | bytes 56 | tf_op jit(solution)/shard_map/ppermute | solution.py:43
  87.9 3.5 %collective-permute-start.9 = (f32[4]{0:T(128)S(1)}, f32[4]{0:T(128)S(1)}, u32[]{:S(2)}, u32[]{:S(2)}) collective-permute-start(f32[4]{0:T(128)S(1)} %add.97), channel_id=1, source_target_pairs={{0,16},{16,0},{32,48},{48,32},{1,17},{17,1},{33,49},{49,33},{2,18}... | collective-permute-start | bytes 56 | tf_op jit(solution)/shard_map/ppermute | solution.py:43
  91.4 5.0 %collective-permute-start.10 = (f32[4]{0:T(128)S(1)}, f32[4]{0:T(128)S(1)}, u32[]{:S(2)}, u32[]{:S(2)}) collective-permute-start(f32[4]{0:T(128)S(1)} %add.98), channel_id=1, source_target_pairs={{0,32},{16,48},{32,0},{48,16},{1,33},{17,49},{33,1},{49,17},{2,34}... | collective-permute-start | bytes 56 | tf_op jit(solution)/shard_map/ppermute | solution.py:43
  96.5 3.5 %collective-permute-start.11 = (f32[4]{0:T(128)S(1)}, f32[4]{0:T(128)S(1)}, u32[]{:S(2)}, u32[]{:S(2)}) collective-permute-start(f32[4]{0:T(128)S(1)} %add.99), channel_id=1, source_target_pairs={{0,4},{4,0},{8,12},{12,8},{1,5},{5,1},{9,13},{13,9},{2,6},{6,2},{1... | collective-permute-start | bytes 56 | tf_op jit(solution)/shard_map/ppermute | solution.py:43
  100.0 5.0 %collective-permute-start.12 = (f32[4]{0:T(128)S(1)}, f32[4]{0:T(128)S(1)}, u32[]{:S(2)}, u32[]{:S(2)}) collective-permute-start(f32[4]{0:T(128)S(1)} %add.100), channel_id=1, source_target_pairs={{0,8},{4,12},{8,0},{12,4},{1,9},{5,13},{9,1},{13,5},{2,10},{6,14},... | collective-permute-start | bytes 56 | tf_op jit(solution)/shard_map/ppermute | solution.py:43
  105.1 7.4 %collective-permute-start.13 = (f32[4]{0:T(128)S(1)}, f32[4]{0:T(128)S(1)}, u32[]{:S(2)}, u32[]{:S(2)}) collective-permute-start(f32[4]{0:T(128)S(1)} %add.101), channel_id=1, source_target_pairs={{0,2},{2,0},{1,3},{3,1},{4,6},{6,4},{5,7},{7,5},{8,10},{10,8},{9,1... | collective-permute-start | bytes 56 | tf_op jit(solution)/shard_map/ppermute | solution.py:43

commit v3 on v2

--- a/solution.py
+++ b/solution.py
@@ -3,6 +3,8 @@
 from jax import lax
 from jax.sharding import Mesh
 from jax.sharding import PartitionSpec as P
+from jax.experimental import pallas as pl
+from jax.experimental.pallas import tpu as pltpu
 
 COL = ("col_0", "col_1", "col_2", "col_3")
 DOUBLING = (
@@ -97,6 +99,101 @@
     return blocks.reshape(16 * (win_rows + 1), 16 * (win_cols + 1))
 
 
+LANES = 128
+WINDOWS_PER_TILE = LANES // 16
+HALF = WINDOWS_PER_TILE * 32
+
+
+def transform_tables(column_table, row_table):
+    first = column_table[:16].reshape(16, 2, 32)
+    second = column_table[16:].reshape(16, 2, 32)
+    same = jnp.eye(2 * WINDOWS_PER_TILE, WINDOWS_PER_TILE, dtype=jnp.float32)
+    shifted = jnp.eye(2 * WINDOWS_PER_TILE, WINDOWS_PER_TILE, k=-1, dtype=jnp.float32)
+    columns = jnp.einsum("Kk,lcw->Klckw", same, first) + jnp.einsum(
+        "Kk,lcw->Klckw", shifted, second
+    )
+    columns = columns.reshape(2 * LANES, 2 * HALF)
+    real = row_table[:32].reshape(32, 2, 16, 2)[..., 0].reshape(32, 32)
+    imag = row_table[32:].reshape(32, 2, 16, 2)[..., 0].reshape(32, 32)
+    forward = jnp.concatenate([real, imag], axis=1)
+    backward = jnp.concatenate([real.T, imag.T], axis=1)
+    return columns, columns.T, forward, backward
+
+
+def transform_kernel(x_ref, m_ref, n_ref, f_ref, g_ref, fw_ref, ww_ref, out_ref):
+    rows = x_ref.shape[0]
+    win_rows = rows // 16 - 1
+    tiles = (x_ref.shape[1] - LANES) // LANES
+    out_ref[...] = jnp.zeros_like(out_ref)
+    forward = f_ref[...]
+    backward = g_ref[...]
+    freq = fw_ref[...]
+
+    def one_tile(t, carry):
+        start = pl.multiple_of(t * LANES, LANES)
+        y = jnp.dot(
+            x_ref[:, pl.ds(start, 2 * LANES)],
+            m_ref[...],
+            precision=lax.Precision.HIGHEST,
+            preferred_element_type=jnp.float32,
+        )
+        weights = ww_ref[:, pl.ds(pl.multiple_of(t * 2 * HALF, 2 * HALF), 2 * HALF)]
+        pieces = []
+        for a in range(win_rows):
+            ya = y[16 * a : 16 * a + 32]
+            turned = jnp.concatenate([-ya[:, HALF:], ya[:, :HALF]], axis=1)
+            z = jnp.dot(
+                forward,
+                jnp.concatenate([ya, turned], axis=0),
+                precision=lax.Precision.HIGHEST,
+                preferred_element_type=jnp.float32,
+            )
+            z = z * freq * weights[a : a + 1]
+            turned = jnp.concatenate([z[:, HALF:], -z[:, :HALF]], axis=1)
+            pieces.append(
+                jnp.dot(
+                    backward,
+                    jnp.concatenate([z, turned], axis=0),
+                    precision=lax.Precision.HIGHEST,
+                    preferred_element_type=jnp.float32,
+                )
+            )
+        blocks = [pieces[0][:16]]
+        for a in range(1, win_rows):
+            blocks.append(pieces[a][:16] + pieces[a - 1][16:])
+        blocks.append(pieces[win_rows - 1][16:])
+        stacked = jnp.concatenate(blocks, axis=0)
+        out_ref[:, pl.ds(start, 2 * LANES)] += jnp.dot(
+            stacked,
+            n_ref[...],
+            precision=lax.Precision.HIGHEST,
+            preferred_element_type=jnp.float32,
+        )
+        return carry
+
+    lax.fori_loop(0, tiles, one_tile, 0)
+
+
+def analyze_weigh_synthesize(region, window_weight, freq_weight, column_table, row_table):
+    rows, cols = region.shape
+    tiles = (cols - 16) // LANES
+    wide = (tiles + 1) * LANES
+    padded = jnp.pad(region, ((0, 0), (0, wide - cols)))
+    columns, columns_t, forward, backward = transform_tables(column_table, row_table)
+    freq = jnp.tile(freq_weight, (1, 2 * WINDOWS_PER_TILE))
+    weights = jnp.repeat(window_weight, 32, axis=1).reshape(
+        window_weight.shape[0], tiles, WINDOWS_PER_TILE, 32
+    )
+    weights = jnp.concatenate([weights, weights], axis=2).reshape(window_weight.shape[0], -1)
+    vmem = pl.BlockSpec(memory_space=pltpu.VMEM)
+    out = pl.pallas_call(
+        transform_kernel,
+        out_shape=jax.ShapeDtypeStruct((rows, wide), jnp.float32),
+        in_specs=[vmem] * 7,
+        out_specs=vmem,
+    )(padded, columns, columns_t, forward, backward, freq, weights)
+    return out[:, :cols]
+
 def per_device(iterate, residual, direction, window_weight, freq_weight):
     column_table, row_table = tables()
     height, breadth = direction.shape
@@ -110,8 +207,7 @@
         ],
         axis=0,
     )
-    coefficients = weigh(analyze(region, column_table, row_table), window_weight, freq_weight)
-    spread = synthesize(coefficients, column_table, row_table)
+    spread = analyze_weigh_synthesize(region, window_weight, freq_weight, column_table, row_table)
     arrived_rows = passed_along(spread[height:, :breadth], "row", 1)
     arrived_cols = passed_along(spread[:height, breadth:], COL, 1)
     arrived_corner = passed_diagonally(spread[height:, breadth:], 1)

time: 120 us -> 120 us (level)
  Pallas kernels: 0 us -> 37 us
  matrix products: 25.9 us -> 0 us
  local copies, waits for them, and re-layouts: 20.1 us -> 11.1 us
  other arithmetic: 4.53 us -> 6.02 us
    pallas_call x0 -> x1, Pallas kernels: none -> 37 us  [analyze_weigh_synthesize(): pl.pallas_call(transform_kernel, out_shape=jax.ShapeDtypeStruct((rows, wi...]
    dot_general x6 -> x0, matrix products: 25.9 us -> none  [the longest x1 8.11 us: analyze(): jnp.einsum('akbl,lp->akpb', blocks[:, :, 1:], column_table[16:], precisio...]
    add x1 -> x0, local copies, waits for them, and re-layouts: 3.89 us -> none  [synthesize(): jnp.pad(lower_piece, ((0, 0), (0, 0), (0, 1), (0, 0)))]
    ppermute x8, starting transfers between devices: 16.5 us -> 13.1 us  [summed_everywhere(): x = x + lax.ppermute(x, axis, [(i, i ^ mask) for i in range(count)])]
    reshape x2 -> x5, local copies, waits for them, and re-layouts: 7.14 us -> 3.93 us  [the longest x1 1.94 us: analyze_weigh_synthesize(): jnp.concatenate([weights, weights], axis=2)]
    ppermute x8, waiting for transfers between devices: 18.7 us -> 21.4 us  [summed_everywhere(): x = x + lax.ppermute(x, axis, [(i, i ^ mask) for i in range(count)])]
    transpose x1 -> x0, local copies, waits for them, and re-layouts: 2.43 us -> none  [synthesize(): jnp.einsum('tm,atvb->amvb', row_table, coefficients, precision=precise)]
    ppermute x2, waiting for transfers between devices: 2.36 us -> 0.01 us  [passed_diagonally(): return lax.ppermute(value, ('row',) + COL, pairs)]
  transfers between devices with their start and end apart: 14 -> 14, of which waited for: 10 -> 10; matrix products, arithmetic and copies ran while one was open for 2% -> 9% of each run, Pallas kernels for 0% -> 0%
where the time goes in v3:
time: 120 us; the launch traced here: 119 us
  Pallas kernels  37 us (31%)
  starting transfers between devices  36.7 us (31%)
  waiting for transfers between devices  23.9 us (20%)
  local copies, waits for them, and re-layouts  11.1 us (9%)
  other arithmetic  6.02 us (5%)
  between operations  4.93 us (4%)
    pallas_call x1, Pallas kernels, analyze_weigh_synthesize(): pl.pallas_call(transform_kernel, out_shape=jax.ShapeDtypeStruct((rows, wi...  37 us
    ppermute x8, waiting for transfers between devices, summed_everywhere(): x = x + lax.ppermute(x, axis, [(i, i ^ mask) for i in range(count)])  21.4 us
    ppermute x4, starting transfers between devices, passed_along(): lax.ppermute(value, axis, [(source, source + steps) for source in range(l...  18.1 us
    ppermute x8, starting transfers between devices, summed_everywhere(): x = x + lax.ppermute(x, axis, [(i, i ^ mask) for i in range(count)])  13.1 us
    ppermute x2, starting transfers between devices, passed_diagonally(): return lax.ppermute(value, ('row',) + COL, pairs)  5.53 us
    ppermute x4, waiting for transfers between devices, passed_along(): lax.ppermute(value, axis, [(source, source + steps) for source in range(l...  2.48 us
  transfers between devices with their start and end apart: 14, of which 10 were waited for; matrix products, arithmetic and copies ran while one was open for 9% of the time, Pallas kernels for 0%

profile of v3, /device:TPU:16, one launch (start us, length us, event | category | flops | bytes accessed | tf_op | source)
XLA Modules:
  0.0 119.5 jit_solution(3630441136695992165)
XLA Ops:
  1.5 1.3 %collective-permute-start.1 = (f32[16,2048]{1,0:T(8,128)S(1)}, f32[16,2048]{1,0:T(8,128)S(1)}, u32[]{:S(2)}, u32[]{:S(2)}) collective-permute-start(f32[16,2048]{1,0:T(8,128)S(1)} %slice.51), channel_id=1, source_target_pairs={{64,0},{128,64},{192,128},{65,1},{129,65},{193,129},{66,2},{130,66... | collective-permute-start | bytes 393224 | tf_op jit(solution)/shard_map/ppermute | solution.py:29
  3.6 10.6 %collective-permute-start = (f32[64,16]{1,0:T(8,128)S(1)}, f32[64,16]{1,0:T(8,128)S(1)}, u32[]{:S(2)}, u32[]{:S(2)}) collective-permute-start(f32[64,16]{1,0:T(8,128)S(1)} %slice.50), channel_id=1, source_target_pairs={{1,0},{2,1},{3,2},{4,3},{5,4},{6,5},{7,6},{8,7},{9,8},{10,9},{11,1... | collective-permute-start | bytes 12296 | tf_op jit(solution)/shard_map/ppermute | solution.py:29
  14.9 1.3 %collective-permute-start.2 = (f32[16,16]{1,0:T(8,128)S(1)}, f32[16,16]{1,0:T(8,128)S(1)}, u32[]{:S(2)}, u32[]{:S(2)}) collective-permute-start(f32[16,16]{1,0:T(8,128)S(1)} %slice.52), channel_id=1, source_target_pairs={{65,0},{66,1},{67,2},{68,3},{69,4},{70,5},{71,6},{72,7},{73,8},{74... | collective-permute-start | bytes 3080 | tf_op jit(solution)/shard_map/ppermute | solution.py:39
  21.5 1.9 %reshape.115.ww_ref = f32[4,8192]{1,0:T(4,128)} reshape(f32[4,16,16,32]{3,2,1,0:T(8,128)} %pad_maximum_fusion) | data formatting | bytes 262144 | tf_op jit(solution)/shard_map/reshape | solution.py:187
  25.2 37.0 %shard_map.76 = f32[80,2176]{1,0:T(8,128)} custom-call(f32[80,2176]{1,0:T(8,128)} %fusion.x_ref, f32[256,512]{1,0:T(8,128)} %copy-done.1, f32[512,256]{1,0:T(8,128)} %bitcast.19, f32[32,64]{1,0:T(8,128)} %get-tuple-element.25.f_ref, f32[32,64]{1,0:T(8,128)} %get-tuple-element.26.g_ref, f32[32,512]{1,0:T(8,128)} %tile.10.fw_ref, f32[4,8192]{1,0:T(4,128)} %reshape.115.ww_ref), custom_call_target="tpu_custom_call" | custom-call | tf_op jit(solution)/shard_map/pallas_call | solution.py:189
  62.9 1.9 %collective-permute-start.4 = (f32[64,16]{1,0:T(8,128)S(1)}, f32[64,16]{1,0:T(8,128)S(1)}, u32[]{:S(2)}, u32[]{:S(2)}) collective-permute-start(f32[64,16]{1,0:T(8,128)S(1)} %slice.67), channel_id=1, source_target_pairs={{0,1},{1,2},{2,3},{3,4},{4,5},{5,6},{6,7},{7,8},{8,9},{9,10},{10,1... | collective-permute-start | bytes 12296 | tf_op jit(solution)/shard_map/ppermute | solution.py:29
  65.5 4.2 %collective-permute-start.5 = (f32[16,16]{1,0:T(8,128)S(1)}, f32[16,16]{1,0:T(8,128)S(1)}, u32[]{:S(2)}, u32[]{:S(2)}) collective-permute-start(f32[16,16]{1,0:T(8,128)S(1)} %slice.68), channel_id=1, source_target_pairs={{0,65},{1,66},{2,67},{3,68},{4,69},{5,70},{6,71},{7,72},{8,73},{9,... | collective-permute-start | bytes 3080 | tf_op jit(solution)/shard_map/ppermute | solution.py:39
  70.7 4.3 %collective-permute-start.3 = (f32[16,2048]{1,0:T(8,128)S(1)}, f32[16,2048]{1,0:T(8,128)S(1)}, u32[]{:S(2)}, u32[]{:S(2)}) collective-permute-start(f32[16,2048]{1,0:T(8,128)S(1)} %slice.66), channel_id=1, source_target_pairs={{0,64},{64,128},{128,192},{1,65},{65,129},{129,193},{2,66},{66,130... | collective-permute-start | bytes 393224 | tf_op jit(solution)/shard_map/ppermute | solution.py:29
  75.0 2.4 %collective-permute-done.3 = f32[16,2048]{1,0:T(8,128)S(1)} collective-permute-done((f32[16,2048]{1,0:T(8,128)S(1)}, f32[16,2048]{1,0:T(8,128)S(1)}, u32[]{:S(2)}, u32[]{:S(2)}) %collective-permute-start.3) | collective-permute-done | bytes 131104 | tf_op jit(solution)/shard_map/ppermute | solution.py:29
  77.5 1.1 multiply_bitcast_fusion.2
  79.2 1.1 collective-permute-done.6
  80.3 2.4 %collective-permute-start.7 = (f32[4]{0:T(128)S(1)}, f32[4]{0:T(128)S(1)}, u32[]{:S(2)}, u32[]{:S(2)}) collective-permute-start(f32[4]{0:T(128)S(1)} %add.91), channel_id=1, source_target_pairs={{0,64},{64,0},{128,192},{192,128},{1,65},{65,1},{129,193},{193,129... | collective-permute-start | bytes 56 | tf_op jit(solution)/shard_map/ppermute | solution.py:45
  82.7 1.5 %collective-permute-done.7 = f32[4]{0:T(128)S(1)} collective-permute-done((f32[4]{0:T(128)S(1)}, f32[4]{0:T(128)S(1)}, u32[]{:S(2)}, u32[]{:S(2)}) %collective-permute-start.7) | collective-permute-done | bytes 48 | tf_op jit(solution)/shard_map/ppermute | solution.py:45
  84.2 3.2 %collective-permute-start.8 = (f32[4]{0:T(128)S(1)}, f32[4]{0:T(128)S(1)}, u32[]{:S(2)}, u32[]{:S(2)}) collective-permute-start(f32[4]{0:T(128)S(1)} %add.92), channel_id=1, source_target_pairs={{0,128},{64,192},{128,0},{192,64},{1,129},{65,193},{129,1},{193,65... | collective-permute-start | bytes 56 | tf_op jit(solution)/shard_map/ppermute | solution.py:45
  87.4 1.5 %collective-permute-done.8 = f32[4]{0:T(128)S(1)} collective-permute-done((f32[4]{0:T(128)S(1)}, f32[4]{0:T(128)S(1)}, u32[]{:S(2)}, u32[]{:S(2)}) %collective-permute-start.8) | collective-permute-done | bytes 48 | tf_op jit(solution)/shard_map/ppermute | solution.py:45
  88.9 1.6 %collective-permute-start.9 = (f32[4]{0:T(128)S(1)}, f32[4]{0:T(128)S(1)}, u32[]{:S(2)}, u32[]{:S(2)}) collective-permute-start(f32[4]{0:T(128)S(1)} %add.93), channel_id=1, source_target_pairs={{0,16},{16,0},{32,48},{48,32},{1,17},{17,1},{33,49},{49,33},{2,18}... | collective-permute-start | bytes 56 | tf_op jit(solution)/shard_map/ppermute | solution.py:45
  90.5 2.0 %collective-permute-done.9 = f32[4]{0:T(128)S(1)} collective-permute-done((f32[4]{0:T(128)S(1)}, f32[4]{0:T(128)S(1)}, u32[]{:S(2)}, u32[]{:S(2)}) %collective-permute-start.9) | collective-permute-done | bytes 48 | tf_op jit(solution)/shard_map/ppermute | solution.py:45
  92.5 5.0 %collective-permute-done.10 = f32[4]{0:T(128)S(1)} collective-permute-done((f32[4]{0:T(128)S(1)}, f32[4]{0:T(128)S(1)}, u32[]{:S(2)}, u32[]{:S(2)}) %collective-permute-start.10) | collective-permute-done | bytes 48 | tf_op jit(solution)/shard_map/ppermute | solution.py:45
  97.5 3.5 %collective-permute-done.11 = f32[4]{0:T(128)S(1)} collective-permute-done((f32[4]{0:T(128)S(1)}, f32[4]{0:T(128)S(1)}, u32[]{:S(2)}, u32[]{:S(2)}) %collective-permute-start.11) | collective-permute-done | bytes 48 | tf_op jit(solution)/shard_map/ppermute | solution.py:45
  101.1 1.0 collective-permute-start.12
  102.1 4.0 %collective-permute-done.12 = f32[4]{0:T(128)S(1)} collective-permute-done((f32[4]{0:T(128)S(1)}, f32[4]{0:T(128)S(1)}, u32[]{:S(2)}, u32[]{:S(2)}) %collective-permute-start.12) | collective-permute-done | bytes 48 | tf_op jit(solution)/shard_map/ppermute | solution.py:45
  106.1 4.8 %collective-permute-start.13 = (f32[4]{0:T(128)S(1)}, f32[4]{0:T(128)S(1)}, u32[]{:S(2)}, u32[]{:S(2)}) collective-permute-start(f32[4]{0:T(128)S(1)} %add.97), channel_id=1, source_target_pairs={{0,2},{2,0},{1,3},{3,1},{4,6},{6,4},{5,7},{7,5},{8,10},{10,8},{9,1... | collective-permute-start | bytes 56 | tf_op jit(solution)/shard_map/ppermute | solution.py:45
  110.9 2.7 %collective-permute-done.13 = f32[4]{0:T(128)S(1)} collective-permute-done((f32[4]{0:T(128)S(1)}, f32[4]{0:T(128)S(1)}, u32[]{:S(2)}, u32[]{:S(2)}) %collective-permute-start.13) | collective-permute-done | bytes 48 | tf_op jit(solution)/shard_map/ppermute | solution.py:45
  118.3 1.2 %multiply_add_fusion = (f32[64,2048]{1,0:T(8,128)}, f32[64,2048]{1,0:T(8,128)}, f32[64,2048]{1,0:T(8,128)}) fusion(f32[64,2048]{1,0:T(8,128)S(1)} %copy-done, f32[]{:T(128)S(6)} %div.66, f32[64,2048]{1,0:T(8,128)S(1)} %copy-done.2, f32[64,2048]{1,0:T(8,128)S(1)} %get-tuple-element.6, f32[]{:T(128)S(6)} %div.65, f32[64,2048]{1,0:T(8,128)S(1)} %copy-done.3), kind=kLoop, calls=%fused_computation.10 | loop fusion | flops 786432 | bytes 3670024 | tf_op jit(solution)/shard_map/add | solution.py:233
  (57 shorter events, 12.9 us)
Async XLA Ops:
  1.5 22.7 %collective-permute-start.1 = (f32[16,2048]{1,0:T(8,128)S(1)}, f32[16,2048]{1,0:T(8,128)S(1)}, u32[]{:S(2)}, u32[]{:S(2)}) collective-permute-start(f32[16,2048]{1,0:T(8,128)S(1)} %slice.51), channel_id=1, source_target_pairs={{64,0},{128,64},{192,128},{65,1},{129,65},{193,129},{66,2},{130,66... | collective-permute-start | bytes 393224 | tf_op jit(solution)/shard_map/ppermute | solution.py:29
  3.6 20.6 %collective-permute-start = (f32[64,16]{1,0:T(8,128)S(1)}, f32[64,16]{1,0:T(8,128)S(1)}, u32[]{:S(2)}, u32[]{:S(2)}) collective-permute-start(f32[64,16]{1,0:T(8,128)S(1)} %slice.50), channel_id=1, source_target_pairs={{1,0},{2,1},{3,2},{4,3},{5,4},{6,5},{7,6},{8,7},{9,8},{10,9},{11,1... | collective-permute-start | bytes 12296 | tf_op jit(solution)/shard_map/ppermute | solution.py:29
  14.9 9.3 %collective-permute-start.2 = (f32[16,16]{1,0:T(8,128)S(1)}, f32[16,16]{1,0:T(8,128)S(1)}, u32[]{:S(2)}, u32[]{:S(2)}) collective-permute-start(f32[16,16]{1,0:T(8,128)S(1)} %slice.52), channel_id=1, source_target_pairs={{65,0},{66,1},{67,2},{68,3},{69,4},{70,5},{71,6},{72,7},{73,8},{74... | collective-permute-start | bytes 3080 | tf_op jit(solution)/shard_map/ppermute | solution.py:39
  19.7 3.8 %copy-start.4 = (f32[32,32]{1,0:T(8,128)S(1)}, f32[32,32]{1,0:T(8,128)}, u32[]{:S(2)}) copy-start(f32[32,32]{1,0:T(8,128)} %param.9) | copy-start | bytes 12292
  19.7 4.6 %copy-start = (f32[64,2048]{1,0:T(8,128)S(1)}, f32[64,2048]{1,0:T(8,128)}, u32[]{:S(2)}) copy-start(f32[64,2048]{1,0:T(8,128)} %param.7) | copy-start | bytes 1572868
  20.5 4.7 %copy-start.1 = (f32[256,512]{1,0:T(8,128)}, f32[256,512]{1,0:T(8,128)S(1)}, u32[]{:S(2)}) copy-start(f32[256,512]{1,0:T(8,128)S(1)} %reshape.114.m_ref) | copy-start | bytes 1572868
  25.2 53.4 %copy-start.2 = (f32[64,2048]{1,0:T(8,128)S(1)}, f32[64,2048]{1,0:T(8,128)}, u32[]{:S(2)}) copy-start(f32[64,2048]{1,0:T(8,128)} %param.6) | copy-start | bytes 1572868
  62.9 12.1 %collective-permute-start.4 = (f32[64,16]{1,0:T(8,128)S(1)}, f32[64,16]{1,0:T(8,128)S(1)}, u32[]{:S(2)}, u32[]{:S(2)}) collective-permute-start(f32[64,16]{1,0:T(8,128)S(1)} %slice.67), channel_id=1, source_target_pairs={{0,1},{1,2},{2,3},{3,4},{4,5},{5,6},{6,7},{7,8},{8,9},{9,10},{10,1... | collective-permute-start | bytes 12296 | tf_op jit(solution)/shard_map/ppermute | solution.py:29
  65.5 9.5 %collective-permute-start.5 = (f32[16,16]{1,0:T(8,128)S(1)}, f32[16,16]{1,0:T(8,128)S(1)}, u32[]{:S(2)}, u32[]{:S(2)}) collective-permute-start(f32[16,16]{1,0:T(8,128)S(1)} %slice.68), channel_id=1, source_target_pairs={{0,65},{1,66},{2,67},{3,68},{4,69},{5,70},{6,71},{7,72},{8,73},{9,... | collective-permute-start | bytes 3080 | tf_op jit(solution)/shard_map/ppermute | solution.py:39
  70.7 6.8 %collective-permute-start.3 = (f32[16,2048]{1,0:T(8,128)S(1)}, f32[16,2048]{1,0:T(8,128)S(1)}, u32[]{:S(2)}, u32[]{:S(2)}) collective-permute-start(f32[16,2048]{1,0:T(8,128)S(1)} %slice.66), channel_id=1, source_target_pairs={{0,64},{64,128},{128,192},{1,65},{65,129},{129,193},{2,66},{66,130... | collective-permute-start | bytes 393224 | tf_op jit(solution)/shard_map/ppermute | solution.py:29
  78.6 39.6 %copy-start.3 = (f32[64,2048]{1,0:T(8,128)S(1)}, f32[64,2048]{1,0:T(8,128)}, u32[]{:S(2)}) copy-start(f32[64,2048]{1,0:T(8,128)} %param.5) | copy-start | bytes 1572868
  79.1 1.2 collective-permute-start.6
  80.3 4.0 %collective-permute-start.7 = (f32[4]{0:T(128)S(1)}, f32[4]{0:T(128)S(1)}, u32[]{:S(2)}, u32[]{:S(2)}) collective-permute-start(f32[4]{0:T(128)S(1)} %add.91), channel_id=1, source_target_pairs={{0,64},{64,0},{128,192},{192,128},{1,65},{65,1},{129,193},{193,129... | collective-permute-start | bytes 56 | tf_op jit(solution)/shard_map/ppermute | solution.py:45
  84.2 4.7 %collective-permute-start.8 = (f32[4]{0:T(128)S(1)}, f32[4]{0:T(128)S(1)}, u32[]{:S(2)}, u32[]{:S(2)}) collective-permute-start(f32[4]{0:T(128)S(1)} %add.92), channel_id=1, source_target_pairs={{0,128},{64,192},{128,0},{192,64},{1,129},{65,193},{129,1},{193,65... | collective-permute-start | bytes 56 | tf_op jit(solution)/shard_map/ppermute | solution.py:45
  88.9 3.5 %collective-permute-start.9 = (f32[4]{0:T(128)S(1)}, f32[4]{0:T(128)S(1)}, u32[]{:S(2)}, u32[]{:S(2)}) collective-permute-start(f32[4]{0:T(128)S(1)} %add.93), channel_id=1, source_target_pairs={{0,16},{16,0},{32,48},{48,32},{1,17},{17,1},{33,49},{49,33},{2,18}... | collective-permute-start | bytes 56 | tf_op jit(solution)/shard_map/ppermute | solution.py:45
  92.5 5.0 %collective-permute-start.10 = (f32[4]{0:T(128)S(1)}, f32[4]{0:T(128)S(1)}, u32[]{:S(2)}, u32[]{:S(2)}) collective-permute-start(f32[4]{0:T(128)S(1)} %add.94), channel_id=1, source_target_pairs={{0,32},{16,48},{32,0},{48,16},{1,33},{17,49},{33,1},{49,17},{2,34}... | collective-permute-start | bytes 56 | tf_op jit(solution)/shard_map/ppermute | solution.py:45
  97.5 3.5 %collective-permute-start.11 = (f32[4]{0:T(128)S(1)}, f32[4]{0:T(128)S(1)}, u32[]{:S(2)}, u32[]{:S(2)}) collective-permute-start(f32[4]{0:T(128)S(1)} %add.95), channel_id=1, source_target_pairs={{0,4},{4,0},{8,12},{12,8},{1,5},{5,1},{9,13},{13,9},{2,6},{6,2},{1... | collective-permute-start | bytes 56 | tf_op jit(solution)/shard_map/ppermute | solution.py:45
  101.1 5.0 %collective-permute-start.12 = (f32[4]{0:T(128)S(1)}, f32[4]{0:T(128)S(1)}, u32[]{:S(2)}, u32[]{:S(2)}) collective-permute-start(f32[4]{0:T(128)S(1)} %add.96), channel_id=1, source_target_pairs={{0,8},{4,12},{8,0},{12,4},{1,9},{5,13},{9,1},{13,5},{2,10},{6,14},... | collective-permute-start | bytes 56 | tf_op jit(solution)/shard_map/ppermute | solution.py:45
  106.1 7.4 %collective-permute-start.13 = (f32[4]{0:T(128)S(1)}, f32[4]{0:T(128)S(1)}, u32[]{:S(2)}, u32[]{:S(2)}) collective-permute-start(f32[4]{0:T(128)S(1)} %add.97), channel_id=1, source_target_pairs={{0,2},{2,0},{1,3},{3,1},{4,6},{6,4},{5,7},{7,5},{8,10},{10,8},{9,1... | collective-permute-start | bytes 56 | tf_op jit(solution)/shard_map/ppermute | solution.py:45

commit v4 on v2

--- a/solution.py
+++ b/solution.py
@@ -1,8 +1,11 @@
 import jax
+import numpy as np
 import jax.numpy as jnp
 from jax import lax
 from jax.sharding import Mesh
 from jax.sharding import PartitionSpec as P
+from jax.experimental import pallas as pl
+from jax.experimental.pallas import tpu as pltpu
 
 COL = ("col_0", "col_1", "col_2", "col_3")
 DOUBLING = (
@@ -97,8 +100,127 @@
     return blocks.reshape(16 * (win_rows + 1), 16 * (win_cols + 1))
 
 
+LANES = 128
+WINDOWS_PER_TILE = LANES // 16
+HALF = WINDOWS_PER_TILE * 32
+
+
+def numpy_tables():
+    positions = np.arange(32, dtype=np.float32)
+    window = np.exp(np.float32(-0.5) * ((positions - np.float32(15.5)) / np.float32(8.0)) ** 2)
+    phases = np.float32(2.0 * np.pi) * np.outer(positions, positions) / np.float32(32.0)
+    scale = np.sqrt(np.float32(32.0))
+    cos_part = np.cos(phases) * window[None, :] / scale
+    sin_part = -np.sin(phases) * window[None, :] / scale
+    return cos_part.astype(np.float32), sin_part.astype(np.float32)
+
+
+def transform_tables(win_rows):
+    cos_part, sin_part = numpy_tables()
+    column_table = np.stack([cos_part.T, sin_part.T], axis=1)
+    columns = np.zeros((2 * WINDOWS_PER_TILE, 16, 2, WINDOWS_PER_TILE, 32), np.float32)
+    for k in range(WINDOWS_PER_TILE):
+        columns[k, :, :, k] = column_table[:16]
+        columns[k + 1, :, :, k] = column_table[16:]
+    columns = columns.reshape(2 * LANES, 2 * HALF)
+    blocks = win_rows + 1
+    real = np.zeros((win_rows, 32, blocks * 16), np.float32)
+    imag = np.zeros((win_rows, 32, blocks * 16), np.float32)
+    for a in range(win_rows):
+        real[a, :, 16 * a : 16 * a + 32] = cos_part
+        imag[a, :, 16 * a : 16 * a + 32] = sin_part
+    real = real.reshape(win_rows * 32, blocks * 16)
+    imag = imag.reshape(win_rows * 32, blocks * 16)
+    forward = np.concatenate([real, imag], axis=1)
+    backward = np.concatenate([real.T, imag.T], axis=1)
+    return [columns, np.ascontiguousarray(columns.T), forward, backward]
+
+
+def split_constant(table):
+    high = table.astype(jnp.bfloat16)
+    low = (table - high.astype(np.float32)).astype(jnp.bfloat16)
+    return [jnp.asarray(high), jnp.asarray(low)]
+
+
+def split_value(value):
+    high = value.astype(jnp.bfloat16)
+    return high, (value - high.astype(jnp.float32)).astype(jnp.bfloat16)
+
+
+def three_pass_dot(a, b):
+    total = jnp.dot(a[0], b[1], preferred_element_type=jnp.float32)
+    total += jnp.dot(a[1], b[0], preferred_element_type=jnp.float32)
+    return total + jnp.dot(a[0], b[0], preferred_element_type=jnp.float32)
+
+
+def transform_kernel(
+    x_ref, mh_ref, ml_ref, nh_ref, nl_ref, fh_ref, fl_ref, gh_ref, gl_ref, fw_ref, ww_ref,
+    out_ref, y_ref, e_ref,
+):
+    rows = x_ref.shape[0]
+    win_rows = rows // 16 - 1
+    tiles = (x_ref.shape[1] - LANES) // LANES
+    stacked_x = jnp.concatenate(
+        [x_ref[:, t * LANES : (t + 2) * LANES] for t in range(tiles)], axis=0
+    )
+    y_ref[...] = three_pass_dot(split_value(stacked_x), (mh_ref[...], ml_ref[...]))
+    forward = (fh_ref[...], fl_ref[...])
+    backward = (gh_ref[...], gl_ref[...])
+    freq = fw_ref[...]
+
+    def one_tile(t, carry):
+        here = pl.ds(pl.multiple_of(t * rows, 8), rows)
+        y = y_ref[here, :]
+        weights = ww_ref[:, pl.ds(pl.multiple_of(t * 2 * HALF, 2 * HALF), 2 * HALF)]
+        turned = jnp.concatenate([-y[:, HALF:], y[:, :HALF]], axis=1)
+        z = three_pass_dot(forward, split_value(jnp.concatenate([y, turned], axis=0)))
+        spread = jnp.concatenate(
+            [jnp.broadcast_to(weights[a : a + 1], (32, 2 * HALF)) for a in range(win_rows)],
+            axis=0,
+        )
+        z = z * freq * spread
+        turned = jnp.concatenate([z[:, HALF:], -z[:, :HALF]], axis=1)
+        e_ref[here, :] = three_pass_dot(backward, split_value(jnp.concatenate([z, turned], axis=0)))
+        return carry
+
+    lax.fori_loop(0, tiles, one_tile, 0)
+    pieces = three_pass_dot(split_value(e_ref[...]), (nh_ref[...], nl_ref[...]))
+    out_ref[...] = jnp.zeros_like(out_ref)
+    for t in range(tiles):
+        out_ref[:, t * LANES : (t + 2) * LANES] += pieces[t * rows : (t + 1) * rows]
+
+
+def analyze_weigh_synthesize(region, window_weight, freq_weight):
+    rows, cols = region.shape
+    tiles = (cols - 16) // LANES
+    wide = (tiles + 1) * LANES
+    padded = jnp.pad(region, ((0, 0), (0, wide - cols)))
+    win_rows = rows // 16 - 1
+    constants = []
+    for table in transform_tables(win_rows):
+        constants += split_constant(table)
+    freq = jnp.broadcast_to(
+        freq_weight.reshape(1, 32, 1, 1, 32), (win_rows, 32, 2, WINDOWS_PER_TILE, 32)
+    ).reshape(win_rows * 32, 2 * HALF)
+    weights = jnp.broadcast_to(
+        window_weight.reshape(win_rows, tiles, 1, WINDOWS_PER_TILE, 1),
+        (win_rows, tiles, 2, WINDOWS_PER_TILE, 32),
+    ).reshape(win_rows, tiles * 2 * HALF)
+    vmem = pl.BlockSpec(memory_space=pltpu.VMEM)
+    out = pl.pallas_call(
+        transform_kernel,
+        out_shape=jax.ShapeDtypeStruct((rows, wide), jnp.float32),
+        in_specs=[vmem] * 11,
+        out_specs=vmem,
+        scratch_shapes=[
+            pltpu.VMEM((tiles * rows, 2 * HALF), jnp.float32),
+            pltpu.VMEM((tiles * rows, 2 * HALF), jnp.float32),
+        ],
+    )(padded, *constants, freq, weights)
+    return out[:, :cols]
+
+
 def per_device(iterate, residual, direction, window_weight, freq_weight):
-    column_table, row_table = tables()
     height, breadth = direction.shape
     beside = passed_along(direction[:, :16], COL, -1)
     below = passed_along(direction[:16], "row", -1)
@@ -110,8 +232,7 @@
         ],
         axis=0,
     )
-    coefficients = weigh(analyze(region, column_table, row_table), window_weight, freq_weight)
-    spread = synthesize(coefficients, column_table, row_table)
+    spread = analyze_weigh_synthesize(region, window_weight, freq_weight)
     arrived_rows = passed_along(spread[height:, :breadth], "row", 1)
     arrived_cols = passed_along(spread[:height, breadth:], COL, 1)
     arrived_corner = passed_diagonally(spread[height:, breadth:], 1)

time: 120 us -> 92.9 us (0.77)
  matrix products: 25.9 us -> 0 us
  Pallas kernels: 0 us -> 13.1 us
  local copies, waits for them, and re-layouts: 20.1 us -> 8.35 us
  starting transfers between devices: 37.9 us -> 36.1 us
    dot_general x6 -> x0, matrix products: 25.9 us -> none  [the longest x1 8.11 us: analyze(): jnp.einsum('akbl,lp->akpb', blocks[:, :, 1:], column_table[16:], precisio...]
    pallas_call x0 -> x1, Pallas kernels: none -> 13.1 us  [analyze_weigh_synthesize(): pl.pallas_call(transform_kernel, out_shape=jax.ShapeDtypeStruct((rows, wi...]
    reshape x2, local copies, waits for them, and re-layouts: 7.14 us -> 2 us  [the longest x1 1.09 us: analyze_weigh_synthesize(): freq = jnp.broadcast_to(freq_weight.reshape(1, 32, 1, 1, 32), (win_rows,...]
    add x1 -> x0, local copies, waits for them, and re-layouts: 3.89 us -> none  [synthesize(): jnp.pad(lower_piece, ((0, 0), (0, 0), (0, 1), (0, 0)))]
    ppermute x8, starting transfers between devices: 16.5 us -> 13.1 us  [summed_everywhere(): x = x + lax.ppermute(x, axis, [(i, i ^ mask) for i in range(count)])]
    another operation x2 -> x0, local copies, waits for them, and re-layouts: 2.44 us -> none  [analyze(): jnp.stack([section_one[:-1], section_one[1:]], axis=1)]
    transpose x1 -> x0, local copies, waits for them, and re-layouts: 2.43 us -> none  [synthesize(): jnp.einsum('tm,atvb->amvb', row_table, coefficients, precision=precise)]
    ppermute x8, waiting for transfers between devices: 18.7 us -> 21.1 us  [summed_everywhere(): x = x + lax.ppermute(x, axis, [(i, i ^ mask) for i in range(count)])]
  transfers between devices with their start and end apart: 14 -> 14, of which waited for: 10 -> 11; matrix products, arithmetic and copies ran while one was open for 2% -> 7% of each run, Pallas kernels for 0% -> 0%
where the time goes in v4:
time: 92.9 us; the launch traced here: 91.6 us
  starting transfers between devices  36.1 us (39%)
  waiting for transfers between devices  25.4 us (27%)
  Pallas kernels  13.1 us (14%)
  local copies, waits for them, and re-layouts  8.35 us (9%)
  between operations  4.89 us (5%)
  other arithmetic  3.76 us (4%)
    ppermute x8, waiting for transfers between devices, summed_everywhere(): x = x + lax.ppermute(x, axis, [(i, i ^ mask) for i in range(count)])  21.1 us
    ppermute x4, starting transfers between devices, passed_along(): lax.ppermute(value, axis, [(source, source + steps) for source in range(l...  18.1 us
    ppermute x8, starting transfers between devices, summed_everywhere(): x = x + lax.ppermute(x, axis, [(i, i ^ mask) for i in range(count)])  13.1 us
    pallas_call x1, Pallas kernels, analyze_weigh_synthesize(): pl.pallas_call(transform_kernel, out_shape=jax.ShapeDtypeStruct((rows, wi...  13.1 us
    ppermute x2, starting transfers between devices, passed_diagonally(): return lax.ppermute(value, ('row',) + COL, pairs)  4.87 us
    ppermute x4, waiting for transfers between devices, passed_along(): lax.ppermute(value, axis, [(source, source + steps) for source in range(l...  3.68 us
  transfers between devices with their start and end apart: 14, of which 11 were waited for; matrix products, arithmetic and copies ran while one was open for 7% of the time, Pallas kernels for 0%

profile of v4, /device:TPU:16, one launch (start us, length us, event | category | flops | bytes accessed | tf_op | source)
XLA Modules:
  0.0 91.6 jit_solution(8340216436935496132)
XLA Ops:
  0.6 0.9 %slice.39 = f32[16,2048]{1,0:T(8,128)S(1)} slice(f32[64,2048]{1,0:T(8,128)} %param.15), slice={[0:16], [0:2048]} | slice | bytes 262144 | tf_op jit(solution)/shard_map/slice | solution.py:226
  1.6 1.3 %collective-permute-start.1 = (f32[16,2048]{1,0:T(8,128)S(1)}, f32[16,2048]{1,0:T(8,128)S(1)}, u32[]{:S(2)}, u32[]{:S(2)}) collective-permute-start(f32[16,2048]{1,0:T(8,128)S(1)} %slice.39), channel_id=1, source_target_pairs={{64,0},{128,64},{192,128},{65,1},{129,65},{193,129},{66,2},{130,66... | collective-permute-start | bytes 393224 | tf_op jit(solution)/shard_map/ppermute | solution.py:30
  3.6 10.6 %collective-permute-start = (f32[64,16]{1,0:T(8,128)S(1)}, f32[64,16]{1,0:T(8,128)S(1)}, u32[]{:S(2)}, u32[]{:S(2)}) collective-permute-start(f32[64,16]{1,0:T(8,128)S(1)} %slice.38), channel_id=1, source_target_pairs={{1,0},{2,1},{3,2},{4,3},{5,4},{6,5},{7,6},{8,7},{9,8},{10,9},{11,1... | collective-permute-start | bytes 12296 | tf_op jit(solution)/shard_map/ppermute | solution.py:30
  14.9 1.3 %collective-permute-start.2 = (f32[16,16]{1,0:T(8,128)S(1)}, f32[16,16]{1,0:T(8,128)S(1)}, u32[]{:S(2)}, u32[]{:S(2)}) collective-permute-start(f32[16,16]{1,0:T(8,128)S(1)} %slice.40), channel_id=1, source_target_pairs={{65,0},{66,1},{67,2},{68,3},{69,4},{70,5},{71,6},{72,7},{73,8},{74... | collective-permute-start | bytes 3080 | tf_op jit(solution)/shard_map/ppermute | solution.py:40
  18.1 1.1 %reshape.16.fw_ref = f32[128,512]{1,0:T(8,128)} reshape(f32[4,32,2,8,32]{4,3,2,1,0:T(8,128)S(1)} %broadcast_in_dim.12) | data formatting | bytes 524288 | tf_op jit(solution)/shard_map/reshape | solution.py:204
  20.8 13.1 %shard_map.148 = f32[80,2176]{1,0:T(8,128)} custom-call(f32[80,2176]{1,0:T(8,128)} %fusion.x_ref, bf16[256,512]{1,0:T(8,128)(2,1)} %constant.24.clone.mh_ref, bf16[256,512]{1,0:T(8,128)(2,1)} %constant.25.clone.ml_ref, bf16[512,256]{1,0:T(8,128)(2,1)} %constant.26.clone.nh_ref, bf16[512,256]{1,0:T(8,128)(2,1)} %constant.27.clone.nl_ref, ...), custom_call_target="tpu_custom_call" | custom-call | tf_op jit(solution)/shard_map/pallas_call | solution.py:210
  34.7 1.9 %collective-permute-start.4 = (f32[64,16]{1,0:T(8,128)S(1)}, f32[64,16]{1,0:T(8,128)S(1)}, u32[]{:S(2)}, u32[]{:S(2)}) collective-permute-start(f32[64,16]{1,0:T(8,128)S(1)} %slice.51), channel_id=1, source_target_pairs={{0,1},{1,2},{2,3},{3,4},{4,5},{5,6},{6,7},{7,8},{8,9},{9,10},{10,1... | collective-permute-start | bytes 12296 | tf_op jit(solution)/shard_map/ppermute | solution.py:30
  37.3 3.6 %collective-permute-start.5 = (f32[16,16]{1,0:T(8,128)S(1)}, f32[16,16]{1,0:T(8,128)S(1)}, u32[]{:S(2)}, u32[]{:S(2)}) collective-permute-start(f32[16,16]{1,0:T(8,128)S(1)} %slice.52), channel_id=1, source_target_pairs={{0,65},{1,66},{2,67},{3,68},{4,69},{5,70},{6,71},{7,72},{8,73},{9,... | collective-permute-start | bytes 3080 | tf_op jit(solution)/shard_map/ppermute | solution.py:40
  41.8 4.3 %collective-permute-start.3 = (f32[16,2048]{1,0:T(8,128)S(1)}, f32[16,2048]{1,0:T(8,128)S(1)}, u32[]{:S(2)}, u32[]{:S(2)}) collective-permute-start(f32[16,2048]{1,0:T(8,128)S(1)} %slice.50), channel_id=1, source_target_pairs={{0,64},{64,128},{128,192},{1,65},{65,129},{129,193},{2,66},{66,130... | collective-permute-start | bytes 393224 | tf_op jit(solution)/shard_map/ppermute | solution.py:30
  46.8 3.0 %collective-permute-done.3 = f32[16,2048]{1,0:T(8,128)S(1)} collective-permute-done((f32[16,2048]{1,0:T(8,128)S(1)}, f32[16,2048]{1,0:T(8,128)S(1)}, u32[]{:S(2)}, u32[]{:S(2)}) %collective-permute-start.3) | collective-permute-done | bytes 131104 | tf_op jit(solution)/shard_map/ppermute | solution.py:30
  49.8 1.1 %multiply_bitcast_fusion.2 = (f32[1,64,2048]{2,1,0:T(8,128)S(1)}, f32[64,2048]{1,0:T(8,128)S(1)}) fusion(f32[64,2048]{1,0:T(8,128)S(1)} %copy-done, f32[64,16]{1,0:T(8,128)S(1)} %pad_add_fusion, f32[16,2048]{1,0:T(8,128)S(1)} %collective-permute-done.3, f32[80,2176]{1,0:T(8,128)} %shard_map.148), kind=kLoop, calls=%fused_computation.13 | loop fusion | flops 655360 | bytes 2232320 | tf_op jit(solution)/shard_map/stack | solution.py:249
  52.6 2.5 %collective-permute-start.7 = (f32[4]{0:T(128)S(1)}, f32[4]{0:T(128)S(1)}, u32[]{:S(2)}, u32[]{:S(2)}) collective-permute-start(f32[4]{0:T(128)S(1)} %add.57), channel_id=1, source_target_pairs={{0,64},{64,0},{128,192},{192,128},{1,65},{65,1},{129,193},{193,129... | collective-permute-start | bytes 56 | tf_op jit(solution)/shard_map/ppermute | solution.py:46
  55.1 1.5 %collective-permute-done.7 = f32[4]{0:T(128)S(1)} collective-permute-done((f32[4]{0:T(128)S(1)}, f32[4]{0:T(128)S(1)}, u32[]{:S(2)}, u32[]{:S(2)}) %collective-permute-start.7) | collective-permute-done | bytes 48 | tf_op jit(solution)/shard_map/ppermute | solution.py:46
  56.6 2.1 %collective-permute-start.8 = (f32[4]{0:T(128)S(1)}, f32[4]{0:T(128)S(1)}, u32[]{:S(2)}, u32[]{:S(2)}) collective-permute-start(f32[4]{0:T(128)S(1)} %add.58), channel_id=1, source_target_pairs={{0,128},{64,192},{128,0},{192,64},{1,129},{65,193},{129,1},{193,65... | collective-permute-start | bytes 56 | tf_op jit(solution)/shard_map/ppermute | solution.py:46
  58.7 2.3 %collective-permute-done.8 = f32[4]{0:T(128)S(1)} collective-permute-done((f32[4]{0:T(128)S(1)}, f32[4]{0:T(128)S(1)}, u32[]{:S(2)}, u32[]{:S(2)}) %collective-permute-start.8) | collective-permute-done | bytes 48 | tf_op jit(solution)/shard_map/ppermute | solution.py:46
  61.0 1.6 %collective-permute-start.9 = (f32[4]{0:T(128)S(1)}, f32[4]{0:T(128)S(1)}, u32[]{:S(2)}, u32[]{:S(2)}) collective-permute-start(f32[4]{0:T(128)S(1)} %add.59), channel_id=1, source_target_pairs={{0,16},{16,0},{32,48},{48,32},{1,17},{17,1},{33,49},{49,33},{2,18}... | collective-permute-start | bytes 56 | tf_op jit(solution)/shard_map/ppermute | solution.py:46
  62.7 1.9 %collective-permute-done.9 = f32[4]{0:T(128)S(1)} collective-permute-done((f32[4]{0:T(128)S(1)}, f32[4]{0:T(128)S(1)}, u32[]{:S(2)}, u32[]{:S(2)}) %collective-permute-start.9) | collective-permute-done | bytes 48 | tf_op jit(solution)/shard_map/ppermute | solution.py:46
  64.6 5.0 %collective-permute-done.10 = f32[4]{0:T(128)S(1)} collective-permute-done((f32[4]{0:T(128)S(1)}, f32[4]{0:T(128)S(1)}, u32[]{:S(2)}, u32[]{:S(2)}) %collective-permute-start.10) | collective-permute-done | bytes 48 | tf_op jit(solution)/shard_map/ppermute | solution.py:46
  69.6 3.5 %collective-permute-done.11 = f32[4]{0:T(128)S(1)} collective-permute-done((f32[4]{0:T(128)S(1)}, f32[4]{0:T(128)S(1)}, u32[]{:S(2)}, u32[]{:S(2)}) %collective-permute-start.11) | collective-permute-done | bytes 48 | tf_op jit(solution)/shard_map/ppermute | solution.py:46
  73.2 2.8 %collective-permute-start.12 = (f32[4]{0:T(128)S(1)}, f32[4]{0:T(128)S(1)}, u32[]{:S(2)}, u32[]{:S(2)}) collective-permute-start(f32[4]{0:T(128)S(1)} %add.62), channel_id=1, source_target_pairs={{0,8},{4,12},{8,0},{12,4},{1,9},{5,13},{9,1},{13,5},{2,10},{6,14},... | collective-permute-start | bytes 56 | tf_op jit(solution)/shard_map/ppermute | solution.py:46
  75.9 2.3 %collective-permute-done.12 = f32[4]{0:T(128)S(1)} collective-permute-done((f32[4]{0:T(128)S(1)}, f32[4]{0:T(128)S(1)}, u32[]{:S(2)}, u32[]{:S(2)}) %collective-permute-start.12) | collective-permute-done | bytes 48 | tf_op jit(solution)/shard_map/ppermute | solution.py:46
  78.2 3.8 %collective-permute-start.13 = (f32[4]{0:T(128)S(1)}, f32[4]{0:T(128)S(1)}, u32[]{:S(2)}, u32[]{:S(2)}) collective-permute-start(f32[4]{0:T(128)S(1)} %add.63), channel_id=1, source_target_pairs={{0,2},{2,0},{1,3},{3,1},{4,6},{6,4},{5,7},{7,5},{8,10},{10,8},{9,1... | collective-permute-start | bytes 56 | tf_op jit(solution)/shard_map/ppermute | solution.py:46
  82.0 3.7 %collective-permute-done.13 = f32[4]{0:T(128)S(1)} collective-permute-done((f32[4]{0:T(128)S(1)}, f32[4]{0:T(128)S(1)}, u32[]{:S(2)}, u32[]{:S(2)}) %collective-permute-start.13) | collective-permute-done | bytes 48 | tf_op jit(solution)/shard_map/ppermute | solution.py:46
  90.4 1.2 %multiply_add_fusion = (f32[64,2048]{1,0:T(8,128)}, f32[64,2048]{1,0:T(8,128)}, f32[64,2048]{1,0:T(8,128)}) fusion(f32[64,2048]{1,0:T(8,128)S(1)} %copy-done, f32[]{:T(128)S(6)} %div.7, f32[64,2048]{1,0:T(8,128)S(1)} %copy-done.1, f32[64,2048]{1,0:T(8,128)S(1)} %get-tuple-element.6, f32[]{:T(128)S(6)} %div.6, f32[64,2048]{1,0:T(8,128)S(1)} %copy-done.2), kind=kLoop, calls=%fused_computation.8 | loop fusion | flops 786432 | bytes 3670024 | tf_op jit(solution)/shard_map/add | solution.py:258
  (39 shorter events, 10.3 us)
Async XLA Ops:
  0.6 17.4 %copy-start.3 = (f32[32,32]{1,0:T(8,128)S(1)}, f32[32,32]{1,0:T(8,128)}, u32[]{:S(2)}) copy-start(f32[32,32]{1,0:T(8,128)} %param.17) | copy-start | bytes 12292
  1.6 18.3 %collective-permute-start.1 = (f32[16,2048]{1,0:T(8,128)S(1)}, f32[16,2048]{1,0:T(8,128)S(1)}, u32[]{:S(2)}, u32[]{:S(2)}) collective-permute-start(f32[16,2048]{1,0:T(8,128)S(1)} %slice.39), channel_id=1, source_target_pairs={{64,0},{128,64},{192,128},{65,1},{129,65},{193,129},{66,2},{130,66... | collective-permute-start | bytes 393224 | tf_op jit(solution)/shard_map/ppermute | solution.py:30
  3.6 16.3 %collective-permute-start = (f32[64,16]{1,0:T(8,128)S(1)}, f32[64,16]{1,0:T(8,128)S(1)}, u32[]{:S(2)}, u32[]{:S(2)}) collective-permute-start(f32[64,16]{1,0:T(8,128)S(1)} %slice.38), channel_id=1, source_target_pairs={{1,0},{2,1},{3,2},{4,3},{5,4},{6,5},{7,6},{8,7},{9,8},{10,9},{11,1... | collective-permute-start | bytes 12296 | tf_op jit(solution)/shard_map/ppermute | solution.py:30
  14.9 5.0 %collective-permute-start.2 = (f32[16,16]{1,0:T(8,128)S(1)}, f32[16,16]{1,0:T(8,128)S(1)}, u32[]{:S(2)}, u32[]{:S(2)}) collective-permute-start(f32[16,16]{1,0:T(8,128)S(1)} %slice.40), channel_id=1, source_target_pairs={{65,0},{66,1},{67,2},{68,3},{69,4},{70,5},{71,6},{72,7},{73,8},{74... | collective-permute-start | bytes 3080 | tf_op jit(solution)/shard_map/ppermute | solution.py:40
  18.1 1.8 %copy-start = (f32[64,2048]{1,0:T(8,128)S(1)}, f32[64,2048]{1,0:T(8,128)}, u32[]{:S(2)}) copy-start(f32[64,2048]{1,0:T(8,128)} %param.15) | copy-start | bytes 1572868
  34.7 12.1 %collective-permute-start.4 = (f32[64,16]{1,0:T(8,128)S(1)}, f32[64,16]{1,0:T(8,128)S(1)}, u32[]{:S(2)}, u32[]{:S(2)}) collective-permute-start(f32[64,16]{1,0:T(8,128)S(1)} %slice.51), channel_id=1, source_target_pairs={{0,1},{1,2},{2,3},{3,4},{4,5},{5,6},{6,7},{7,8},{8,9},{9,10},{10,1... | collective-permute-start | bytes 12296 | tf_op jit(solution)/shard_map/ppermute | solution.py:30
  37.3 8.8 %collective-permute-start.5 = (f32[16,16]{1,0:T(8,128)S(1)}, f32[16,16]{1,0:T(8,128)S(1)}, u32[]{:S(2)}, u32[]{:S(2)}) collective-permute-start(f32[16,16]{1,0:T(8,128)S(1)} %slice.52), channel_id=1, source_target_pairs={{0,65},{1,66},{2,67},{3,68},{4,69},{5,70},{6,71},{7,72},{8,73},{9,... | collective-permute-start | bytes 3080 | tf_op jit(solution)/shard_map/ppermute | solution.py:40
  41.8 8.0 %collective-permute-start.3 = (f32[16,2048]{1,0:T(8,128)S(1)}, f32[16,2048]{1,0:T(8,128)S(1)}, u32[]{:S(2)}, u32[]{:S(2)}) collective-permute-start(f32[16,2048]{1,0:T(8,128)S(1)} %slice.50), channel_id=1, source_target_pairs={{0,64},{64,128},{128,192},{1,65},{65,129},{129,193},{2,66},{66,130... | collective-permute-start | bytes 393224 | tf_op jit(solution)/shard_map/ppermute | solution.py:30
  46.8 4.1 %copy-start.1 = (f32[64,2048]{1,0:T(8,128)S(1)}, f32[64,2048]{1,0:T(8,128)}, u32[]{:S(2)}) copy-start(f32[64,2048]{1,0:T(8,128)} %param.14) | copy-start | bytes 1572868
  51.1 39.2 %copy-start.2 = (f32[64,2048]{1,0:T(8,128)S(1)}, f32[64,2048]{1,0:T(8,128)}, u32[]{:S(2)}) copy-start(f32[64,2048]{1,0:T(8,128)} %param.13) | copy-start | bytes 1572868
  51.4 1.2 %collective-permute-start.6 = (f32[4]{0:T(128)S(1)}, f32[4]{0:T(128)S(1)}, u32[]{:S(2)}, u32[]{:S(2)}) collective-permute-start(f32[4]{0:T(128)S(1)} %maximum_reduce_fusion), channel_id=1, source_target_pairs={{0,1},{1,0},{2,3},{3,2},{4,5},{5,4},{6,7},{7,6},{8,9},{9,8},{10,11... | collective-permute-start | bytes 56 | tf_op jit(solution)/shard_map/ppermute | solution.py:46
  52.6 4.0 %collective-permute-start.7 = (f32[4]{0:T(128)S(1)}, f32[4]{0:T(128)S(1)}, u32[]{:S(2)}, u32[]{:S(2)}) collective-permute-start(f32[4]{0:T(128)S(1)} %add.57), channel_id=1, source_target_pairs={{0,64},{64,0},{128,192},{192,128},{1,65},{65,1},{129,193},{193,129... | collective-permute-start | bytes 56 | tf_op jit(solution)/shard_map/ppermute | solution.py:46
  56.6 4.4 %collective-permute-start.8 = (f32[4]{0:T(128)S(1)}, f32[4]{0:T(128)S(1)}, u32[]{:S(2)}, u32[]{:S(2)}) collective-permute-start(f32[4]{0:T(128)S(1)} %add.58), channel_id=1, source_target_pairs={{0,128},{64,192},{128,0},{192,64},{1,129},{65,193},{129,1},{193,65... | collective-permute-start | bytes 56 | tf_op jit(solution)/shard_map/ppermute | solution.py:46
  61.0 3.5 %collective-permute-start.9 = (f32[4]{0:T(128)S(1)}, f32[4]{0:T(128)S(1)}, u32[]{:S(2)}, u32[]{:S(2)}) collective-permute-start(f32[4]{0:T(128)S(1)} %add.59), channel_id=1, source_target_pairs={{0,16},{16,0},{32,48},{48,32},{1,17},{17,1},{33,49},{49,33},{2,18}... | collective-permute-start | bytes 56 | tf_op jit(solution)/shard_map/ppermute | solution.py:46
  64.6 5.0 %collective-permute-start.10 = (f32[4]{0:T(128)S(1)}, f32[4]{0:T(128)S(1)}, u32[]{:S(2)}, u32[]{:S(2)}) collective-permute-start(f32[4]{0:T(128)S(1)} %add.60), channel_id=1, source_target_pairs={{0,32},{16,48},{32,0},{48,16},{1,33},{17,49},{33,1},{49,17},{2,34}... | collective-permute-start | bytes 56 | tf_op jit(solution)/shard_map/ppermute | solution.py:46
  69.6 3.5 %collective-permute-start.11 = (f32[4]{0:T(128)S(1)}, f32[4]{0:T(128)S(1)}, u32[]{:S(2)}, u32[]{:S(2)}) collective-permute-start(f32[4]{0:T(128)S(1)} %add.61), channel_id=1, source_target_pairs={{0,4},{4,0},{8,12},{12,8},{1,5},{5,1},{9,13},{13,9},{2,6},{6,2},{1... | collective-permute-start | bytes 56 | tf_op jit(solution)/shard_map/ppermute | solution.py:46
  73.2 5.0 %collective-permute-start.12 = (f32[4]{0:T(128)S(1)}, f32[4]{0:T(128)S(1)}, u32[]{:S(2)}, u32[]{:S(2)}) collective-permute-start(f32[4]{0:T(128)S(1)} %add.62), channel_id=1, source_target_pairs={{0,8},{4,12},{8,0},{12,4},{1,9},{5,13},{9,1},{13,5},{2,10},{6,14},... | collective-permute-start | bytes 56 | tf_op jit(solution)/shard_map/ppermute | solution.py:46
  78.2 7.4 %collective-permute-start.13 = (f32[4]{0:T(128)S(1)}, f32[4]{0:T(128)S(1)}, u32[]{:S(2)}, u32[]{:S(2)}) collective-permute-start(f32[4]{0:T(128)S(1)} %add.63), channel_id=1, source_target_pairs={{0,2},{2,0},{1,3},{3,1},{4,6},{6,4},{5,7},{7,5},{8,10},{10,8},{9,1... | collective-permute-start | bytes 56 | tf_op jit(solution)/shard_map/ppermute | solution.py:46

commit v5 on v4

--- a/solution.py
+++ b/solution.py
@@ -192,8 +192,10 @@
 
 def analyze_weigh_synthesize(region, window_weight, freq_weight):
     rows, cols = region.shape
-    tiles = (cols - 16) // LANES
+    windows = (cols - 16) // 16
+    tiles = -(-windows // WINDOWS_PER_TILE)
     wide = (tiles + 1) * LANES
+    window_weight = jnp.pad(window_weight, ((0, 0), (0, tiles * WINDOWS_PER_TILE - windows)))
     padded = jnp.pad(region, ((0, 0), (0, wide - cols)))
     win_rows = rows // 16 - 1
     constants = []
@@ -222,29 +224,24 @@
 
 def per_device(iterate, residual, direction, window_weight, freq_weight):
     height, breadth = direction.shape
-    beside = passed_along(direction[:, :16], COL, -1)
-    below = passed_along(direction[:16], "row", -1)
-    corner = passed_diagonally(direction[:16, :16], -1)
-    region = jnp.concatenate(
-        [
-            jnp.concatenate([direction, beside], axis=1),
-            jnp.concatenate([below, corner], axis=1),
-        ],
-        axis=0,
-    )
-    spread = analyze_weigh_synthesize(region, window_weight, freq_weight)
-    arrived_rows = passed_along(spread[height:, :breadth], "row", 1)
-    arrived_cols = passed_along(spread[:height, breadth:], COL, 1)
-    arrived_corner = passed_diagonally(spread[height:, breadth:], 1)
-    synthesized = (
-        spread[:height, :breadth]
-        + jnp.pad(arrived_rows, ((0, height - 16), (0, 0)))
-        + jnp.pad(
-            arrived_cols
-            + jnp.pad(arrived_corner, ((0, height - 16), (0, 0))),
-            ((0, 0), (0, breadth - 16)),
-        )
-    )
+    rim_weight = jnp.pad(window_weight[:, -1:], ((0, 0), (0, 15)))
+    from_left = passed_along(
+        jnp.concatenate([direction[:, -16:], rim_weight], axis=0), COL, 1
+    )
+    from_right = passed_along(direction[:, :16], COL, -1)
+    widened = jnp.concatenate([from_left[:height], direction, from_right], axis=1)
+    weights_wide = jnp.concatenate([from_left[height:, :1], window_weight], axis=1)
+    top_weight = jnp.pad(weights_wide[-1:], ((0, 0), (0, widened.shape[1] - weights_wide.shape[1])))
+    from_above = passed_along(
+        jnp.concatenate([widened[-16:], top_weight], axis=0), "row", 1
+    )
+    from_below = passed_along(widened[:16], "row", -1)
+    region = jnp.concatenate([from_above[:16], widened, from_below], axis=0)
+    weights_all = jnp.concatenate(
+        [from_above[16:, : weights_wide.shape[1]], weights_wide], axis=0
+    )
+    spread = analyze_weigh_synthesize(region, weights_all, freq_weight)
+    synthesized = spread[16 : 16 + height, 16 : 16 + breadth]
     applied = synthesized + damping * direction
     products = jnp.stack(
         [residual * residual, direction * applied, residual * applied, applied * applied]

time: 92.9 us -> 90.2 us (0.971)
  starting transfers between devices: 36.1 us -> 31.8 us
  Pallas kernels: 13.1 us -> 16.4 us
  local copies, waits for them, and re-layouts: 8.35 us -> 6.42 us
  other arithmetic: 3.76 us -> 5.01 us
    ppermute x2 -> x0, starting transfers between devices: 4.87 us -> none  [passed_diagonally(): return lax.ppermute(value, ('row',) + COL, pairs)]
    pallas_call x1, Pallas kernels: 13.1 us -> 16.4 us  [analyze_weigh_synthesize(): pl.pallas_call(transform_kernel, out_shape=jax.ShapeDtypeStruct((rows, wi...]
    slice x6 -> x7, local copies, waits for them, and re-layouts: 4.77 us -> 1.64 us  [the longest x1 0.85 us: per_device(): from_right = passed_along(direction[:, :16], COL, -1)]
    concatenate x0 -> x2, local copies, waits for them, and re-layouts: none -> 1.46 us  [the longest x1 1.36 us: per_device(): jnp.concatenate([from_left[:height], direction, from_right], axis=1)]
    concatenate x1 -> x5, other arithmetic: 0.92 us -> 1.99 us  [the longest x1 1.05 us: per_device(): region = jnp.concatenate([from_above[:16], widened, from_below], axis=0)]
    ppermute x8, starting transfers between devices: 13.1 us -> 14.2 us  [summed_everywhere(): x = x + lax.ppermute(x, axis, [(i, i ^ mask) for i in range(count)])]
  transfers between devices with their start and end apart: 14 -> 12, of which waited for: 11 -> 11; matrix products, arithmetic and copies ran while one was open for 7% -> 4% of each run, Pallas kernels for 0% -> 0%
where the time goes in v5:
time: 90.2 us; the launch traced here: 89.7 us
  starting transfers between devices  31.8 us (35%)
  waiting for transfers between devices  25.3 us (28%)
  Pallas kernels  16.4 us (18%)
  local copies, waits for them, and re-layouts  6.42 us (7%)
  other arithmetic  5.01 us (6%)
  between operations  4.75 us (5%)
    ppermute x8, waiting for transfers between devices, summed_everywhere(): x = x + lax.ppermute(x, axis, [(i, i ^ mask) for i in range(count)])  21.5 us
    ppermute x4, starting transfers between devices, passed_along(): lax.ppermute(value, axis, [(source, source + steps) for source in range(l...  17.6 us
    pallas_call x1, Pallas kernels, analyze_weigh_synthesize(): pl.pallas_call(transform_kernel, out_shape=jax.ShapeDtypeStruct((rows, wi...  16.4 us
    ppermute x8, starting transfers between devices, summed_everywhere(): x = x + lax.ppermute(x, axis, [(i, i ^ mask) for i in range(count)])  14.2 us
    ppermute x4, waiting for transfers between devices, passed_along(): lax.ppermute(value, axis, [(source, source + steps) for source in range(l...  3.77 us
  transfers between devices with their start and end apart: 12, of which 11 were waited for; matrix products, arithmetic and copies ran while one was open for 4% of the time, Pallas kernels for 0%

profile of v5, /device:TPU:16, one launch (start us, length us, event | category | flops | bytes accessed | tf_op | source)
XLA Modules:
  0.0 89.7 jit_solution(11946977981174963236)
XLA Ops:
  2.6 1.9 %collective-permute-start = (f32[68,16]{1,0:T(8,128)S(1)}, f32[68,16]{1,0:T(8,128)S(1)}, u32[]{:S(2)}, u32[]{:S(2)}) collective-permute-start(f32[68,16]{1,0:T(8,128)S(1)} %copy.18), channel_id=1, source_target_pairs={{0,1},{1,2},{2,3},{3,4},{4,5},{5,6},{6,7},{7,8},{8,9},{9,10},{10,1... | collective-permute-start | bytes 13064 | tf_op jit(solution)/shard_map/ppermute | solution.py:30
  4.5 10.6 %collective-permute-start.1 = (f32[64,16]{1,0:T(8,128)S(1)}, f32[64,16]{1,0:T(8,128)S(1)}, u32[]{:S(2)}, u32[]{:S(2)}) collective-permute-start(f32[64,16]{1,0:T(8,128)S(1)} %get-tuple-element.12), channel_id=1, source_target_pairs={{1,0},{2,1},{3,2},{4,3},{5,4},{6,5},{7,6},{8,7},{9,8},{10,9},{11,1... | collective-permute-start | bytes 12296 | tf_op jit(solution)/shard_map/ppermute | solution.py:30
  16.7 1.4 %concatenate.19 = f32[64,2080]{1,0:T(8,128)S(1)} concatenate(f32[64,16]{1,0:T(8,128)S(1)} %slice.62, f32[64,2048]{1,0:T(8,128)} %param.15, f32[64,16]{1,0:T(8,128)S(1)} %collective-permute-done.1), dimensions={1} | concatenate | bytes 1064960 | tf_op jit(solution)/shard_map/concatenate | solution.py:232
  18.1 3.8 %collective-permute-start.2 = (f32[17,2080]{1,0:T(8,128)S(1)}, f32[17,2080]{1,0:T(8,128)S(1)}, u32[]{:S(2)}, u32[]{:S(2)}) collective-permute-start(f32[17,2080]{1,0:T(8,128)S(1)} %pad_maximum_fusion), channel_id=1, source_target_pairs={{0,64},{64,128},{128,192},{1,65},{65,129},{129,193},{2,66},{66,130... | collective-permute-start | bytes 424328 | tf_op jit(solution)/shard_map/ppermute | solution.py:30
  21.9 1.3 %collective-permute-start.3 = (f32[16,2080]{1,0:T(8,128)S(1)}, f32[16,2080]{1,0:T(8,128)S(1)}, u32[]{:S(2)}, u32[]{:S(2)}) collective-permute-start(f32[16,2080]{1,0:T(8,128)S(1)} %get-tuple-element.9), channel_id=1, source_target_pairs={{64,0},{128,64},{192,128},{65,1},{129,65},{193,129},{66,2},{130,66... | collective-permute-start | bytes 399368 | tf_op jit(solution)/shard_map/ppermute | solution.py:30
  23.3 1.2 %reshape.16.fw_ref = f32[160,512]{1,0:T(8,128)} reshape(f32[5,32,2,8,32]{4,3,2,1,0:T(8,128)S(1)} %broadcast_in_dim.12) | data formatting | bytes 655360 | tf_op jit(solution)/shard_map/reshape | solution.py:206
  26.5 2.3 %collective-permute-done.3 = f32[16,2080]{1,0:T(8,128)S(1)} collective-permute-done((f32[16,2080]{1,0:T(8,128)S(1)}, f32[16,2080]{1,0:T(8,128)S(1)}, u32[]{:S(2)}, u32[]{:S(2)}) %collective-permute-start.3) | collective-permute-done | bytes 133152 | tf_op jit(solution)/shard_map/ppermute | solution.py:30
  29.9 16.4 %shard_map.148 = f32[96,2304]{1,0:T(8,128)} custom-call(f32[96,2304]{1,0:T(8,128)} %select_maximum_fusion.x_ref, bf16[256,512]{1,0:T(8,128)(2,1)} %constant.24.clone.mh_ref, bf16[256,512]{1,0:T(8,128)(2,1)} %constant.25.clone.ml_ref, bf16[512,256]{1,0:T(8,128)(2,1)} %constant.26.clone.nh_ref, bf16[512,256]{1,0:T(8,128)(2,1)} %constant.27.clone.nl_ref, ...), custom_call_target="tpu_custom_call" | custom-call | tf_op jit(solution)/shard_map/pallas_call | solution.py:212
  46.4 1.3 %multiply_bitcast_fusion.2 = (f32[1,64,2048]{2,1,0:T(8,128)S(1)}, f32[1,64,2048]{2,1,0:T(8,128)S(1)}, f32[1,64,2048]{2,1,0:T(8,128)S(1)}, f32[1,64,2048]{2,1,0:T(8,128)S(1)}) fusion(f32[64,2048]{1,0:T(8,128)S(1)} %copy-done, f32[96,2304]{1,0:T(8,128)} %shard_map.148, f32[64,2048]{1,0:T(8,128)S(1)} %copy-done.2), kind=kLoop, calls=%fused_computation.10 | loop fusion | flops 786432 | bytes 3670016 | tf_op jit(solution)/shard_map/stack | solution.py:246
  48.0 2.1 %collective-permute-start.4 = (f32[4]{0:T(128)S(1)}, f32[4]{0:T(128)S(1)}, u32[]{:S(2)}, u32[]{:S(2)}) collective-permute-start(f32[4]{0:T(128)S(1)} %maximum_reduce_fusion), channel_id=1, source_target_pairs={{0,1},{1,0},{2,3},{3,2},{4,5},{5,4},{6,7},{7,6},{8,9},{9,8},{10,11... | collective-permute-start | bytes 56 | tf_op jit(solution)/shard_map/ppermute | solution.py:46
  50.9 1.3 %collective-permute-start.5 = (f32[4]{0:T(128)S(1)}, f32[4]{0:T(128)S(1)}, u32[]{:S(2)}, u32[]{:S(2)}) collective-permute-start(f32[4]{0:T(128)S(1)} %add.45), channel_id=1, source_target_pairs={{0,64},{64,0},{128,192},{192,128},{1,65},{65,1},{129,193},{193,129... | collective-permute-start | bytes 56 | tf_op jit(solution)/shard_map/ppermute | solution.py:46
  52.2 2.3 %collective-permute-done.5 = f32[4]{0:T(128)S(1)} collective-permute-done((f32[4]{0:T(128)S(1)}, f32[4]{0:T(128)S(1)}, u32[]{:S(2)}, u32[]{:S(2)}) %collective-permute-start.5) | collective-permute-done | bytes 48 | tf_op jit(solution)/shard_map/ppermute | solution.py:46
  54.5 3.1 %collective-permute-start.6 = (f32[4]{0:T(128)S(1)}, f32[4]{0:T(128)S(1)}, u32[]{:S(2)}, u32[]{:S(2)}) collective-permute-start(f32[4]{0:T(128)S(1)} %add.46), channel_id=1, source_target_pairs={{0,128},{64,192},{128,0},{192,64},{1,129},{65,193},{129,1},{193,65... | collective-permute-start | bytes 56 | tf_op jit(solution)/shard_map/ppermute | solution.py:46
  57.6 1.5 %collective-permute-done.6 = f32[4]{0:T(128)S(1)} collective-permute-done((f32[4]{0:T(128)S(1)}, f32[4]{0:T(128)S(1)}, u32[]{:S(2)}, u32[]{:S(2)}) %collective-permute-start.6) | collective-permute-done | bytes 48 | tf_op jit(solution)/shard_map/ppermute | solution.py:46
  59.1 1.3 %collective-permute-start.7 = (f32[4]{0:T(128)S(1)}, f32[4]{0:T(128)S(1)}, u32[]{:S(2)}, u32[]{:S(2)}) collective-permute-start(f32[4]{0:T(128)S(1)} %add.47), channel_id=1, source_target_pairs={{0,16},{16,0},{32,48},{48,32},{1,17},{17,1},{33,49},{49,33},{2,18}... | collective-permute-start | bytes 56 | tf_op jit(solution)/shard_map/ppermute | solution.py:46
  60.4 2.3 %collective-permute-done.7 = f32[4]{0:T(128)S(1)} collective-permute-done((f32[4]{0:T(128)S(1)}, f32[4]{0:T(128)S(1)}, u32[]{:S(2)}, u32[]{:S(2)}) %collective-permute-start.7) | collective-permute-done | bytes 48 | tf_op jit(solution)/shard_map/ppermute | solution.py:46
  62.7 5.0 %collective-permute-done.8 = f32[4]{0:T(128)S(1)} collective-permute-done((f32[4]{0:T(128)S(1)}, f32[4]{0:T(128)S(1)}, u32[]{:S(2)}, u32[]{:S(2)}) %collective-permute-start.8) | collective-permute-done | bytes 48 | tf_op jit(solution)/shard_map/ppermute | solution.py:46
  67.7 1.2 %collective-permute-start.9 = (f32[4]{0:T(128)S(1)}, f32[4]{0:T(128)S(1)}, u32[]{:S(2)}, u32[]{:S(2)}) collective-permute-start(f32[4]{0:T(128)S(1)} %add.49), channel_id=1, source_target_pairs={{0,4},{4,0},{8,12},{12,8},{1,5},{5,1},{9,13},{13,9},{2,6},{6,2},{1... | collective-permute-start | bytes 56 | tf_op jit(solution)/shard_map/ppermute | solution.py:46
  68.9 2.3 %collective-permute-done.9 = f32[4]{0:T(128)S(1)} collective-permute-done((f32[4]{0:T(128)S(1)}, f32[4]{0:T(128)S(1)}, u32[]{:S(2)}, u32[]{:S(2)}) %collective-permute-start.9) | collective-permute-done | bytes 48 | tf_op jit(solution)/shard_map/ppermute | solution.py:46
  71.2 2.8 %collective-permute-start.10 = (f32[4]{0:T(128)S(1)}, f32[4]{0:T(128)S(1)}, u32[]{:S(2)}, u32[]{:S(2)}) collective-permute-start(f32[4]{0:T(128)S(1)} %add.50), channel_id=1, source_target_pairs={{0,8},{4,12},{8,0},{12,4},{1,9},{5,13},{9,1},{13,5},{2,10},{6,14},... | collective-permute-start | bytes 56 | tf_op jit(solution)/shard_map/ppermute | solution.py:46
  74.0 2.3 %collective-permute-done.10 = f32[4]{0:T(128)S(1)} collective-permute-done((f32[4]{0:T(128)S(1)}, f32[4]{0:T(128)S(1)}, u32[]{:S(2)}, u32[]{:S(2)}) %collective-permute-start.10) | collective-permute-done | bytes 48 | tf_op jit(solution)/shard_map/ppermute | solution.py:46
  76.3 2.4 %collective-permute-start.11 = (f32[4]{0:T(128)S(1)}, f32[4]{0:T(128)S(1)}, u32[]{:S(2)}, u32[]{:S(2)}) collective-permute-start(f32[4]{0:T(128)S(1)} %add.51), channel_id=1, source_target_pairs={{0,2},{2,0},{1,3},{3,1},{4,6},{6,4},{5,7},{7,5},{8,10},{10,8},{9,1... | collective-permute-start | bytes 56 | tf_op jit(solution)/shard_map/ppermute | solution.py:46
  78.7 5.1 %collective-permute-done.11 = f32[4]{0:T(128)S(1)} collective-permute-done((f32[4]{0:T(128)S(1)}, f32[4]{0:T(128)S(1)}, u32[]{:S(2)}, u32[]{:S(2)}) %collective-permute-start.11) | collective-permute-done | bytes 48 | tf_op jit(solution)/shard_map/ppermute | solution.py:46
  88.3 1.4 %multiply_add_fusion = (f32[64,2048]{1,0:T(8,128)}, f32[64,2048]{1,0:T(8,128)}, f32[64,2048]{1,0:T(8,128)}) fusion(f32[64,2048]{1,0:T(8,128)S(1)} %copy-done, f32[]{:T(128)S(6)} %div.7, f32[64,2048]{1,0:T(8,128)S(1)} %copy-done.2, f32[96,2304]{1,0:T(8,128)S(1)} %copy-done.1, f32[]{:T(128)S(6)} %div.6, f32[64,2048]{1,0:T(8,128)S(1)} %copy-done.3), kind=kLoop, calls=%fused_computation.5 | loop fusion | flops 1048576 | bytes 3670024 | tf_op jit(solution)/shard_map/add | solution.py:255
  (46 shorter events, 8.5 us)
Async XLA Ops:
  0.6 22.6 %copy-start.5 = (f32[32,32]{1,0:T(8,128)S(1)}, f32[32,32]{1,0:T(8,128)}, u32[]{:S(2)}) copy-start(f32[32,32]{1,0:T(8,128)} %param.17) | copy-start | bytes 12292
  2.6 12.6 %collective-permute-start = (f32[68,16]{1,0:T(8,128)S(1)}, f32[68,16]{1,0:T(8,128)S(1)}, u32[]{:S(2)}, u32[]{:S(2)}) collective-permute-start(f32[68,16]{1,0:T(8,128)S(1)} %copy.18), channel_id=1, source_target_pairs={{0,1},{1,2},{2,3},{3,4},{4,5},{5,6},{6,7},{7,8},{8,9},{9,10},{10,1... | collective-permute-start | bytes 13064 | tf_op jit(solution)/shard_map/ppermute | solution.py:30
  4.5 12.2 %collective-permute-start.1 = (f32[64,16]{1,0:T(8,128)S(1)}, f32[64,16]{1,0:T(8,128)S(1)}, u32[]{:S(2)}, u32[]{:S(2)}) collective-permute-start(f32[64,16]{1,0:T(8,128)S(1)} %get-tuple-element.12), channel_id=1, source_target_pairs={{1,0},{2,1},{3,2},{4,3},{5,4},{6,5},{7,6},{8,7},{9,8},{10,9},{11,1... | collective-permute-start | bytes 12296 | tf_op jit(solution)/shard_map/ppermute | solution.py:30
  18.1 7.1 %collective-permute-start.2 = (f32[17,2080]{1,0:T(8,128)S(1)}, f32[17,2080]{1,0:T(8,128)S(1)}, u32[]{:S(2)}, u32[]{:S(2)}) collective-permute-start(f32[17,2080]{1,0:T(8,128)S(1)} %pad_maximum_fusion), channel_id=1, source_target_pairs={{0,64},{64,128},{128,192},{1,65},{65,129},{129,193},{2,66},{66,130... | collective-permute-start | bytes 424328 | tf_op jit(solution)/shard_map/ppermute | solution.py:30
  21.9 3.3 %copy-start.4 = (f32[4,128]{1,0:T(4,128)S(1)}, f32[4,128]{1,0:T(4,128)}, u32[]{:S(2)}) copy-start(f32[4,128]{1,0:T(4,128)} %param.16) | copy-start | bytes 6148
  21.9 6.9 %collective-permute-start.3 = (f32[16,2080]{1,0:T(8,128)S(1)}, f32[16,2080]{1,0:T(8,128)S(1)}, u32[]{:S(2)}, u32[]{:S(2)}) collective-permute-start(f32[16,2080]{1,0:T(8,128)S(1)} %get-tuple-element.9), channel_id=1, source_target_pairs={{64,0},{128,64},{192,128},{65,1},{129,65},{193,129},{66,2},{130,66... | collective-permute-start | bytes 399368 | tf_op jit(solution)/shard_map/ppermute | solution.py:30
  29.9 16.4 %copy-start = (f32[64,2048]{1,0:T(8,128)S(1)}, f32[64,2048]{1,0:T(8,128)}, u32[]{:S(2)}) copy-start(f32[64,2048]{1,0:T(8,128)} %param.15) | copy-start | bytes 1572868
  29.9 16.4 %copy-start.2 = (f32[64,2048]{1,0:T(8,128)S(1)}, f32[64,2048]{1,0:T(8,128)}, u32[]{:S(2)}) copy-start(f32[64,2048]{1,0:T(8,128)} %param.14) | copy-start | bytes 1572868
  47.7 40.5 %copy-start.1 = (f32[96,2304]{1,0:T(8,128)S(1)}, f32[96,2304]{1,0:T(8,128)}, u32[]{:S(2)}) copy-start(f32[96,2304]{1,0:T(8,128)} %shard_map.148) | copy-start | bytes 2654212
  47.7 40.5 %copy-start.3 = (f32[64,2048]{1,0:T(8,128)S(1)}, f32[64,2048]{1,0:T(8,128)}, u32[]{:S(2)}) copy-start(f32[64,2048]{1,0:T(8,128)} %param.13) | copy-start | bytes 1572868
  48.0 2.9 %collective-permute-start.4 = (f32[4]{0:T(128)S(1)}, f32[4]{0:T(128)S(1)}, u32[]{:S(2)}, u32[]{:S(2)}) collective-permute-start(f32[4]{0:T(128)S(1)} %maximum_reduce_fusion), channel_id=1, source_target_pairs={{0,1},{1,0},{2,3},{3,2},{4,5},{5,4},{6,7},{7,6},{8,9},{9,8},{10,11... | collective-permute-start | bytes 56 | tf_op jit(solution)/shard_map/ppermute | solution.py:46
  50.9 3.5 %collective-permute-start.5 = (f32[4]{0:T(128)S(1)}, f32[4]{0:T(128)S(1)}, u32[]{:S(2)}, u32[]{:S(2)}) collective-permute-start(f32[4]{0:T(128)S(1)} %add.45), channel_id=1, source_target_pairs={{0,64},{64,0},{128,192},{192,128},{1,65},{65,1},{129,193},{193,129... | collective-permute-start | bytes 56 | tf_op jit(solution)/shard_map/ppermute | solution.py:46
  54.5 4.6 %collective-permute-start.6 = (f32[4]{0:T(128)S(1)}, f32[4]{0:T(128)S(1)}, u32[]{:S(2)}, u32[]{:S(2)}) collective-permute-start(f32[4]{0:T(128)S(1)} %add.46), channel_id=1, source_target_pairs={{0,128},{64,192},{128,0},{192,64},{1,129},{65,193},{129,1},{193,65... | collective-permute-start | bytes 56 | tf_op jit(solution)/shard_map/ppermute | solution.py:46
  59.1 3.5 %collective-permute-start.7 = (f32[4]{0:T(128)S(1)}, f32[4]{0:T(128)S(1)}, u32[]{:S(2)}, u32[]{:S(2)}) collective-permute-start(f32[4]{0:T(128)S(1)} %add.47), channel_id=1, source_target_pairs={{0,16},{16,0},{32,48},{48,32},{1,17},{17,1},{33,49},{49,33},{2,18}... | collective-permute-start | bytes 56 | tf_op jit(solution)/shard_map/ppermute | solution.py:46
  62.6 5.0 %collective-permute-start.8 = (f32[4]{0:T(128)S(1)}, f32[4]{0:T(128)S(1)}, u32[]{:S(2)}, u32[]{:S(2)}) collective-permute-start(f32[4]{0:T(128)S(1)} %add.48), channel_id=1, source_target_pairs={{0,32},{16,48},{32,0},{48,16},{1,33},{17,49},{33,1},{49,17},{2,34}... | collective-permute-start | bytes 56 | tf_op jit(solution)/shard_map/ppermute | solution.py:46
  67.7 3.5 %collective-permute-start.9 = (f32[4]{0:T(128)S(1)}, f32[4]{0:T(128)S(1)}, u32[]{:S(2)}, u32[]{:S(2)}) collective-permute-start(f32[4]{0:T(128)S(1)} %add.49), channel_id=1, source_target_pairs={{0,4},{4,0},{8,12},{12,8},{1,5},{5,1},{9,13},{13,9},{2,6},{6,2},{1... | collective-permute-start | bytes 56 | tf_op jit(solution)/shard_map/ppermute | solution.py:46
  71.2 5.0 %collective-permute-start.10 = (f32[4]{0:T(128)S(1)}, f32[4]{0:T(128)S(1)}, u32[]{:S(2)}, u32[]{:S(2)}) collective-permute-start(f32[4]{0:T(128)S(1)} %add.50), channel_id=1, source_target_pairs={{0,8},{4,12},{8,0},{12,4},{1,9},{5,13},{9,1},{13,5},{2,10},{6,14},... | collective-permute-start | bytes 56 | tf_op jit(solution)/shard_map/ppermute | solution.py:46
  76.3 7.4 %collective-permute-start.11 = (f32[4]{0:T(128)S(1)}, f32[4]{0:T(128)S(1)}, u32[]{:S(2)}, u32[]{:S(2)}) collective-permute-start(f32[4]{0:T(128)S(1)} %add.51), channel_id=1, source_target_pairs={{0,2},{2,0},{1,3},{3,1},{4,6},{6,4},{5,7},{7,5},{8,10},{10,8},{9,1... | collective-permute-start | bytes 56 | tf_op jit(solution)/shard_map/ppermute | solution.py:46

commit v6 on v5

--- a/solution.py
+++ b/solution.py
@@ -231,17 +231,27 @@
     from_right = passed_along(direction[:, :16], COL, -1)
     widened = jnp.concatenate([from_left[:height], direction, from_right], axis=1)
     weights_wide = jnp.concatenate([from_left[height:, :1], window_weight], axis=1)
+    middle = analyze_weigh_synthesize(widened, weights_wide[:-1], freq_weight)
     top_weight = jnp.pad(weights_wide[-1:], ((0, 0), (0, widened.shape[1] - weights_wide.shape[1])))
     from_above = passed_along(
         jnp.concatenate([widened[-16:], top_weight], axis=0), "row", 1
     )
     from_below = passed_along(widened[:16], "row", -1)
-    region = jnp.concatenate([from_above[:16], widened, from_below], axis=0)
-    weights_all = jnp.concatenate(
-        [from_above[16:, : weights_wide.shape[1]], weights_wide], axis=0
-    )
-    spread = analyze_weigh_synthesize(region, weights_all, freq_weight)
-    synthesized = spread[16 : 16 + height, 16 : 16 + breadth]
+    top = analyze_weigh_synthesize(
+        jnp.concatenate([from_above[:16], widened[:16]], axis=0),
+        from_above[16:, : weights_wide.shape[1]],
+        freq_weight,
+    )
+    bottom = analyze_weigh_synthesize(
+        jnp.concatenate([widened[-16:], from_below], axis=0),
+        weights_wide[-1:],
+        freq_weight,
+    )
+    inner = slice(16, 16 + breadth)
+    synthesized = middle[:, inner] + jnp.concatenate(
+        [top[16:, inner], jnp.zeros((height - 32, breadth), jnp.float32), bottom[:16, inner]],
+        axis=0,
+    )
     applied = synthesized + damping * direction
     products = jnp.stack(
         [residual * residual, direction * applied, residual * applied, applied * applied]

time: 90.2 us -> 105 us (1.16)
  Pallas kernels: 16.4 us -> 29.6 us
  local copies, waits for them, and re-layouts: 6.42 us -> 12 us
  waiting for transfers between devices: 25.3 us -> 22.2 us
  other arithmetic: 5.01 us -> 3.63 us
    pallas_call x1 -> x3, Pallas kernels: 16.4 us -> 29.6 us  [analyze_weigh_synthesize(): pl.pallas_call(transform_kernel, out_shape=jax.ShapeDtypeStruct((rows, wi...]
    ppermute x4, waiting for transfers between devices: 3.77 us -> 0.01 us  [passed_along(): lax.ppermute(value, axis, [(source, source + steps) for source in range(l...]
    slice x1 -> x3, local copies, waits for them, and re-layouts: 0.01 us -> 2.01 us  [the longest x1 1 us: per_device(): bottom[:16, inner]]
    broadcast_in_dim x2 -> x8, local copies, waits for them, and re-layouts: 0.24 us -> 1.99 us  [analyze_weigh_synthesize(): jnp.broadcast_to(window_weight.reshape(win_rows, tiles, 1, WINDOWS_PER_TI...]
    broadcast_in_dim x1 -> x3, local copies, waits for them, and re-layouts: 0.1 us -> 1.56 us  [analyze_weigh_synthesize(): jnp.broadcast_to(freq_weight.reshape(1, 32, 1, 1, 32), (win_rows, 32, 2,...]
    concatenate x1, local copies, waits for them, and re-layouts: 1.36 us -> 0.27 us  [per_device(): jnp.concatenate([from_left[:height], direction, from_right], axis=1)]
  transfers between devices with their start and end apart: 12 -> 12, of which waited for: 11 -> 8; matrix products, arithmetic and copies ran while one was open for 4% -> 7% of each run, Pallas kernels for 0% -> 20%
where the time goes in v6:
time: 105 us; the launch traced here: 104 us
  starting transfers between devices  32.2 us (31%)
  Pallas kernels  29.6 us (28%)
  waiting for transfers between devices  22.2 us (21%)
  local copies, waits for them, and re-layouts  12 us (11%)
  between operations  4.74 us (5%)
  other arithmetic  3.63 us (3%)
    pallas_call x3, Pallas kernels, analyze_weigh_synthesize(): pl.pallas_call(transform_kernel, out_shape=jax.ShapeDtypeStruct((rows, wi...  29.6 us
    ppermute x8, waiting for transfers between devices, summed_everywhere(): x = x + lax.ppermute(x, axis, [(i, i ^ mask) for i in range(count)])  22.2 us
    ppermute x4, starting transfers between devices, passed_along(): lax.ppermute(value, axis, [(source, source + steps) for source in range(l...  18.4 us
    ppermute x8, starting transfers between devices, summed_everywhere(): x = x + lax.ppermute(x, axis, [(i, i ^ mask) for i in range(count)])  13.8 us
  transfers between devices with their start and end apart: 12, of which 8 were waited for; matrix products, arithmetic and copies ran while one was open for 7% of the time, Pallas kernels for 20%

profile of v6, /device:TPU:16, one launch (start us, length us, event | category | flops | bytes accessed | tf_op | source)
XLA Modules:
  0.0 104.3 jit_solution(11606183564570667044)
XLA Ops:
  2.6 1.9 %collective-permute-start = (f32[68,16]{1,0:T(8,128)S(1)}, f32[68,16]{1,0:T(8,128)S(1)}, u32[]{:S(2)}, u32[]{:S(2)}) collective-permute-start(f32[68,16]{1,0:T(8,128)S(1)} %copy.34), channel_id=1, source_target_pairs={{0,1},{1,2},{2,3},{3,4},{4,5},{5,6},{6,7},{7,8},{8,9},{9,10},{10,1... | collective-permute-start | bytes 13064 | tf_op jit(solution)/shard_map/ppermute | solution.py:30
  4.5 10.6 %collective-permute-start.1 = (f32[64,16]{1,0:T(8,128)S(1)}, f32[64,16]{1,0:T(8,128)S(1)}, u32[]{:S(2)}, u32[]{:S(2)}) collective-permute-start(f32[64,16]{1,0:T(8,128)S(1)} %get-tuple-element.13), channel_id=1, source_target_pairs={{1,0},{2,1},{3,2},{4,3},{5,4},{6,5},{7,6},{8,7},{9,8},{10,9},{11,1... | collective-permute-start | bytes 12296 | tf_op jit(solution)/shard_map/ppermute | solution.py:30
  18.2 1.3 %collective-permute-start.3 = (f32[16,2080]{1,0:T(8,128)S(1)}, f32[16,2080]{1,0:T(8,128)S(1)}, u32[]{:S(2)}, u32[]{:S(2)}) collective-permute-start(f32[16,2080]{1,0:T(8,128)S(1)} %get-tuple-element.8), channel_id=1, source_target_pairs={{64,0},{128,64},{192,128},{65,1},{129,65},{193,129},{66,2},{130,66... | collective-permute-start | bytes 399368 | tf_op jit(solution)/shard_map/ppermute | solution.py:30
  22.4 4.5 %collective-permute-start.2 = (f32[17,2080]{1,0:T(8,128)S(1)}, f32[17,2080]{1,0:T(8,128)S(1)}, u32[]{:S(2)}, u32[]{:S(2)}) collective-permute-start(f32[17,2080]{1,0:T(8,128)S(1)} %select_maximum_fusion.2), channel_id=1, source_target_pairs={{0,64},{64,128},{128,192},{1,65},{65,129},{129,193},{2,66},{66,130... | collective-permute-start | bytes 424328 | tf_op jit(solution)/shard_map/ppermute | solution.py:30
  27.0 12.1 %shard_map.292 = f32[64,2304]{1,0:T(8,128)} custom-call(f32[64,2304]{1,0:T(8,128)} %pad.31.x_ref, bf16[256,512]{1,0:T(8,128)(2,1)} %constant.14.clone.mh_ref, bf16[256,512]{1,0:T(8,128)(2,1)} %constant.34.clone.ml_ref, bf16[512,256]{1,0:T(8,128)(2,1)} %constant.35.clone.nh_ref, bf16[512,256]{1,0:T(8,128)(2,1)} %constant.36.clone.nl_ref, ...), custom_call_target="tpu_custom_call" | custom-call | tf_op jit(solution)/shard_map/pallas_call | solution.py:212
  39.8 8.7 %shard_map.294 = f32[32,2304]{1,0:T(8,128)} custom-call(f32[32,2304]{1,0:T(8,128)} %select_maximum_fusion.x_ref, bf16[256,512]{1,0:T(8,128)(2,1)} %constant.14.clone.mh_ref, bf16[256,512]{1,0:T(8,128)(2,1)} %constant.34.clone.ml_ref, bf16[512,256]{1,0:T(8,128)(2,1)} %constant.35.clone.nh_ref, bf16[512,256]{1,0:T(8,128)(2,1)} %constant.36.clone.nl_ref, ...), custom_call_target="tpu_custom_call" | custom-call | tf_op jit(solution)/shard_map/pallas_call | solution.py:212
  48.5 1.0 slice.91
  51.2 8.8 %shard_map.293 = f32[32,2304]{1,0:T(8,128)} custom-call(f32[32,2304]{1,0:T(8,128)} %select_maximum_fusion.1.x_ref, bf16[256,512]{1,0:T(8,128)(2,1)} %constant.14.clone.mh_ref, bf16[256,512]{1,0:T(8,128)(2,1)} %constant.34.clone.ml_ref, bf16[512,256]{1,0:T(8,128)(2,1)} %constant.35.clone.nh_ref, bf16[512,256]{1,0:T(8,128)(2,1)} %constant.36.clone.nl_ref, ...), custom_call_target="tpu_custom_call" | custom-call | tf_op jit(solution)/shard_map/pallas_call | solution.py:212
  60.0 1.0 slice.90
  62.6 2.6 %collective-permute-start.4 = (f32[4]{0:T(128)S(1)}, f32[4]{0:T(128)S(1)}, u32[]{:S(2)}, u32[]{:S(2)}) collective-permute-start(f32[4]{0:T(128)S(1)} %maximum_reduce_fusion), channel_id=1, source_target_pairs={{0,1},{1,0},{2,3},{3,2},{4,5},{5,4},{6,7},{7,6},{8,9},{9,8},{10,11... | collective-permute-start | bytes 56 | tf_op jit(solution)/shard_map/ppermute | solution.py:46
  66.0 1.1 %collective-permute-start.5 = (f32[4]{0:T(128)S(1)}, f32[4]{0:T(128)S(1)}, u32[]{:S(2)}, u32[]{:S(2)}) collective-permute-start(f32[4]{0:T(128)S(1)} %add.57), channel_id=1, source_target_pairs={{0,64},{64,0},{128,192},{192,128},{1,65},{65,1},{129,193},{193,129... | collective-permute-start | bytes 56 | tf_op jit(solution)/shard_map/ppermute | solution.py:46
  67.1 2.4 %collective-permute-done.5 = f32[4]{0:T(128)S(1)} collective-permute-done((f32[4]{0:T(128)S(1)}, f32[4]{0:T(128)S(1)}, u32[]{:S(2)}, u32[]{:S(2)}) %collective-permute-start.5) | collective-permute-done | bytes 48 | tf_op jit(solution)/shard_map/ppermute | solution.py:46
  69.5 1.5 %collective-permute-start.6 = (f32[4]{0:T(128)S(1)}, f32[4]{0:T(128)S(1)}, u32[]{:S(2)}, u32[]{:S(2)}) collective-permute-start(f32[4]{0:T(128)S(1)} %add.58), channel_id=1, source_target_pairs={{0,128},{64,192},{128,0},{192,64},{1,129},{65,193},{129,1},{193,65... | collective-permute-start | bytes 56 | tf_op jit(solution)/shard_map/ppermute | solution.py:46
  71.0 3.0 %collective-permute-done.6 = f32[4]{0:T(128)S(1)} collective-permute-done((f32[4]{0:T(128)S(1)}, f32[4]{0:T(128)S(1)}, u32[]{:S(2)}, u32[]{:S(2)}) %collective-permute-start.6) | collective-permute-done | bytes 48 | tf_op jit(solution)/shard_map/ppermute | solution.py:46
  73.9 1.3 %collective-permute-start.7 = (f32[4]{0:T(128)S(1)}, f32[4]{0:T(128)S(1)}, u32[]{:S(2)}, u32[]{:S(2)}) collective-permute-start(f32[4]{0:T(128)S(1)} %add.59), channel_id=1, source_target_pairs={{0,16},{16,0},{32,48},{48,32},{1,17},{17,1},{33,49},{49,33},{2,18}... | collective-permute-start | bytes 56 | tf_op jit(solution)/shard_map/ppermute | solution.py:46
  75.2 2.3 %collective-permute-done.7 = f32[4]{0:T(128)S(1)} collective-permute-done((f32[4]{0:T(128)S(1)}, f32[4]{0:T(128)S(1)}, u32[]{:S(2)}, u32[]{:S(2)}) %collective-permute-start.7) | collective-permute-done | bytes 48 | tf_op jit(solution)/shard_map/ppermute | solution.py:46
  77.8 4.7 %collective-permute-done.8 = f32[4]{0:T(128)S(1)} collective-permute-done((f32[4]{0:T(128)S(1)}, f32[4]{0:T(128)S(1)}, u32[]{:S(2)}, u32[]{:S(2)}) %collective-permute-start.8) | collective-permute-done | bytes 48 | tf_op jit(solution)/shard_map/ppermute | solution.py:46
  82.5 1.8 %collective-permute-start.9 = (f32[4]{0:T(128)S(1)}, f32[4]{0:T(128)S(1)}, u32[]{:S(2)}, u32[]{:S(2)}) collective-permute-start(f32[4]{0:T(128)S(1)} %add.61), channel_id=1, source_target_pairs={{0,4},{4,0},{8,12},{12,8},{1,5},{5,1},{9,13},{13,9},{2,6},{6,2},{1... | collective-permute-start | bytes 56 | tf_op jit(solution)/shard_map/ppermute | solution.py:46
  84.4 1.7 %collective-permute-done.9 = f32[4]{0:T(128)S(1)} collective-permute-done((f32[4]{0:T(128)S(1)}, f32[4]{0:T(128)S(1)}, u32[]{:S(2)}, u32[]{:S(2)}) %collective-permute-start.9) | collective-permute-done | bytes 48 | tf_op jit(solution)/shard_map/ppermute | solution.py:46
  86.1 3.4 %collective-permute-start.10 = (f32[4]{0:T(128)S(1)}, f32[4]{0:T(128)S(1)}, u32[]{:S(2)}, u32[]{:S(2)}) collective-permute-start(f32[4]{0:T(128)S(1)} %add.62), channel_id=1, source_target_pairs={{0,8},{4,12},{8,0},{12,4},{1,9},{5,13},{9,1},{13,5},{2,10},{6,14},... | collective-permute-start | bytes 56 | tf_op jit(solution)/shard_map/ppermute | solution.py:46
  89.5 1.7 %collective-permute-done.10 = f32[4]{0:T(128)S(1)} collective-permute-done((f32[4]{0:T(128)S(1)}, f32[4]{0:T(128)S(1)}, u32[]{:S(2)}, u32[]{:S(2)}) %collective-permute-start.10) | collective-permute-done | bytes 48 | tf_op jit(solution)/shard_map/ppermute | solution.py:46
  91.1 1.9 %collective-permute-start.11 = (f32[4]{0:T(128)S(1)}, f32[4]{0:T(128)S(1)}, u32[]{:S(2)}, u32[]{:S(2)}) collective-permute-start(f32[4]{0:T(128)S(1)} %add.63), channel_id=1, source_target_pairs={{0,2},{2,0},{1,3},{3,1},{4,6},{6,4},{5,7},{7,5},{8,10},{10,8},{9,1... | collective-permute-start | bytes 56 | tf_op jit(solution)/shard_map/ppermute | solution.py:46
  93.0 5.6 %collective-permute-done.11 = f32[4]{0:T(128)S(1)} collective-permute-done((f32[4]{0:T(128)S(1)}, f32[4]{0:T(128)S(1)}, u32[]{:S(2)}, u32[]{:S(2)}) %collective-permute-start.11) | collective-permute-done | bytes 48 | tf_op jit(solution)/shard_map/ppermute | solution.py:46
  103.1 1.2 %multiply_add_fusion = (f32[64,2048]{1,0:T(8,128)}, f32[64,2048]{1,0:T(8,128)}, f32[64,2048]{1,0:T(8,128)}) fusion(f32[64,2048]{1,0:T(8,128)S(1)} %copy-done, f32[]{:T(128)S(6)} %div.7, f32[64,2048]{1,0:T(8,128)S(1)} %copy-done.2, f32[64,2048]{1,0:T(8,128)S(1)} %get-tuple-element.6, f32[]{:T(128)S(6)} %div.6, f32[64,2048]{1,0:T(8,128)S(1)} %copy-done.3), kind=kLoop, calls=%fused_computation.3 | loop fusion | flops 786432 | bytes 3670024 | tf_op jit(solution)/shard_map/add | solution.py:265
  (66 shorter events, 13.5 us)
Async XLA Ops:
  0.6 16.0 %copy-start.4 = (f32[32,32]{1,0:T(8,128)S(1)}, f32[32,32]{1,0:T(8,128)}, u32[]{:S(2)}) copy-start(f32[32,32]{1,0:T(8,128)} %param.33) | copy-start | bytes 12292
  2.6 15.2 %collective-permute-start = (f32[68,16]{1,0:T(8,128)S(1)}, f32[68,16]{1,0:T(8,128)S(1)}, u32[]{:S(2)}, u32[]{:S(2)}) collective-permute-start(f32[68,16]{1,0:T(8,128)S(1)} %copy.34), channel_id=1, source_target_pairs={{0,1},{1,2},{2,3},{3,4},{4,5},{5,6},{6,7},{7,8},{8,9},{9,10},{10,1... | collective-permute-start | bytes 13064 | tf_op jit(solution)/shard_map/ppermute | solution.py:30
  4.5 13.3 %collective-permute-start.1 = (f32[64,16]{1,0:T(8,128)S(1)}, f32[64,16]{1,0:T(8,128)S(1)}, u32[]{:S(2)}, u32[]{:S(2)}) collective-permute-start(f32[64,16]{1,0:T(8,128)S(1)} %get-tuple-element.13), channel_id=1, source_target_pairs={{1,0},{2,1},{3,2},{4,3},{5,4},{6,5},{7,6},{8,7},{9,8},{10,9},{11,1... | collective-permute-start | bytes 12296 | tf_op jit(solution)/shard_map/ppermute | solution.py:30
  16.7 1.1 %copy-start.5 = (f32[4,128]{1,0:T(4,128)S(1)}, f32[4,128]{1,0:T(4,128)}, u32[]{:S(2)}) copy-start(f32[4,128]{1,0:T(4,128)} %param.32) | copy-start | bytes 6148
  16.7 1.2 %copy-start = (f32[64,2048]{1,0:T(8,128)S(1)}, f32[64,2048]{1,0:T(8,128)}, u32[]{:S(2)}) copy-start(f32[64,2048]{1,0:T(8,128)} %param.31) | copy-start | bytes 1572868
  18.2 20.9 %collective-permute-start.3 = (f32[16,2080]{1,0:T(8,128)S(1)}, f32[16,2080]{1,0:T(8,128)S(1)}, u32[]{:S(2)}, u32[]{:S(2)}) collective-permute-start(f32[16,2080]{1,0:T(8,128)S(1)} %get-tuple-element.8), channel_id=1, source_target_pairs={{64,0},{128,64},{192,128},{65,1},{129,65},{193,129},{66,2},{130,66... | collective-permute-start | bytes 399368 | tf_op jit(solution)/shard_map/ppermute | solution.py:30
  22.4 27.1 %collective-permute-start.2 = (f32[17,2080]{1,0:T(8,128)S(1)}, f32[17,2080]{1,0:T(8,128)S(1)}, u32[]{:S(2)}, u32[]{:S(2)}) collective-permute-start(f32[17,2080]{1,0:T(8,128)S(1)} %select_maximum_fusion.2), channel_id=1, source_target_pairs={{0,64},{64,128},{128,192},{1,65},{65,129},{129,193},{2,66},{66,130... | collective-permute-start | bytes 424328 | tf_op jit(solution)/shard_map/ppermute | solution.py:30
  51.2 9.8 %copy-start.1 = (f32[64,2304]{1,0:T(8,128)S(1)}, f32[64,2304]{1,0:T(8,128)}, u32[]{:S(2)}) copy-start(f32[64,2304]{1,0:T(8,128)} %shard_map.292) | copy-start | bytes 1769476
  61.1 1.0 %copy-start.2 = (f32[64,2048]{1,0:T(8,128)S(1)}, f32[64,2048]{1,0:T(8,128)}, u32[]{:S(2)}) copy-start(f32[64,2048]{1,0:T(8,128)} %param.30) | copy-start | bytes 1572868
  62.3 40.8 %copy-start.3 = (f32[64,2048]{1,0:T(8,128)S(1)}, f32[64,2048]{1,0:T(8,128)}, u32[]{:S(2)}) copy-start(f32[64,2048]{1,0:T(8,128)} %param.29) | copy-start | bytes 1572868
  62.6 3.4 %collective-permute-start.4 = (f32[4]{0:T(128)S(1)}, f32[4]{0:T(128)S(1)}, u32[]{:S(2)}, u32[]{:S(2)}) collective-permute-start(f32[4]{0:T(128)S(1)} %maximum_reduce_fusion), channel_id=1, source_target_pairs={{0,1},{1,0},{2,3},{3,2},{4,5},{5,4},{6,7},{7,6},{8,9},{9,8},{10,11... | collective-permute-start | bytes 56 | tf_op jit(solution)/shard_map/ppermute | solution.py:46
  66.0 3.5 %collective-permute-start.5 = (f32[4]{0:T(128)S(1)}, f32[4]{0:T(128)S(1)}, u32[]{:S(2)}, u32[]{:S(2)}) collective-permute-start(f32[4]{0:T(128)S(1)} %add.57), channel_id=1, source_target_pairs={{0,64},{64,0},{128,192},{192,128},{1,65},{65,1},{129,193},{193,129... | collective-permute-start | bytes 56 | tf_op jit(solution)/shard_map/ppermute | solution.py:46
  69.5 4.4 %collective-permute-start.6 = (f32[4]{0:T(128)S(1)}, f32[4]{0:T(128)S(1)}, u32[]{:S(2)}, u32[]{:S(2)}) collective-permute-start(f32[4]{0:T(128)S(1)} %add.58), channel_id=1, source_target_pairs={{0,128},{64,192},{128,0},{192,64},{1,129},{65,193},{129,1},{193,65... | collective-permute-start | bytes 56 | tf_op jit(solution)/shard_map/ppermute | solution.py:46
  73.9 3.5 %collective-permute-start.7 = (f32[4]{0:T(128)S(1)}, f32[4]{0:T(128)S(1)}, u32[]{:S(2)}, u32[]{:S(2)}) collective-permute-start(f32[4]{0:T(128)S(1)} %add.59), channel_id=1, source_target_pairs={{0,16},{16,0},{32,48},{48,32},{1,17},{17,1},{33,49},{49,33},{2,18}... | collective-permute-start | bytes 56 | tf_op jit(solution)/shard_map/ppermute | solution.py:46
  77.5 5.0 %collective-permute-start.8 = (f32[4]{0:T(128)S(1)}, f32[4]{0:T(128)S(1)}, u32[]{:S(2)}, u32[]{:S(2)}) collective-permute-start(f32[4]{0:T(128)S(1)} %add.60), channel_id=1, source_target_pairs={{0,32},{16,48},{32,0},{48,16},{1,33},{17,49},{33,1},{49,17},{2,34}... | collective-permute-start | bytes 56 | tf_op jit(solution)/shard_map/ppermute | solution.py:46
  82.5 3.5 %collective-permute-start.9 = (f32[4]{0:T(128)S(1)}, f32[4]{0:T(128)S(1)}, u32[]{:S(2)}, u32[]{:S(2)}) collective-permute-start(f32[4]{0:T(128)S(1)} %add.61), channel_id=1, source_target_pairs={{0,4},{4,0},{8,12},{12,8},{1,5},{5,1},{9,13},{13,9},{2,6},{6,2},{1... | collective-permute-start | bytes 56 | tf_op jit(solution)/shard_map/ppermute | solution.py:46
  86.1 5.0 %collective-permute-start.10 = (f32[4]{0:T(128)S(1)}, f32[4]{0:T(128)S(1)}, u32[]{:S(2)}, u32[]{:S(2)}) collective-permute-start(f32[4]{0:T(128)S(1)} %add.62), channel_id=1, source_target_pairs={{0,8},{4,12},{8,0},{12,4},{1,9},{5,13},{9,1},{13,5},{2,10},{6,14},... | collective-permute-start | bytes 56 | tf_op jit(solution)/shard_map/ppermute | solution.py:46
  91.1 7.4 %collective-permute-start.11 = (f32[4]{0:T(128)S(1)}, f32[4]{0:T(128)S(1)}, u32[]{:S(2)}, u32[]{:S(2)}) collective-permute-start(f32[4]{0:T(128)S(1)} %add.63), channel_id=1, source_target_pairs={{0,2},{2,0},{1,3},{3,1},{4,6},{6,4},{5,7},{7,5},{8,10},{10,8},{9,1... | collective-permute-start | bytes 56 | tf_op jit(solution)/shard_map/ppermute | solution.py:46

commit v7 on v5

--- a/solution.py
+++ b/solution.py
@@ -153,6 +153,16 @@
     return total + jnp.dot(a[0], b[0], preferred_element_type=jnp.float32)
 
 
+def constant_first_dot(a, b):
+    rows = a[0].shape[0]
+    both = jnp.dot(
+        jnp.concatenate([a[0], a[1]], axis=0), b[0], preferred_element_type=jnp.float32
+    )
+    total = jnp.dot(a[0], b[1], preferred_element_type=jnp.float32)
+    total += both[rows:]
+    return total + both[:rows]
+
+
 def transform_kernel(
     x_ref, mh_ref, ml_ref, nh_ref, nl_ref, fh_ref, fl_ref, gh_ref, gl_ref, fw_ref, ww_ref,
     out_ref, y_ref, e_ref,
@@ -173,17 +183,17 @@
         y = y_ref[here, :]
         weights = ww_ref[:, pl.ds(pl.multiple_of(t * 2 * HALF, 2 * HALF), 2 * HALF)]
         turned = jnp.concatenate([-y[:, HALF:], y[:, :HALF]], axis=1)
-        z = three_pass_dot(forward, split_value(jnp.concatenate([y, turned], axis=0)))
+        z = constant_first_dot(forward, split_value(jnp.concatenate([y, turned], axis=0)))
         spread = jnp.concatenate(
             [jnp.broadcast_to(weights[a : a + 1], (32, 2 * HALF)) for a in range(win_rows)],
             axis=0,
         )
         z = z * freq * spread
         turned = jnp.concatenate([z[:, HALF:], -z[:, :HALF]], axis=1)
-        e_ref[here, :] = three_pass_dot(backward, split_value(jnp.concatenate([z, turned], axis=0)))
+        e_ref[here, :] = constant_first_dot(backward, split_value(jnp.concatenate([z, turned], axis=0)))
         return carry
 
-    lax.fori_loop(0, tiles, one_tile, 0)
+    lax.fori_loop(0, tiles, one_tile, 0, unroll=True)
     pieces = three_pass_dot(split_value(e_ref[...]), (nh_ref[...], nl_ref[...]))
     out_ref[...] = jnp.zeros_like(out_ref)
     for t in range(tiles):
@@ -224,24 +234,34 @@
 
 def per_device(iterate, residual, direction, window_weight, freq_weight):
     height, breadth = direction.shape
-    rim_weight = jnp.pad(window_weight[:, -1:], ((0, 0), (0, 15)))
-    from_left = passed_along(
-        jnp.concatenate([direction[:, -16:], rim_weight], axis=0), COL, 1
-    )
-    from_right = passed_along(direction[:, :16], COL, -1)
-    widened = jnp.concatenate([from_left[:height], direction, from_right], axis=1)
-    weights_wide = jnp.concatenate([from_left[height:, :1], window_weight], axis=1)
-    top_weight = jnp.pad(weights_wide[-1:], ((0, 0), (0, widened.shape[1] - weights_wide.shape[1])))
-    from_above = passed_along(
-        jnp.concatenate([widened[-16:], top_weight], axis=0), "row", 1
-    )
-    from_below = passed_along(widened[:16], "row", -1)
-    region = jnp.concatenate([from_above[:16], widened, from_below], axis=0)
-    weights_all = jnp.concatenate(
-        [from_above[16:, : weights_wide.shape[1]], weights_wide], axis=0
-    )
-    spread = analyze_weigh_synthesize(region, weights_all, freq_weight)
-    synthesized = spread[16 : 16 + height, 16 : 16 + breadth]
+    count = window_weight.shape[1]
+    top_weight = jnp.pad(window_weight[-1:], ((0, 0), (0, breadth - count)))
+    from_above = passed_along(jnp.concatenate([direction[-16:], top_weight], axis=0), "row", 1)
+    from_below = passed_along(direction[:16], "row", -1)
+    tall = jnp.concatenate([from_above[:16], direction, from_below], axis=0)
+    weights_tall = jnp.concatenate([from_above[16:, :count], window_weight], axis=0)
+    middle = analyze_weigh_synthesize(tall, weights_tall[:, :-1], freq_weight)
+    rim_weight = jnp.pad(weights_tall[:, -1:], ((0, 0), (0, 15)))
+    from_left = passed_along(jnp.concatenate([tall[:, -16:], rim_weight], axis=0), COL, 1)
+    from_right = passed_along(tall[:, :16], COL, -1)
+    rows = tall.shape[0]
+    edges = analyze_weigh_synthesize(
+        jnp.concatenate([from_left[:rows], tall[:, :16], tall[:, -16:], from_right], axis=1),
+        jnp.concatenate(
+            [from_left[rows:, :1], jnp.zeros_like(weights_tall[:, :1]), weights_tall[:, -1:]],
+            axis=1,
+        ),
+        freq_weight,
+    )
+    own = slice(16, 16 + height)
+    synthesized = middle[own, :breadth] + jnp.concatenate(
+        [
+            edges[own, 16:32],
+            jnp.zeros((height, breadth - 32), jnp.float32),
+            edges[own, 32:48],
+        ],
+        axis=1,
+    )
     applied = synthesized + damping * direction
     products = jnp.stack(
         [residual * residual, direction * applied, residual * applied, applied * applied]

time: 90.2 us -> 90.4 us (level)
  local copies, waits for them, and re-layouts: 6.42 us -> 10.6 us
  starting transfers between devices: 31.8 us -> 28 us
  other arithmetic: 5.01 us -> 2.71 us
  Pallas kernels: 16.4 us -> 17.6 us
  waiting for transfers between devices: 25.3 us -> 26.5 us
    ppermute x8, starting transfers between devices: 14.2 us -> 10.4 us  [summed_everywhere(): x = x + lax.ppermute(x, axis, [(i, i ^ mask) for i in range(count)])]
    ppermute x8, waiting for transfers between devices: 21.5 us -> 23.7 us  [summed_everywhere(): x = x + lax.ppermute(x, axis, [(i, i ^ mask) for i in range(count)])]
    pallas_call x1 -> x2, Pallas kernels: 16.4 us -> 17.6 us  [analyze_weigh_synthesize(): pl.pallas_call(transform_kernel, out_shape=jax.ShapeDtypeStruct((rows, wi...]
    slice x7 -> x9, local copies, waits for them, and re-layouts: 1.64 us -> 2.79 us  [the longest x1 0.99 us: per_device(): direction[-16:]]
    concatenate x5 -> x6, other arithmetic: 1.99 us -> 0.91 us  [the longest x1 0.75 us: per_device(): jnp.concatenate([from_left[:rows], tall[:, :16], tall[:, -16:], from_righ...]
    another operation x1 -> x2, other arithmetic: 1.33 us -> 0.26 us  [per_device(): jnp.stack([residual * residual, direction * applied, residual * applied,...]
    pad x0 -> x2, local copies, waits for them, and re-layouts: none -> 1.03 us  [the longest x1 1.02 us: analyze_weigh_synthesize(): padded = jnp.pad(region, ((0, 0), (0, wide - cols)))]
    ppermute x4, waiting for transfers between devices: 3.77 us -> 2.75 us  [passed_along(): lax.ppermute(value, axis, [(source, source + steps) for source in range(l...]
  transfers between devices with their start and end apart: 12 -> 12, of which waited for: 11 -> 9; matrix products, arithmetic and copies ran while one was open for 4% -> 6% of each run, Pallas kernels for 0% -> 16%
where the time goes in v7:
time: 90.4 us; the launch traced here: 90 us
  starting transfers between devices  28 us (31%)
  waiting for transfers between devices  26.5 us (29%)
  Pallas kernels  17.6 us (19%)
  local copies, waits for them, and re-layouts  10.6 us (12%)
  between operations  4.55 us (5%)
  other arithmetic  2.71 us (3%)
    ppermute x8, waiting for transfers between devices, summed_everywhere(): x = x + lax.ppermute(x, axis, [(i, i ^ mask) for i in range(count)])  23.7 us
    pallas_call x2, Pallas kernels, analyze_weigh_synthesize(): pl.pallas_call(transform_kernel, out_shape=jax.ShapeDtypeStruct((rows, wi...  17.6 us
    ppermute x4, starting transfers between devices, passed_along(): lax.ppermute(value, axis, [(source, source + steps) for source in range(l...  17.6 us
    ppermute x8, starting transfers between devices, summed_everywhere(): x = x + lax.ppermute(x, axis, [(i, i ^ mask) for i in range(count)])  10.4 us
    ppermute x4, waiting for transfers between devices, passed_along(): lax.ppermute(value, axis, [(source, source + steps) for source in range(l...  2.75 us
  transfers between devices with their start and end apart: 12, of which 9 were waited for; matrix products, arithmetic and copies ran while one was open for 6% of the time, Pallas kernels for 16%

profile of v7, /device:TPU:16, one launch (start us, length us, event | category | flops | bytes accessed | tf_op | source)
XLA Modules:
  0.0 90.0 jit_solution(3825201003773247983)
XLA Ops:
  0.6 1.0 %fusion.3 = (f32[16,2048]{1,0:T(8,128)S(1)}, f32[16,2048]{1,0:T(8,128)S(1)}) fusion(f32[64,2048]{1,0:T(8,128)} %param.23), kind=kLoop, calls=%fused_computation.24 | loop fusion | bytes 524288 | tf_op jit(solution)/shard_map/slice | solution.py:239
  2.3 3.8 %collective-permute-start = (f32[17,2048]{1,0:T(8,128)S(1)}, f32[17,2048]{1,0:T(8,128)S(1)}, u32[]{:S(2)}, u32[]{:S(2)}) collective-permute-start(f32[17,2048]{1,0:T(8,128)S(1)} %select_maximum_fusion), channel_id=1, source_target_pairs={{0,64},{64,128},{128,192},{1,65},{65,129},{129,193},{2,66},{66,130... | collective-permute-start | bytes 417800 | tf_op jit(solution)/shard_map/ppermute | solution.py:30
  6.2 1.3 %collective-permute-start.1 = (f32[16,2048]{1,0:T(8,128)S(1)}, f32[16,2048]{1,0:T(8,128)S(1)}, u32[]{:S(2)}, u32[]{:S(2)}) collective-permute-start(f32[16,2048]{1,0:T(8,128)S(1)} %get-tuple-element.14), channel_id=1, source_target_pairs={{64,0},{128,64},{192,128},{65,1},{129,65},{193,129},{66,2},{130,66... | collective-permute-start | bytes 393224 | tf_op jit(solution)/shard_map/ppermute | solution.py:30
  9.1 1.2 %reshape.30.fw_ref = f32[160,512]{1,0:T(8,128)} reshape(f32[5,32,2,8,32]{4,3,2,1,0:T(8,128)S(1)} %broadcast_in_dim.10) | data formatting | bytes 655360 | tf_op jit(solution)/shard_map/reshape | solution.py:216
  10.4 2.7 %collective-permute-done.1 = f32[16,2048]{1,0:T(8,128)S(1)} collective-permute-done((f32[16,2048]{1,0:T(8,128)S(1)}, f32[16,2048]{1,0:T(8,128)S(1)}, u32[]{:S(2)}, u32[]{:S(2)}) %collective-permute-start.1) | collective-permute-done | bytes 131104 | tf_op jit(solution)/shard_map/ppermute | solution.py:30
  13.3 1.0 %pad.25.x_ref = f32[96,2176]{1,0:T(8,128)} pad(f32[96,2048]{1,0:T(8,128)S(1)} %pad_maximum_fusion, f32[]{:T(128)} %constant.12.clone.1), padding=0_0x0_128 | pad | bytes 1622020 | tf_op jit(solution)/shard_map/jit(_pad)/pad | solution.py:209
  14.5 1.9 %collective-permute-start.2 = (f32[101,16]{1,0:T(8,128)S(1)}, f32[101,16]{1,0:T(8,128)S(1)}, u32[]{:S(2)}, u32[]{:S(2)}) collective-permute-start(f32[101,16]{1,0:T(8,128)S(1)} %select_maximum_fusion.4), channel_id=1, source_target_pairs={{0,1},{1,2},{2,3},{3,4},{4,5},{5,6},{6,7},{7,8},{8,9},{9,10},{10,1... | collective-permute-start | bytes 19400 | tf_op jit(solution)/shard_map/ppermute | solution.py:30
  16.4 10.6 %collective-permute-start.3 = (f32[96,16]{1,0:T(8,128)S(1)}, f32[96,16]{1,0:T(8,128)S(1)}, u32[]{:S(2)}, u32[]{:S(2)}) collective-permute-start(f32[96,16]{1,0:T(8,128)S(1)} %get-tuple-element.8), channel_id=1, source_target_pairs={{1,0},{2,1},{3,2},{4,3},{5,4},{6,5},{7,6},{8,7},{9,8},{10,9},{11,1... | collective-permute-start | bytes 18440 | tf_op jit(solution)/shard_map/ppermute | solution.py:30
  27.2 1.0 %reshape.31.ww_ref = f32[5,8192]{1,0:T(8,128)} reshape(f32[5,16,2,8,32]{4,3,2,1,0:T(8,128)S(1)} %broadcast_in_dim.11) | data formatting | bytes 327680 | tf_op jit(solution)/shard_map/reshape | solution.py:220
  28.2 14.4 %shard_map.220 = f32[96,2176]{1,0:T(8,128)} custom-call(f32[96,2176]{1,0:T(8,128)} %pad.25.x_ref, bf16[256,512]{1,0:T(8,128)(2,1)} %constant.29.clone.mh_ref, bf16[256,512]{1,0:T(8,128)(2,1)} %constant.30.clone.ml_ref, bf16[512,256]{1,0:T(8,128)(2,1)} %constant.31.clone.nh_ref, bf16[512,256]{1,0:T(8,128)(2,1)} %constant.32.clone.nl_ref, ...), custom_call_target="tpu_custom_call" | custom-call | tf_op jit(solution)/shard_map/pallas_call | solution.py:222
  44.3 3.2 %shard_map.221 = f32[96,256]{1,0:T(8,128)} custom-call(f32[96,256]{1,0:T(8,128)} %select_maximum_fusion.1.x_ref, bf16[256,512]{1,0:T(8,128)(2,1)} %constant.29.clone.mh_ref, bf16[256,512]{1,0:T(8,128)(2,1)} %constant.30.clone.ml_ref, bf16[512,256]{1,0:T(8,128)(2,1)} %constant.31.clone.nh_ref, bf16[512,256]{1,0:T(8,128)(2,1)} %constant.32.clone.nl_ref, ...), custom_call_target="tpu_custom_call" | custom-call | tf_op jit(solution)/shard_map/pallas_call | solution.py:222
  50.5 1.1 %collective-permute-done.4 = f32[4]{0:T(128)S(1)} collective-permute-done((f32[4]{0:T(128)S(1)}, f32[4]{0:T(128)S(1)}, u32[]{:S(2)}, u32[]{:S(2)}) %collective-permute-start.4) | collective-permute-done | bytes 48 | tf_op jit(solution)/shard_map/ppermute | solution.py:46
  51.6 1.9 %collective-permute-start.5 = (f32[4]{0:T(128)S(1)}, f32[4]{0:T(128)S(1)}, u32[]{:S(2)}, u32[]{:S(2)}) collective-permute-start(f32[4]{0:T(128)S(1)} %add.51), channel_id=1, source_target_pairs={{0,64},{64,0},{128,192},{192,128},{1,65},{65,1},{129,193},{193,129... | collective-permute-start | bytes 56 | tf_op jit(solution)/shard_map/ppermute | solution.py:46
  53.5 1.6 %collective-permute-done.5 = f32[4]{0:T(128)S(1)} collective-permute-done((f32[4]{0:T(128)S(1)}, f32[4]{0:T(128)S(1)}, u32[]{:S(2)}, u32[]{:S(2)}) %collective-permute-start.5) | collective-permute-done | bytes 48 | tf_op jit(solution)/shard_map/ppermute | solution.py:46
  55.1 3.1 %collective-permute-start.6 = (f32[4]{0:T(128)S(1)}, f32[4]{0:T(128)S(1)}, u32[]{:S(2)}, u32[]{:S(2)}) collective-permute-start(f32[4]{0:T(128)S(1)} %add.52), channel_id=1, source_target_pairs={{0,128},{64,192},{128,0},{192,64},{1,129},{65,193},{129,1},{193,65... | collective-permute-start | bytes 56 | tf_op jit(solution)/shard_map/ppermute | solution.py:46
  58.2 1.5 %collective-permute-done.6 = f32[4]{0:T(128)S(1)} collective-permute-done((f32[4]{0:T(128)S(1)}, f32[4]{0:T(128)S(1)}, u32[]{:S(2)}, u32[]{:S(2)}) %collective-permute-start.6) | collective-permute-done | bytes 48 | tf_op jit(solution)/shard_map/ppermute | solution.py:46
  59.8 1.3 %collective-permute-start.7 = (f32[4]{0:T(128)S(1)}, f32[4]{0:T(128)S(1)}, u32[]{:S(2)}, u32[]{:S(2)}) collective-permute-start(f32[4]{0:T(128)S(1)} %add.53), channel_id=1, source_target_pairs={{0,16},{16,0},{32,48},{48,32},{1,17},{17,1},{33,49},{49,33},{2,18}... | collective-permute-start | bytes 56 | tf_op jit(solution)/shard_map/ppermute | solution.py:46
  61.0 2.3 %collective-permute-done.7 = f32[4]{0:T(128)S(1)} collective-permute-done((f32[4]{0:T(128)S(1)}, f32[4]{0:T(128)S(1)}, u32[]{:S(2)}, u32[]{:S(2)}) %collective-permute-start.7) | collective-permute-done | bytes 48 | tf_op jit(solution)/shard_map/ppermute | solution.py:46
  63.3 5.0 %collective-permute-done.8 = f32[4]{0:T(128)S(1)} collective-permute-done((f32[4]{0:T(128)S(1)}, f32[4]{0:T(128)S(1)}, u32[]{:S(2)}, u32[]{:S(2)}) %collective-permute-start.8) | collective-permute-done | bytes 48 | tf_op jit(solution)/shard_map/ppermute | solution.py:46
  68.4 3.5 %collective-permute-done.9 = f32[4]{0:T(128)S(1)} collective-permute-done((f32[4]{0:T(128)S(1)}, f32[4]{0:T(128)S(1)}, u32[]{:S(2)}, u32[]{:S(2)}) %collective-permute-start.9) | collective-permute-done | bytes 48 | tf_op jit(solution)/shard_map/ppermute | solution.py:46
  72.8 4.1 %collective-permute-done.10 = f32[4]{0:T(128)S(1)} collective-permute-done((f32[4]{0:T(128)S(1)}, f32[4]{0:T(128)S(1)}, u32[]{:S(2)}, u32[]{:S(2)}) %collective-permute-start.10) | collective-permute-done | bytes 48 | tf_op jit(solution)/shard_map/ppermute | solution.py:46
  76.9 3.0 %collective-permute-start.11 = (f32[4]{0:T(128)S(1)}, f32[4]{0:T(128)S(1)}, u32[]{:S(2)}, u32[]{:S(2)}) collective-permute-start(f32[4]{0:T(128)S(1)} %add.57), channel_id=1, source_target_pairs={{0,2},{2,0},{1,3},{3,1},{4,6},{6,4},{5,7},{7,5},{8,10},{10,8},{9,1... | collective-permute-start | bytes 56 | tf_op jit(solution)/shard_map/ppermute | solution.py:46
  79.9 4.5 %collective-permute-done.11 = f32[4]{0:T(128)S(1)} collective-permute-done((f32[4]{0:T(128)S(1)}, f32[4]{0:T(128)S(1)}, u32[]{:S(2)}, u32[]{:S(2)}) %collective-permute-start.11) | collective-permute-done | bytes 48 | tf_op jit(solution)/shard_map/ppermute | solution.py:46
  88.7 1.2 %multiply_add_fusion = (f32[64,2048]{1,0:T(8,128)}, f32[64,2048]{1,0:T(8,128)}, f32[64,2048]{1,0:T(8,128)}) fusion(f32[64,2048]{1,0:T(8,128)S(1)} %copy-done, f32[]{:T(128)S(6)} %div.7, f32[64,2048]{1,0:T(8,128)S(1)} %copy-done.2, f32[64,2048]{1,0:T(8,128)S(1)} %get-tuple-element.6, f32[]{:T(128)S(6)} %div.6, f32[64,2048]{1,0:T(8,128)S(1)} %copy-done.3), kind=kLoop, calls=%fused_computation.4 | loop fusion | flops 786432 | bytes 3670024 | tf_op jit(solution)/shard_map/add | solution.py:275
  (56 shorter events, 9.0 us)
Async XLA Ops:
  2.3 8.1 %collective-permute-start = (f32[17,2048]{1,0:T(8,128)S(1)}, f32[17,2048]{1,0:T(8,128)S(1)}, u32[]{:S(2)}, u32[]{:S(2)}) collective-permute-start(f32[17,2048]{1,0:T(8,128)S(1)} %select_maximum_fusion), channel_id=1, source_target_pairs={{0,64},{64,128},{128,192},{1,65},{65,129},{129,193},{2,66},{66,130... | collective-permute-start | bytes 417800 | tf_op jit(solution)/shard_map/ppermute | solution.py:30
  6.2 7.0 %collective-permute-start.1 = (f32[16,2048]{1,0:T(8,128)S(1)}, f32[16,2048]{1,0:T(8,128)S(1)}, u32[]{:S(2)}, u32[]{:S(2)}) collective-permute-start(f32[16,2048]{1,0:T(8,128)S(1)} %get-tuple-element.14), channel_id=1, source_target_pairs={{64,0},{128,64},{192,128},{65,1},{129,65},{193,129},{66,2},{130,66... | collective-permute-start | bytes 393224 | tf_op jit(solution)/shard_map/ppermute | solution.py:30
  8.2 5.0 %copy-start = (f32[64,2048]{1,0:T(8,128)S(1)}, f32[64,2048]{1,0:T(8,128)}, u32[]{:S(2)}) copy-start(f32[64,2048]{1,0:T(8,128)} %param.23) | copy-start | bytes 1572868
  10.4 4.0 %copy-start.4 = (f32[4,128]{1,0:T(4,128)S(1)}, f32[4,128]{1,0:T(4,128)}, u32[]{:S(2)}) copy-start(f32[4,128]{1,0:T(4,128)} %param.24) | copy-start | bytes 6148
  13.3 13.8 %copy-start.5 = (pred[16,8]{1,0:T(8,128)(4,1)S(1)}, pred[16,8]{1,0:T(8,128)(4,1)}, u32[]{:S(2)}) copy-start(pred[16,8]{1,0:T(8,128)(4,1)} %constant.13.clone.1) | copy-start | bytes 388
  14.5 28.2 %collective-permute-start.2 = (f32[101,16]{1,0:T(8,128)S(1)}, f32[101,16]{1,0:T(8,128)S(1)}, u32[]{:S(2)}, u32[]{:S(2)}) collective-permute-start(f32[101,16]{1,0:T(8,128)S(1)} %select_maximum_fusion.4), channel_id=1, source_target_pairs={{0,1},{1,2},{2,3},{3,4},{4,5},{5,6},{6,7},{7,8},{8,9},{9,10},{10,1... | collective-permute-start | bytes 19400 | tf_op jit(solution)/shard_map/ppermute | solution.py:30
  16.4 27.1 %collective-permute-start.3 = (f32[96,16]{1,0:T(8,128)S(1)}, f32[96,16]{1,0:T(8,128)S(1)}, u32[]{:S(2)}, u32[]{:S(2)}) collective-permute-start(f32[96,16]{1,0:T(8,128)S(1)} %get-tuple-element.8), channel_id=1, source_target_pairs={{1,0},{2,1},{3,2},{4,3},{5,4},{6,5},{7,6},{8,7},{9,8},{10,9},{11,1... | collective-permute-start | bytes 18440 | tf_op jit(solution)/shard_map/ppermute | solution.py:30
  47.5 1.3 %copy-start.1 = (f32[96,2176]{1,0:T(8,128)S(1)}, f32[96,2176]{1,0:T(8,128)}, u32[]{:S(2)}) copy-start(f32[96,2176]{1,0:T(8,128)} %shard_map.220) | copy-start | bytes 2506756
  48.7 1.0 %copy-start.2 = (f32[64,2048]{1,0:T(8,128)S(1)}, f32[64,2048]{1,0:T(8,128)}, u32[]{:S(2)}) copy-start(f32[64,2048]{1,0:T(8,128)} %param.22) | copy-start | bytes 1572868
  50.0 38.7 %copy-start.3 = (f32[64,2048]{1,0:T(8,128)S(1)}, f32[64,2048]{1,0:T(8,128)}, u32[]{:S(2)}) copy-start(f32[64,2048]{1,0:T(8,128)} %param.21) | copy-start | bytes 1572868
  50.2 1.3 %collective-permute-start.4 = (f32[4]{0:T(128)S(1)}, f32[4]{0:T(128)S(1)}, u32[]{:S(2)}, u32[]{:S(2)}) collective-permute-start(f32[4]{0:T(128)S(1)} %maximum_reduce_fusion), channel_id=1, source_target_pairs={{0,1},{1,0},{2,3},{3,2},{4,5},{5,4},{6,7},{7,6},{8,9},{9,8},{10,11... | collective-permute-start | bytes 56 | tf_op jit(solution)/shard_map/ppermute | solution.py:46
  51.6 3.5 %collective-permute-start.5 = (f32[4]{0:T(128)S(1)}, f32[4]{0:T(128)S(1)}, u32[]{:S(2)}, u32[]{:S(2)}) collective-permute-start(f32[4]{0:T(128)S(1)} %add.51), channel_id=1, source_target_pairs={{0,64},{64,0},{128,192},{192,128},{1,65},{65,1},{129,193},{193,129... | collective-permute-start | bytes 56 | tf_op jit(solution)/shard_map/ppermute | solution.py:46
  55.1 4.6 %collective-permute-start.6 = (f32[4]{0:T(128)S(1)}, f32[4]{0:T(128)S(1)}, u32[]{:S(2)}, u32[]{:S(2)}) collective-permute-start(f32[4]{0:T(128)S(1)} %add.52), channel_id=1, source_target_pairs={{0,128},{64,192},{128,0},{192,64},{1,129},{65,193},{129,1},{193,65... | collective-permute-start | bytes 56 | tf_op jit(solution)/shard_map/ppermute | solution.py:46
  59.8 3.5 %collective-permute-start.7 = (f32[4]{0:T(128)S(1)}, f32[4]{0:T(128)S(1)}, u32[]{:S(2)}, u32[]{:S(2)}) collective-permute-start(f32[4]{0:T(128)S(1)} %add.53), channel_id=1, source_target_pairs={{0,16},{16,0},{32,48},{48,32},{1,17},{17,1},{33,49},{49,33},{2,18}... | collective-permute-start | bytes 56 | tf_op jit(solution)/shard_map/ppermute | solution.py:46
  63.3 5.0 %collective-permute-start.8 = (f32[4]{0:T(128)S(1)}, f32[4]{0:T(128)S(1)}, u32[]{:S(2)}, u32[]{:S(2)}) collective-permute-start(f32[4]{0:T(128)S(1)} %add.54), channel_id=1, source_target_pairs={{0,32},{16,48},{32,0},{48,16},{1,33},{17,49},{33,1},{49,17},{2,34}... | collective-permute-start | bytes 56 | tf_op jit(solution)/shard_map/ppermute | solution.py:46
  68.4 3.5 %collective-permute-start.9 = (f32[4]{0:T(128)S(1)}, f32[4]{0:T(128)S(1)}, u32[]{:S(2)}, u32[]{:S(2)}) collective-permute-start(f32[4]{0:T(128)S(1)} %add.55), channel_id=1, source_target_pairs={{0,4},{4,0},{8,12},{12,8},{1,5},{5,1},{9,13},{13,9},{2,6},{6,2},{1... | collective-permute-start | bytes 56 | tf_op jit(solution)/shard_map/ppermute | solution.py:46
  71.9 5.0 %collective-permute-start.10 = (f32[4]{0:T(128)S(1)}, f32[4]{0:T(128)S(1)}, u32[]{:S(2)}, u32[]{:S(2)}) collective-permute-start(f32[4]{0:T(128)S(1)} %add.56), channel_id=1, source_target_pairs={{0,8},{4,12},{8,0},{12,4},{1,9},{5,13},{9,1},{13,5},{2,10},{6,14},... | collective-permute-start | bytes 56 | tf_op jit(solution)/shard_map/ppermute | solution.py:46
  76.9 7.4 %collective-permute-start.11 = (f32[4]{0:T(128)S(1)}, f32[4]{0:T(128)S(1)}, u32[]{:S(2)}, u32[]{:S(2)}) collective-permute-start(f32[4]{0:T(128)S(1)} %add.57), channel_id=1, source_target_pairs={{0,2},{2,0},{1,3},{3,1},{4,6},{6,4},{5,7},{7,5},{8,10},{10,8},{9,1... | collective-permute-start | bytes 56 | tf_op jit(solution)/shard_map/ppermute | solution.py:46

commit v8 on v5

--- a/solution.py
+++ b/solution.py
@@ -133,7 +133,7 @@
     imag = imag.reshape(win_rows * 32, blocks * 16)
     forward = np.concatenate([real, imag], axis=1)
     backward = np.concatenate([real.T, imag.T], axis=1)
-    return [columns, np.ascontiguousarray(columns.T), forward, backward]
+    return [columns, forward, backward]
 
 
 def split_constant(table):
@@ -153,8 +153,26 @@
     return total + jnp.dot(a[0], b[0], preferred_element_type=jnp.float32)
 
 
+def transposed_dot(a, b):
+    def one(x, y):
+        return lax.dot_general(
+            x, y, (((1,), (1,)), ((), ())), preferred_element_type=jnp.float32
+        )
+    return one(a[0], b[1]) + one(a[1], b[0]) + one(a[0], b[0])
+
+
+def constant_first_dot(a, b):
+    rows = a[0].shape[0]
+    both = jnp.dot(
+        jnp.concatenate([a[0], a[1]], axis=0), b[0], preferred_element_type=jnp.float32
+    )
+    total = jnp.dot(a[0], b[1], preferred_element_type=jnp.float32)
+    total += both[rows:]
+    return total + both[:rows]
+
+
 def transform_kernel(
-    x_ref, mh_ref, ml_ref, nh_ref, nl_ref, fh_ref, fl_ref, gh_ref, gl_ref, fw_ref, ww_ref,
+    x_ref, mh_ref, ml_ref, fh_ref, fl_ref, gh_ref, gl_ref, fw_ref, ww_ref,
     out_ref, y_ref, e_ref,
 ):
     rows = x_ref.shape[0]
@@ -173,18 +191,18 @@
         y = y_ref[here, :]
         weights = ww_ref[:, pl.ds(pl.multiple_of(t * 2 * HALF, 2 * HALF), 2 * HALF)]
         turned = jnp.concatenate([-y[:, HALF:], y[:, :HALF]], axis=1)
-        z = three_pass_dot(forward, split_value(jnp.concatenate([y, turned], axis=0)))
+        z = constant_first_dot(forward, split_value(jnp.concatenate([y, turned], axis=0)))
         spread = jnp.concatenate(
             [jnp.broadcast_to(weights[a : a + 1], (32, 2 * HALF)) for a in range(win_rows)],
             axis=0,
         )
         z = z * freq * spread
         turned = jnp.concatenate([z[:, HALF:], -z[:, :HALF]], axis=1)
-        e_ref[here, :] = three_pass_dot(backward, split_value(jnp.concatenate([z, turned], axis=0)))
+        e_ref[here, :] = constant_first_dot(backward, split_value(jnp.concatenate([z, turned], axis=0)))
         return carry
 
-    lax.fori_loop(0, tiles, one_tile, 0)
-    pieces = three_pass_dot(split_value(e_ref[...]), (nh_ref[...], nl_ref[...]))
+    lax.fori_loop(0, tiles, one_tile, 0, unroll=True)
+    pieces = transposed_dot(split_value(e_ref[...]), (mh_ref[...], ml_ref[...]))
     out_ref[...] = jnp.zeros_like(out_ref)
     for t in range(tiles):
         out_ref[:, t * LANES : (t + 2) * LANES] += pieces[t * rows : (t + 1) * rows]
@@ -212,7 +230,7 @@
     out = pl.pallas_call(
         transform_kernel,
         out_shape=jax.ShapeDtypeStruct((rows, wide), jnp.float32),
-        in_specs=[vmem] * 11,
+        in_specs=[vmem] * 9,
         out_specs=vmem,
         scratch_shapes=[
             pltpu.VMEM((tiles * rows, 2 * HALF), jnp.float32),

time: 90.2 us -> 89.1 us (0.988)
  Pallas kernels: 16.4 us -> 15.2 us
    pallas_call x1, Pallas kernels: 16.4 us -> 15.2 us  [analyze_weigh_synthesize(): pl.pallas_call(transform_kernel, out_shape=jax.ShapeDtypeStruct((rows, wi...]
where the time goes in v8:
time: 89.1 us; the launch traced here: 88.6 us
  starting transfers between devices  32 us (36%)
  waiting for transfers between devices  25.3 us (28%)
  Pallas kernels  15.2 us (17%)
  local copies, waits for them, and re-layouts  6.42 us (7%)
  other arithmetic  5.01 us (6%)
  between operations  4.74 us (5%)
    ppermute x8, waiting for transfers between devices, summed_everywhere(): x = x + lax.ppermute(x, axis, [(i, i ^ mask) for i in range(count)])  21.5 us
    ppermute x4, starting transfers between devices, passed_along(): lax.ppermute(value, axis, [(source, source + steps) for source in range(l...  17.6 us
    pallas_call x1, Pallas kernels, analyze_weigh_synthesize(): pl.pallas_call(transform_kernel, out_shape=jax.ShapeDtypeStruct((rows, wi...  15.2 us
    ppermute x8, starting transfers between devices, summed_everywhere(): x = x + lax.ppermute(x, axis, [(i, i ^ mask) for i in range(count)])  14.4 us
    ppermute x4, waiting for transfers between devices, passed_along(): lax.ppermute(value, axis, [(source, source + steps) for source in range(l...  3.77 us
  transfers between devices with their start and end apart: 12, of which 11 were waited for; matrix products, arithmetic and copies ran while one was open for 4% of the time, Pallas kernels for 0%

profile of v8, /device:TPU:16, one launch (start us, length us, event | category | flops | bytes accessed | tf_op | source)
XLA Modules:
  0.0 88.6 jit_solution(3164045641085961242)
XLA Ops:
  2.6 1.9 %collective-permute-start = (f32[68,16]{1,0:T(8,128)S(1)}, f32[68,16]{1,0:T(8,128)S(1)}, u32[]{:S(2)}, u32[]{:S(2)}) collective-permute-start(f32[68,16]{1,0:T(8,128)S(1)} %copy.16), channel_id=1, source_target_pairs={{0,1},{1,2},{2,3},{3,4},{4,5},{5,6},{6,7},{7,8},{8,9},{9,10},{10,1... | collective-permute-start | bytes 13064 | tf_op jit(solution)/shard_map/ppermute | solution.py:30
  4.5 10.6 %collective-permute-start.1 = (f32[64,16]{1,0:T(8,128)S(1)}, f32[64,16]{1,0:T(8,128)S(1)}, u32[]{:S(2)}, u32[]{:S(2)}) collective-permute-start(f32[64,16]{1,0:T(8,128)S(1)} %get-tuple-element.12), channel_id=1, source_target_pairs={{1,0},{2,1},{3,2},{4,3},{5,4},{6,5},{7,6},{8,7},{9,8},{10,9},{11,1... | collective-permute-start | bytes 12296 | tf_op jit(solution)/shard_map/ppermute | solution.py:30
  16.7 1.4 %concatenate.19 = f32[64,2080]{1,0:T(8,128)S(1)} concatenate(f32[64,16]{1,0:T(8,128)S(1)} %slice.62, f32[64,2048]{1,0:T(8,128)} %param.13, f32[64,16]{1,0:T(8,128)S(1)} %collective-permute-done.1), dimensions={1} | concatenate | bytes 1064960 | tf_op jit(solution)/shard_map/concatenate | solution.py:250
  18.1 3.8 %collective-permute-start.2 = (f32[17,2080]{1,0:T(8,128)S(1)}, f32[17,2080]{1,0:T(8,128)S(1)}, u32[]{:S(2)}, u32[]{:S(2)}) collective-permute-start(f32[17,2080]{1,0:T(8,128)S(1)} %pad_maximum_fusion), channel_id=1, source_target_pairs={{0,64},{64,128},{128,192},{1,65},{65,129},{129,193},{2,66},{66,130... | collective-permute-start | bytes 424328 | tf_op jit(solution)/shard_map/ppermute | solution.py:30
  21.9 1.3 %collective-permute-start.3 = (f32[16,2080]{1,0:T(8,128)S(1)}, f32[16,2080]{1,0:T(8,128)S(1)}, u32[]{:S(2)}, u32[]{:S(2)}) collective-permute-start(f32[16,2080]{1,0:T(8,128)S(1)} %get-tuple-element.9), channel_id=1, source_target_pairs={{64,0},{128,64},{192,128},{65,1},{129,65},{193,129},{66,2},{130,66... | collective-permute-start | bytes 399368 | tf_op jit(solution)/shard_map/ppermute | solution.py:30
  23.3 1.2 %reshape.16.fw_ref = f32[160,512]{1,0:T(8,128)} reshape(f32[5,32,2,8,32]{4,3,2,1,0:T(8,128)S(1)} %broadcast_in_dim.12) | data formatting | bytes 655360 | tf_op jit(solution)/shard_map/reshape | solution.py:224
  26.5 2.3 %collective-permute-done.3 = f32[16,2080]{1,0:T(8,128)S(1)} collective-permute-done((f32[16,2080]{1,0:T(8,128)S(1)}, f32[16,2080]{1,0:T(8,128)S(1)}, u32[]{:S(2)}, u32[]{:S(2)}) %collective-permute-start.3) | collective-permute-done | bytes 133152 | tf_op jit(solution)/shard_map/ppermute | solution.py:30
  29.9 15.2 %shard_map.130 = f32[96,2304]{1,0:T(8,128)} custom-call(f32[96,2304]{1,0:T(8,128)} %select_maximum_fusion.x_ref, bf16[256,512]{1,0:T(8,128)(2,1)} %constant.20.clone.mh_ref, bf16[256,512]{1,0:T(8,128)(2,1)} %constant.21.clone.ml_ref, bf16[160,192]{1,0:T(8,128)(2,1)} %constant.22.clone.fh_ref, bf16[160,192]{1,0:T(8,128)(2,1)} %constant.23.clone.fl_ref, ...), custom_call_target="tpu_custom_call" | custom-call | tf_op jit(solution)/shard_map/pallas_call | solution.py:230
  45.1 1.3 %multiply_bitcast_fusion.2 = (f32[1,64,2048]{2,1,0:T(8,128)S(1)}, f32[1,64,2048]{2,1,0:T(8,128)S(1)}, f32[1,64,2048]{2,1,0:T(8,128)S(1)}, f32[1,64,2048]{2,1,0:T(8,128)S(1)}) fusion(f32[64,2048]{1,0:T(8,128)S(1)} %copy-done, f32[96,2304]{1,0:T(8,128)} %shard_map.130, f32[64,2048]{1,0:T(8,128)S(1)} %copy-done.2), kind=kLoop, calls=%fused_computation.10 | loop fusion | flops 786432 | bytes 3670016 | tf_op jit(solution)/shard_map/stack | solution.py:264
  46.8 2.3 %collective-permute-start.4 = (f32[4]{0:T(128)S(1)}, f32[4]{0:T(128)S(1)}, u32[]{:S(2)}, u32[]{:S(2)}) collective-permute-start(f32[4]{0:T(128)S(1)} %maximum_reduce_fusion), channel_id=1, source_target_pairs={{0,1},{1,0},{2,3},{3,2},{4,5},{5,4},{6,7},{7,6},{8,9},{9,8},{10,11... | collective-permute-start | bytes 56 | tf_op jit(solution)/shard_map/ppermute | solution.py:46
  49.9 1.3 %collective-permute-start.5 = (f32[4]{0:T(128)S(1)}, f32[4]{0:T(128)S(1)}, u32[]{:S(2)}, u32[]{:S(2)}) collective-permute-start(f32[4]{0:T(128)S(1)} %add.45), channel_id=1, source_target_pairs={{0,64},{64,0},{128,192},{192,128},{1,65},{65,1},{129,193},{193,129... | collective-permute-start | bytes 56 | tf_op jit(solution)/shard_map/ppermute | solution.py:46
  51.2 2.3 %collective-permute-done.5 = f32[4]{0:T(128)S(1)} collective-permute-done((f32[4]{0:T(128)S(1)}, f32[4]{0:T(128)S(1)}, u32[]{:S(2)}, u32[]{:S(2)}) %collective-permute-start.5) | collective-permute-done | bytes 48 | tf_op jit(solution)/shard_map/ppermute | solution.py:46
  53.4 3.1 %collective-permute-start.6 = (f32[4]{0:T(128)S(1)}, f32[4]{0:T(128)S(1)}, u32[]{:S(2)}, u32[]{:S(2)}) collective-permute-start(f32[4]{0:T(128)S(1)} %add.46), channel_id=1, source_target_pairs={{0,128},{64,192},{128,0},{192,64},{1,129},{65,193},{129,1},{193,65... | collective-permute-start | bytes 56 | tf_op jit(solution)/shard_map/ppermute | solution.py:46
  56.5 1.5 %collective-permute-done.6 = f32[4]{0:T(128)S(1)} collective-permute-done((f32[4]{0:T(128)S(1)}, f32[4]{0:T(128)S(1)}, u32[]{:S(2)}, u32[]{:S(2)}) %collective-permute-start.6) | collective-permute-done | bytes 48 | tf_op jit(solution)/shard_map/ppermute | solution.py:46
  58.0 1.3 %collective-permute-start.7 = (f32[4]{0:T(128)S(1)}, f32[4]{0:T(128)S(1)}, u32[]{:S(2)}, u32[]{:S(2)}) collective-permute-start(f32[4]{0:T(128)S(1)} %add.47), channel_id=1, source_target_pairs={{0,16},{16,0},{32,48},{48,32},{1,17},{17,1},{33,49},{49,33},{2,18}... | collective-permute-start | bytes 56 | tf_op jit(solution)/shard_map/ppermute | solution.py:46
  59.3 2.3 %collective-permute-done.7 = f32[4]{0:T(128)S(1)} collective-permute-done((f32[4]{0:T(128)S(1)}, f32[4]{0:T(128)S(1)}, u32[]{:S(2)}, u32[]{:S(2)}) %collective-permute-start.7) | collective-permute-done | bytes 48 | tf_op jit(solution)/shard_map/ppermute | solution.py:46
  61.6 5.0 %collective-permute-done.8 = f32[4]{0:T(128)S(1)} collective-permute-done((f32[4]{0:T(128)S(1)}, f32[4]{0:T(128)S(1)}, u32[]{:S(2)}, u32[]{:S(2)}) %collective-permute-start.8) | collective-permute-done | bytes 48 | tf_op jit(solution)/shard_map/ppermute | solution.py:46
  66.6 1.2 %collective-permute-start.9 = (f32[4]{0:T(128)S(1)}, f32[4]{0:T(128)S(1)}, u32[]{:S(2)}, u32[]{:S(2)}) collective-permute-start(f32[4]{0:T(128)S(1)} %add.49), channel_id=1, source_target_pairs={{0,4},{4,0},{8,12},{12,8},{1,5},{5,1},{9,13},{13,9},{2,6},{6,2},{1... | collective-permute-start | bytes 56 | tf_op jit(solution)/shard_map/ppermute | solution.py:46
  67.8 2.3 %collective-permute-done.9 = f32[4]{0:T(128)S(1)} collective-permute-done((f32[4]{0:T(128)S(1)}, f32[4]{0:T(128)S(1)}, u32[]{:S(2)}, u32[]{:S(2)}) %collective-permute-start.9) | collective-permute-done | bytes 48 | tf_op jit(solution)/shard_map/ppermute | solution.py:46
  70.2 2.7 %collective-permute-start.10 = (f32[4]{0:T(128)S(1)}, f32[4]{0:T(128)S(1)}, u32[]{:S(2)}, u32[]{:S(2)}) collective-permute-start(f32[4]{0:T(128)S(1)} %add.50), channel_id=1, source_target_pairs={{0,8},{4,12},{8,0},{12,4},{1,9},{5,13},{9,1},{13,5},{2,10},{6,14},... | collective-permute-start | bytes 56 | tf_op jit(solution)/shard_map/ppermute | solution.py:46
  72.9 2.3 %collective-permute-done.10 = f32[4]{0:T(128)S(1)} collective-permute-done((f32[4]{0:T(128)S(1)}, f32[4]{0:T(128)S(1)}, u32[]{:S(2)}, u32[]{:S(2)}) %collective-permute-start.10) | collective-permute-done | bytes 48 | tf_op jit(solution)/shard_map/ppermute | solution.py:46
  75.2 2.4 %collective-permute-start.11 = (f32[4]{0:T(128)S(1)}, f32[4]{0:T(128)S(1)}, u32[]{:S(2)}, u32[]{:S(2)}) collective-permute-start(f32[4]{0:T(128)S(1)} %add.51), channel_id=1, source_target_pairs={{0,2},{2,0},{1,3},{3,1},{4,6},{6,4},{5,7},{7,5},{8,10},{10,8},{9,1... | collective-permute-start | bytes 56 | tf_op jit(solution)/shard_map/ppermute | solution.py:46
  77.6 5.1 %collective-permute-done.11 = f32[4]{0:T(128)S(1)} collective-permute-done((f32[4]{0:T(128)S(1)}, f32[4]{0:T(128)S(1)}, u32[]{:S(2)}, u32[]{:S(2)}) %collective-permute-start.11) | collective-permute-done | bytes 48 | tf_op jit(solution)/shard_map/ppermute | solution.py:46
  87.2 1.4 %multiply_add_fusion = (f32[64,2048]{1,0:T(8,128)}, f32[64,2048]{1,0:T(8,128)}, f32[64,2048]{1,0:T(8,128)}) fusion(f32[64,2048]{1,0:T(8,128)S(1)} %copy-done, f32[]{:T(128)S(6)} %div.7, f32[64,2048]{1,0:T(8,128)S(1)} %copy-done.2, f32[96,2304]{1,0:T(8,128)S(1)} %copy-done.1, f32[]{:T(128)S(6)} %div.6, f32[64,2048]{1,0:T(8,128)S(1)} %copy-done.3), kind=kLoop, calls=%fused_computation.5 | loop fusion | flops 1048576 | bytes 3670024 | tf_op jit(solution)/shard_map/add | solution.py:273
  (46 shorter events, 8.5 us)
Async XLA Ops:
  0.6 22.6 %copy-start.5 = (f32[32,32]{1,0:T(8,128)S(1)}, f32[32,32]{1,0:T(8,128)}, u32[]{:S(2)}) copy-start(f32[32,32]{1,0:T(8,128)} %param.15) | copy-start | bytes 12292
  2.6 12.6 %collective-permute-start = (f32[68,16]{1,0:T(8,128)S(1)}, f32[68,16]{1,0:T(8,128)S(1)}, u32[]{:S(2)}, u32[]{:S(2)}) collective-permute-start(f32[68,16]{1,0:T(8,128)S(1)} %copy.16), channel_id=1, source_target_pairs={{0,1},{1,2},{2,3},{3,4},{4,5},{5,6},{6,7},{7,8},{8,9},{9,10},{10,1... | collective-permute-start | bytes 13064 | tf_op jit(solution)/shard_map/ppermute | solution.py:30
  4.5 12.2 %collective-permute-start.1 = (f32[64,16]{1,0:T(8,128)S(1)}, f32[64,16]{1,0:T(8,128)S(1)}, u32[]{:S(2)}, u32[]{:S(2)}) collective-permute-start(f32[64,16]{1,0:T(8,128)S(1)} %get-tuple-element.12), channel_id=1, source_target_pairs={{1,0},{2,1},{3,2},{4,3},{5,4},{6,5},{7,6},{8,7},{9,8},{10,9},{11,1... | collective-permute-start | bytes 12296 | tf_op jit(solution)/shard_map/ppermute | solution.py:30
  18.1 7.1 %collective-permute-start.2 = (f32[17,2080]{1,0:T(8,128)S(1)}, f32[17,2080]{1,0:T(8,128)S(1)}, u32[]{:S(2)}, u32[]{:S(2)}) collective-permute-start(f32[17,2080]{1,0:T(8,128)S(1)} %pad_maximum_fusion), channel_id=1, source_target_pairs={{0,64},{64,128},{128,192},{1,65},{65,129},{129,193},{2,66},{66,130... | collective-permute-start | bytes 424328 | tf_op jit(solution)/shard_map/ppermute | solution.py:30
  21.9 3.3 %copy-start.4 = (f32[4,128]{1,0:T(4,128)S(1)}, f32[4,128]{1,0:T(4,128)}, u32[]{:S(2)}) copy-start(f32[4,128]{1,0:T(4,128)} %param.14) | copy-start | bytes 6148
  21.9 6.9 %collective-permute-start.3 = (f32[16,2080]{1,0:T(8,128)S(1)}, f32[16,2080]{1,0:T(8,128)S(1)}, u32[]{:S(2)}, u32[]{:S(2)}) collective-permute-start(f32[16,2080]{1,0:T(8,128)S(1)} %get-tuple-element.9), channel_id=1, source_target_pairs={{64,0},{128,64},{192,128},{65,1},{129,65},{193,129},{66,2},{130,66... | collective-permute-start | bytes 399368 | tf_op jit(solution)/shard_map/ppermute | solution.py:30
  29.9 15.2 %copy-start = (f32[64,2048]{1,0:T(8,128)S(1)}, f32[64,2048]{1,0:T(8,128)}, u32[]{:S(2)}) copy-start(f32[64,2048]{1,0:T(8,128)} %param.13) | copy-start | bytes 1572868
  29.9 15.2 %copy-start.2 = (f32[64,2048]{1,0:T(8,128)S(1)}, f32[64,2048]{1,0:T(8,128)}, u32[]{:S(2)}) copy-start(f32[64,2048]{1,0:T(8,128)} %param.12) | copy-start | bytes 1572868
  46.5 40.7 %copy-start.1 = (f32[96,2304]{1,0:T(8,128)S(1)}, f32[96,2304]{1,0:T(8,128)}, u32[]{:S(2)}) copy-start(f32[96,2304]{1,0:T(8,128)} %shard_map.130) | copy-start | bytes 2654212
  46.5 40.7 %copy-start.3 = (f32[64,2048]{1,0:T(8,128)S(1)}, f32[64,2048]{1,0:T(8,128)}, u32[]{:S(2)}) copy-start(f32[64,2048]{1,0:T(8,128)} %param.11) | copy-start | bytes 1572868
  46.8 3.1 %collective-permute-start.4 = (f32[4]{0:T(128)S(1)}, f32[4]{0:T(128)S(1)}, u32[]{:S(2)}, u32[]{:S(2)}) collective-permute-start(f32[4]{0:T(128)S(1)} %maximum_reduce_fusion), channel_id=1, source_target_pairs={{0,1},{1,0},{2,3},{3,2},{4,5},{5,4},{6,7},{7,6},{8,9},{9,8},{10,11... | collective-permute-start | bytes 56 | tf_op jit(solution)/shard_map/ppermute | solution.py:46
  49.9 3.5 %collective-permute-start.5 = (f32[4]{0:T(128)S(1)}, f32[4]{0:T(128)S(1)}, u32[]{:S(2)}, u32[]{:S(2)}) collective-permute-start(f32[4]{0:T(128)S(1)} %add.45), channel_id=1, source_target_pairs={{0,64},{64,0},{128,192},{192,128},{1,65},{65,1},{129,193},{193,129... | collective-permute-start | bytes 56 | tf_op jit(solution)/shard_map/ppermute | solution.py:46
  53.4 4.6 %collective-permute-start.6 = (f32[4]{0:T(128)S(1)}, f32[4]{0:T(128)S(1)}, u32[]{:S(2)}, u32[]{:S(2)}) collective-permute-start(f32[4]{0:T(128)S(1)} %add.46), channel_id=1, source_target_pairs={{0,128},{64,192},{128,0},{192,64},{1,129},{65,193},{129,1},{193,65... | collective-permute-start | bytes 56 | tf_op jit(solution)/shard_map/ppermute | solution.py:46
  58.0 3.5 %collective-permute-start.7 = (f32[4]{0:T(128)S(1)}, f32[4]{0:T(128)S(1)}, u32[]{:S(2)}, u32[]{:S(2)}) collective-permute-start(f32[4]{0:T(128)S(1)} %add.47), channel_id=1, source_target_pairs={{0,16},{16,0},{32,48},{48,32},{1,17},{17,1},{33,49},{49,33},{2,18}... | collective-permute-start | bytes 56 | tf_op jit(solution)/shard_map/ppermute | solution.py:46
  61.6 5.0 %collective-permute-start.8 = (f32[4]{0:T(128)S(1)}, f32[4]{0:T(128)S(1)}, u32[]{:S(2)}, u32[]{:S(2)}) collective-permute-start(f32[4]{0:T(128)S(1)} %add.48), channel_id=1, source_target_pairs={{0,32},{16,48},{32,0},{48,16},{1,33},{17,49},{33,1},{49,17},{2,34}... | collective-permute-start | bytes 56 | tf_op jit(solution)/shard_map/ppermute | solution.py:46
  66.6 3.5 %collective-permute-start.9 = (f32[4]{0:T(128)S(1)}, f32[4]{0:T(128)S(1)}, u32[]{:S(2)}, u32[]{:S(2)}) collective-permute-start(f32[4]{0:T(128)S(1)} %add.49), channel_id=1, source_target_pairs={{0,4},{4,0},{8,12},{12,8},{1,5},{5,1},{9,13},{13,9},{2,6},{6,2},{1... | collective-permute-start | bytes 56 | tf_op jit(solution)/shard_map/ppermute | solution.py:46
  70.2 5.0 %collective-permute-start.10 = (f32[4]{0:T(128)S(1)}, f32[4]{0:T(128)S(1)}, u32[]{:S(2)}, u32[]{:S(2)}) collective-permute-start(f32[4]{0:T(128)S(1)} %add.50), channel_id=1, source_target_pairs={{0,8},{4,12},{8,0},{12,4},{1,9},{5,13},{9,1},{13,5},{2,10},{6,14},... | collective-permute-start | bytes 56 | tf_op jit(solution)/shard_map/ppermute | solution.py:46
  75.2 7.4 %collective-permute-start.11 = (f32[4]{0:T(128)S(1)}, f32[4]{0:T(128)S(1)}, u32[]{:S(2)}, u32[]{:S(2)}) collective-permute-start(f32[4]{0:T(128)S(1)} %add.51), channel_id=1, source_target_pairs={{0,2},{2,0},{1,3},{3,1},{4,6},{6,4},{5,7},{7,5},{8,10},{10,8},{9,1... | collective-permute-start | bytes 56 | tf_op jit(solution)/shard_map/ppermute | solution.py:46

commit v9 on v8

--- a/solution.py
+++ b/solution.py
@@ -240,6 +240,34 @@
     return out[:, :cols]
 
 
+def update_kernel(sums_ref, iterate_ref, residual_ref, direction_ref, applied_ref,
+                  iterate_out, residual_out, direction_out):
+    sums = sums_ref[...]
+    norm_now, curvature, cross_term, image_norm = (sums[:, i : i + 1] for i in range(4))
+    step_length = norm_now / curvature
+    norm_next = norm_now - 2.0 * step_length * cross_term + step_length * step_length * image_norm
+    ratio = norm_next / norm_now
+    direction = direction_ref[...]
+    iterate_out[...] = iterate_ref[...] + step_length * direction
+    new_residual = residual_ref[...] - step_length * applied_ref[...]
+    residual_out[...] = new_residual
+    direction_out[...] = new_residual + ratio * direction
+
+
+def updated(sums, iterate, residual, direction, applied):
+    height, breadth = iterate.shape
+    rows = 8
+    block = pl.BlockSpec((rows, breadth), lambda i: (i, 0))
+    shape = jax.ShapeDtypeStruct(iterate.shape, jnp.float32)
+    return pl.pallas_call(
+        update_kernel,
+        grid=(height // rows,),
+        out_shape=(shape, shape, shape),
+        in_specs=[pl.BlockSpec((1, 4), lambda i: (0, 0))] + [block] * 4,
+        out_specs=(block, block, block),
+    )(sums, iterate, residual, direction, applied)
+
+
 def per_device(iterate, residual, direction, window_weight, freq_weight):
     height, breadth = direction.shape
     rim_weight = jnp.pad(window_weight[:, -1:], ((0, 0), (0, 15)))
@@ -265,13 +293,7 @@
         [residual * residual, direction * applied, residual * applied, applied * applied]
     )
     sums = summed_everywhere(jnp.sum(products, axis=(1, 2)), DOUBLING)
-    norm_now, curvature, cross_term, image_norm = sums[0], sums[1], sums[2], sums[3]
-    step_length = norm_now / curvature
-    new_iterate = iterate + step_length * direction
-    new_residual = residual - step_length * applied
-    norm_next = norm_now - 2.0 * step_length * cross_term + step_length * step_length * image_norm
-    new_direction = new_residual + norm_next / norm_now * direction
-    return (new_iterate, new_residual, new_direction)
+    return updated(sums.reshape(1, 4), iterate, residual, direction, applied)
 
 
 def solution(mesh):

time: 89.1 us -> 90.8 us (1.019)
  Pallas kernels: 15.2 us -> 21.2 us
  between operations: 4.74 us -> 0.82 us
  other arithmetic: 5.01 us -> 3.58 us
    pallas_call x0 -> x1, Pallas kernels: none -> 5.95 us  [updated(): pl.pallas_call(update_kernel, grid=(height // rows,), out_shape=(shape, s...]
    add x1 -> x0, other arithmetic: 1.4 us -> none  [per_device(): new_direction = new_residual + norm_next / norm_now * direction]
  transfers between devices with their start and end apart: 12 -> 12, of which waited for: 11 -> 11; matrix products, arithmetic and copies ran while one was open for 4% -> 3% of each run, Pallas kernels for 0% -> 0%
where the time goes in v9:
time: 90.8 us; the launch traced here: 90.1 us
  starting transfers between devices  32 us (35%)
  waiting for transfers between devices  26 us (29%)
  Pallas kernels  21.2 us (23%)
  local copies, waits for them, and re-layouts  6.49 us (7%)
  other arithmetic  3.58 us (4%)
    ppermute x8, waiting for transfers between devices, summed_everywhere(): x = x + lax.ppermute(x, axis, [(i, i ^ mask) for i in range(count)])  21.5 us
    ppermute x4, starting transfers between devices, passed_along(): lax.ppermute(value, axis, [(source, source + steps) for source in range(l...  17.6 us
    pallas_call x1, Pallas kernels, analyze_weigh_synthesize(): pl.pallas_call(transform_kernel, out_shape=jax.ShapeDtypeStruct((rows, wi...  15.2 us
    ppermute x8, starting transfers between devices, summed_everywhere(): x = x + lax.ppermute(x, axis, [(i, i ^ mask) for i in range(count)])  14.4 us
    pallas_call x1, Pallas kernels, updated(): pl.pallas_call(update_kernel, grid=(height // rows,), out_shape=(shape, s...  5.95 us
    ppermute x4, waiting for transfers between devices, passed_along(): lax.ppermute(value, axis, [(source, source + steps) for source in range(l...  4.54 us
  transfers between devices with their start and end apart: 12, of which 11 were waited for; matrix products, arithmetic and copies ran while one was open for 3% of the time, Pallas kernels for 0%

profile of v9, /device:TPU:16, one launch (start us, length us, event | category | flops | bytes accessed | tf_op | source)
XLA Modules:
  0.0 90.1 jit_solution(17672334554453601736)
XLA Ops:
  2.6 1.9 %collective-permute-start = (f32[68,16]{1,0:T(8,128)S(1)}, f32[68,16]{1,0:T(8,128)S(1)}, u32[]{:S(2)}, u32[]{:S(2)}) collective-permute-start(f32[68,16]{1,0:T(8,128)S(1)} %copy.16), channel_id=1, source_target_pairs={{0,1},{1,2},{2,3},{3,4},{4,5},{5,6},{6,7},{7,8},{8,9},{9,10},{10,1... | collective-permute-start | bytes 13064 | tf_op jit(solution)/shard_map/ppermute | solution.py:30
  4.6 10.6 %collective-permute-start.1 = (f32[64,16]{1,0:T(8,128)S(1)}, f32[64,16]{1,0:T(8,128)S(1)}, u32[]{:S(2)}, u32[]{:S(2)}) collective-permute-start(f32[64,16]{1,0:T(8,128)S(1)} %get-tuple-element.10), channel_id=1, source_target_pairs={{1,0},{2,1},{3,2},{4,3},{5,4},{6,5},{7,6},{8,7},{9,8},{10,9},{11,1... | collective-permute-start | bytes 12296 | tf_op jit(solution)/shard_map/ppermute | solution.py:30
  15.2 1.6 %collective-permute-done.1 = f32[64,16]{1,0:T(8,128)S(1)} collective-permute-done((f32[64,16]{1,0:T(8,128)S(1)}, f32[64,16]{1,0:T(8,128)S(1)}, u32[]{:S(2)}, u32[]{:S(2)}) %collective-permute-start.1) | collective-permute-done | bytes 4128 | tf_op jit(solution)/shard_map/ppermute | solution.py:30
  16.8 1.4 %concatenate.19 = f32[64,2080]{1,0:T(8,128)S(1)} concatenate(f32[64,16]{1,0:T(8,128)S(1)} %slice.46, f32[64,2048]{1,0:T(8,128)} %direction_ref.1, f32[64,16]{1,0:T(8,128)S(1)} %collective-permute-done.1), dimensions={1} | concatenate | bytes 1064960 | tf_op jit(solution)/shard_map/concatenate | solution.py:278
  18.3 3.8 %collective-permute-start.2 = (f32[17,2080]{1,0:T(8,128)S(1)}, f32[17,2080]{1,0:T(8,128)S(1)}, u32[]{:S(2)}, u32[]{:S(2)}) collective-permute-start(f32[17,2080]{1,0:T(8,128)S(1)} %pad_maximum_fusion), channel_id=1, source_target_pairs={{0,64},{64,128},{128,192},{1,65},{65,129},{129,193},{2,66},{66,130... | collective-permute-start | bytes 424328 | tf_op jit(solution)/shard_map/ppermute | solution.py:30
  22.1 1.3 %collective-permute-start.3 = (f32[16,2080]{1,0:T(8,128)S(1)}, f32[16,2080]{1,0:T(8,128)S(1)}, u32[]{:S(2)}, u32[]{:S(2)}) collective-permute-start(f32[16,2080]{1,0:T(8,128)S(1)} %get-tuple-element.6), channel_id=1, source_target_pairs={{64,0},{128,64},{192,128},{65,1},{129,65},{193,129},{66,2},{130,66... | collective-permute-start | bytes 399368 | tf_op jit(solution)/shard_map/ppermute | solution.py:30
  26.7 2.3 %collective-permute-done.3 = f32[16,2080]{1,0:T(8,128)S(1)} collective-permute-done((f32[16,2080]{1,0:T(8,128)S(1)}, f32[16,2080]{1,0:T(8,128)S(1)}, u32[]{:S(2)}, u32[]{:S(2)}) %collective-permute-start.3) | collective-permute-done | bytes 133152 | tf_op jit(solution)/shard_map/ppermute | solution.py:30
  30.0 15.2 %shard_map.130 = f32[96,2304]{1,0:T(8,128)} custom-call(f32[96,2304]{1,0:T(8,128)} %select_maximum_fusion.x_ref, bf16[256,512]{1,0:T(8,128)(2,1)} %constant.18.clone.mh_ref, bf16[256,512]{1,0:T(8,128)(2,1)} %constant.19.clone.ml_ref, bf16[160,192]{1,0:T(8,128)(2,1)} %constant.20.clone.fh_ref, bf16[160,192]{1,0:T(8,128)(2,1)} %constant.21.clone.fl_ref, ...), custom_call_target="tpu_custom_call" | custom-call | tf_op jit(solution)/shard_map/pallas_call | solution.py:230
  45.3 1.3 %multiply_bitcast_fusion.2 = (f32[1,64,2048]{2,1,0:T(8,128)S(1)}, f32[64,2048]{1,0:T(8,128)S(1)}) fusion(f32[64,2048]{1,0:T(8,128)S(1)} %copy-done, f32[96,2304]{1,0:T(8,128)} %shard_map.130), kind=kLoop, calls=%fused_computation.7 | loop fusion | flops 393216 | bytes 2097152 | tf_op jit(solution)/shard_map/stack | solution.py:292
  47.7 2.3 %collective-permute-start.4 = (f32[4]{0:T(128)S(1)}, f32[4]{0:T(128)S(1)}, u32[]{:S(2)}, u32[]{:S(2)}) collective-permute-start(f32[4]{0:T(128)S(1)} %maximum_reduce_fusion), channel_id=1, source_target_pairs={{0,1},{1,0},{2,3},{3,2},{4,5},{5,4},{6,7},{7,6},{8,9},{9,8},{10,11... | collective-permute-start | bytes 56 | tf_op jit(solution)/shard_map/ppermute | solution.py:46
  50.8 1.3 %collective-permute-start.5 = (f32[4]{0:T(128)S(1)}, f32[4]{0:T(128)S(1)}, u32[]{:S(2)}, u32[]{:S(2)}) collective-permute-start(f32[4]{0:T(128)S(1)} %add.36), channel_id=1, source_target_pairs={{0,64},{64,0},{128,192},{192,128},{1,65},{65,1},{129,193},{193,129... | collective-permute-start | bytes 56 | tf_op jit(solution)/shard_map/ppermute | solution.py:46
  52.0 2.3 %collective-permute-done.5 = f32[4]{0:T(128)S(1)} collective-permute-done((f32[4]{0:T(128)S(1)}, f32[4]{0:T(128)S(1)}, u32[]{:S(2)}, u32[]{:S(2)}) %collective-permute-start.5) | collective-permute-done | bytes 48 | tf_op jit(solution)/shard_map/ppermute | solution.py:46
  54.3 3.1 %collective-permute-start.6 = (f32[4]{0:T(128)S(1)}, f32[4]{0:T(128)S(1)}, u32[]{:S(2)}, u32[]{:S(2)}) collective-permute-start(f32[4]{0:T(128)S(1)} %add.37), channel_id=1, source_target_pairs={{0,128},{64,192},{128,0},{192,64},{1,129},{65,193},{129,1},{193,65... | collective-permute-start | bytes 56 | tf_op jit(solution)/shard_map/ppermute | solution.py:46
  57.4 1.5 %collective-permute-done.6 = f32[4]{0:T(128)S(1)} collective-permute-done((f32[4]{0:T(128)S(1)}, f32[4]{0:T(128)S(1)}, u32[]{:S(2)}, u32[]{:S(2)}) %collective-permute-start.6) | collective-permute-done | bytes 48 | tf_op jit(solution)/shard_map/ppermute | solution.py:46
  58.9 1.3 %collective-permute-start.7 = (f32[4]{0:T(128)S(1)}, f32[4]{0:T(128)S(1)}, u32[]{:S(2)}, u32[]{:S(2)}) collective-permute-start(f32[4]{0:T(128)S(1)} %add.38), channel_id=1, source_target_pairs={{0,16},{16,0},{32,48},{48,32},{1,17},{17,1},{33,49},{49,33},{2,18}... | collective-permute-start | bytes 56 | tf_op jit(solution)/shard_map/ppermute | solution.py:46
  60.2 2.3 %collective-permute-done.7 = f32[4]{0:T(128)S(1)} collective-permute-done((f32[4]{0:T(128)S(1)}, f32[4]{0:T(128)S(1)}, u32[]{:S(2)}, u32[]{:S(2)}) %collective-permute-start.7) | collective-permute-done | bytes 48 | tf_op jit(solution)/shard_map/ppermute | solution.py:46
  62.5 5.0 %collective-permute-done.8 = f32[4]{0:T(128)S(1)} collective-permute-done((f32[4]{0:T(128)S(1)}, f32[4]{0:T(128)S(1)}, u32[]{:S(2)}, u32[]{:S(2)}) %collective-permute-start.8) | collective-permute-done | bytes 48 | tf_op jit(solution)/shard_map/ppermute | solution.py:46
  67.5 1.2 %collective-permute-start.9 = (f32[4]{0:T(128)S(1)}, f32[4]{0:T(128)S(1)}, u32[]{:S(2)}, u32[]{:S(2)}) collective-permute-start(f32[4]{0:T(128)S(1)} %add.40), channel_id=1, source_target_pairs={{0,4},{4,0},{8,12},{12,8},{1,5},{5,1},{9,13},{13,9},{2,6},{6,2},{1... | collective-permute-start | bytes 56 | tf_op jit(solution)/shard_map/ppermute | solution.py:46
  68.7 2.3 %collective-permute-done.9 = f32[4]{0:T(128)S(1)} collective-permute-done((f32[4]{0:T(128)S(1)}, f32[4]{0:T(128)S(1)}, u32[]{:S(2)}, u32[]{:S(2)}) %collective-permute-start.9) | collective-permute-done | bytes 48 | tf_op jit(solution)/shard_map/ppermute | solution.py:46
  71.0 2.8 %collective-permute-start.10 = (f32[4]{0:T(128)S(1)}, f32[4]{0:T(128)S(1)}, u32[]{:S(2)}, u32[]{:S(2)}) collective-permute-start(f32[4]{0:T(128)S(1)} %add.41), channel_id=1, source_target_pairs={{0,8},{4,12},{8,0},{12,4},{1,9},{5,13},{9,1},{13,5},{2,10},{6,14},... | collective-permute-start | bytes 56 | tf_op jit(solution)/shard_map/ppermute | solution.py:46
  73.8 2.3 %collective-permute-done.10 = f32[4]{0:T(128)S(1)} collective-permute-done((f32[4]{0:T(128)S(1)}, f32[4]{0:T(128)S(1)}, u32[]{:S(2)}, u32[]{:S(2)}) %collective-permute-start.10) | collective-permute-done | bytes 48 | tf_op jit(solution)/shard_map/ppermute | solution.py:46
  76.1 2.4 %collective-permute-start.11 = (f32[4]{0:T(128)S(1)}, f32[4]{0:T(128)S(1)}, u32[]{:S(2)}, u32[]{:S(2)}) collective-permute-start(f32[4]{0:T(128)S(1)} %add.42), channel_id=1, source_target_pairs={{0,2},{2,0},{1,3},{3,1},{4,6},{6,4},{5,7},{7,5},{8,10},{10,8},{9,1... | collective-permute-start | bytes 56 | tf_op jit(solution)/shard_map/ppermute | solution.py:46
  78.5 5.1 %collective-permute-done.11 = f32[4]{0:T(128)S(1)} collective-permute-done((f32[4]{0:T(128)S(1)}, f32[4]{0:T(128)S(1)}, u32[]{:S(2)}, u32[]{:S(2)}) %collective-permute-start.11) | collective-permute-done | bytes 48 | tf_op jit(solution)/shard_map/ppermute | solution.py:46
  84.1 5.9 %shard_map.131 = (f32[64,2048]{1,0:T(8,128)}, f32[64,2048]{1,0:T(8,128)}, f32[64,2048]{1,0:T(8,128)}) custom-call(f32[1,4]{1,0:T(1,128)} %add_bitcast_fusion.sums_ref, f32[64,2048]{1,0:T(8,128)} %iterate_ref.1, f32[64,2048]{1,0:T(8,128)} %residual_ref.1, f32[64,2048]{1,0:T(8,128)} %direction_ref.1, f32[64,2048]{1,0:T(8,128)} %copy-done.1), custom_call_target="tpu_custom_call" | custom-call | tf_op jit(solution)/shard_map/pallas_call | solution.py:262
  (44 shorter events, 9.0 us)
Async XLA Ops:
  0.6 17.6 %copy-start.3 = (f32[4,128]{1,0:T(4,128)S(1)}, f32[4,128]{1,0:T(4,128)}, u32[]{:S(2)}) copy-start(f32[4,128]{1,0:T(4,128)} %param.14) | copy-start | bytes 6148
  0.6 22.7 %copy-start.4 = (f32[32,32]{1,0:T(8,128)S(1)}, f32[32,32]{1,0:T(8,128)}, u32[]{:S(2)}) copy-start(f32[32,32]{1,0:T(8,128)} %param.15) | copy-start | bytes 12292
  2.6 12.6 %collective-permute-start = (f32[68,16]{1,0:T(8,128)S(1)}, f32[68,16]{1,0:T(8,128)S(1)}, u32[]{:S(2)}, u32[]{:S(2)}) collective-permute-start(f32[68,16]{1,0:T(8,128)S(1)} %copy.16), channel_id=1, source_target_pairs={{0,1},{1,2},{2,3},{3,4},{4,5},{5,6},{6,7},{7,8},{8,9},{9,10},{10,1... | collective-permute-start | bytes 13064 | tf_op jit(solution)/shard_map/ppermute | solution.py:30
  4.6 12.2 %collective-permute-start.1 = (f32[64,16]{1,0:T(8,128)S(1)}, f32[64,16]{1,0:T(8,128)S(1)}, u32[]{:S(2)}, u32[]{:S(2)}) collective-permute-start(f32[64,16]{1,0:T(8,128)S(1)} %get-tuple-element.10), channel_id=1, source_target_pairs={{1,0},{2,1},{3,2},{4,3},{5,4},{6,5},{7,6},{8,7},{9,8},{10,9},{11,1... | collective-permute-start | bytes 12296 | tf_op jit(solution)/shard_map/ppermute | solution.py:30
  18.3 7.1 %collective-permute-start.2 = (f32[17,2080]{1,0:T(8,128)S(1)}, f32[17,2080]{1,0:T(8,128)S(1)}, u32[]{:S(2)}, u32[]{:S(2)}) collective-permute-start(f32[17,2080]{1,0:T(8,128)S(1)} %pad_maximum_fusion), channel_id=1, source_target_pairs={{0,64},{64,128},{128,192},{1,65},{65,129},{129,193},{2,66},{66,130... | collective-permute-start | bytes 424328 | tf_op jit(solution)/shard_map/ppermute | solution.py:30
  22.1 6.9 %collective-permute-start.3 = (f32[16,2080]{1,0:T(8,128)S(1)}, f32[16,2080]{1,0:T(8,128)S(1)}, u32[]{:S(2)}, u32[]{:S(2)}) collective-permute-start(f32[16,2080]{1,0:T(8,128)S(1)} %get-tuple-element.6), channel_id=1, source_target_pairs={{64,0},{128,64},{192,128},{65,1},{129,65},{193,129},{66,2},{130,66... | collective-permute-start | bytes 399368 | tf_op jit(solution)/shard_map/ppermute | solution.py:30
  30.0 15.2 %copy-start = (f32[64,2048]{1,0:T(8,128)S(1)}, f32[64,2048]{1,0:T(8,128)}, u32[]{:S(2)}) copy-start(f32[64,2048]{1,0:T(8,128)} %direction_ref.1) | copy-start | bytes 1572868
  45.3 1.3 %copy-start.2 = (f32[64,2048]{1,0:T(8,128)S(1)}, f32[64,2048]{1,0:T(8,128)}, u32[]{:S(2)}) copy-start(f32[64,2048]{1,0:T(8,128)} %residual_ref.1) | copy-start | bytes 1572868
  46.6 0.8 copy-start.1
  47.7 3.1 %collective-permute-start.4 = (f32[4]{0:T(128)S(1)}, f32[4]{0:T(128)S(1)}, u32[]{:S(2)}, u32[]{:S(2)}) collective-permute-start(f32[4]{0:T(128)S(1)} %maximum_reduce_fusion), channel_id=1, source_target_pairs={{0,1},{1,0},{2,3},{3,2},{4,5},{5,4},{6,7},{7,6},{8,9},{9,8},{10,11... | collective-permute-start | bytes 56 | tf_op jit(solution)/shard_map/ppermute | solution.py:46
  50.8 3.5 %collective-permute-start.5 = (f32[4]{0:T(128)S(1)}, f32[4]{0:T(128)S(1)}, u32[]{:S(2)}, u32[]{:S(2)}) collective-permute-start(f32[4]{0:T(128)S(1)} %add.36), channel_id=1, source_target_pairs={{0,64},{64,0},{128,192},{192,128},{1,65},{65,1},{129,193},{193,129... | collective-permute-start | bytes 56 | tf_op jit(solution)/shard_map/ppermute | solution.py:46
  54.3 4.6 %collective-permute-start.6 = (f32[4]{0:T(128)S(1)}, f32[4]{0:T(128)S(1)}, u32[]{:S(2)}, u32[]{:S(2)}) collective-permute-start(f32[4]{0:T(128)S(1)} %add.37), channel_id=1, source_target_pairs={{0,128},{64,192},{128,0},{192,64},{1,129},{65,193},{129,1},{193,65... | collective-permute-start | bytes 56 | tf_op jit(solution)/shard_map/ppermute | solution.py:46
  58.9 3.5 %collective-permute-start.7 = (f32[4]{0:T(128)S(1)}, f32[4]{0:T(128)S(1)}, u32[]{:S(2)}, u32[]{:S(2)}) collective-permute-start(f32[4]{0:T(128)S(1)} %add.38), channel_id=1, source_target_pairs={{0,16},{16,0},{32,48},{48,32},{1,17},{17,1},{33,49},{49,33},{2,18}... | collective-permute-start | bytes 56 | tf_op jit(solution)/shard_map/ppermute | solution.py:46
  62.4 5.0 %collective-permute-start.8 = (f32[4]{0:T(128)S(1)}, f32[4]{0:T(128)S(1)}, u32[]{:S(2)}, u32[]{:S(2)}) collective-permute-start(f32[4]{0:T(128)S(1)} %add.39), channel_id=1, source_target_pairs={{0,32},{16,48},{32,0},{48,16},{1,33},{17,49},{33,1},{49,17},{2,34}... | collective-permute-start | bytes 56 | tf_op jit(solution)/shard_map/ppermute | solution.py:46
  67.5 3.5 %collective-permute-start.9 = (f32[4]{0:T(128)S(1)}, f32[4]{0:T(128)S(1)}, u32[]{:S(2)}, u32[]{:S(2)}) collective-permute-start(f32[4]{0:T(128)S(1)} %add.40), channel_id=1, source_target_pairs={{0,4},{4,0},{8,12},{12,8},{1,5},{5,1},{9,13},{13,9},{2,6},{6,2},{1... | collective-permute-start | bytes 56 | tf_op jit(solution)/shard_map/ppermute | solution.py:46
  71.0 5.0 %collective-permute-start.10 = (f32[4]{0:T(128)S(1)}, f32[4]{0:T(128)S(1)}, u32[]{:S(2)}, u32[]{:S(2)}) collective-permute-start(f32[4]{0:T(128)S(1)} %add.41), channel_id=1, source_target_pairs={{0,8},{4,12},{8,0},{12,4},{1,9},{5,13},{9,1},{13,5},{2,10},{6,14},... | collective-permute-start | bytes 56 | tf_op jit(solution)/shard_map/ppermute | solution.py:46
  76.1 7.4 %collective-permute-start.11 = (f32[4]{0:T(128)S(1)}, f32[4]{0:T(128)S(1)}, u32[]{:S(2)}, u32[]{:S(2)}) collective-permute-start(f32[4]{0:T(128)S(1)} %add.42), channel_id=1, source_target_pairs={{0,2},{2,0},{1,3},{3,1},{4,6},{6,4},{5,7},{7,5},{8,10},{10,8},{9,1... | collective-permute-start | bytes 56 | tf_op jit(solution)/shard_map/ppermute | solution.py:46

commit v10 on v9

--- a/solution.py
+++ b/solution.py
@@ -101,6 +101,7 @@
 
 
 LANES = 128
+UPDATE_ROWS = 32
 WINDOWS_PER_TILE = LANES // 16
 HALF = WINDOWS_PER_TILE * 32
 
@@ -256,7 +257,7 @@
 
 def updated(sums, iterate, residual, direction, applied):
     height, breadth = iterate.shape
-    rows = 8
+    rows = UPDATE_ROWS
     block = pl.BlockSpec((rows, breadth), lambda i: (i, 0))
     shape = jax.ShapeDtypeStruct(iterate.shape, jnp.float32)
     return pl.pallas_call(

time: 90.8 us -> 87.1 us (0.959)
  Pallas kernels: 21.2 us -> 17.8 us
    pallas_call x1, Pallas kernels: 5.95 us -> 2.57 us  [updated(): pl.pallas_call(update_kernel, grid=(height // rows,), out_shape=(shape, s...]
where the time goes in v10:
time: 87.1 us; the launch traced here: 86.7 us
  starting transfers between devices  32 us (37%)
  waiting for transfers between devices  26 us (30%)
  Pallas kernels  17.8 us (20%)
  local copies, waits for them, and re-layouts  6.49 us (7%)
  other arithmetic  3.58 us (4%)
    ppermute x8, waiting for transfers between devices, summed_everywhere(): x = x + lax.ppermute(x, axis, [(i, i ^ mask) for i in range(count)])  21.5 us
    ppermute x4, starting transfers between devices, passed_along(): lax.ppermute(value, axis, [(source, source + steps) for source in range(l...  17.6 us
    pallas_call x1, Pallas kernels, analyze_weigh_synthesize(): pl.pallas_call(transform_kernel, out_shape=jax.ShapeDtypeStruct((rows, wi...  15.2 us
    ppermute x8, starting transfers between devices, summed_everywhere(): x = x + lax.ppermute(x, axis, [(i, i ^ mask) for i in range(count)])  14.4 us
    ppermute x4, waiting for transfers between devices, passed_along(): lax.ppermute(value, axis, [(source, source + steps) for source in range(l...  4.54 us
    pallas_call x1, Pallas kernels, updated(): pl.pallas_call(update_kernel, grid=(height // rows,), out_shape=(shape, s...  2.57 us
  transfers between devices with their start and end apart: 12, of which 11 were waited for; matrix products, arithmetic and copies ran while one was open for 3% of the time, Pallas kernels for 0%

profile of v10, /device:TPU:16, one launch (start us, length us, event | category | flops | bytes accessed | tf_op | source)
XLA Modules:
  0.0 86.7 jit_solution(10354410884053815865)
XLA Ops:
  2.6 1.9 %collective-permute-start = (f32[68,16]{1,0:T(8,128)S(1)}, f32[68,16]{1,0:T(8,128)S(1)}, u32[]{:S(2)}, u32[]{:S(2)}) collective-permute-start(f32[68,16]{1,0:T(8,128)S(1)} %copy.16), channel_id=1, source_target_pairs={{0,1},{1,2},{2,3},{3,4},{4,5},{5,6},{6,7},{7,8},{8,9},{9,10},{10,1... | collective-permute-start | bytes 13064 | tf_op jit(solution)/shard_map/ppermute | solution.py:30
  4.6 10.6 %collective-permute-start.1 = (f32[64,16]{1,0:T(8,128)S(1)}, f32[64,16]{1,0:T(8,128)S(1)}, u32[]{:S(2)}, u32[]{:S(2)}) collective-permute-start(f32[64,16]{1,0:T(8,128)S(1)} %get-tuple-element.10), channel_id=1, source_target_pairs={{1,0},{2,1},{3,2},{4,3},{5,4},{6,5},{7,6},{8,7},{9,8},{10,9},{11,1... | collective-permute-start | bytes 12296 | tf_op jit(solution)/shard_map/ppermute | solution.py:30
  15.2 1.6 %collective-permute-done.1 = f32[64,16]{1,0:T(8,128)S(1)} collective-permute-done((f32[64,16]{1,0:T(8,128)S(1)}, f32[64,16]{1,0:T(8,128)S(1)}, u32[]{:S(2)}, u32[]{:S(2)}) %collective-permute-start.1) | collective-permute-done | bytes 4128 | tf_op jit(solution)/shard_map/ppermute | solution.py:30
  16.8 1.4 %concatenate.19 = f32[64,2080]{1,0:T(8,128)S(1)} concatenate(f32[64,16]{1,0:T(8,128)S(1)} %slice.46, f32[64,2048]{1,0:T(8,128)} %direction_ref.1, f32[64,16]{1,0:T(8,128)S(1)} %collective-permute-done.1), dimensions={1} | concatenate | bytes 1064960 | tf_op jit(solution)/shard_map/concatenate | solution.py:279
  18.3 3.8 %collective-permute-start.2 = (f32[17,2080]{1,0:T(8,128)S(1)}, f32[17,2080]{1,0:T(8,128)S(1)}, u32[]{:S(2)}, u32[]{:S(2)}) collective-permute-start(f32[17,2080]{1,0:T(8,128)S(1)} %pad_maximum_fusion), channel_id=1, source_target_pairs={{0,64},{64,128},{128,192},{1,65},{65,129},{129,193},{2,66},{66,130... | collective-permute-start | bytes 424328 | tf_op jit(solution)/shard_map/ppermute | solution.py:30
  22.1 1.3 %collective-permute-start.3 = (f32[16,2080]{1,0:T(8,128)S(1)}, f32[16,2080]{1,0:T(8,128)S(1)}, u32[]{:S(2)}, u32[]{:S(2)}) collective-permute-start(f32[16,2080]{1,0:T(8,128)S(1)} %get-tuple-element.6), channel_id=1, source_target_pairs={{64,0},{128,64},{192,128},{65,1},{129,65},{193,129},{66,2},{130,66... | collective-permute-start | bytes 399368 | tf_op jit(solution)/shard_map/ppermute | solution.py:30
  26.7 2.3 %collective-permute-done.3 = f32[16,2080]{1,0:T(8,128)S(1)} collective-permute-done((f32[16,2080]{1,0:T(8,128)S(1)}, f32[16,2080]{1,0:T(8,128)S(1)}, u32[]{:S(2)}, u32[]{:S(2)}) %collective-permute-start.3) | collective-permute-done | bytes 133152 | tf_op jit(solution)/shard_map/ppermute | solution.py:30
  30.0 15.2 %shard_map.130 = f32[96,2304]{1,0:T(8,128)} custom-call(f32[96,2304]{1,0:T(8,128)} %select_maximum_fusion.x_ref, bf16[256,512]{1,0:T(8,128)(2,1)} %constant.18.clone.mh_ref, bf16[256,512]{1,0:T(8,128)(2,1)} %constant.19.clone.ml_ref, bf16[160,192]{1,0:T(8,128)(2,1)} %constant.20.clone.fh_ref, bf16[160,192]{1,0:T(8,128)(2,1)} %constant.21.clone.fl_ref, ...), custom_call_target="tpu_custom_call" | custom-call | tf_op jit(solution)/shard_map/pallas_call | solution.py:231
  45.3 1.3 %multiply_bitcast_fusion.2 = (f32[1,64,2048]{2,1,0:T(8,128)S(1)}, f32[64,2048]{1,0:T(8,128)S(1)}) fusion(f32[64,2048]{1,0:T(8,128)S(1)} %copy-done, f32[96,2304]{1,0:T(8,128)} %shard_map.130), kind=kLoop, calls=%fused_computation.7 | loop fusion | flops 393216 | bytes 2097152 | tf_op jit(solution)/shard_map/stack | solution.py:293
  47.7 2.3 %collective-permute-start.4 = (f32[4]{0:T(128)S(1)}, f32[4]{0:T(128)S(1)}, u32[]{:S(2)}, u32[]{:S(2)}) collective-permute-start(f32[4]{0:T(128)S(1)} %maximum_reduce_fusion), channel_id=1, source_target_pairs={{0,1},{1,0},{2,3},{3,2},{4,5},{5,4},{6,7},{7,6},{8,9},{9,8},{10,11... | collective-permute-start | bytes 56 | tf_op jit(solution)/shard_map/ppermute | solution.py:46
  50.8 1.3 %collective-permute-start.5 = (f32[4]{0:T(128)S(1)}, f32[4]{0:T(128)S(1)}, u32[]{:S(2)}, u32[]{:S(2)}) collective-permute-start(f32[4]{0:T(128)S(1)} %add.36), channel_id=1, source_target_pairs={{0,64},{64,0},{128,192},{192,128},{1,65},{65,1},{129,193},{193,129... | collective-permute-start | bytes 56 | tf_op jit(solution)/shard_map/ppermute | solution.py:46
  52.0 2.3 %collective-permute-done.5 = f32[4]{0:T(128)S(1)} collective-permute-done((f32[4]{0:T(128)S(1)}, f32[4]{0:T(128)S(1)}, u32[]{:S(2)}, u32[]{:S(2)}) %collective-permute-start.5) | collective-permute-done | bytes 48 | tf_op jit(solution)/shard_map/ppermute | solution.py:46
  54.3 3.1 %collective-permute-start.6 = (f32[4]{0:T(128)S(1)}, f32[4]{0:T(128)S(1)}, u32[]{:S(2)}, u32[]{:S(2)}) collective-permute-start(f32[4]{0:T(128)S(1)} %add.37), channel_id=1, source_target_pairs={{0,128},{64,192},{128,0},{192,64},{1,129},{65,193},{129,1},{193,65... | collective-permute-start | bytes 56 | tf_op jit(solution)/shard_map/ppermute | solution.py:46
  57.4 1.5 %collective-permute-done.6 = f32[4]{0:T(128)S(1)} collective-permute-done((f32[4]{0:T(128)S(1)}, f32[4]{0:T(128)S(1)}, u32[]{:S(2)}, u32[]{:S(2)}) %collective-permute-start.6) | collective-permute-done | bytes 48 | tf_op jit(solution)/shard_map/ppermute | solution.py:46
  58.9 1.3 %collective-permute-start.7 = (f32[4]{0:T(128)S(1)}, f32[4]{0:T(128)S(1)}, u32[]{:S(2)}, u32[]{:S(2)}) collective-permute-start(f32[4]{0:T(128)S(1)} %add.38), channel_id=1, source_target_pairs={{0,16},{16,0},{32,48},{48,32},{1,17},{17,1},{33,49},{49,33},{2,18}... | collective-permute-start | bytes 56 | tf_op jit(solution)/shard_map/ppermute | solution.py:46
  60.2 2.3 %collective-permute-done.7 = f32[4]{0:T(128)S(1)} collective-permute-done((f32[4]{0:T(128)S(1)}, f32[4]{0:T(128)S(1)}, u32[]{:S(2)}, u32[]{:S(2)}) %collective-permute-start.7) | collective-permute-done | bytes 48 | tf_op jit(solution)/shard_map/ppermute | solution.py:46
  62.5 5.0 %collective-permute-done.8 = f32[4]{0:T(128)S(1)} collective-permute-done((f32[4]{0:T(128)S(1)}, f32[4]{0:T(128)S(1)}, u32[]{:S(2)}, u32[]{:S(2)}) %collective-permute-start.8) | collective-permute-done | bytes 48 | tf_op jit(solution)/shard_map/ppermute | solution.py:46
  67.5 1.2 %collective-permute-start.9 = (f32[4]{0:T(128)S(1)}, f32[4]{0:T(128)S(1)}, u32[]{:S(2)}, u32[]{:S(2)}) collective-permute-start(f32[4]{0:T(128)S(1)} %add.40), channel_id=1, source_target_pairs={{0,4},{4,0},{8,12},{12,8},{1,5},{5,1},{9,13},{13,9},{2,6},{6,2},{1... | collective-permute-start | bytes 56 | tf_op jit(solution)/shard_map/ppermute | solution.py:46
  68.7 2.3 %collective-permute-done.9 = f32[4]{0:T(128)S(1)} collective-permute-done((f32[4]{0:T(128)S(1)}, f32[4]{0:T(128)S(1)}, u32[]{:S(2)}, u32[]{:S(2)}) %collective-permute-start.9) | collective-permute-done | bytes 48 | tf_op jit(solution)/shard_map/ppermute | solution.py:46
  71.0 2.8 %collective-permute-start.10 = (f32[4]{0:T(128)S(1)}, f32[4]{0:T(128)S(1)}, u32[]{:S(2)}, u32[]{:S(2)}) collective-permute-start(f32[4]{0:T(128)S(1)} %add.41), channel_id=1, source_target_pairs={{0,8},{4,12},{8,0},{12,4},{1,9},{5,13},{9,1},{13,5},{2,10},{6,14},... | collective-permute-start | bytes 56 | tf_op jit(solution)/shard_map/ppermute | solution.py:46
  73.8 2.3 %collective-permute-done.10 = f32[4]{0:T(128)S(1)} collective-permute-done((f32[4]{0:T(128)S(1)}, f32[4]{0:T(128)S(1)}, u32[]{:S(2)}, u32[]{:S(2)}) %collective-permute-start.10) | collective-permute-done | bytes 48 | tf_op jit(solution)/shard_map/ppermute | solution.py:46
  76.1 2.4 %collective-permute-start.11 = (f32[4]{0:T(128)S(1)}, f32[4]{0:T(128)S(1)}, u32[]{:S(2)}, u32[]{:S(2)}) collective-permute-start(f32[4]{0:T(128)S(1)} %add.42), channel_id=1, source_target_pairs={{0,2},{2,0},{1,3},{3,1},{4,6},{6,4},{5,7},{7,5},{8,10},{10,8},{9,1... | collective-permute-start | bytes 56 | tf_op jit(solution)/shard_map/ppermute | solution.py:46
  78.5 5.1 %collective-permute-done.11 = f32[4]{0:T(128)S(1)} collective-permute-done((f32[4]{0:T(128)S(1)}, f32[4]{0:T(128)S(1)}, u32[]{:S(2)}, u32[]{:S(2)}) %collective-permute-start.11) | collective-permute-done | bytes 48 | tf_op jit(solution)/shard_map/ppermute | solution.py:46
  84.1 2.6 %shard_map.131 = (f32[64,2048]{1,0:T(8,128)}, f32[64,2048]{1,0:T(8,128)}, f32[64,2048]{1,0:T(8,128)}) custom-call(f32[1,4]{1,0:T(1,128)} %add_bitcast_fusion.sums_ref, f32[64,2048]{1,0:T(8,128)} %iterate_ref.1, f32[64,2048]{1,0:T(8,128)} %residual_ref.1, f32[64,2048]{1,0:T(8,128)} %direction_ref.1, f32[64,2048]{1,0:T(8,128)} %copy-done.1), custom_call_target="tpu_custom_call" | custom-call | tf_op jit(solution)/shard_map/pallas_call | solution.py:263
  (44 shorter events, 9.0 us)
Async XLA Ops:
  0.6 17.6 %copy-start.3 = (f32[4,128]{1,0:T(4,128)S(1)}, f32[4,128]{1,0:T(4,128)}, u32[]{:S(2)}) copy-start(f32[4,128]{1,0:T(4,128)} %param.14) | copy-start | bytes 6148
  0.6 22.7 %copy-start.4 = (f32[32,32]{1,0:T(8,128)S(1)}, f32[32,32]{1,0:T(8,128)}, u32[]{:S(2)}) copy-start(f32[32,32]{1,0:T(8,128)} %param.15) | copy-start | bytes 12292
  2.6 12.6 %collective-permute-start = (f32[68,16]{1,0:T(8,128)S(1)}, f32[68,16]{1,0:T(8,128)S(1)}, u32[]{:S(2)}, u32[]{:S(2)}) collective-permute-start(f32[68,16]{1,0:T(8,128)S(1)} %copy.16), channel_id=1, source_target_pairs={{0,1},{1,2},{2,3},{3,4},{4,5},{5,6},{6,7},{7,8},{8,9},{9,10},{10,1... | collective-permute-start | bytes 13064 | tf_op jit(solution)/shard_map/ppermute | solution.py:30
  4.6 12.2 %collective-permute-start.1 = (f32[64,16]{1,0:T(8,128)S(1)}, f32[64,16]{1,0:T(8,128)S(1)}, u32[]{:S(2)}, u32[]{:S(2)}) collective-permute-start(f32[64,16]{1,0:T(8,128)S(1)} %get-tuple-element.10), channel_id=1, source_target_pairs={{1,0},{2,1},{3,2},{4,3},{5,4},{6,5},{7,6},{8,7},{9,8},{10,9},{11,1... | collective-permute-start | bytes 12296 | tf_op jit(solution)/shard_map/ppermute | solution.py:30
  18.3 7.1 %collective-permute-start.2 = (f32[17,2080]{1,0:T(8,128)S(1)}, f32[17,2080]{1,0:T(8,128)S(1)}, u32[]{:S(2)}, u32[]{:S(2)}) collective-permute-start(f32[17,2080]{1,0:T(8,128)S(1)} %pad_maximum_fusion), channel_id=1, source_target_pairs={{0,64},{64,128},{128,192},{1,65},{65,129},{129,193},{2,66},{66,130... | collective-permute-start | bytes 424328 | tf_op jit(solution)/shard_map/ppermute | solution.py:30
  22.1 6.9 %collective-permute-start.3 = (f32[16,2080]{1,0:T(8,128)S(1)}, f32[16,2080]{1,0:T(8,128)S(1)}, u32[]{:S(2)}, u32[]{:S(2)}) collective-permute-start(f32[16,2080]{1,0:T(8,128)S(1)} %get-tuple-element.6), channel_id=1, source_target_pairs={{64,0},{128,64},{192,128},{65,1},{129,65},{193,129},{66,2},{130,66... | collective-permute-start | bytes 399368 | tf_op jit(solution)/shard_map/ppermute | solution.py:30
  30.0 15.2 %copy-start = (f32[64,2048]{1,0:T(8,128)S(1)}, f32[64,2048]{1,0:T(8,128)}, u32[]{:S(2)}) copy-start(f32[64,2048]{1,0:T(8,128)} %direction_ref.1) | copy-start | bytes 1572868
  45.3 1.3 %copy-start.2 = (f32[64,2048]{1,0:T(8,128)S(1)}, f32[64,2048]{1,0:T(8,128)}, u32[]{:S(2)}) copy-start(f32[64,2048]{1,0:T(8,128)} %residual_ref.1) | copy-start | bytes 1572868
  46.6 0.8 copy-start.1
  47.7 3.1 %collective-permute-start.4 = (f32[4]{0:T(128)S(1)}, f32[4]{0:T(128)S(1)}, u32[]{:S(2)}, u32[]{:S(2)}) collective-permute-start(f32[4]{0:T(128)S(1)} %maximum_reduce_fusion), channel_id=1, source_target_pairs={{0,1},{1,0},{2,3},{3,2},{4,5},{5,4},{6,7},{7,6},{8,9},{9,8},{10,11... | collective-permute-start | bytes 56 | tf_op jit(solution)/shard_map/ppermute | solution.py:46
  50.8 3.5 %collective-permute-start.5 = (f32[4]{0:T(128)S(1)}, f32[4]{0:T(128)S(1)}, u32[]{:S(2)}, u32[]{:S(2)}) collective-permute-start(f32[4]{0:T(128)S(1)} %add.36), channel_id=1, source_target_pairs={{0,64},{64,0},{128,192},{192,128},{1,65},{65,1},{129,193},{193,129... | collective-permute-start | bytes 56 | tf_op jit(solution)/shard_map/ppermute | solution.py:46
  54.3 4.6 %collective-permute-start.6 = (f32[4]{0:T(128)S(1)}, f32[4]{0:T(128)S(1)}, u32[]{:S(2)}, u32[]{:S(2)}) collective-permute-start(f32[4]{0:T(128)S(1)} %add.37), channel_id=1, source_target_pairs={{0,128},{64,192},{128,0},{192,64},{1,129},{65,193},{129,1},{193,65... | collective-permute-start | bytes 56 | tf_op jit(solution)/shard_map/ppermute | solution.py:46
  58.9 3.5 %collective-permute-start.7 = (f32[4]{0:T(128)S(1)}, f32[4]{0:T(128)S(1)}, u32[]{:S(2)}, u32[]{:S(2)}) collective-permute-start(f32[4]{0:T(128)S(1)} %add.38), channel_id=1, source_target_pairs={{0,16},{16,0},{32,48},{48,32},{1,17},{17,1},{33,49},{49,33},{2,18}... | collective-permute-start | bytes 56 | tf_op jit(solution)/shard_map/ppermute | solution.py:46
  62.4 5.0 %collective-permute-start.8 = (f32[4]{0:T(128)S(1)}, f32[4]{0:T(128)S(1)}, u32[]{:S(2)}, u32[]{:S(2)}) collective-permute-start(f32[4]{0:T(128)S(1)} %add.39), channel_id=1, source_target_pairs={{0,32},{16,48},{32,0},{48,16},{1,33},{17,49},{33,1},{49,17},{2,34}... | collective-permute-start | bytes 56 | tf_op jit(solution)/shard_map/ppermute | solution.py:46
  67.5 3.5 %collective-permute-start.9 = (f32[4]{0:T(128)S(1)}, f32[4]{0:T(128)S(1)}, u32[]{:S(2)}, u32[]{:S(2)}) collective-permute-start(f32[4]{0:T(128)S(1)} %add.40), channel_id=1, source_target_pairs={{0,4},{4,0},{8,12},{12,8},{1,5},{5,1},{9,13},{13,9},{2,6},{6,2},{1... | collective-permute-start | bytes 56 | tf_op jit(solution)/shard_map/ppermute | solution.py:46
  71.0 5.0 %collective-permute-start.10 = (f32[4]{0:T(128)S(1)}, f32[4]{0:T(128)S(1)}, u32[]{:S(2)}, u32[]{:S(2)}) collective-permute-start(f32[4]{0:T(128)S(1)} %add.41), channel_id=1, source_target_pairs={{0,8},{4,12},{8,0},{12,4},{1,9},{5,13},{9,1},{13,5},{2,10},{6,14},... | collective-permute-start | bytes 56 | tf_op jit(solution)/shard_map/ppermute | solution.py:46
  76.1 7.4 %collective-permute-start.11 = (f32[4]{0:T(128)S(1)}, f32[4]{0:T(128)S(1)}, u32[]{:S(2)}, u32[]{:S(2)}) collective-permute-start(f32[4]{0:T(128)S(1)} %add.42), channel_id=1, source_target_pairs={{0,2},{2,0},{1,3},{3,1},{4,6},{6,4},{5,7},{7,5},{8,10},{10,8},{9,1... | collective-permute-start | bytes 56 | tf_op jit(solution)/shard_map/ppermute | solution.py:46

commit v11 on v10

--- a/solution.py
+++ b/solution.py
@@ -173,14 +173,15 @@
 
 
 def transform_kernel(
-    x_ref, mh_ref, ml_ref, fh_ref, fl_ref, gh_ref, gl_ref, fw_ref, ww_ref,
-    out_ref, y_ref, e_ref,
+    above_ref, middle_ref, below_ref, mh_ref, ml_ref, fh_ref, fl_ref, gh_ref, gl_ref, fw_ref,
+    ww_ref, out_ref, y_ref, e_ref,
 ):
-    rows = x_ref.shape[0]
+    x = jnp.concatenate([above_ref[:16], middle_ref[...], below_ref[...]], axis=0)
+    rows = x.shape[0]
     win_rows = rows // 16 - 1
-    tiles = (x_ref.shape[1] - LANES) // LANES
+    tiles = (x.shape[1] - LANES) // LANES
     stacked_x = jnp.concatenate(
-        [x_ref[:, t * LANES : (t + 2) * LANES] for t in range(tiles)], axis=0
+        [x[:, t * LANES : (t + 2) * LANES] for t in range(tiles)], axis=0
     )
     y_ref[...] = three_pass_dot(split_value(stacked_x), (mh_ref[...], ml_ref[...]))
     forward = (fh_ref[...], fl_ref[...])
@@ -209,13 +210,17 @@
         out_ref[:, t * LANES : (t + 2) * LANES] += pieces[t * rows : (t + 1) * rows]
 
 
-def analyze_weigh_synthesize(region, window_weight, freq_weight):
-    rows, cols = region.shape
+def padded_width(cols):
+    windows = (cols - 16) // 16
+    return (-(-windows // WINDOWS_PER_TILE) + 1) * LANES
+
+
+def analyze_weigh_synthesize(above, middle, below, window_weight, freq_weight, cols):
+    rows = middle.shape[0] + 32
     windows = (cols - 16) // 16
     tiles = -(-windows // WINDOWS_PER_TILE)
     wide = (tiles + 1) * LANES
     window_weight = jnp.pad(window_weight, ((0, 0), (0, tiles * WINDOWS_PER_TILE - windows)))
-    padded = jnp.pad(region, ((0, 0), (0, wide - cols)))
     win_rows = rows // 16 - 1
     constants = []
     for table in transform_tables(win_rows):
@@ -231,13 +236,13 @@
     out = pl.pallas_call(
         transform_kernel,
         out_shape=jax.ShapeDtypeStruct((rows, wide), jnp.float32),
-        in_specs=[vmem] * 9,
+        in_specs=[vmem] * 11,
         out_specs=vmem,
         scratch_shapes=[
             pltpu.VMEM((tiles * rows, 2 * HALF), jnp.float32),
             pltpu.VMEM((tiles * rows, 2 * HALF), jnp.float32),
         ],
-    )(padded, *constants, freq, weights)
+    )(above, middle, below, *constants, freq, weights)
     return out[:, :cols]
 
 
@@ -276,18 +281,24 @@
         jnp.concatenate([direction[:, -16:], rim_weight], axis=0), COL, 1
     )
     from_right = passed_along(direction[:, :16], COL, -1)
-    widened = jnp.concatenate([from_left[:height], direction, from_right], axis=1)
+    cols = breadth + 32
+    wide = padded_width(cols)
+    widened = jnp.concatenate(
+        [from_left[:height], direction, from_right, jnp.zeros((height, wide - cols), jnp.float32)],
+        axis=1,
+    )
     weights_wide = jnp.concatenate([from_left[height:, :1], window_weight], axis=1)
     top_weight = jnp.pad(weights_wide[-1:], ((0, 0), (0, widened.shape[1] - weights_wide.shape[1])))
     from_above = passed_along(
         jnp.concatenate([widened[-16:], top_weight], axis=0), "row", 1
     )
     from_below = passed_along(widened[:16], "row", -1)
-    region = jnp.concatenate([from_above[:16], widened, from_below], axis=0)
     weights_all = jnp.concatenate(
         [from_above[16:, : weights_wide.shape[1]], weights_wide], axis=0
     )
-    spread = analyze_weigh_synthesize(region, weights_all, freq_weight)
+    spread = analyze_weigh_synthesize(
+        from_above, widened, from_below, weights_all, freq_weight, cols
+    )
     synthesized = spread[16 : 16 + height, 16 : 16 + breadth]
     applied = synthesized + damping * direction
     products = jnp.stack(

time: 87.1 us -> 86.7 us (level)
    concatenate x1 -> x0, other arithmetic: 0.98 us -> none  [per_device(): region = jnp.concatenate([from_above[:16], widened, from_below], axis=0)]
  transfers between devices with their start and end apart: 12 -> 12, of which waited for: 11 -> 11; matrix products, arithmetic and copies ran while one was open for 3% -> 4% of each run, Pallas kernels for 0% -> 0%
where the time goes in v11:
time: 86.7 us; the launch traced here: 86.2 us
  starting transfers between devices  31.9 us (37%)
  waiting for transfers between devices  25.5 us (29%)
  Pallas kernels  17.7 us (20%)
  local copies, waits for them, and re-layouts  7.12 us (8%)
  other arithmetic  3.21 us (4%)
    ppermute x8, waiting for transfers between devices, summed_everywhere(): x = x + lax.ppermute(x, axis, [(i, i ^ mask) for i in range(count)])  21.6 us
    ppermute x4, starting transfers between devices, passed_along(): lax.ppermute(value, axis, [(source, source + steps) for source in range(l...  17.6 us
    pallas_call x1, Pallas kernels, analyze_weigh_synthesize(): pl.pallas_call(transform_kernel, out_shape=jax.ShapeDtypeStruct((rows, wi...  15.1 us
    ppermute x8, starting transfers between devices, summed_everywhere(): x = x + lax.ppermute(x, axis, [(i, i ^ mask) for i in range(count)])  14.3 us
    ppermute x4, waiting for transfers between devices, passed_along(): lax.ppermute(value, axis, [(source, source + steps) for source in range(l...  3.87 us
    pallas_call x1, Pallas kernels, updated(): pl.pallas_call(update_kernel, grid=(height // rows,), out_shape=(shape, s...  2.57 us
  transfers between devices with their start and end apart: 12, of which 11 were waited for; matrix products, arithmetic and copies ran while one was open for 4% of the time, Pallas kernels for 0%

profile of v11, /device:TPU:16, one launch (start us, length us, event | category | flops | bytes accessed | tf_op | source)
XLA Modules:
  0.0 86.2 jit_solution(9509179361710411567)
XLA Ops:
  2.6 1.9 %collective-permute-start = (f32[68,16]{1,0:T(8,128)S(1)}, f32[68,16]{1,0:T(8,128)S(1)}, u32[]{:S(2)}, u32[]{:S(2)}) collective-permute-start(f32[68,16]{1,0:T(8,128)S(1)} %copy.16), channel_id=1, source_target_pairs={{0,1},{1,2},{2,3},{3,4},{4,5},{5,6},{6,7},{7,8},{8,9},{9,10},{10,1... | collective-permute-start | bytes 13064 | tf_op jit(solution)/shard_map/ppermute | solution.py:30
  4.5 10.6 %collective-permute-start.1 = (f32[64,16]{1,0:T(8,128)S(1)}, f32[64,16]{1,0:T(8,128)S(1)}, u32[]{:S(2)}, u32[]{:S(2)}) collective-permute-start(f32[64,16]{1,0:T(8,128)S(1)} %get-tuple-element.10), channel_id=1, source_target_pairs={{1,0},{2,1},{3,2},{4,3},{5,4},{6,5},{7,6},{8,7},{9,8},{10,9},{11,1... | collective-permute-start | bytes 12296 | tf_op jit(solution)/shard_map/ppermute | solution.py:30
  16.7 1.4 %concatenate.16.middle_ref = f32[64,2304]{1,0:T(8,128)S(1)} concatenate(f32[64,16]{1,0:T(8,128)S(1)} %slice.42, f32[64,2048]{1,0:T(8,128)} %direction_ref.1, f32[64,16]{1,0:T(8,128)S(1)} %collective-permute-done.1, f32[64,224]{1,0:T(8,128)S(1)} %broadcast_in_dim.15), dimensions={1} | concatenate | bytes 1179648 | tf_op jit(solution)/shard_map/concatenate | solution.py:286
  18.2 3.8 %collective-permute-start.2 = (f32[17,2304]{1,0:T(8,128)S(1)}, f32[17,2304]{1,0:T(8,128)S(1)}, u32[]{:S(2)}, u32[]{:S(2)}) collective-permute-start(f32[17,2304]{1,0:T(8,128)S(1)} %pad_maximum_fusion), channel_id=1, source_target_pairs={{0,64},{64,128},{128,192},{1,65},{65,129},{129,193},{2,66},{66,130... | collective-permute-start | bytes 470024 | tf_op jit(solution)/shard_map/ppermute | solution.py:30
  22.0 1.3 %collective-permute-start.3 = (f32[16,2304]{1,0:T(8,128)S(1)}, f32[16,2304]{1,0:T(8,128)S(1)}, u32[]{:S(2)}, u32[]{:S(2)}) collective-permute-start(f32[16,2304]{1,0:T(8,128)S(1)} %get-tuple-element.5), channel_id=1, source_target_pairs={{64,0},{128,64},{192,128},{65,1},{129,65},{193,129},{66,2},{130,66... | collective-permute-start | bytes 442376 | tf_op jit(solution)/shard_map/ppermute | solution.py:30
  23.4 1.2 %reshape.19.fw_ref = f32[160,512]{1,0:T(8,128)} reshape(f32[5,32,2,8,32]{4,3,2,1,0:T(8,128)S(1)} %broadcast_in_dim.16) | data formatting | bytes 655360 | tf_op jit(solution)/shard_map/reshape | solution.py:230
  26.7 2.3 %collective-permute-done.3.below_ref = f32[16,2304]{1,0:T(8,128)S(1)} collective-permute-done((f32[16,2304]{1,0:T(8,128)S(1)}, f32[16,2304]{1,0:T(8,128)S(1)}, u32[]{:S(2)}, u32[]{:S(2)}) %collective-permute-start.3) | collective-permute-done | bytes 147488 | tf_op jit(solution)/shard_map/ppermute | solution.py:30
  29.7 15.1 %shard_map.130 = f32[96,2304]{1,0:T(8,128)} custom-call(f32[17,2304]{1,0:T(8,128)} %copy-done.4, f32[64,2304]{1,0:T(8,128)} %copy-done.2, f32[16,2304]{1,0:T(8,128)} %copy-done.5, bf16[256,512]{1,0:T(8,128)(2,1)} %constant.7.clone.mh_ref, bf16[256,512]{1,0:T(8,128)(2,1)} %constant.20.clone.ml_ref, bf16[160,192]{1,0:T(8,128)(2,1)} %constant.21.clone.fh_ref, ...), custom_call_target="tpu_custom_call" | custom-call | tf_op jit(solution)/shard_map/pallas_call | solution.py:236
  44.8 1.3 %multiply_bitcast_fusion.2 = (f32[1,64,2048]{2,1,0:T(8,128)S(1)}, f32[64,2048]{1,0:T(8,128)S(1)}) fusion(f32[64,2048]{1,0:T(8,128)S(1)} %copy-done, f32[96,2304]{1,0:T(8,128)} %shard_map.130), kind=kLoop, calls=%fused_computation.4 | loop fusion | flops 393216 | bytes 2097152 | tf_op jit(solution)/shard_map/stack | solution.py:304
  47.2 2.3 %collective-permute-start.4 = (f32[4]{0:T(128)S(1)}, f32[4]{0:T(128)S(1)}, u32[]{:S(2)}, u32[]{:S(2)}) collective-permute-start(f32[4]{0:T(128)S(1)} %maximum_reduce_fusion), channel_id=1, source_target_pairs={{0,1},{1,0},{2,3},{3,2},{4,5},{5,4},{6,7},{7,6},{8,9},{9,8},{10,11... | collective-permute-start | bytes 56 | tf_op jit(solution)/shard_map/ppermute | solution.py:46
  50.3 1.4 %collective-permute-start.5 = (f32[4]{0:T(128)S(1)}, f32[4]{0:T(128)S(1)}, u32[]{:S(2)}, u32[]{:S(2)}) collective-permute-start(f32[4]{0:T(128)S(1)} %add.34), channel_id=1, source_target_pairs={{0,64},{64,0},{128,192},{192,128},{1,65},{65,1},{129,193},{193,129... | collective-permute-start | bytes 56 | tf_op jit(solution)/shard_map/ppermute | solution.py:46
  51.6 2.2 %collective-permute-done.5 = f32[4]{0:T(128)S(1)} collective-permute-done((f32[4]{0:T(128)S(1)}, f32[4]{0:T(128)S(1)}, u32[]{:S(2)}, u32[]{:S(2)}) %collective-permute-start.5) | collective-permute-done | bytes 48 | tf_op jit(solution)/shard_map/ppermute | solution.py:46
  53.8 3.1 %collective-permute-start.6 = (f32[4]{0:T(128)S(1)}, f32[4]{0:T(128)S(1)}, u32[]{:S(2)}, u32[]{:S(2)}) collective-permute-start(f32[4]{0:T(128)S(1)} %add.35), channel_id=1, source_target_pairs={{0,128},{64,192},{128,0},{192,64},{1,129},{65,193},{129,1},{193,65... | collective-permute-start | bytes 56 | tf_op jit(solution)/shard_map/ppermute | solution.py:46
  57.0 1.5 %collective-permute-done.6 = f32[4]{0:T(128)S(1)} collective-permute-done((f32[4]{0:T(128)S(1)}, f32[4]{0:T(128)S(1)}, u32[]{:S(2)}, u32[]{:S(2)}) %collective-permute-start.6) | collective-permute-done | bytes 48 | tf_op jit(solution)/shard_map/ppermute | solution.py:46
  58.5 1.3 %collective-permute-start.7 = (f32[4]{0:T(128)S(1)}, f32[4]{0:T(128)S(1)}, u32[]{:S(2)}, u32[]{:S(2)}) collective-permute-start(f32[4]{0:T(128)S(1)} %add.36), channel_id=1, source_target_pairs={{0,16},{16,0},{32,48},{48,32},{1,17},{17,1},{33,49},{49,33},{2,18}... | collective-permute-start | bytes 56 | tf_op jit(solution)/shard_map/ppermute | solution.py:46
  59.8 2.3 %collective-permute-done.7 = f32[4]{0:T(128)S(1)} collective-permute-done((f32[4]{0:T(128)S(1)}, f32[4]{0:T(128)S(1)}, u32[]{:S(2)}, u32[]{:S(2)}) %collective-permute-start.7) | collective-permute-done | bytes 48 | tf_op jit(solution)/shard_map/ppermute | solution.py:46
  62.0 5.0 %collective-permute-done.8 = f32[4]{0:T(128)S(1)} collective-permute-done((f32[4]{0:T(128)S(1)}, f32[4]{0:T(128)S(1)}, u32[]{:S(2)}, u32[]{:S(2)}) %collective-permute-start.8) | collective-permute-done | bytes 48 | tf_op jit(solution)/shard_map/ppermute | solution.py:46
  67.1 1.2 %collective-permute-start.9 = (f32[4]{0:T(128)S(1)}, f32[4]{0:T(128)S(1)}, u32[]{:S(2)}, u32[]{:S(2)}) collective-permute-start(f32[4]{0:T(128)S(1)} %add.38), channel_id=1, source_target_pairs={{0,4},{4,0},{8,12},{12,8},{1,5},{5,1},{9,13},{13,9},{2,6},{6,2},{1... | collective-permute-start | bytes 56 | tf_op jit(solution)/shard_map/ppermute | solution.py:46
  68.2 2.4 %collective-permute-done.9 = f32[4]{0:T(128)S(1)} collective-permute-done((f32[4]{0:T(128)S(1)}, f32[4]{0:T(128)S(1)}, u32[]{:S(2)}, u32[]{:S(2)}) %collective-permute-start.9) | collective-permute-done | bytes 48 | tf_op jit(solution)/shard_map/ppermute | solution.py:46
  70.6 2.7 %collective-permute-start.10 = (f32[4]{0:T(128)S(1)}, f32[4]{0:T(128)S(1)}, u32[]{:S(2)}, u32[]{:S(2)}) collective-permute-start(f32[4]{0:T(128)S(1)} %add.39), channel_id=1, source_target_pairs={{0,8},{4,12},{8,0},{12,4},{1,9},{5,13},{9,1},{13,5},{2,10},{6,14},... | collective-permute-start | bytes 56 | tf_op jit(solution)/shard_map/ppermute | solution.py:46
  73.3 2.3 %collective-permute-done.10 = f32[4]{0:T(128)S(1)} collective-permute-done((f32[4]{0:T(128)S(1)}, f32[4]{0:T(128)S(1)}, u32[]{:S(2)}, u32[]{:S(2)}) %collective-permute-start.10) | collective-permute-done | bytes 48 | tf_op jit(solution)/shard_map/ppermute | solution.py:46
  75.7 2.4 %collective-permute-start.11 = (f32[4]{0:T(128)S(1)}, f32[4]{0:T(128)S(1)}, u32[]{:S(2)}, u32[]{:S(2)}) collective-permute-start(f32[4]{0:T(128)S(1)} %add.40), channel_id=1, source_target_pairs={{0,2},{2,0},{1,3},{3,1},{4,6},{6,4},{5,7},{7,5},{8,10},{10,8},{9,1... | collective-permute-start | bytes 56 | tf_op jit(solution)/shard_map/ppermute | solution.py:46
  78.1 5.0 %collective-permute-done.11 = f32[4]{0:T(128)S(1)} collective-permute-done((f32[4]{0:T(128)S(1)}, f32[4]{0:T(128)S(1)}, u32[]{:S(2)}, u32[]{:S(2)}) %collective-permute-start.11) | collective-permute-done | bytes 48 | tf_op jit(solution)/shard_map/ppermute | solution.py:46
  83.6 2.6 %shard_map.131 = (f32[64,2048]{1,0:T(8,128)}, f32[64,2048]{1,0:T(8,128)}, f32[64,2048]{1,0:T(8,128)}) custom-call(f32[1,4]{1,0:T(1,128)} %add_bitcast_fusion.sums_ref, f32[64,2048]{1,0:T(8,128)} %iterate_ref.1, f32[64,2048]{1,0:T(8,128)} %residual_ref.1, f32[64,2048]{1,0:T(8,128)} %direction_ref.1, f32[64,2048]{1,0:T(8,128)} %copy-done.1), custom_call_target="tpu_custom_call" | custom-call | tf_op jit(solution)/shard_map/pallas_call | solution.py:268
  (49 shorter events, 8.8 us)
Async XLA Ops:
  0.6 22.6 %copy-start.7 = (f32[32,32]{1,0:T(8,128)S(1)}, f32[32,32]{1,0:T(8,128)}, u32[]{:S(2)}) copy-start(f32[32,32]{1,0:T(8,128)} %param.15) | copy-start | bytes 12292
  2.6 12.6 %collective-permute-start = (f32[68,16]{1,0:T(8,128)S(1)}, f32[68,16]{1,0:T(8,128)S(1)}, u32[]{:S(2)}, u32[]{:S(2)}) collective-permute-start(f32[68,16]{1,0:T(8,128)S(1)} %copy.16), channel_id=1, source_target_pairs={{0,1},{1,2},{2,3},{3,4},{4,5},{5,6},{6,7},{7,8},{8,9},{9,10},{10,1... | collective-permute-start | bytes 13064 | tf_op jit(solution)/shard_map/ppermute | solution.py:30
  4.5 12.2 %collective-permute-start.1 = (f32[64,16]{1,0:T(8,128)S(1)}, f32[64,16]{1,0:T(8,128)S(1)}, u32[]{:S(2)}, u32[]{:S(2)}) collective-permute-start(f32[64,16]{1,0:T(8,128)S(1)} %get-tuple-element.10), channel_id=1, source_target_pairs={{1,0},{2,1},{3,2},{4,3},{5,4},{6,5},{7,6},{8,7},{9,8},{10,9},{11,1... | collective-permute-start | bytes 12296 | tf_op jit(solution)/shard_map/ppermute | solution.py:30
  18.1 6.5 %copy-start.2 = (f32[64,2304]{1,0:T(8,128)}, f32[64,2304]{1,0:T(8,128)S(1)}, u32[]{:S(2)}) copy-start(f32[64,2304]{1,0:T(8,128)S(1)} %concatenate.16.middle_ref) | copy-start | bytes 1769476
  18.2 7.2 %collective-permute-start.2 = (f32[17,2304]{1,0:T(8,128)S(1)}, f32[17,2304]{1,0:T(8,128)S(1)}, u32[]{:S(2)}, u32[]{:S(2)}) collective-permute-start(f32[17,2304]{1,0:T(8,128)S(1)} %pad_maximum_fusion), channel_id=1, source_target_pairs={{0,64},{64,128},{128,192},{1,65},{65,129},{129,193},{2,66},{66,130... | collective-permute-start | bytes 470024 | tf_op jit(solution)/shard_map/ppermute | solution.py:30
  22.0 3.4 %copy-start.6 = (f32[4,128]{1,0:T(4,128)S(1)}, f32[4,128]{1,0:T(4,128)}, u32[]{:S(2)}) copy-start(f32[4,128]{1,0:T(4,128)} %param.14) | copy-start | bytes 6148
  22.0 7.0 %collective-permute-start.3 = (f32[16,2304]{1,0:T(8,128)S(1)}, f32[16,2304]{1,0:T(8,128)S(1)}, u32[]{:S(2)}, u32[]{:S(2)}) collective-permute-start(f32[16,2304]{1,0:T(8,128)S(1)} %get-tuple-element.5), channel_id=1, source_target_pairs={{64,0},{128,64},{192,128},{65,1},{129,65},{193,129},{66,2},{130,66... | collective-permute-start | bytes 442376 | tf_op jit(solution)/shard_map/ppermute | solution.py:30
  25.4 3.6 %copy-start.4 = (f32[17,2304]{1,0:T(8,128)}, f32[17,2304]{1,0:T(8,128)S(1)}, u32[]{:S(2)}) copy-start(f32[17,2304]{1,0:T(8,128)S(1)} %collective-permute-done.2.above_ref) | copy-start | bytes 470020
  26.7 18.1 %copy-start = (f32[64,2048]{1,0:T(8,128)S(1)}, f32[64,2048]{1,0:T(8,128)}, u32[]{:S(2)}) copy-start(f32[64,2048]{1,0:T(8,128)} %direction_ref.1) | copy-start | bytes 1572868
  29.0 0.7 copy-start.5
  44.8 1.3 %copy-start.3 = (f32[64,2048]{1,0:T(8,128)S(1)}, f32[64,2048]{1,0:T(8,128)}, u32[]{:S(2)}) copy-start(f32[64,2048]{1,0:T(8,128)} %residual_ref.1) | copy-start | bytes 1572868
  46.1 0.8 copy-start.1
  47.2 3.1 %collective-permute-start.4 = (f32[4]{0:T(128)S(1)}, f32[4]{0:T(128)S(1)}, u32[]{:S(2)}, u32[]{:S(2)}) collective-permute-start(f32[4]{0:T(128)S(1)} %maximum_reduce_fusion), channel_id=1, source_target_pairs={{0,1},{1,0},{2,3},{3,2},{4,5},{5,4},{6,7},{7,6},{8,9},{9,8},{10,11... | collective-permute-start | bytes 56 | tf_op jit(solution)/shard_map/ppermute | solution.py:46
  50.3 3.5 %collective-permute-start.5 = (f32[4]{0:T(128)S(1)}, f32[4]{0:T(128)S(1)}, u32[]{:S(2)}, u32[]{:S(2)}) collective-permute-start(f32[4]{0:T(128)S(1)} %add.34), channel_id=1, source_target_pairs={{0,64},{64,0},{128,192},{192,128},{1,65},{65,1},{129,193},{193,129... | collective-permute-start | bytes 56 | tf_op jit(solution)/shard_map/ppermute | solution.py:46
  53.8 4.7 %collective-permute-start.6 = (f32[4]{0:T(128)S(1)}, f32[4]{0:T(128)S(1)}, u32[]{:S(2)}, u32[]{:S(2)}) collective-permute-start(f32[4]{0:T(128)S(1)} %add.35), channel_id=1, source_target_pairs={{0,128},{64,192},{128,0},{192,64},{1,129},{65,193},{129,1},{193,65... | collective-permute-start | bytes 56 | tf_op jit(solution)/shard_map/ppermute | solution.py:46
  58.5 3.5 %collective-permute-start.7 = (f32[4]{0:T(128)S(1)}, f32[4]{0:T(128)S(1)}, u32[]{:S(2)}, u32[]{:S(2)}) collective-permute-start(f32[4]{0:T(128)S(1)} %add.36), channel_id=1, source_target_pairs={{0,16},{16,0},{32,48},{48,32},{1,17},{17,1},{33,49},{49,33},{2,18}... | collective-permute-start | bytes 56 | tf_op jit(solution)/shard_map/ppermute | solution.py:46
  62.0 5.0 %collective-permute-start.8 = (f32[4]{0:T(128)S(1)}, f32[4]{0:T(128)S(1)}, u32[]{:S(2)}, u32[]{:S(2)}) collective-permute-start(f32[4]{0:T(128)S(1)} %add.37), channel_id=1, source_target_pairs={{0,32},{16,48},{32,0},{48,16},{1,33},{17,49},{33,1},{49,17},{2,34}... | collective-permute-start | bytes 56 | tf_op jit(solution)/shard_map/ppermute | solution.py:46
  67.1 3.5 %collective-permute-start.9 = (f32[4]{0:T(128)S(1)}, f32[4]{0:T(128)S(1)}, u32[]{:S(2)}, u32[]{:S(2)}) collective-permute-start(f32[4]{0:T(128)S(1)} %add.38), channel_id=1, source_target_pairs={{0,4},{4,0},{8,12},{12,8},{1,5},{5,1},{9,13},{13,9},{2,6},{6,2},{1... | collective-permute-start | bytes 56 | tf_op jit(solution)/shard_map/ppermute | solution.py:46
  70.6 5.0 %collective-permute-start.10 = (f32[4]{0:T(128)S(1)}, f32[4]{0:T(128)S(1)}, u32[]{:S(2)}, u32[]{:S(2)}) collective-permute-start(f32[4]{0:T(128)S(1)} %add.39), channel_id=1, source_target_pairs={{0,8},{4,12},{8,0},{12,4},{1,9},{5,13},{9,1},{13,5},{2,10},{6,14},... | collective-permute-start | bytes 56 | tf_op jit(solution)/shard_map/ppermute | solution.py:46
  75.7 7.4 %collective-permute-start.11 = (f32[4]{0:T(128)S(1)}, f32[4]{0:T(128)S(1)}, u32[]{:S(2)}, u32[]{:S(2)}) collective-permute-start(f32[4]{0:T(128)S(1)} %add.40), channel_id=1, source_target_pairs={{0,2},{2,0},{1,3},{3,1},{4,6},{6,4},{5,7},{7,5},{8,10},{10,8},{9,1... | collective-permute-start | bytes 56 | tf_op jit(solution)/shard_map/ppermute | solution.py:46

commit v12 on v11

--- a/solution.py
+++ b/solution.py
@@ -276,29 +276,45 @@
 
 def per_device(iterate, residual, direction, window_weight, freq_weight):
     height, breadth = direction.shape
+    count = window_weight.shape[1]
     rim_weight = jnp.pad(window_weight[:, -1:], ((0, 0), (0, 15)))
     from_left = passed_along(
         jnp.concatenate([direction[:, -16:], rim_weight], axis=0), COL, 1
     )
     from_right = passed_along(direction[:, :16], COL, -1)
+    top_weight = jnp.pad(window_weight[-1:], ((0, 0), (0, breadth - count)))
+    from_above = passed_along(jnp.concatenate([direction[-16:], top_weight], axis=0), "row", 1)
+    from_below = passed_along(direction[:16], "row", -1)
+    corner_weight = jnp.pad(from_left[-1:, :1], ((0, 0), (0, 31)))
+    upper_corners = passed_along(
+        jnp.concatenate(
+            [jnp.concatenate([from_left[height - 16 : height], from_right[-16:]], axis=1), corner_weight],
+            axis=0,
+        ),
+        "row",
+        1,
+    )
+    lower_corners = passed_along(
+        jnp.concatenate([from_left[:16], from_right[:16]], axis=1), "row", -1
+    )
     cols = breadth + 32
     wide = padded_width(cols)
-    widened = jnp.concatenate(
-        [from_left[:height], direction, from_right, jnp.zeros((height, wide - cols), jnp.float32)],
-        axis=1,
-    )
-    weights_wide = jnp.concatenate([from_left[height:, :1], window_weight], axis=1)
-    top_weight = jnp.pad(weights_wide[-1:], ((0, 0), (0, widened.shape[1] - weights_wide.shape[1])))
-    from_above = passed_along(
-        jnp.concatenate([widened[-16:], top_weight], axis=0), "row", 1
-    )
-    from_below = passed_along(widened[:16], "row", -1)
+    def band(left, middle, right):
+        rows = middle.shape[0]
+        return jnp.concatenate(
+            [left, middle, right, jnp.zeros((rows, wide - cols), jnp.float32)], axis=1
+        )
+    widened = band(from_left[:height], direction, from_right)
+    above = band(upper_corners[:16, :16], from_above[:16], upper_corners[:16, 16:])
+    below = band(lower_corners[:, :16], from_below, lower_corners[:, 16:])
     weights_all = jnp.concatenate(
-        [from_above[16:, : weights_wide.shape[1]], weights_wide], axis=0
-    )
-    spread = analyze_weigh_synthesize(
-        from_above, widened, from_below, weights_all, freq_weight, cols
-    )
+        [
+            jnp.concatenate([upper_corners[16:, :1], from_above[16:, :count]], axis=1),
+            jnp.concatenate([from_left[height:, :1], window_weight], axis=1),
+        ],
+        axis=0,
+    )
+    spread = analyze_weigh_synthesize(above, widened, below, weights_all, freq_weight, cols)
     synthesized = spread[16 : 16 + height, 16 : 16 + breadth]
     applied = synthesized + damping * direction
     products = jnp.stack(

time: 86.7 us -> 93.3 us (1.076)
  local copies, waits for them, and re-layouts: 7.12 us -> 11.2 us
  starting transfers between devices: 31.9 us -> 35.7 us
  waiting for transfers between devices: 25.5 us -> 23.5 us
    ppermute x4 -> x6, starting transfers between devices: 17.6 us -> 24.2 us  [passed_along(): lax.ppermute(value, axis, [(source, source + steps) for source in range(l...]
    ppermute x4 -> x6, waiting for transfers between devices: 3.87 us -> 0.19 us  [passed_along(): lax.ppermute(value, axis, [(source, source + steps) for source in range(l...]
    ppermute x8, starting transfers between devices: 14.3 us -> 11.5 us  [summed_everywhere(): x = x + lax.ppermute(x, axis, [(i, i ^ mask) for i in range(count)])]
    slice x3 -> x11, local copies, waits for them, and re-layouts: 0.03 us -> 2.86 us  [the longest x1 0.99 us: per_device(): from_below = passed_along(direction[:16], 'row', -1)]
    ppermute x8, waiting for transfers between devices: 21.6 us -> 23.3 us  [summed_everywhere(): x = x + lax.ppermute(x, axis, [(i, i ^ mask) for i in range(count)])]
    concatenate x1 -> x3, local copies, waits for them, and re-layouts: 1.38 us -> 2.63 us  [band(): jnp.concatenate([left, middle, right, jnp.zeros((rows, wide - cols), jnp....]
  transfers between devices with their start and end apart: 12 -> 14, of which waited for: 11 -> 9; matrix products, arithmetic and copies ran while one was open for 4% -> 8% of each run, Pallas kernels for 0% -> 0%
where the time goes in v12:
time: 93.3 us; the launch traced here: 92.8 us
  starting transfers between devices  35.7 us (38%)
  waiting for transfers between devices  23.5 us (25%)
  Pallas kernels  17.6 us (19%)
  local copies, waits for them, and re-layouts  11.2 us (12%)
  other arithmetic  3.92 us (4%)
    ppermute x6, starting transfers between devices, passed_along(): lax.ppermute(value, axis, [(source, source + steps) for source in range(l...  24.2 us
    ppermute x8, waiting for transfers between devices, summed_everywhere(): x = x + lax.ppermute(x, axis, [(i, i ^ mask) for i in range(count)])  23.3 us
    pallas_call x1, Pallas kernels, analyze_weigh_synthesize(): pl.pallas_call(transform_kernel, out_shape=jax.ShapeDtypeStruct((rows, wi...  15.1 us
    ppermute x8, starting transfers between devices, summed_everywhere(): x = x + lax.ppermute(x, axis, [(i, i ^ mask) for i in range(count)])  11.5 us
    concatenate x3, local copies, waits for them, and re-layouts, band(): jnp.concatenate([left, middle, right, jnp.zeros((rows, wide - cols), jnp....  2.63 us
    pallas_call x1, Pallas kernels, updated(): pl.pallas_call(update_kernel, grid=(height // rows,), out_shape=(shape, s...  2.57 us
  transfers between devices with their start and end apart: 14, of which 9 were waited for; matrix products, arithmetic and copies ran while one was open for 8% of the time, Pallas kernels for 0%

profile of v12, /device:TPU:16, one launch (start us, length us, event | category | flops | bytes accessed | tf_op | source)
XLA Modules:
  0.0 92.8 jit_solution(4787787842569347612)
XLA Ops:
  2.6 1.9 %collective-permute-start = (f32[68,16]{1,0:T(8,128)S(1)}, f32[68,16]{1,0:T(8,128)S(1)}, u32[]{:S(2)}, u32[]{:S(2)}) collective-permute-start(f32[68,16]{1,0:T(8,128)S(1)} %copy.16), channel_id=1, source_target_pairs={{0,1},{1,2},{2,3},{3,4},{4,5},{5,6},{6,7},{7,8},{8,9},{9,10},{10,1... | collective-permute-start | bytes 13064 | tf_op jit(solution)/shard_map/ppermute | solution.py:30
  4.5 10.6 %collective-permute-start.1 = (f32[64,16]{1,0:T(8,128)S(1)}, f32[64,16]{1,0:T(8,128)S(1)}, u32[]{:S(2)}, u32[]{:S(2)}) collective-permute-start(f32[64,16]{1,0:T(8,128)S(1)} %get-tuple-element.10), channel_id=1, source_target_pairs={{1,0},{2,1},{3,2},{4,3},{5,4},{6,5},{7,6},{8,7},{9,8},{10,9},{11,1... | collective-permute-start | bytes 12296 | tf_op jit(solution)/shard_map/ppermute | solution.py:30
  16.8 3.8 %collective-permute-start.3 = (f32[17,2048]{1,0:T(8,128)S(1)}, f32[17,2048]{1,0:T(8,128)S(1)}, u32[]{:S(2)}, u32[]{:S(2)}) collective-permute-start(f32[17,2048]{1,0:T(8,128)S(1)} %select_maximum_fusion), channel_id=1, source_target_pairs={{0,64},{64,128},{128,192},{1,65},{65,129},{129,193},{2,66},{66,130... | collective-permute-start | bytes 417800 | tf_op jit(solution)/shard_map/ppermute | solution.py:30
  20.6 1.4 %collective-permute-start.5 = (f32[16,2048]{1,0:T(8,128)S(1)}, f32[16,2048]{1,0:T(8,128)S(1)}, u32[]{:S(2)}, u32[]{:S(2)}) collective-permute-start(f32[16,2048]{1,0:T(8,128)S(1)} %get-tuple-element.8), channel_id=1, source_target_pairs={{64,0},{128,64},{192,128},{65,1},{129,65},{193,129},{66,2},{130,66... | collective-permute-start | bytes 393224 | tf_op jit(solution)/shard_map/ppermute | solution.py:30
  22.9 1.2 %reshape.19.fw_ref = f32[160,512]{1,0:T(8,128)} reshape(f32[5,32,2,8,32]{4,3,2,1,0:T(8,128)S(1)} %broadcast_in_dim.16) | data formatting | bytes 655360 | tf_op jit(solution)/shard_map/reshape | solution.py:230
  24.2 1.3 %collective-permute-start.4 = (f32[16,32]{1,0:T(8,128)S(1)}, f32[16,32]{1,0:T(8,128)S(1)}, u32[]{:S(2)}, u32[]{:S(2)}) collective-permute-start(f32[16,32]{1,0:T(8,128)S(1)} %pad_maximum_fusion), channel_id=1, source_target_pairs={{64,0},{128,64},{192,128},{65,1},{129,65},{193,129},{66,2},{130,66... | collective-permute-start | bytes 6152 | tf_op jit(solution)/shard_map/ppermute | solution.py:30
  26.7 5.2 %collective-permute-start.2 = (f32[17,32]{1,0:T(8,128)S(1)}, f32[17,32]{1,0:T(8,128)S(1)}, u32[]{:S(2)}, u32[]{:S(2)}) collective-permute-start(f32[17,32]{1,0:T(8,128)S(1)} %select_maximum_fusion.1), channel_id=1, source_target_pairs={{0,64},{64,128},{128,192},{1,65},{65,129},{129,193},{2,66},{66,130... | collective-permute-start | bytes 6536 | tf_op jit(solution)/shard_map/ppermute | solution.py:30
  31.9 1.1 %concatenate.38.middle_ref = f32[64,2304]{1,0:T(8,128)} concatenate(f32[64,16]{1,0:T(8,128)S(1)} %slice.92, f32[64,2048]{1,0:T(8,128)S(1)} %copy-done, f32[64,16]{1,0:T(8,128)S(1)} %collective-permute-done.1, f32[64,224]{1,0:T(8,128)S(1)} %broadcast_in_dim.15), dimensions={1} | concatenate | bytes 1179648 | tf_op jit(solution)/shard_map/concatenate | solution.py:304
  35.6 1.0 %reshape.20.ww_ref = f32[5,8704]{1,0:T(8,128)} reshape(f32[5,17,2,8,32]{4,3,2,1,0:T(8,128)S(1)} %broadcast_in_dim.18) | data formatting | bytes 348160 | tf_op jit(solution)/shard_map/reshape | solution.py:234
  37.4 15.1 %shard_map.130 = f32[96,2304]{1,0:T(8,128)} custom-call(f32[16,2304]{1,0:T(8,128)} %concatenate.37.above_ref, f32[64,2304]{1,0:T(8,128)} %concatenate.38.middle_ref, f32[16,2304]{1,0:T(8,128)} %concatenate.40.below_ref, bf16[256,512]{1,0:T(8,128)(2,1)} %constant.10.clone.mh_ref, bf16[256,512]{1,0:T(8,128)(2,1)} %constant.7.clone.ml_ref, ...), custom_call_target="tpu_custom_call" | custom-call | tf_op jit(solution)/shard_map/pallas_call | solution.py:236
  52.5 1.3 %multiply_bitcast_fusion.2 = (f32[1,64,2048]{2,1,0:T(8,128)S(1)}, f32[64,2048]{1,0:T(8,128)S(1)}) fusion(f32[64,2048]{1,0:T(8,128)S(1)} %copy-done, f32[96,2304]{1,0:T(8,128)} %shard_map.130), kind=kLoop, calls=%fused_computation.4 | loop fusion | flops 393216 | bytes 2097152 | tf_op jit(solution)/shard_map/stack | solution.py:320
  55.1 1.1 %collective-permute-done.6 = f32[4]{0:T(128)S(1)} collective-permute-done((f32[4]{0:T(128)S(1)}, f32[4]{0:T(128)S(1)}, u32[]{:S(2)}, u32[]{:S(2)}) %collective-permute-start.6) | collective-permute-done | bytes 48 | tf_op jit(solution)/shard_map/ppermute | solution.py:46
  56.2 2.3 %collective-permute-start.7 = (f32[4]{0:T(128)S(1)}, f32[4]{0:T(128)S(1)}, u32[]{:S(2)}, u32[]{:S(2)}) collective-permute-start(f32[4]{0:T(128)S(1)} %add.36), channel_id=1, source_target_pairs={{0,64},{64,0},{128,192},{192,128},{1,65},{65,1},{129,193},{193,129... | collective-permute-start | bytes 56 | tf_op jit(solution)/shard_map/ppermute | solution.py:46
  58.5 1.5 %collective-permute-done.7 = f32[4]{0:T(128)S(1)} collective-permute-done((f32[4]{0:T(128)S(1)}, f32[4]{0:T(128)S(1)}, u32[]{:S(2)}, u32[]{:S(2)}) %collective-permute-start.7) | collective-permute-done | bytes 48 | tf_op jit(solution)/shard_map/ppermute | solution.py:46
  60.0 3.5 %collective-permute-start.8 = (f32[4]{0:T(128)S(1)}, f32[4]{0:T(128)S(1)}, u32[]{:S(2)}, u32[]{:S(2)}) collective-permute-start(f32[4]{0:T(128)S(1)} %add.37), channel_id=1, source_target_pairs={{0,128},{64,192},{128,0},{192,64},{1,129},{65,193},{129,1},{193,65... | collective-permute-start | bytes 56 | tf_op jit(solution)/shard_map/ppermute | solution.py:46
  63.5 1.5 %collective-permute-done.8 = f32[4]{0:T(128)S(1)} collective-permute-done((f32[4]{0:T(128)S(1)}, f32[4]{0:T(128)S(1)}, u32[]{:S(2)}, u32[]{:S(2)}) %collective-permute-start.8) | collective-permute-done | bytes 48 | tf_op jit(solution)/shard_map/ppermute | solution.py:46
  65.0 1.3 %collective-permute-start.9 = (f32[4]{0:T(128)S(1)}, f32[4]{0:T(128)S(1)}, u32[]{:S(2)}, u32[]{:S(2)}) collective-permute-start(f32[4]{0:T(128)S(1)} %add.38), channel_id=1, source_target_pairs={{0,16},{16,0},{32,48},{48,32},{1,17},{17,1},{33,49},{49,33},{2,18}... | collective-permute-start | bytes 56 | tf_op jit(solution)/shard_map/ppermute | solution.py:46
  66.3 2.3 %collective-permute-done.9 = f32[4]{0:T(128)S(1)} collective-permute-done((f32[4]{0:T(128)S(1)}, f32[4]{0:T(128)S(1)}, u32[]{:S(2)}, u32[]{:S(2)}) %collective-permute-start.9) | collective-permute-done | bytes 48 | tf_op jit(solution)/shard_map/ppermute | solution.py:46
  68.6 5.0 %collective-permute-done.10 = f32[4]{0:T(128)S(1)} collective-permute-done((f32[4]{0:T(128)S(1)}, f32[4]{0:T(128)S(1)}, u32[]{:S(2)}, u32[]{:S(2)}) %collective-permute-start.10) | collective-permute-done | bytes 48 | tf_op jit(solution)/shard_map/ppermute | solution.py:46
  73.6 3.5 %collective-permute-done.11 = f32[4]{0:T(128)S(1)} collective-permute-done((f32[4]{0:T(128)S(1)}, f32[4]{0:T(128)S(1)}, u32[]{:S(2)}, u32[]{:S(2)}) %collective-permute-start.11) | collective-permute-done | bytes 48 | tf_op jit(solution)/shard_map/ppermute | solution.py:46
  78.1 4.1 %collective-permute-done.12 = f32[4]{0:T(128)S(1)} collective-permute-done((f32[4]{0:T(128)S(1)}, f32[4]{0:T(128)S(1)}, u32[]{:S(2)}, u32[]{:S(2)}) %collective-permute-start.12) | collective-permute-done | bytes 48 | tf_op jit(solution)/shard_map/ppermute | solution.py:46
  82.2 3.3 %collective-permute-start.13 = (f32[4]{0:T(128)S(1)}, f32[4]{0:T(128)S(1)}, u32[]{:S(2)}, u32[]{:S(2)}) collective-permute-start(f32[4]{0:T(128)S(1)} %add.42), channel_id=1, source_target_pairs={{0,2},{2,0},{1,3},{3,1},{4,6},{6,4},{5,7},{7,5},{8,10},{10,8},{9,1... | collective-permute-start | bytes 56 | tf_op jit(solution)/shard_map/ppermute | solution.py:46
  85.5 4.2 %collective-permute-done.13 = f32[4]{0:T(128)S(1)} collective-permute-done((f32[4]{0:T(128)S(1)}, f32[4]{0:T(128)S(1)}, u32[]{:S(2)}, u32[]{:S(2)}) %collective-permute-start.13) | collective-permute-done | bytes 48 | tf_op jit(solution)/shard_map/ppermute | solution.py:46
  90.2 2.6 %shard_map.131 = (f32[64,2048]{1,0:T(8,128)}, f32[64,2048]{1,0:T(8,128)}, f32[64,2048]{1,0:T(8,128)}) custom-call(f32[1,4]{1,0:T(1,128)} %add_bitcast_fusion.sums_ref, f32[64,2048]{1,0:T(8,128)} %iterate_ref.1, f32[64,2048]{1,0:T(8,128)} %residual_ref.1, f32[64,2048]{1,0:T(8,128)} %direction_ref.1, f32[64,2048]{1,0:T(8,128)} %copy-done.1), custom_call_target="tpu_custom_call" | custom-call | tf_op jit(solution)/shard_map/pallas_call | solution.py:268
  (57 shorter events, 11.9 us)
Async XLA Ops:
  2.6 21.5 %collective-permute-start = (f32[68,16]{1,0:T(8,128)S(1)}, f32[68,16]{1,0:T(8,128)S(1)}, u32[]{:S(2)}, u32[]{:S(2)}) collective-permute-start(f32[68,16]{1,0:T(8,128)S(1)} %copy.16), channel_id=1, source_target_pairs={{0,1},{1,2},{2,3},{3,4},{4,5},{5,6},{6,7},{7,8},{8,9},{9,10},{10,1... | collective-permute-start | bytes 13064 | tf_op jit(solution)/shard_map/ppermute | solution.py:30
  4.5 19.6 %collective-permute-start.1 = (f32[64,16]{1,0:T(8,128)S(1)}, f32[64,16]{1,0:T(8,128)S(1)}, u32[]{:S(2)}, u32[]{:S(2)}) collective-permute-start(f32[64,16]{1,0:T(8,128)S(1)} %get-tuple-element.10), channel_id=1, source_target_pairs={{1,0},{2,1},{3,2},{4,3},{5,4},{6,5},{7,6},{8,7},{9,8},{10,9},{11,1... | collective-permute-start | bytes 12296 | tf_op jit(solution)/shard_map/ppermute | solution.py:30
  16.8 17.8 %collective-permute-start.3 = (f32[17,2048]{1,0:T(8,128)S(1)}, f32[17,2048]{1,0:T(8,128)S(1)}, u32[]{:S(2)}, u32[]{:S(2)}) collective-permute-start(f32[17,2048]{1,0:T(8,128)S(1)} %select_maximum_fusion), channel_id=1, source_target_pairs={{0,64},{64,128},{128,192},{1,65},{65,129},{129,193},{2,66},{66,130... | collective-permute-start | bytes 417800 | tf_op jit(solution)/shard_map/ppermute | solution.py:30
  20.6 11.3 %copy-start = (f32[64,2048]{1,0:T(8,128)S(1)}, f32[64,2048]{1,0:T(8,128)}, u32[]{:S(2)}) copy-start(f32[64,2048]{1,0:T(8,128)} %direction_ref.1) | copy-start | bytes 1572868
  20.6 13.2 %collective-permute-start.5 = (f32[16,2048]{1,0:T(8,128)S(1)}, f32[16,2048]{1,0:T(8,128)S(1)}, u32[]{:S(2)}, u32[]{:S(2)}) collective-permute-start(f32[16,2048]{1,0:T(8,128)S(1)} %get-tuple-element.8), channel_id=1, source_target_pairs={{64,0},{128,64},{192,128},{65,1},{129,65},{193,129},{66,2},{130,66... | collective-permute-start | bytes 393224 | tf_op jit(solution)/shard_map/ppermute | solution.py:30
  24.1 10.6 %copy-start.3 = (f32[4,128]{1,0:T(4,128)S(1)}, f32[4,128]{1,0:T(4,128)}, u32[]{:S(2)}) copy-start(f32[4,128]{1,0:T(4,128)} %param.14) | copy-start | bytes 6148
  24.2 8.8 %collective-permute-start.4 = (f32[16,32]{1,0:T(8,128)S(1)}, f32[16,32]{1,0:T(8,128)S(1)}, u32[]{:S(2)}, u32[]{:S(2)}) collective-permute-start(f32[16,32]{1,0:T(8,128)S(1)} %pad_maximum_fusion), channel_id=1, source_target_pairs={{64,0},{128,64},{192,128},{65,1},{129,65},{193,129},{66,2},{130,66... | collective-permute-start | bytes 6152 | tf_op jit(solution)/shard_map/ppermute | solution.py:30
  26.7 6.6 %collective-permute-start.2 = (f32[17,32]{1,0:T(8,128)S(1)}, f32[17,32]{1,0:T(8,128)S(1)}, u32[]{:S(2)}, u32[]{:S(2)}) collective-permute-start(f32[17,32]{1,0:T(8,128)S(1)} %select_maximum_fusion.1), channel_id=1, source_target_pairs={{0,64},{64,128},{128,192},{1,65},{65,129},{129,193},{2,66},{66,130... | collective-permute-start | bytes 6536 | tf_op jit(solution)/shard_map/ppermute | solution.py:30
  52.5 1.3 %copy-start.2 = (f32[64,2048]{1,0:T(8,128)S(1)}, f32[64,2048]{1,0:T(8,128)}, u32[]{:S(2)}) copy-start(f32[64,2048]{1,0:T(8,128)} %residual_ref.1) | copy-start | bytes 1572868
  53.8 0.8 copy-start.1
  54.9 1.3 %collective-permute-start.6 = (f32[4]{0:T(128)S(1)}, f32[4]{0:T(128)S(1)}, u32[]{:S(2)}, u32[]{:S(2)}) collective-permute-start(f32[4]{0:T(128)S(1)} %maximum_reduce_fusion), channel_id=1, source_target_pairs={{0,1},{1,0},{2,3},{3,2},{4,5},{5,4},{6,7},{7,6},{8,9},{9,8},{10,11... | collective-permute-start | bytes 56 | tf_op jit(solution)/shard_map/ppermute | solution.py:46
  56.2 3.8 %collective-permute-start.7 = (f32[4]{0:T(128)S(1)}, f32[4]{0:T(128)S(1)}, u32[]{:S(2)}, u32[]{:S(2)}) collective-permute-start(f32[4]{0:T(128)S(1)} %add.36), channel_id=1, source_target_pairs={{0,64},{64,0},{128,192},{192,128},{1,65},{65,1},{129,193},{193,129... | collective-permute-start | bytes 56 | tf_op jit(solution)/shard_map/ppermute | solution.py:46
  60.0 5.0 %collective-permute-start.8 = (f32[4]{0:T(128)S(1)}, f32[4]{0:T(128)S(1)}, u32[]{:S(2)}, u32[]{:S(2)}) collective-permute-start(f32[4]{0:T(128)S(1)} %add.37), channel_id=1, source_target_pairs={{0,128},{64,192},{128,0},{192,64},{1,129},{65,193},{129,1},{193,65... | collective-permute-start | bytes 56 | tf_op jit(solution)/shard_map/ppermute | solution.py:46
  65.0 3.5 %collective-permute-start.9 = (f32[4]{0:T(128)S(1)}, f32[4]{0:T(128)S(1)}, u32[]{:S(2)}, u32[]{:S(2)}) collective-permute-start(f32[4]{0:T(128)S(1)} %add.38), channel_id=1, source_target_pairs={{0,16},{16,0},{32,48},{48,32},{1,17},{17,1},{33,49},{49,33},{2,18}... | collective-permute-start | bytes 56 | tf_op jit(solution)/shard_map/ppermute | solution.py:46
  68.6 5.0 %collective-permute-start.10 = (f32[4]{0:T(128)S(1)}, f32[4]{0:T(128)S(1)}, u32[]{:S(2)}, u32[]{:S(2)}) collective-permute-start(f32[4]{0:T(128)S(1)} %add.39), channel_id=1, source_target_pairs={{0,32},{16,48},{32,0},{48,16},{1,33},{17,49},{33,1},{49,17},{2,34}... | collective-permute-start | bytes 56 | tf_op jit(solution)/shard_map/ppermute | solution.py:46
  73.6 3.5 %collective-permute-start.11 = (f32[4]{0:T(128)S(1)}, f32[4]{0:T(128)S(1)}, u32[]{:S(2)}, u32[]{:S(2)}) collective-permute-start(f32[4]{0:T(128)S(1)} %add.40), channel_id=1, source_target_pairs={{0,4},{4,0},{8,12},{12,8},{1,5},{5,1},{9,13},{13,9},{2,6},{6,2},{1... | collective-permute-start | bytes 56 | tf_op jit(solution)/shard_map/ppermute | solution.py:46
  77.2 5.0 %collective-permute-start.12 = (f32[4]{0:T(128)S(1)}, f32[4]{0:T(128)S(1)}, u32[]{:S(2)}, u32[]{:S(2)}) collective-permute-start(f32[4]{0:T(128)S(1)} %add.41), channel_id=1, source_target_pairs={{0,8},{4,12},{8,0},{12,4},{1,9},{5,13},{9,1},{13,5},{2,10},{6,14},... | collective-permute-start | bytes 56 | tf_op jit(solution)/shard_map/ppermute | solution.py:46
  82.2 7.4 %collective-permute-start.13 = (f32[4]{0:T(128)S(1)}, f32[4]{0:T(128)S(1)}, u32[]{:S(2)}, u32[]{:S(2)}) collective-permute-start(f32[4]{0:T(128)S(1)} %add.42), channel_id=1, source_target_pairs={{0,2},{2,0},{1,3},{3,1},{4,6},{6,4},{5,7},{7,5},{8,10},{10,8},{9,1... | collective-permute-start | bytes 56 | tf_op jit(solution)/shard_map/ppermute | solution.py:46

commit v13 on v11

--- a/solution.py
+++ b/solution.py
@@ -102,6 +102,7 @@
 
 LANES = 128
 UPDATE_ROWS = 32
+TILE_GROUP = 6
 WINDOWS_PER_TILE = LANES // 16
 HALF = WINDOWS_PER_TILE * 32
 
@@ -188,22 +189,27 @@
     backward = (gh_ref[...], gl_ref[...])
     freq = fw_ref[...]
 
-    def one_tile(t, carry):
-        here = pl.ds(pl.multiple_of(t * rows, 8), rows)
-        y = y_ref[here, :]
-        weights = ww_ref[:, pl.ds(pl.multiple_of(t * 2 * HALF, 2 * HALF), 2 * HALF)]
-        turned = jnp.concatenate([-y[:, HALF:], y[:, :HALF]], axis=1)
-        z = constant_first_dot(forward, split_value(jnp.concatenate([y, turned], axis=0)))
+    def turn(value, sign):
+        blocks = []
+        for g in range(value.shape[1] // (2 * HALF)):
+            re = value[:, 2 * HALF * g : 2 * HALF * g + HALF]
+            im = value[:, 2 * HALF * g + HALF : 2 * HALF * (g + 1)]
+            blocks += [-im, re] if sign else [im, -re]
+        return jnp.concatenate(blocks, axis=1)
+
+    for first in range(0, tiles, TILE_GROUP):
+        group = range(first, min(first + TILE_GROUP, tiles))
+        y = jnp.concatenate([y_ref[t * rows : (t + 1) * rows, :] for t in group], axis=1)
+        weights = ww_ref[:, first * 2 * HALF : (group[-1] + 1) * 2 * HALF]
+        z = constant_first_dot(forward, split_value(jnp.concatenate([y, turn(y, True)], axis=0)))
         spread = jnp.concatenate(
-            [jnp.broadcast_to(weights[a : a + 1], (32, 2 * HALF)) for a in range(win_rows)],
+            [jnp.broadcast_to(weights[a : a + 1], (32, weights.shape[1])) for a in range(win_rows)],
             axis=0,
         )
-        z = z * freq * spread
-        turned = jnp.concatenate([z[:, HALF:], -z[:, :HALF]], axis=1)
-        e_ref[here, :] = constant_first_dot(backward, split_value(jnp.concatenate([z, turned], axis=0)))
-        return carry
-
-    lax.fori_loop(0, tiles, one_tile, 0, unroll=True)
+        z = z * jnp.concatenate([freq] * len(group), axis=1) * spread
+        e = constant_first_dot(backward, split_value(jnp.concatenate([z, turn(z, False)], axis=0)))
+        for g, t in enumerate(group):
+            e_ref[t * rows : (t + 1) * rows, :] = e[:, 2 * HALF * g : 2 * HALF * (g + 1)]
     pieces = transposed_dot(split_value(e_ref[...]), (mh_ref[...], ml_ref[...]))
     out_ref[...] = jnp.zeros_like(out_ref)
     for t in range(tiles):

time: 86.7 us -> 84.3 us (0.972)
  Pallas kernels: 17.7 us -> 15.5 us
    pallas_call x1, Pallas kernels: 15.1 us -> 12.9 us  [analyze_weigh_synthesize(): pl.pallas_call(transform_kernel, out_shape=jax.ShapeDtypeStruct((rows, wi...]
where the time goes in v13:
time: 84.3 us; the launch traced here: 83.9 us
  starting transfers between devices  31.7 us (38%)
  waiting for transfers between devices  25.5 us (30%)
  Pallas kernels  15.5 us (18%)
  local copies, waits for them, and re-layouts  7.12 us (8%)
  other arithmetic  3.21 us (4%)
    ppermute x8, waiting for transfers between devices, summed_everywhere(): x = x + lax.ppermute(x, axis, [(i, i ^ mask) for i in range(count)])  21.6 us
    ppermute x4, starting transfers between devices, passed_along(): lax.ppermute(value, axis, [(source, source + steps) for source in range(l...  17.6 us
    ppermute x8, starting transfers between devices, summed_everywhere(): x = x + lax.ppermute(x, axis, [(i, i ^ mask) for i in range(count)])  14.1 us
    pallas_call x1, Pallas kernels, analyze_weigh_synthesize(): pl.pallas_call(transform_kernel, out_shape=jax.ShapeDtypeStruct((rows, wi...  12.9 us
    ppermute x4, waiting for transfers between devices, passed_along(): lax.ppermute(value, axis, [(source, source + steps) for source in range(l...  3.87 us
    pallas_call x1, Pallas kernels, updated(): pl.pallas_call(update_kernel, grid=(height // rows,), out_shape=(shape, s...  2.57 us
  transfers between devices with their start and end apart: 12, of which 11 were waited for; matrix products, arithmetic and copies ran while one was open for 4% of the time, Pallas kernels for 0%

profile of v13, /device:TPU:16, one launch (start us, length us, event | category | flops | bytes accessed | tf_op | source)
XLA Modules:
  0.0 83.9 jit_solution(16763443572667175622)
XLA Ops:
  2.6 1.9 %collective-permute-start = (f32[68,16]{1,0:T(8,128)S(1)}, f32[68,16]{1,0:T(8,128)S(1)}, u32[]{:S(2)}, u32[]{:S(2)}) collective-permute-start(f32[68,16]{1,0:T(8,128)S(1)} %copy.16), channel_id=1, source_target_pairs={{0,1},{1,2},{2,3},{3,4},{4,5},{5,6},{6,7},{7,8},{8,9},{9,10},{10,1... | collective-permute-start | bytes 13064 | tf_op jit(solution)/shard_map/ppermute | solution.py:30
  4.5 10.6 %collective-permute-start.1 = (f32[64,16]{1,0:T(8,128)S(1)}, f32[64,16]{1,0:T(8,128)S(1)}, u32[]{:S(2)}, u32[]{:S(2)}) collective-permute-start(f32[64,16]{1,0:T(8,128)S(1)} %get-tuple-element.10), channel_id=1, source_target_pairs={{1,0},{2,1},{3,2},{4,3},{5,4},{6,5},{7,6},{8,7},{9,8},{10,9},{11,1... | collective-permute-start | bytes 12296 | tf_op jit(solution)/shard_map/ppermute | solution.py:30
  16.7 1.4 %concatenate.16.middle_ref = f32[64,2304]{1,0:T(8,128)S(1)} concatenate(f32[64,16]{1,0:T(8,128)S(1)} %slice.42, f32[64,2048]{1,0:T(8,128)} %direction_ref.1, f32[64,16]{1,0:T(8,128)S(1)} %collective-permute-done.1, f32[64,224]{1,0:T(8,128)S(1)} %broadcast_in_dim.15), dimensions={1} | concatenate | bytes 1179648 | tf_op jit(solution)/shard_map/concatenate | solution.py:292
  18.2 3.8 %collective-permute-start.2 = (f32[17,2304]{1,0:T(8,128)S(1)}, f32[17,2304]{1,0:T(8,128)S(1)}, u32[]{:S(2)}, u32[]{:S(2)}) collective-permute-start(f32[17,2304]{1,0:T(8,128)S(1)} %pad_maximum_fusion), channel_id=1, source_target_pairs={{0,64},{64,128},{128,192},{1,65},{65,129},{129,193},{2,66},{66,130... | collective-permute-start | bytes 470024 | tf_op jit(solution)/shard_map/ppermute | solution.py:30
  22.0 1.3 %collective-permute-start.3 = (f32[16,2304]{1,0:T(8,128)S(1)}, f32[16,2304]{1,0:T(8,128)S(1)}, u32[]{:S(2)}, u32[]{:S(2)}) collective-permute-start(f32[16,2304]{1,0:T(8,128)S(1)} %get-tuple-element.5), channel_id=1, source_target_pairs={{64,0},{128,64},{192,128},{65,1},{129,65},{193,129},{66,2},{130,66... | collective-permute-start | bytes 442376 | tf_op jit(solution)/shard_map/ppermute | solution.py:30
  23.4 1.2 %reshape.19.fw_ref = f32[160,512]{1,0:T(8,128)} reshape(f32[5,32,2,8,32]{4,3,2,1,0:T(8,128)S(1)} %broadcast_in_dim.16) | data formatting | bytes 655360 | tf_op jit(solution)/shard_map/reshape | solution.py:236
  26.7 2.3 %collective-permute-done.3.below_ref = f32[16,2304]{1,0:T(8,128)S(1)} collective-permute-done((f32[16,2304]{1,0:T(8,128)S(1)}, f32[16,2304]{1,0:T(8,128)S(1)}, u32[]{:S(2)}, u32[]{:S(2)}) %collective-permute-start.3) | collective-permute-done | bytes 147488 | tf_op jit(solution)/shard_map/ppermute | solution.py:30
  29.7 12.9 %shard_map.130 = f32[96,2304]{1,0:T(8,128)} custom-call(f32[17,2304]{1,0:T(8,128)} %copy-done.4, f32[64,2304]{1,0:T(8,128)} %copy-done.2, f32[16,2304]{1,0:T(8,128)} %copy-done.5, bf16[256,512]{1,0:T(8,128)(2,1)} %constant.7.clone.mh_ref, bf16[256,512]{1,0:T(8,128)(2,1)} %constant.20.clone.ml_ref, bf16[160,192]{1,0:T(8,128)(2,1)} %constant.21.clone.fh_ref, ...), custom_call_target="tpu_custom_call" | custom-call | tf_op jit(solution)/shard_map/pallas_call | solution.py:242
  42.6 1.3 %multiply_bitcast_fusion.2 = (f32[1,64,2048]{2,1,0:T(8,128)S(1)}, f32[64,2048]{1,0:T(8,128)S(1)}) fusion(f32[64,2048]{1,0:T(8,128)S(1)} %copy-done, f32[96,2304]{1,0:T(8,128)} %shard_map.130), kind=kLoop, calls=%fused_computation.4 | loop fusion | flops 393216 | bytes 2097152 | tf_op jit(solution)/shard_map/stack | solution.py:310
  45.0 2.1 %collective-permute-start.4 = (f32[4]{0:T(128)S(1)}, f32[4]{0:T(128)S(1)}, u32[]{:S(2)}, u32[]{:S(2)}) collective-permute-start(f32[4]{0:T(128)S(1)} %maximum_reduce_fusion), channel_id=1, source_target_pairs={{0,1},{1,0},{2,3},{3,2},{4,5},{5,4},{6,7},{7,6},{8,9},{9,8},{10,11... | collective-permute-start | bytes 56 | tf_op jit(solution)/shard_map/ppermute | solution.py:46
  47.9 1.4 %collective-permute-start.5 = (f32[4]{0:T(128)S(1)}, f32[4]{0:T(128)S(1)}, u32[]{:S(2)}, u32[]{:S(2)}) collective-permute-start(f32[4]{0:T(128)S(1)} %add.34), channel_id=1, source_target_pairs={{0,64},{64,0},{128,192},{192,128},{1,65},{65,1},{129,193},{193,129... | collective-permute-start | bytes 56 | tf_op jit(solution)/shard_map/ppermute | solution.py:46
  49.3 2.2 %collective-permute-done.5 = f32[4]{0:T(128)S(1)} collective-permute-done((f32[4]{0:T(128)S(1)}, f32[4]{0:T(128)S(1)}, u32[]{:S(2)}, u32[]{:S(2)}) %collective-permute-start.5) | collective-permute-done | bytes 48 | tf_op jit(solution)/shard_map/ppermute | solution.py:46
  51.5 3.2 %collective-permute-start.6 = (f32[4]{0:T(128)S(1)}, f32[4]{0:T(128)S(1)}, u32[]{:S(2)}, u32[]{:S(2)}) collective-permute-start(f32[4]{0:T(128)S(1)} %add.35), channel_id=1, source_target_pairs={{0,128},{64,192},{128,0},{192,64},{1,129},{65,193},{129,1},{193,65... | collective-permute-start | bytes 56 | tf_op jit(solution)/shard_map/ppermute | solution.py:46
  54.6 1.5 %collective-permute-done.6 = f32[4]{0:T(128)S(1)} collective-permute-done((f32[4]{0:T(128)S(1)}, f32[4]{0:T(128)S(1)}, u32[]{:S(2)}, u32[]{:S(2)}) %collective-permute-start.6) | collective-permute-done | bytes 48 | tf_op jit(solution)/shard_map/ppermute | solution.py:46
  56.2 1.3 %collective-permute-start.7 = (f32[4]{0:T(128)S(1)}, f32[4]{0:T(128)S(1)}, u32[]{:S(2)}, u32[]{:S(2)}) collective-permute-start(f32[4]{0:T(128)S(1)} %add.36), channel_id=1, source_target_pairs={{0,16},{16,0},{32,48},{48,32},{1,17},{17,1},{33,49},{49,33},{2,18}... | collective-permute-start | bytes 56 | tf_op jit(solution)/shard_map/ppermute | solution.py:46
  57.4 2.3 %collective-permute-done.7 = f32[4]{0:T(128)S(1)} collective-permute-done((f32[4]{0:T(128)S(1)}, f32[4]{0:T(128)S(1)}, u32[]{:S(2)}, u32[]{:S(2)}) %collective-permute-start.7) | collective-permute-done | bytes 48 | tf_op jit(solution)/shard_map/ppermute | solution.py:46
  59.7 5.0 %collective-permute-done.8 = f32[4]{0:T(128)S(1)} collective-permute-done((f32[4]{0:T(128)S(1)}, f32[4]{0:T(128)S(1)}, u32[]{:S(2)}, u32[]{:S(2)}) %collective-permute-start.8) | collective-permute-done | bytes 48 | tf_op jit(solution)/shard_map/ppermute | solution.py:46
  64.7 1.1 %collective-permute-start.9 = (f32[4]{0:T(128)S(1)}, f32[4]{0:T(128)S(1)}, u32[]{:S(2)}, u32[]{:S(2)}) collective-permute-start(f32[4]{0:T(128)S(1)} %add.38), channel_id=1, source_target_pairs={{0,4},{4,0},{8,12},{12,8},{1,5},{5,1},{9,13},{13,9},{2,6},{6,2},{1... | collective-permute-start | bytes 56 | tf_op jit(solution)/shard_map/ppermute | solution.py:46
  65.9 2.4 %collective-permute-done.9 = f32[4]{0:T(128)S(1)} collective-permute-done((f32[4]{0:T(128)S(1)}, f32[4]{0:T(128)S(1)}, u32[]{:S(2)}, u32[]{:S(2)}) %collective-permute-start.9) | collective-permute-done | bytes 48 | tf_op jit(solution)/shard_map/ppermute | solution.py:46
  68.3 2.7 %collective-permute-start.10 = (f32[4]{0:T(128)S(1)}, f32[4]{0:T(128)S(1)}, u32[]{:S(2)}, u32[]{:S(2)}) collective-permute-start(f32[4]{0:T(128)S(1)} %add.39), channel_id=1, source_target_pairs={{0,8},{4,12},{8,0},{12,4},{1,9},{5,13},{9,1},{13,5},{2,10},{6,14},... | collective-permute-start | bytes 56 | tf_op jit(solution)/shard_map/ppermute | solution.py:46
  71.0 2.4 %collective-permute-done.10 = f32[4]{0:T(128)S(1)} collective-permute-done((f32[4]{0:T(128)S(1)}, f32[4]{0:T(128)S(1)}, u32[]{:S(2)}, u32[]{:S(2)}) %collective-permute-start.10) | collective-permute-done | bytes 48 | tf_op jit(solution)/shard_map/ppermute | solution.py:46
  73.3 2.4 %collective-permute-start.11 = (f32[4]{0:T(128)S(1)}, f32[4]{0:T(128)S(1)}, u32[]{:S(2)}, u32[]{:S(2)}) collective-permute-start(f32[4]{0:T(128)S(1)} %add.40), channel_id=1, source_target_pairs={{0,2},{2,0},{1,3},{3,1},{4,6},{6,4},{5,7},{7,5},{8,10},{10,8},{9,1... | collective-permute-start | bytes 56 | tf_op jit(solution)/shard_map/ppermute | solution.py:46
  75.7 5.1 %collective-permute-done.11 = f32[4]{0:T(128)S(1)} collective-permute-done((f32[4]{0:T(128)S(1)}, f32[4]{0:T(128)S(1)}, u32[]{:S(2)}, u32[]{:S(2)}) %collective-permute-start.11) | collective-permute-done | bytes 48 | tf_op jit(solution)/shard_map/ppermute | solution.py:46
  81.3 2.6 %shard_map.131 = (f32[64,2048]{1,0:T(8,128)}, f32[64,2048]{1,0:T(8,128)}, f32[64,2048]{1,0:T(8,128)}) custom-call(f32[1,4]{1,0:T(1,128)} %add_bitcast_fusion.sums_ref, f32[64,2048]{1,0:T(8,128)} %iterate_ref.1, f32[64,2048]{1,0:T(8,128)} %residual_ref.1, f32[64,2048]{1,0:T(8,128)} %direction_ref.1, f32[64,2048]{1,0:T(8,128)} %copy-done.1), custom_call_target="tpu_custom_call" | custom-call | tf_op jit(solution)/shard_map/pallas_call | solution.py:274
  (49 shorter events, 8.8 us)
Async XLA Ops:
  0.6 22.6 %copy-start.7 = (f32[32,32]{1,0:T(8,128)S(1)}, f32[32,32]{1,0:T(8,128)}, u32[]{:S(2)}) copy-start(f32[32,32]{1,0:T(8,128)} %param.15) | copy-start | bytes 12292
  2.6 12.6 %collective-permute-start = (f32[68,16]{1,0:T(8,128)S(1)}, f32[68,16]{1,0:T(8,128)S(1)}, u32[]{:S(2)}, u32[]{:S(2)}) collective-permute-start(f32[68,16]{1,0:T(8,128)S(1)} %copy.16), channel_id=1, source_target_pairs={{0,1},{1,2},{2,3},{3,4},{4,5},{5,6},{6,7},{7,8},{8,9},{9,10},{10,1... | collective-permute-start | bytes 13064 | tf_op jit(solution)/shard_map/ppermute | solution.py:30
  4.5 12.2 %collective-permute-start.1 = (f32[64,16]{1,0:T(8,128)S(1)}, f32[64,16]{1,0:T(8,128)S(1)}, u32[]{:S(2)}, u32[]{:S(2)}) collective-permute-start(f32[64,16]{1,0:T(8,128)S(1)} %get-tuple-element.10), channel_id=1, source_target_pairs={{1,0},{2,1},{3,2},{4,3},{5,4},{6,5},{7,6},{8,7},{9,8},{10,9},{11,1... | collective-permute-start | bytes 12296 | tf_op jit(solution)/shard_map/ppermute | solution.py:30
  18.1 6.5 %copy-start.2 = (f32[64,2304]{1,0:T(8,128)}, f32[64,2304]{1,0:T(8,128)S(1)}, u32[]{:S(2)}) copy-start(f32[64,2304]{1,0:T(8,128)S(1)} %concatenate.16.middle_ref) | copy-start | bytes 1769476
  18.2 7.2 %collective-permute-start.2 = (f32[17,2304]{1,0:T(8,128)S(1)}, f32[17,2304]{1,0:T(8,128)S(1)}, u32[]{:S(2)}, u32[]{:S(2)}) collective-permute-start(f32[17,2304]{1,0:T(8,128)S(1)} %pad_maximum_fusion), channel_id=1, source_target_pairs={{0,64},{64,128},{128,192},{1,65},{65,129},{129,193},{2,66},{66,130... | collective-permute-start | bytes 470024 | tf_op jit(solution)/shard_map/ppermute | solution.py:30
  22.0 3.4 %copy-start.6 = (f32[4,128]{1,0:T(4,128)S(1)}, f32[4,128]{1,0:T(4,128)}, u32[]{:S(2)}) copy-start(f32[4,128]{1,0:T(4,128)} %param.14) | copy-start | bytes 6148
  22.0 7.0 %collective-permute-start.3 = (f32[16,2304]{1,0:T(8,128)S(1)}, f32[16,2304]{1,0:T(8,128)S(1)}, u32[]{:S(2)}, u32[]{:S(2)}) collective-permute-start(f32[16,2304]{1,0:T(8,128)S(1)} %get-tuple-element.5), channel_id=1, source_target_pairs={{64,0},{128,64},{192,128},{65,1},{129,65},{193,129},{66,2},{130,66... | collective-permute-start | bytes 442376 | tf_op jit(solution)/shard_map/ppermute | solution.py:30
  25.4 3.6 %copy-start.4 = (f32[17,2304]{1,0:T(8,128)}, f32[17,2304]{1,0:T(8,128)S(1)}, u32[]{:S(2)}) copy-start(f32[17,2304]{1,0:T(8,128)S(1)} %collective-permute-done.2.above_ref) | copy-start | bytes 470020
  26.7 15.9 %copy-start = (f32[64,2048]{1,0:T(8,128)S(1)}, f32[64,2048]{1,0:T(8,128)}, u32[]{:S(2)}) copy-start(f32[64,2048]{1,0:T(8,128)} %direction_ref.1) | copy-start | bytes 1572868
  29.0 0.7 copy-start.5
  42.6 1.3 %copy-start.3 = (f32[64,2048]{1,0:T(8,128)S(1)}, f32[64,2048]{1,0:T(8,128)}, u32[]{:S(2)}) copy-start(f32[64,2048]{1,0:T(8,128)} %residual_ref.1) | copy-start | bytes 1572868
  43.9 0.8 copy-start.1
  45.0 2.9 %collective-permute-start.4 = (f32[4]{0:T(128)S(1)}, f32[4]{0:T(128)S(1)}, u32[]{:S(2)}, u32[]{:S(2)}) collective-permute-start(f32[4]{0:T(128)S(1)} %maximum_reduce_fusion), channel_id=1, source_target_pairs={{0,1},{1,0},{2,3},{3,2},{4,5},{5,4},{6,7},{7,6},{8,9},{9,8},{10,11... | collective-permute-start | bytes 56 | tf_op jit(solution)/shard_map/ppermute | solution.py:46
  47.9 3.5 %collective-permute-start.5 = (f32[4]{0:T(128)S(1)}, f32[4]{0:T(128)S(1)}, u32[]{:S(2)}, u32[]{:S(2)}) collective-permute-start(f32[4]{0:T(128)S(1)} %add.34), channel_id=1, source_target_pairs={{0,64},{64,0},{128,192},{192,128},{1,65},{65,1},{129,193},{193,129... | collective-permute-start | bytes 56 | tf_op jit(solution)/shard_map/ppermute | solution.py:46
  51.5 4.7 %collective-permute-start.6 = (f32[4]{0:T(128)S(1)}, f32[4]{0:T(128)S(1)}, u32[]{:S(2)}, u32[]{:S(2)}) collective-permute-start(f32[4]{0:T(128)S(1)} %add.35), channel_id=1, source_target_pairs={{0,128},{64,192},{128,0},{192,64},{1,129},{65,193},{129,1},{193,65... | collective-permute-start | bytes 56 | tf_op jit(solution)/shard_map/ppermute | solution.py:46
  56.2 3.5 %collective-permute-start.7 = (f32[4]{0:T(128)S(1)}, f32[4]{0:T(128)S(1)}, u32[]{:S(2)}, u32[]{:S(2)}) collective-permute-start(f32[4]{0:T(128)S(1)} %add.36), channel_id=1, source_target_pairs={{0,16},{16,0},{32,48},{48,32},{1,17},{17,1},{33,49},{49,33},{2,18}... | collective-permute-start | bytes 56 | tf_op jit(solution)/shard_map/ppermute | solution.py:46
  59.7 5.0 %collective-permute-start.8 = (f32[4]{0:T(128)S(1)}, f32[4]{0:T(128)S(1)}, u32[]{:S(2)}, u32[]{:S(2)}) collective-permute-start(f32[4]{0:T(128)S(1)} %add.37), channel_id=1, source_target_pairs={{0,32},{16,48},{32,0},{48,16},{1,33},{17,49},{33,1},{49,17},{2,34}... | collective-permute-start | bytes 56 | tf_op jit(solution)/shard_map/ppermute | solution.py:46
  64.7 3.5 %collective-permute-start.9 = (f32[4]{0:T(128)S(1)}, f32[4]{0:T(128)S(1)}, u32[]{:S(2)}, u32[]{:S(2)}) collective-permute-start(f32[4]{0:T(128)S(1)} %add.38), channel_id=1, source_target_pairs={{0,4},{4,0},{8,12},{12,8},{1,5},{5,1},{9,13},{13,9},{2,6},{6,2},{1... | collective-permute-start | bytes 56 | tf_op jit(solution)/shard_map/ppermute | solution.py:46
  68.3 5.0 %collective-permute-start.10 = (f32[4]{0:T(128)S(1)}, f32[4]{0:T(128)S(1)}, u32[]{:S(2)}, u32[]{:S(2)}) collective-permute-start(f32[4]{0:T(128)S(1)} %add.39), channel_id=1, source_target_pairs={{0,8},{4,12},{8,0},{12,4},{1,9},{5,13},{9,1},{13,5},{2,10},{6,14},... | collective-permute-start | bytes 56 | tf_op jit(solution)/shard_map/ppermute | solution.py:46
  73.3 7.4 %collective-permute-start.11 = (f32[4]{0:T(128)S(1)}, f32[4]{0:T(128)S(1)}, u32[]{:S(2)}, u32[]{:S(2)}) collective-permute-start(f32[4]{0:T(128)S(1)} %add.40), channel_id=1, source_target_pairs={{0,2},{2,0},{1,3},{3,1},{4,6},{6,4},{5,7},{7,5},{8,10},{10,8},{9,1... | collective-permute-start | bytes 56 | tf_op jit(solution)/shard_map/ppermute | solution.py:46

commit v14 on v13

--- a/solution.py
+++ b/solution.py
@@ -211,9 +211,10 @@
         for g, t in enumerate(group):
             e_ref[t * rows : (t + 1) * rows, :] = e[:, 2 * HALF * g : 2 * HALF * (g + 1)]
     pieces = transposed_dot(split_value(e_ref[...]), (mh_ref[...], ml_ref[...]))
+    kept = out_ref.shape[0]
     out_ref[...] = jnp.zeros_like(out_ref)
     for t in range(tiles):
-        out_ref[:, t * LANES : (t + 2) * LANES] += pieces[t * rows : (t + 1) * rows]
+        out_ref[:, t * LANES : (t + 2) * LANES] += pieces[t * rows + 16 : t * rows + 16 + kept]
 
 
 def padded_width(cols):
@@ -241,7 +242,7 @@
     vmem = pl.BlockSpec(memory_space=pltpu.VMEM)
     out = pl.pallas_call(
         transform_kernel,
-        out_shape=jax.ShapeDtypeStruct((rows, wide), jnp.float32),
+        out_shape=jax.ShapeDtypeStruct((rows - 32, wide), jnp.float32),
         in_specs=[vmem] * 11,
         out_specs=vmem,
         scratch_shapes=[
@@ -305,7 +306,7 @@
     spread = analyze_weigh_synthesize(
         from_above, widened, from_below, weights_all, freq_weight, cols
     )
-    synthesized = spread[16 : 16 + height, 16 : 16 + breadth]
+    synthesized = spread[:, 16 : 16 + breadth]
     applied = synthesized + damping * direction
     products = jnp.stack(
         [residual * residual, direction * applied, residual * applied, applied * applied]

time: 84.3 us -> 84.3 us (level)
  no operation moved by 1% of the time
where the time goes in v14:
time: 84.3 us; the launch traced here: 83.8 us
  starting transfers between devices  31.7 us (38%)
  waiting for transfers between devices  25.5 us (30%)
  Pallas kernels  15.4 us (18%)
  local copies, waits for them, and re-layouts  7.12 us (8%)
  other arithmetic  3.21 us (4%)
    ppermute x8, waiting for transfers between devices, summed_everywhere(): x = x + lax.ppermute(x, axis, [(i, i ^ mask) for i in range(count)])  21.7 us
    ppermute x4, starting transfers between devices, passed_along(): lax.ppermute(value, axis, [(source, source + steps) for source in range(l...  17.6 us
    ppermute x8, starting transfers between devices, summed_everywhere(): x = x + lax.ppermute(x, axis, [(i, i ^ mask) for i in range(count)])  14.1 us
    pallas_call x1, Pallas kernels, analyze_weigh_synthesize(): pl.pallas_call(transform_kernel, out_shape=jax.ShapeDtypeStruct((rows - 3...  12.8 us
    ppermute x4, waiting for transfers between devices, passed_along(): lax.ppermute(value, axis, [(source, source + steps) for source in range(l...  3.87 us
    pallas_call x1, Pallas kernels, updated(): pl.pallas_call(update_kernel, grid=(height // rows,), out_shape=(shape, s...  2.57 us
  transfers between devices with their start and end apart: 12, of which 11 were waited for; matrix products, arithmetic and copies ran while one was open for 4% of the time, Pallas kernels for 0%

profile of v14, /device:TPU:16, one launch (start us, length us, event | category | flops | bytes accessed | tf_op | source)
XLA Modules:
  0.0 83.8 jit_solution(1233247230996202807)
XLA Ops:
  2.6 1.9 %collective-permute-start = (f32[68,16]{1,0:T(8,128)S(1)}, f32[68,16]{1,0:T(8,128)S(1)}, u32[]{:S(2)}, u32[]{:S(2)}) collective-permute-start(f32[68,16]{1,0:T(8,128)S(1)} %copy.16), channel_id=1, source_target_pairs={{0,1},{1,2},{2,3},{3,4},{4,5},{5,6},{6,7},{7,8},{8,9},{9,10},{10,1... | collective-permute-start | bytes 13064 | tf_op jit(solution)/shard_map/ppermute | solution.py:30
  4.5 10.6 %collective-permute-start.1 = (f32[64,16]{1,0:T(8,128)S(1)}, f32[64,16]{1,0:T(8,128)S(1)}, u32[]{:S(2)}, u32[]{:S(2)}) collective-permute-start(f32[64,16]{1,0:T(8,128)S(1)} %get-tuple-element.10), channel_id=1, source_target_pairs={{1,0},{2,1},{3,2},{4,3},{5,4},{6,5},{7,6},{8,7},{9,8},{10,9},{11,1... | collective-permute-start | bytes 12296 | tf_op jit(solution)/shard_map/ppermute | solution.py:30
  16.7 1.4 %concatenate.16.middle_ref = f32[64,2304]{1,0:T(8,128)S(1)} concatenate(f32[64,16]{1,0:T(8,128)S(1)} %slice.42, f32[64,2048]{1,0:T(8,128)} %direction_ref.1, f32[64,16]{1,0:T(8,128)S(1)} %collective-permute-done.1, f32[64,224]{1,0:T(8,128)S(1)} %broadcast_in_dim.15), dimensions={1} | concatenate | bytes 1179648 | tf_op jit(solution)/shard_map/concatenate | solution.py:293
  18.2 3.8 %collective-permute-start.2 = (f32[17,2304]{1,0:T(8,128)S(1)}, f32[17,2304]{1,0:T(8,128)S(1)}, u32[]{:S(2)}, u32[]{:S(2)}) collective-permute-start(f32[17,2304]{1,0:T(8,128)S(1)} %pad_maximum_fusion), channel_id=1, source_target_pairs={{0,64},{64,128},{128,192},{1,65},{65,129},{129,193},{2,66},{66,130... | collective-permute-start | bytes 470024 | tf_op jit(solution)/shard_map/ppermute | solution.py:30
  22.0 1.3 %collective-permute-start.3 = (f32[16,2304]{1,0:T(8,128)S(1)}, f32[16,2304]{1,0:T(8,128)S(1)}, u32[]{:S(2)}, u32[]{:S(2)}) collective-permute-start(f32[16,2304]{1,0:T(8,128)S(1)} %get-tuple-element.5), channel_id=1, source_target_pairs={{64,0},{128,64},{192,128},{65,1},{129,65},{193,129},{66,2},{130,66... | collective-permute-start | bytes 442376 | tf_op jit(solution)/shard_map/ppermute | solution.py:30
  23.4 1.2 %reshape.19.fw_ref = f32[160,512]{1,0:T(8,128)} reshape(f32[5,32,2,8,32]{4,3,2,1,0:T(8,128)S(1)} %broadcast_in_dim.16) | data formatting | bytes 655360 | tf_op jit(solution)/shard_map/reshape | solution.py:237
  26.7 2.3 %collective-permute-done.3.below_ref = f32[16,2304]{1,0:T(8,128)S(1)} collective-permute-done((f32[16,2304]{1,0:T(8,128)S(1)}, f32[16,2304]{1,0:T(8,128)S(1)}, u32[]{:S(2)}, u32[]{:S(2)}) %collective-permute-start.3) | collective-permute-done | bytes 147488 | tf_op jit(solution)/shard_map/ppermute | solution.py:30
  29.7 12.8 %shard_map.130 = f32[64,2304]{1,0:T(8,128)} custom-call(f32[17,2304]{1,0:T(8,128)} %copy-done.4, f32[64,2304]{1,0:T(8,128)} %copy-done.2, f32[16,2304]{1,0:T(8,128)} %copy-done.5, bf16[256,512]{1,0:T(8,128)(2,1)} %constant.7.clone.mh_ref, bf16[256,512]{1,0:T(8,128)(2,1)} %constant.20.clone.ml_ref, bf16[160,192]{1,0:T(8,128)(2,1)} %constant.21.clone.fh_ref, ...), custom_call_target="tpu_custom_call" | custom-call | tf_op jit(solution)/shard_map/pallas_call | solution.py:243
  42.5 1.3 %multiply_bitcast_fusion.2 = (f32[1,64,2048]{2,1,0:T(8,128)S(1)}, f32[64,2048]{1,0:T(8,128)S(1)}) fusion(f32[64,2048]{1,0:T(8,128)S(1)} %copy-done, f32[64,2304]{1,0:T(8,128)} %shard_map.130), kind=kLoop, calls=%fused_computation.4 | loop fusion | flops 393216 | bytes 2097152 | tf_op jit(solution)/shard_map/stack | solution.py:311
  44.9 2.1 %collective-permute-start.4 = (f32[4]{0:T(128)S(1)}, f32[4]{0:T(128)S(1)}, u32[]{:S(2)}, u32[]{:S(2)}) collective-permute-start(f32[4]{0:T(128)S(1)} %maximum_reduce_fusion), channel_id=1, source_target_pairs={{0,1},{1,0},{2,3},{3,2},{4,5},{5,4},{6,7},{7,6},{8,9},{9,8},{10,11... | collective-permute-start | bytes 56 | tf_op jit(solution)/shard_map/ppermute | solution.py:46
  47.8 1.4 %collective-permute-start.5 = (f32[4]{0:T(128)S(1)}, f32[4]{0:T(128)S(1)}, u32[]{:S(2)}, u32[]{:S(2)}) collective-permute-start(f32[4]{0:T(128)S(1)} %add.34), channel_id=1, source_target_pairs={{0,64},{64,0},{128,192},{192,128},{1,65},{65,1},{129,193},{193,129... | collective-permute-start | bytes 56 | tf_op jit(solution)/shard_map/ppermute | solution.py:46
  49.2 2.2 %collective-permute-done.5 = f32[4]{0:T(128)S(1)} collective-permute-done((f32[4]{0:T(128)S(1)}, f32[4]{0:T(128)S(1)}, u32[]{:S(2)}, u32[]{:S(2)}) %collective-permute-start.5) | collective-permute-done | bytes 48 | tf_op jit(solution)/shard_map/ppermute | solution.py:46
  51.4 3.2 %collective-permute-start.6 = (f32[4]{0:T(128)S(1)}, f32[4]{0:T(128)S(1)}, u32[]{:S(2)}, u32[]{:S(2)}) collective-permute-start(f32[4]{0:T(128)S(1)} %add.35), channel_id=1, source_target_pairs={{0,128},{64,192},{128,0},{192,64},{1,129},{65,193},{129,1},{193,65... | collective-permute-start | bytes 56 | tf_op jit(solution)/shard_map/ppermute | solution.py:46
  54.6 1.5 %collective-permute-done.6 = f32[4]{0:T(128)S(1)} collective-permute-done((f32[4]{0:T(128)S(1)}, f32[4]{0:T(128)S(1)}, u32[]{:S(2)}, u32[]{:S(2)}) %collective-permute-start.6) | collective-permute-done | bytes 48 | tf_op jit(solution)/shard_map/ppermute | solution.py:46
  56.1 1.3 %collective-permute-start.7 = (f32[4]{0:T(128)S(1)}, f32[4]{0:T(128)S(1)}, u32[]{:S(2)}, u32[]{:S(2)}) collective-permute-start(f32[4]{0:T(128)S(1)} %add.36), channel_id=1, source_target_pairs={{0,16},{16,0},{32,48},{48,32},{1,17},{17,1},{33,49},{49,33},{2,18}... | collective-permute-start | bytes 56 | tf_op jit(solution)/shard_map/ppermute | solution.py:46
  57.4 2.3 %collective-permute-done.7 = f32[4]{0:T(128)S(1)} collective-permute-done((f32[4]{0:T(128)S(1)}, f32[4]{0:T(128)S(1)}, u32[]{:S(2)}, u32[]{:S(2)}) %collective-permute-start.7) | collective-permute-done | bytes 48 | tf_op jit(solution)/shard_map/ppermute | solution.py:46
  59.6 5.0 %collective-permute-done.8 = f32[4]{0:T(128)S(1)} collective-permute-done((f32[4]{0:T(128)S(1)}, f32[4]{0:T(128)S(1)}, u32[]{:S(2)}, u32[]{:S(2)}) %collective-permute-start.8) | collective-permute-done | bytes 48 | tf_op jit(solution)/shard_map/ppermute | solution.py:46
  64.7 1.1 %collective-permute-start.9 = (f32[4]{0:T(128)S(1)}, f32[4]{0:T(128)S(1)}, u32[]{:S(2)}, u32[]{:S(2)}) collective-permute-start(f32[4]{0:T(128)S(1)} %add.38), channel_id=1, source_target_pairs={{0,4},{4,0},{8,12},{12,8},{1,5},{5,1},{9,13},{13,9},{2,6},{6,2},{1... | collective-permute-start | bytes 56 | tf_op jit(solution)/shard_map/ppermute | solution.py:46
  65.8 2.4 %collective-permute-done.9 = f32[4]{0:T(128)S(1)} collective-permute-done((f32[4]{0:T(128)S(1)}, f32[4]{0:T(128)S(1)}, u32[]{:S(2)}, u32[]{:S(2)}) %collective-permute-start.9) | collective-permute-done | bytes 48 | tf_op jit(solution)/shard_map/ppermute | solution.py:46
  68.2 2.7 %collective-permute-start.10 = (f32[4]{0:T(128)S(1)}, f32[4]{0:T(128)S(1)}, u32[]{:S(2)}, u32[]{:S(2)}) collective-permute-start(f32[4]{0:T(128)S(1)} %add.39), channel_id=1, source_target_pairs={{0,8},{4,12},{8,0},{12,4},{1,9},{5,13},{9,1},{13,5},{2,10},{6,14},... | collective-permute-start | bytes 56 | tf_op jit(solution)/shard_map/ppermute | solution.py:46
  70.9 2.4 %collective-permute-done.10 = f32[4]{0:T(128)S(1)} collective-permute-done((f32[4]{0:T(128)S(1)}, f32[4]{0:T(128)S(1)}, u32[]{:S(2)}, u32[]{:S(2)}) %collective-permute-start.10) | collective-permute-done | bytes 48 | tf_op jit(solution)/shard_map/ppermute | solution.py:46
  73.3 2.4 %collective-permute-start.11 = (f32[4]{0:T(128)S(1)}, f32[4]{0:T(128)S(1)}, u32[]{:S(2)}, u32[]{:S(2)}) collective-permute-start(f32[4]{0:T(128)S(1)} %add.40), channel_id=1, source_target_pairs={{0,2},{2,0},{1,3},{3,1},{4,6},{6,4},{5,7},{7,5},{8,10},{10,8},{9,1... | collective-permute-start | bytes 56 | tf_op jit(solution)/shard_map/ppermute | solution.py:46
  75.6 5.1 %collective-permute-done.11 = f32[4]{0:T(128)S(1)} collective-permute-done((f32[4]{0:T(128)S(1)}, f32[4]{0:T(128)S(1)}, u32[]{:S(2)}, u32[]{:S(2)}) %collective-permute-start.11) | collective-permute-done | bytes 48 | tf_op jit(solution)/shard_map/ppermute | solution.py:46
  81.2 2.6 %shard_map.131 = (f32[64,2048]{1,0:T(8,128)}, f32[64,2048]{1,0:T(8,128)}, f32[64,2048]{1,0:T(8,128)}) custom-call(f32[1,4]{1,0:T(1,128)} %add_bitcast_fusion.sums_ref, f32[64,2048]{1,0:T(8,128)} %iterate_ref.1, f32[64,2048]{1,0:T(8,128)} %residual_ref.1, f32[64,2048]{1,0:T(8,128)} %direction_ref.1, f32[64,2048]{1,0:T(8,128)} %copy-done.1), custom_call_target="tpu_custom_call" | custom-call | tf_op jit(solution)/shard_map/pallas_call | solution.py:275
  (49 shorter events, 8.8 us)
Async XLA Ops:
  0.6 22.6 %copy-start.7 = (f32[32,32]{1,0:T(8,128)S(1)}, f32[32,32]{1,0:T(8,128)}, u32[]{:S(2)}) copy-start(f32[32,32]{1,0:T(8,128)} %param.15) | copy-start | bytes 12292
  2.6 12.6 %collective-permute-start = (f32[68,16]{1,0:T(8,128)S(1)}, f32[68,16]{1,0:T(8,128)S(1)}, u32[]{:S(2)}, u32[]{:S(2)}) collective-permute-start(f32[68,16]{1,0:T(8,128)S(1)} %copy.16), channel_id=1, source_target_pairs={{0,1},{1,2},{2,3},{3,4},{4,5},{5,6},{6,7},{7,8},{8,9},{9,10},{10,1... | collective-permute-start | bytes 13064 | tf_op jit(solution)/shard_map/ppermute | solution.py:30
  4.5 12.2 %collective-permute-start.1 = (f32[64,16]{1,0:T(8,128)S(1)}, f32[64,16]{1,0:T(8,128)S(1)}, u32[]{:S(2)}, u32[]{:S(2)}) collective-permute-start(f32[64,16]{1,0:T(8,128)S(1)} %get-tuple-element.10), channel_id=1, source_target_pairs={{1,0},{2,1},{3,2},{4,3},{5,4},{6,5},{7,6},{8,7},{9,8},{10,9},{11,1... | collective-permute-start | bytes 12296 | tf_op jit(solution)/shard_map/ppermute | solution.py:30
  18.1 6.5 %copy-start.2 = (f32[64,2304]{1,0:T(8,128)}, f32[64,2304]{1,0:T(8,128)S(1)}, u32[]{:S(2)}) copy-start(f32[64,2304]{1,0:T(8,128)S(1)} %concatenate.16.middle_ref) | copy-start | bytes 1769476
  18.2 7.2 %collective-permute-start.2 = (f32[17,2304]{1,0:T(8,128)S(1)}, f32[17,2304]{1,0:T(8,128)S(1)}, u32[]{:S(2)}, u32[]{:S(2)}) collective-permute-start(f32[17,2304]{1,0:T(8,128)S(1)} %pad_maximum_fusion), channel_id=1, source_target_pairs={{0,64},{64,128},{128,192},{1,65},{65,129},{129,193},{2,66},{66,130... | collective-permute-start | bytes 470024 | tf_op jit(solution)/shard_map/ppermute | solution.py:30
  22.0 3.4 %copy-start.6 = (f32[4,128]{1,0:T(4,128)S(1)}, f32[4,128]{1,0:T(4,128)}, u32[]{:S(2)}) copy-start(f32[4,128]{1,0:T(4,128)} %param.14) | copy-start | bytes 6148
  22.0 7.0 %collective-permute-start.3 = (f32[16,2304]{1,0:T(8,128)S(1)}, f32[16,2304]{1,0:T(8,128)S(1)}, u32[]{:S(2)}, u32[]{:S(2)}) collective-permute-start(f32[16,2304]{1,0:T(8,128)S(1)} %get-tuple-element.5), channel_id=1, source_target_pairs={{64,0},{128,64},{192,128},{65,1},{129,65},{193,129},{66,2},{130,66... | collective-permute-start | bytes 442376 | tf_op jit(solution)/shard_map/ppermute | solution.py:30
  25.4 3.6 %copy-start.4 = (f32[17,2304]{1,0:T(8,128)}, f32[17,2304]{1,0:T(8,128)S(1)}, u32[]{:S(2)}) copy-start(f32[17,2304]{1,0:T(8,128)S(1)} %collective-permute-done.2.above_ref) | copy-start | bytes 470020
  26.7 15.8 %copy-start = (f32[64,2048]{1,0:T(8,128)S(1)}, f32[64,2048]{1,0:T(8,128)}, u32[]{:S(2)}) copy-start(f32[64,2048]{1,0:T(8,128)} %direction_ref.1) | copy-start | bytes 1572868
  29.0 0.7 copy-start.5
  42.5 1.3 %copy-start.3 = (f32[64,2048]{1,0:T(8,128)S(1)}, f32[64,2048]{1,0:T(8,128)}, u32[]{:S(2)}) copy-start(f32[64,2048]{1,0:T(8,128)} %residual_ref.1) | copy-start | bytes 1572868
  43.8 0.8 copy-start.1
  44.9 2.9 %collective-permute-start.4 = (f32[4]{0:T(128)S(1)}, f32[4]{0:T(128)S(1)}, u32[]{:S(2)}, u32[]{:S(2)}) collective-permute-start(f32[4]{0:T(128)S(1)} %maximum_reduce_fusion), channel_id=1, source_target_pairs={{0,1},{1,0},{2,3},{3,2},{4,5},{5,4},{6,7},{7,6},{8,9},{9,8},{10,11... | collective-permute-start | bytes 56 | tf_op jit(solution)/shard_map/ppermute | solution.py:46
  47.8 3.5 %collective-permute-start.5 = (f32[4]{0:T(128)S(1)}, f32[4]{0:T(128)S(1)}, u32[]{:S(2)}, u32[]{:S(2)}) collective-permute-start(f32[4]{0:T(128)S(1)} %add.34), channel_id=1, source_target_pairs={{0,64},{64,0},{128,192},{192,128},{1,65},{65,1},{129,193},{193,129... | collective-permute-start | bytes 56 | tf_op jit(solution)/shard_map/ppermute | solution.py:46
  51.4 4.7 %collective-permute-start.6 = (f32[4]{0:T(128)S(1)}, f32[4]{0:T(128)S(1)}, u32[]{:S(2)}, u32[]{:S(2)}) collective-permute-start(f32[4]{0:T(128)S(1)} %add.35), channel_id=1, source_target_pairs={{0,128},{64,192},{128,0},{192,64},{1,129},{65,193},{129,1},{193,65... | collective-permute-start | bytes 56 | tf_op jit(solution)/shard_map/ppermute | solution.py:46
  56.1 3.5 %collective-permute-start.7 = (f32[4]{0:T(128)S(1)}, f32[4]{0:T(128)S(1)}, u32[]{:S(2)}, u32[]{:S(2)}) collective-permute-start(f32[4]{0:T(128)S(1)} %add.36), channel_id=1, source_target_pairs={{0,16},{16,0},{32,48},{48,32},{1,17},{17,1},{33,49},{49,33},{2,18}... | collective-permute-start | bytes 56 | tf_op jit(solution)/shard_map/ppermute | solution.py:46
  59.6 5.0 %collective-permute-start.8 = (f32[4]{0:T(128)S(1)}, f32[4]{0:T(128)S(1)}, u32[]{:S(2)}, u32[]{:S(2)}) collective-permute-start(f32[4]{0:T(128)S(1)} %add.37), channel_id=1, source_target_pairs={{0,32},{16,48},{32,0},{48,16},{1,33},{17,49},{33,1},{49,17},{2,34}... | collective-permute-start | bytes 56 | tf_op jit(solution)/shard_map/ppermute | solution.py:46
  64.7 3.5 %collective-permute-start.9 = (f32[4]{0:T(128)S(1)}, f32[4]{0:T(128)S(1)}, u32[]{:S(2)}, u32[]{:S(2)}) collective-permute-start(f32[4]{0:T(128)S(1)} %add.38), channel_id=1, source_target_pairs={{0,4},{4,0},{8,12},{12,8},{1,5},{5,1},{9,13},{13,9},{2,6},{6,2},{1... | collective-permute-start | bytes 56 | tf_op jit(solution)/shard_map/ppermute | solution.py:46
  68.2 5.0 %collective-permute-start.10 = (f32[4]{0:T(128)S(1)}, f32[4]{0:T(128)S(1)}, u32[]{:S(2)}, u32[]{:S(2)}) collective-permute-start(f32[4]{0:T(128)S(1)} %add.39), channel_id=1, source_target_pairs={{0,8},{4,12},{8,0},{12,4},{1,9},{5,13},{9,1},{13,5},{2,10},{6,14},... | collective-permute-start | bytes 56 | tf_op jit(solution)/shard_map/ppermute | solution.py:46
  73.3 7.4 %collective-permute-start.11 = (f32[4]{0:T(128)S(1)}, f32[4]{0:T(128)S(1)}, u32[]{:S(2)}, u32[]{:S(2)}) collective-permute-start(f32[4]{0:T(128)S(1)} %add.40), channel_id=1, source_target_pairs={{0,2},{2,0},{1,3},{3,1},{4,6},{6,4},{5,7},{7,5},{8,10},{10,8},{9,1... | collective-permute-start | bytes 56 | tf_op jit(solution)/shard_map/ppermute | solution.py:46

commit v15 on v14

--- a/solution.py
+++ b/solution.py
@@ -102,7 +102,7 @@
 
 LANES = 128
 UPDATE_ROWS = 32
-TILE_GROUP = 6
+TILE_GROUP = 17
 WINDOWS_PER_TILE = LANES // 16
 HALF = WINDOWS_PER_TILE * 32
 

time: 84.3 us -> 84 us (level)
  no operation moved by 1% of the time
where the time goes in v15:
time: 84 us; the launch traced here: 83.6 us
  starting transfers between devices  31.7 us (38%)
  waiting for transfers between devices  25.5 us (30%)
  Pallas kernels  15.2 us (18%)
  local copies, waits for them, and re-layouts  7.12 us (8%)
  other arithmetic  3.21 us (4%)
    ppermute x8, waiting for transfers between devices, summed_everywhere(): x = x + lax.ppermute(x, axis, [(i, i ^ mask) for i in range(count)])  21.6 us
    ppermute x4, starting transfers between devices, passed_along(): lax.ppermute(value, axis, [(source, source + steps) for source in range(l...  17.6 us
    ppermute x8, starting transfers between devices, summed_everywhere(): x = x + lax.ppermute(x, axis, [(i, i ^ mask) for i in range(count)])  14.1 us
    pallas_call x1, Pallas kernels, analyze_weigh_synthesize(): pl.pallas_call(transform_kernel, out_shape=jax.ShapeDtypeStruct((rows - 3...  12.6 us
    ppermute x4, waiting for transfers between devices, passed_along(): lax.ppermute(value, axis, [(source, source + steps) for source in range(l...  3.87 us
    pallas_call x1, Pallas kernels, updated(): pl.pallas_call(update_kernel, grid=(height // rows,), out_shape=(shape, s...  2.57 us
  transfers between devices with their start and end apart: 12, of which 11 were waited for; matrix products, arithmetic and copies ran while one was open for 4% of the time, Pallas kernels for 0%

profile of v15, /device:TPU:16, one launch (start us, length us, event | category | flops | bytes accessed | tf_op | source)
XLA Modules:
  0.0 83.6 jit_solution(12884145968124733493)
XLA Ops:
  2.6 1.9 %collective-permute-start = (f32[68,16]{1,0:T(8,128)S(1)}, f32[68,16]{1,0:T(8,128)S(1)}, u32[]{:S(2)}, u32[]{:S(2)}) collective-permute-start(f32[68,16]{1,0:T(8,128)S(1)} %copy.16), channel_id=1, source_target_pairs={{0,1},{1,2},{2,3},{3,4},{4,5},{5,6},{6,7},{7,8},{8,9},{9,10},{10,1... | collective-permute-start | bytes 13064 | tf_op jit(solution)/shard_map/ppermute | solution.py:30
  4.5 10.6 %collective-permute-start.1 = (f32[64,16]{1,0:T(8,128)S(1)}, f32[64,16]{1,0:T(8,128)S(1)}, u32[]{:S(2)}, u32[]{:S(2)}) collective-permute-start(f32[64,16]{1,0:T(8,128)S(1)} %get-tuple-element.10), channel_id=1, source_target_pairs={{1,0},{2,1},{3,2},{4,3},{5,4},{6,5},{7,6},{8,7},{9,8},{10,9},{11,1... | collective-permute-start | bytes 12296 | tf_op jit(solution)/shard_map/ppermute | solution.py:30
  16.7 1.4 %concatenate.16.middle_ref = f32[64,2304]{1,0:T(8,128)S(1)} concatenate(f32[64,16]{1,0:T(8,128)S(1)} %slice.42, f32[64,2048]{1,0:T(8,128)} %direction_ref.1, f32[64,16]{1,0:T(8,128)S(1)} %collective-permute-done.1, f32[64,224]{1,0:T(8,128)S(1)} %broadcast_in_dim.15), dimensions={1} | concatenate | bytes 1179648 | tf_op jit(solution)/shard_map/concatenate | solution.py:293
  18.2 3.8 %collective-permute-start.2 = (f32[17,2304]{1,0:T(8,128)S(1)}, f32[17,2304]{1,0:T(8,128)S(1)}, u32[]{:S(2)}, u32[]{:S(2)}) collective-permute-start(f32[17,2304]{1,0:T(8,128)S(1)} %pad_maximum_fusion), channel_id=1, source_target_pairs={{0,64},{64,128},{128,192},{1,65},{65,129},{129,193},{2,66},{66,130... | collective-permute-start | bytes 470024 | tf_op jit(solution)/shard_map/ppermute | solution.py:30
  22.0 1.3 %collective-permute-start.3 = (f32[16,2304]{1,0:T(8,128)S(1)}, f32[16,2304]{1,0:T(8,128)S(1)}, u32[]{:S(2)}, u32[]{:S(2)}) collective-permute-start(f32[16,2304]{1,0:T(8,128)S(1)} %get-tuple-element.5), channel_id=1, source_target_pairs={{64,0},{128,64},{192,128},{65,1},{129,65},{193,129},{66,2},{130,66... | collective-permute-start | bytes 442376 | tf_op jit(solution)/shard_map/ppermute | solution.py:30
  23.4 1.2 %reshape.19.fw_ref = f32[160,512]{1,0:T(8,128)} reshape(f32[5,32,2,8,32]{4,3,2,1,0:T(8,128)S(1)} %broadcast_in_dim.16) | data formatting | bytes 655360 | tf_op jit(solution)/shard_map/reshape | solution.py:237
  26.7 2.3 %collective-permute-done.3.below_ref = f32[16,2304]{1,0:T(8,128)S(1)} collective-permute-done((f32[16,2304]{1,0:T(8,128)S(1)}, f32[16,2304]{1,0:T(8,128)S(1)}, u32[]{:S(2)}, u32[]{:S(2)}) %collective-permute-start.3) | collective-permute-done | bytes 147488 | tf_op jit(solution)/shard_map/ppermute | solution.py:30
  29.7 12.6 %shard_map.130 = f32[64,2304]{1,0:T(8,128)} custom-call(f32[17,2304]{1,0:T(8,128)} %copy-done.4, f32[64,2304]{1,0:T(8,128)} %copy-done.2, f32[16,2304]{1,0:T(8,128)} %copy-done.5, bf16[256,512]{1,0:T(8,128)(2,1)} %constant.7.clone.mh_ref, bf16[256,512]{1,0:T(8,128)(2,1)} %constant.20.clone.ml_ref, bf16[160,192]{1,0:T(8,128)(2,1)} %constant.21.clone.fh_ref, ...), custom_call_target="tpu_custom_call" | custom-call | tf_op jit(solution)/shard_map/pallas_call | solution.py:243
  42.3 1.3 %multiply_bitcast_fusion.2 = (f32[1,64,2048]{2,1,0:T(8,128)S(1)}, f32[64,2048]{1,0:T(8,128)S(1)}) fusion(f32[64,2048]{1,0:T(8,128)S(1)} %copy-done, f32[64,2304]{1,0:T(8,128)} %shard_map.130), kind=kLoop, calls=%fused_computation.4 | loop fusion | flops 393216 | bytes 2097152 | tf_op jit(solution)/shard_map/stack | solution.py:311
  44.7 2.1 %collective-permute-start.4 = (f32[4]{0:T(128)S(1)}, f32[4]{0:T(128)S(1)}, u32[]{:S(2)}, u32[]{:S(2)}) collective-permute-start(f32[4]{0:T(128)S(1)} %maximum_reduce_fusion), channel_id=1, source_target_pairs={{0,1},{1,0},{2,3},{3,2},{4,5},{5,4},{6,7},{7,6},{8,9},{9,8},{10,11... | collective-permute-start | bytes 56 | tf_op jit(solution)/shard_map/ppermute | solution.py:46
  47.6 1.4 %collective-permute-start.5 = (f32[4]{0:T(128)S(1)}, f32[4]{0:T(128)S(1)}, u32[]{:S(2)}, u32[]{:S(2)}) collective-permute-start(f32[4]{0:T(128)S(1)} %add.34), channel_id=1, source_target_pairs={{0,64},{64,0},{128,192},{192,128},{1,65},{65,1},{129,193},{193,129... | collective-permute-start | bytes 56 | tf_op jit(solution)/shard_map/ppermute | solution.py:46
  49.0 2.2 %collective-permute-done.5 = f32[4]{0:T(128)S(1)} collective-permute-done((f32[4]{0:T(128)S(1)}, f32[4]{0:T(128)S(1)}, u32[]{:S(2)}, u32[]{:S(2)}) %collective-permute-start.5) | collective-permute-done | bytes 48 | tf_op jit(solution)/shard_map/ppermute | solution.py:46
  51.2 3.2 %collective-permute-start.6 = (f32[4]{0:T(128)S(1)}, f32[4]{0:T(128)S(1)}, u32[]{:S(2)}, u32[]{:S(2)}) collective-permute-start(f32[4]{0:T(128)S(1)} %add.35), channel_id=1, source_target_pairs={{0,128},{64,192},{128,0},{192,64},{1,129},{65,193},{129,1},{193,65... | collective-permute-start | bytes 56 | tf_op jit(solution)/shard_map/ppermute | solution.py:46
  54.3 1.5 %collective-permute-done.6 = f32[4]{0:T(128)S(1)} collective-permute-done((f32[4]{0:T(128)S(1)}, f32[4]{0:T(128)S(1)}, u32[]{:S(2)}, u32[]{:S(2)}) %collective-permute-start.6) | collective-permute-done | bytes 48 | tf_op jit(solution)/shard_map/ppermute | solution.py:46
  55.9 1.3 %collective-permute-start.7 = (f32[4]{0:T(128)S(1)}, f32[4]{0:T(128)S(1)}, u32[]{:S(2)}, u32[]{:S(2)}) collective-permute-start(f32[4]{0:T(128)S(1)} %add.36), channel_id=1, source_target_pairs={{0,16},{16,0},{32,48},{48,32},{1,17},{17,1},{33,49},{49,33},{2,18}... | collective-permute-start | bytes 56 | tf_op jit(solution)/shard_map/ppermute | solution.py:46
  57.1 2.3 %collective-permute-done.7 = f32[4]{0:T(128)S(1)} collective-permute-done((f32[4]{0:T(128)S(1)}, f32[4]{0:T(128)S(1)}, u32[]{:S(2)}, u32[]{:S(2)}) %collective-permute-start.7) | collective-permute-done | bytes 48 | tf_op jit(solution)/shard_map/ppermute | solution.py:46
  59.4 5.0 %collective-permute-done.8 = f32[4]{0:T(128)S(1)} collective-permute-done((f32[4]{0:T(128)S(1)}, f32[4]{0:T(128)S(1)}, u32[]{:S(2)}, u32[]{:S(2)}) %collective-permute-start.8) | collective-permute-done | bytes 48 | tf_op jit(solution)/shard_map/ppermute | solution.py:46
  64.4 1.1 %collective-permute-start.9 = (f32[4]{0:T(128)S(1)}, f32[4]{0:T(128)S(1)}, u32[]{:S(2)}, u32[]{:S(2)}) collective-permute-start(f32[4]{0:T(128)S(1)} %add.38), channel_id=1, source_target_pairs={{0,4},{4,0},{8,12},{12,8},{1,5},{5,1},{9,13},{13,9},{2,6},{6,2},{1... | collective-permute-start | bytes 56 | tf_op jit(solution)/shard_map/ppermute | solution.py:46
  65.6 2.4 %collective-permute-done.9 = f32[4]{0:T(128)S(1)} collective-permute-done((f32[4]{0:T(128)S(1)}, f32[4]{0:T(128)S(1)}, u32[]{:S(2)}, u32[]{:S(2)}) %collective-permute-start.9) | collective-permute-done | bytes 48 | tf_op jit(solution)/shard_map/ppermute | solution.py:46
  68.0 2.7 %collective-permute-start.10 = (f32[4]{0:T(128)S(1)}, f32[4]{0:T(128)S(1)}, u32[]{:S(2)}, u32[]{:S(2)}) collective-permute-start(f32[4]{0:T(128)S(1)} %add.39), channel_id=1, source_target_pairs={{0,8},{4,12},{8,0},{12,4},{1,9},{5,13},{9,1},{13,5},{2,10},{6,14},... | collective-permute-start | bytes 56 | tf_op jit(solution)/shard_map/ppermute | solution.py:46
  70.7 2.4 %collective-permute-done.10 = f32[4]{0:T(128)S(1)} collective-permute-done((f32[4]{0:T(128)S(1)}, f32[4]{0:T(128)S(1)}, u32[]{:S(2)}, u32[]{:S(2)}) %collective-permute-start.10) | collective-permute-done | bytes 48 | tf_op jit(solution)/shard_map/ppermute | solution.py:46
  73.0 2.4 %collective-permute-start.11 = (f32[4]{0:T(128)S(1)}, f32[4]{0:T(128)S(1)}, u32[]{:S(2)}, u32[]{:S(2)}) collective-permute-start(f32[4]{0:T(128)S(1)} %add.40), channel_id=1, source_target_pairs={{0,2},{2,0},{1,3},{3,1},{4,6},{6,4},{5,7},{7,5},{8,10},{10,8},{9,1... | collective-permute-start | bytes 56 | tf_op jit(solution)/shard_map/ppermute | solution.py:46
  75.4 5.1 %collective-permute-done.11 = f32[4]{0:T(128)S(1)} collective-permute-done((f32[4]{0:T(128)S(1)}, f32[4]{0:T(128)S(1)}, u32[]{:S(2)}, u32[]{:S(2)}) %collective-permute-start.11) | collective-permute-done | bytes 48 | tf_op jit(solution)/shard_map/ppermute | solution.py:46
  81.0 2.6 %shard_map.131 = (f32[64,2048]{1,0:T(8,128)}, f32[64,2048]{1,0:T(8,128)}, f32[64,2048]{1,0:T(8,128)}) custom-call(f32[1,4]{1,0:T(1,128)} %add_bitcast_fusion.sums_ref, f32[64,2048]{1,0:T(8,128)} %iterate_ref.1, f32[64,2048]{1,0:T(8,128)} %residual_ref.1, f32[64,2048]{1,0:T(8,128)} %direction_ref.1, f32[64,2048]{1,0:T(8,128)} %copy-done.1), custom_call_target="tpu_custom_call" | custom-call | tf_op jit(solution)/shard_map/pallas_call | solution.py:275
  (49 shorter events, 8.8 us)
Async XLA Ops:
  0.6 22.6 %copy-start.7 = (f32[32,32]{1,0:T(8,128)S(1)}, f32[32,32]{1,0:T(8,128)}, u32[]{:S(2)}) copy-start(f32[32,32]{1,0:T(8,128)} %param.15) | copy-start | bytes 12292
  2.6 12.6 %collective-permute-start = (f32[68,16]{1,0:T(8,128)S(1)}, f32[68,16]{1,0:T(8,128)S(1)}, u32[]{:S(2)}, u32[]{:S(2)}) collective-permute-start(f32[68,16]{1,0:T(8,128)S(1)} %copy.16), channel_id=1, source_target_pairs={{0,1},{1,2},{2,3},{3,4},{4,5},{5,6},{6,7},{7,8},{8,9},{9,10},{10,1... | collective-permute-start | bytes 13064 | tf_op jit(solution)/shard_map/ppermute | solution.py:30
  4.5 12.2 %collective-permute-start.1 = (f32[64,16]{1,0:T(8,128)S(1)}, f32[64,16]{1,0:T(8,128)S(1)}, u32[]{:S(2)}, u32[]{:S(2)}) collective-permute-start(f32[64,16]{1,0:T(8,128)S(1)} %get-tuple-element.10), channel_id=1, source_target_pairs={{1,0},{2,1},{3,2},{4,3},{5,4},{6,5},{7,6},{8,7},{9,8},{10,9},{11,1... | collective-permute-start | bytes 12296 | tf_op jit(solution)/shard_map/ppermute | solution.py:30
  18.1 6.5 %copy-start.2 = (f32[64,2304]{1,0:T(8,128)}, f32[64,2304]{1,0:T(8,128)S(1)}, u32[]{:S(2)}) copy-start(f32[64,2304]{1,0:T(8,128)S(1)} %concatenate.16.middle_ref) | copy-start | bytes 1769476
  18.2 7.2 %collective-permute-start.2 = (f32[17,2304]{1,0:T(8,128)S(1)}, f32[17,2304]{1,0:T(8,128)S(1)}, u32[]{:S(2)}, u32[]{:S(2)}) collective-permute-start(f32[17,2304]{1,0:T(8,128)S(1)} %pad_maximum_fusion), channel_id=1, source_target_pairs={{0,64},{64,128},{128,192},{1,65},{65,129},{129,193},{2,66},{66,130... | collective-permute-start | bytes 470024 | tf_op jit(solution)/shard_map/ppermute | solution.py:30
  22.0 3.4 %copy-start.6 = (f32[4,128]{1,0:T(4,128)S(1)}, f32[4,128]{1,0:T(4,128)}, u32[]{:S(2)}) copy-start(f32[4,128]{1,0:T(4,128)} %param.14) | copy-start | bytes 6148
  22.0 7.0 %collective-permute-start.3 = (f32[16,2304]{1,0:T(8,128)S(1)}, f32[16,2304]{1,0:T(8,128)S(1)}, u32[]{:S(2)}, u32[]{:S(2)}) collective-permute-start(f32[16,2304]{1,0:T(8,128)S(1)} %get-tuple-element.5), channel_id=1, source_target_pairs={{64,0},{128,64},{192,128},{65,1},{129,65},{193,129},{66,2},{130,66... | collective-permute-start | bytes 442376 | tf_op jit(solution)/shard_map/ppermute | solution.py:30
  25.4 3.6 %copy-start.4 = (f32[17,2304]{1,0:T(8,128)}, f32[17,2304]{1,0:T(8,128)S(1)}, u32[]{:S(2)}) copy-start(f32[17,2304]{1,0:T(8,128)S(1)} %collective-permute-done.2.above_ref) | copy-start | bytes 470020
  26.7 15.6 %copy-start = (f32[64,2048]{1,0:T(8,128)S(1)}, f32[64,2048]{1,0:T(8,128)}, u32[]{:S(2)}) copy-start(f32[64,2048]{1,0:T(8,128)} %direction_ref.1) | copy-start | bytes 1572868
  29.0 0.7 copy-start.5
  42.3 1.3 %copy-start.3 = (f32[64,2048]{1,0:T(8,128)S(1)}, f32[64,2048]{1,0:T(8,128)}, u32[]{:S(2)}) copy-start(f32[64,2048]{1,0:T(8,128)} %residual_ref.1) | copy-start | bytes 1572868
  43.6 0.8 copy-start.1
  44.7 2.9 %collective-permute-start.4 = (f32[4]{0:T(128)S(1)}, f32[4]{0:T(128)S(1)}, u32[]{:S(2)}, u32[]{:S(2)}) collective-permute-start(f32[4]{0:T(128)S(1)} %maximum_reduce_fusion), channel_id=1, source_target_pairs={{0,1},{1,0},{2,3},{3,2},{4,5},{5,4},{6,7},{7,6},{8,9},{9,8},{10,11... | collective-permute-start | bytes 56 | tf_op jit(solution)/shard_map/ppermute | solution.py:46
  47.6 3.5 %collective-permute-start.5 = (f32[4]{0:T(128)S(1)}, f32[4]{0:T(128)S(1)}, u32[]{:S(2)}, u32[]{:S(2)}) collective-permute-start(f32[4]{0:T(128)S(1)} %add.34), channel_id=1, source_target_pairs={{0,64},{64,0},{128,192},{192,128},{1,65},{65,1},{129,193},{193,129... | collective-permute-start | bytes 56 | tf_op jit(solution)/shard_map/ppermute | solution.py:46
  51.2 4.7 %collective-permute-start.6 = (f32[4]{0:T(128)S(1)}, f32[4]{0:T(128)S(1)}, u32[]{:S(2)}, u32[]{:S(2)}) collective-permute-start(f32[4]{0:T(128)S(1)} %add.35), channel_id=1, source_target_pairs={{0,128},{64,192},{128,0},{192,64},{1,129},{65,193},{129,1},{193,65... | collective-permute-start | bytes 56 | tf_op jit(solution)/shard_map/ppermute | solution.py:46
  55.9 3.5 %collective-permute-start.7 = (f32[4]{0:T(128)S(1)}, f32[4]{0:T(128)S(1)}, u32[]{:S(2)}, u32[]{:S(2)}) collective-permute-start(f32[4]{0:T(128)S(1)} %add.36), channel_id=1, source_target_pairs={{0,16},{16,0},{32,48},{48,32},{1,17},{17,1},{33,49},{49,33},{2,18}... | collective-permute-start | bytes 56 | tf_op jit(solution)/shard_map/ppermute | solution.py:46
  59.4 5.0 %collective-permute-start.8 = (f32[4]{0:T(128)S(1)}, f32[4]{0:T(128)S(1)}, u32[]{:S(2)}, u32[]{:S(2)}) collective-permute-start(f32[4]{0:T(128)S(1)} %add.37), channel_id=1, source_target_pairs={{0,32},{16,48},{32,0},{48,16},{1,33},{17,49},{33,1},{49,17},{2,34}... | collective-permute-start | bytes 56 | tf_op jit(solution)/shard_map/ppermute | solution.py:46
  64.4 3.5 %collective-permute-start.9 = (f32[4]{0:T(128)S(1)}, f32[4]{0:T(128)S(1)}, u32[]{:S(2)}, u32[]{:S(2)}) collective-permute-start(f32[4]{0:T(128)S(1)} %add.38), channel_id=1, source_target_pairs={{0,4},{4,0},{8,12},{12,8},{1,5},{5,1},{9,13},{13,9},{2,6},{6,2},{1... | collective-permute-start | bytes 56 | tf_op jit(solution)/shard_map/ppermute | solution.py:46
  68.0 5.0 %collective-permute-start.10 = (f32[4]{0:T(128)S(1)}, f32[4]{0:T(128)S(1)}, u32[]{:S(2)}, u32[]{:S(2)}) collective-permute-start(f32[4]{0:T(128)S(1)} %add.39), channel_id=1, source_target_pairs={{0,8},{4,12},{8,0},{12,4},{1,9},{5,13},{9,1},{13,5},{2,10},{6,14},... | collective-permute-start | bytes 56 | tf_op jit(solution)/shard_map/ppermute | solution.py:46
  73.0 7.4 %collective-permute-start.11 = (f32[4]{0:T(128)S(1)}, f32[4]{0:T(128)S(1)}, u32[]{:S(2)}, u32[]{:S(2)}) collective-permute-start(f32[4]{0:T(128)S(1)} %add.40), channel_id=1, source_target_pairs={{0,2},{2,0},{1,3},{3,1},{4,6},{6,4},{5,7},{7,5},{8,10},{10,8},{9,1... | collective-permute-start | bytes 56 | tf_op jit(solution)/shard_map/ppermute | solution.py:46

commit v16 on v15

--- a/solution.py
+++ b/solution.py
@@ -311,7 +311,8 @@
     products = jnp.stack(
         [residual * residual, direction * applied, residual * applied, applied * applied]
     )
-    sums = summed_everywhere(jnp.sum(products, axis=(1, 2)), DOUBLING)
+    partial = lax.optimization_barrier(jnp.sum(products, axis=1))
+    sums = summed_everywhere(jnp.sum(partial, axis=1), DOUBLING)
     return updated(sums.reshape(1, 4), iterate, residual, direction, applied)
 
 

time: 84 us -> 84.2 us (level)
  no operation moved by 1% of the time
where the time goes in v16:
time: 84.2 us; the launch traced here: 83.7 us
  starting transfers between devices  31.8 us (38%)
  waiting for transfers between devices  25.5 us (30%)
  Pallas kernels  15.2 us (18%)
  local copies, waits for them, and re-layouts  7.11 us (8%)
  other arithmetic  3.34 us (4%)
    ppermute x8, waiting for transfers between devices, summed_everywhere(): x = x + lax.ppermute(x, axis, [(i, i ^ mask) for i in range(count)])  21.6 us
    ppermute x4, starting transfers between devices, passed_along(): lax.ppermute(value, axis, [(source, source + steps) for source in range(l...  17.6 us
    ppermute x8, starting transfers between devices, summed_everywhere(): x = x + lax.ppermute(x, axis, [(i, i ^ mask) for i in range(count)])  14.2 us
    pallas_call x1, Pallas kernels, analyze_weigh_synthesize(): pl.pallas_call(transform_kernel, out_shape=jax.ShapeDtypeStruct((rows - 3...  12.6 us
    ppermute x4, waiting for transfers between devices, passed_along(): lax.ppermute(value, axis, [(source, source + steps) for source in range(l...  3.87 us
    pallas_call x1, Pallas kernels, updated(): pl.pallas_call(update_kernel, grid=(height // rows,), out_shape=(shape, s...  2.57 us
  transfers between devices with their start and end apart: 12, of which 11 were waited for; matrix products, arithmetic and copies ran while one was open for 4% of the time, Pallas kernels for 0%

profile of v16, /device:TPU:16, one launch (start us, length us, event | category | flops | bytes accessed | tf_op | source)
XLA Modules:
  0.0 83.7 jit_solution(17054306845180702557)
XLA Ops:
  2.6 1.9 %collective-permute-start = (f32[68,16]{1,0:T(8,128)S(1)}, f32[68,16]{1,0:T(8,128)S(1)}, u32[]{:S(2)}, u32[]{:S(2)}) collective-permute-start(f32[68,16]{1,0:T(8,128)S(1)} %copy.16), channel_id=1, source_target_pairs={{0,1},{1,2},{2,3},{3,4},{4,5},{5,6},{6,7},{7,8},{8,9},{9,10},{10,1... | collective-permute-start | bytes 13064 | tf_op jit(solution)/shard_map/ppermute | solution.py:30
  4.5 10.6 %collective-permute-start.1 = (f32[64,16]{1,0:T(8,128)S(1)}, f32[64,16]{1,0:T(8,128)S(1)}, u32[]{:S(2)}, u32[]{:S(2)}) collective-permute-start(f32[64,16]{1,0:T(8,128)S(1)} %get-tuple-element.10), channel_id=1, source_target_pairs={{1,0},{2,1},{3,2},{4,3},{5,4},{6,5},{7,6},{8,7},{9,8},{10,9},{11,1... | collective-permute-start | bytes 12296 | tf_op jit(solution)/shard_map/ppermute | solution.py:30
  16.7 1.4 %concatenate.16.middle_ref = f32[64,2304]{1,0:T(8,128)S(1)} concatenate(f32[64,16]{1,0:T(8,128)S(1)} %slice.42, f32[64,2048]{1,0:T(8,128)} %direction_ref.1, f32[64,16]{1,0:T(8,128)S(1)} %collective-permute-done.1, f32[64,224]{1,0:T(8,128)S(1)} %broadcast_in_dim.15), dimensions={1} | concatenate | bytes 1179648 | tf_op jit(solution)/shard_map/concatenate | solution.py:293
  18.2 3.8 %collective-permute-start.2 = (f32[17,2304]{1,0:T(8,128)S(1)}, f32[17,2304]{1,0:T(8,128)S(1)}, u32[]{:S(2)}, u32[]{:S(2)}) collective-permute-start(f32[17,2304]{1,0:T(8,128)S(1)} %pad_maximum_fusion), channel_id=1, source_target_pairs={{0,64},{64,128},{128,192},{1,65},{65,129},{129,193},{2,66},{66,130... | collective-permute-start | bytes 470024 | tf_op jit(solution)/shard_map/ppermute | solution.py:30
  22.0 1.3 %collective-permute-start.3 = (f32[16,2304]{1,0:T(8,128)S(1)}, f32[16,2304]{1,0:T(8,128)S(1)}, u32[]{:S(2)}, u32[]{:S(2)}) collective-permute-start(f32[16,2304]{1,0:T(8,128)S(1)} %get-tuple-element.5), channel_id=1, source_target_pairs={{64,0},{128,64},{192,128},{65,1},{129,65},{193,129},{66,2},{130,66... | collective-permute-start | bytes 442376 | tf_op jit(solution)/shard_map/ppermute | solution.py:30
  23.4 1.2 %reshape.19.fw_ref = f32[160,512]{1,0:T(8,128)} reshape(f32[5,32,2,8,32]{4,3,2,1,0:T(8,128)S(1)} %broadcast_in_dim.16) | data formatting | bytes 655360 | tf_op jit(solution)/shard_map/reshape | solution.py:237
  26.7 2.3 %collective-permute-done.3.below_ref = f32[16,2304]{1,0:T(8,128)S(1)} collective-permute-done((f32[16,2304]{1,0:T(8,128)S(1)}, f32[16,2304]{1,0:T(8,128)S(1)}, u32[]{:S(2)}, u32[]{:S(2)}) %collective-permute-start.3) | collective-permute-done | bytes 147488 | tf_op jit(solution)/shard_map/ppermute | solution.py:30
  29.7 12.6 %shard_map.130 = f32[64,2304]{1,0:T(8,128)} custom-call(f32[17,2304]{1,0:T(8,128)} %copy-done.4, f32[64,2304]{1,0:T(8,128)} %copy-done.2, f32[16,2304]{1,0:T(8,128)} %copy-done.5, bf16[256,512]{1,0:T(8,128)(2,1)} %constant.7.clone.mh_ref, bf16[256,512]{1,0:T(8,128)(2,1)} %constant.20.clone.ml_ref, bf16[160,192]{1,0:T(8,128)(2,1)} %constant.21.clone.fh_ref, ...), custom_call_target="tpu_custom_call" | custom-call | tf_op jit(solution)/shard_map/pallas_call | solution.py:243
  42.3 1.3 %multiply_bitcast_fusion.2 = (f32[1,64,2048]{2,1,0:T(8,128)S(1)}, f32[64,2048]{1,0:T(8,128)S(1)}) fusion(f32[64,2048]{1,0:T(8,128)S(1)} %copy-done, f32[64,2304]{1,0:T(8,128)} %shard_map.130), kind=kLoop, calls=%fused_computation.4 | loop fusion | flops 393216 | bytes 2097152 | tf_op jit(solution)/shard_map/stack | solution.py:311
  44.7 2.1 %collective-permute-start.4 = (f32[4]{0:T(128)S(1)}, f32[4]{0:T(128)S(1)}, u32[]{:S(2)}, u32[]{:S(2)}) collective-permute-start(f32[4]{0:T(128)S(1)} %reduce_sum.19), channel_id=1, source_target_pairs={{0,1},{1,0},{2,3},{3,2},{4,5},{5,4},{6,7},{7,6},{8,9},{9,8},{10,11... | collective-permute-start | bytes 56 | tf_op jit(solution)/shard_map/ppermute | solution.py:46
  47.7 1.4 %collective-permute-start.5 = (f32[4]{0:T(128)S(1)}, f32[4]{0:T(128)S(1)}, u32[]{:S(2)}, u32[]{:S(2)}) collective-permute-start(f32[4]{0:T(128)S(1)} %add.34), channel_id=1, source_target_pairs={{0,64},{64,0},{128,192},{192,128},{1,65},{65,1},{129,193},{193,129... | collective-permute-start | bytes 56 | tf_op jit(solution)/shard_map/ppermute | solution.py:46
  49.1 2.2 %collective-permute-done.5 = f32[4]{0:T(128)S(1)} collective-permute-done((f32[4]{0:T(128)S(1)}, f32[4]{0:T(128)S(1)}, u32[]{:S(2)}, u32[]{:S(2)}) %collective-permute-start.5) | collective-permute-done | bytes 48 | tf_op jit(solution)/shard_map/ppermute | solution.py:46
  51.2 3.2 %collective-permute-start.6 = (f32[4]{0:T(128)S(1)}, f32[4]{0:T(128)S(1)}, u32[]{:S(2)}, u32[]{:S(2)}) collective-permute-start(f32[4]{0:T(128)S(1)} %add.35), channel_id=1, source_target_pairs={{0,128},{64,192},{128,0},{192,64},{1,129},{65,193},{129,1},{193,65... | collective-permute-start | bytes 56 | tf_op jit(solution)/shard_map/ppermute | solution.py:46
  54.4 1.5 %collective-permute-done.6 = f32[4]{0:T(128)S(1)} collective-permute-done((f32[4]{0:T(128)S(1)}, f32[4]{0:T(128)S(1)}, u32[]{:S(2)}, u32[]{:S(2)}) %collective-permute-start.6) | collective-permute-done | bytes 48 | tf_op jit(solution)/shard_map/ppermute | solution.py:46
  55.9 1.3 %collective-permute-start.7 = (f32[4]{0:T(128)S(1)}, f32[4]{0:T(128)S(1)}, u32[]{:S(2)}, u32[]{:S(2)}) collective-permute-start(f32[4]{0:T(128)S(1)} %add.36), channel_id=1, source_target_pairs={{0,16},{16,0},{32,48},{48,32},{1,17},{17,1},{33,49},{49,33},{2,18}... | collective-permute-start | bytes 56 | tf_op jit(solution)/shard_map/ppermute | solution.py:46
  57.2 2.3 %collective-permute-done.7 = f32[4]{0:T(128)S(1)} collective-permute-done((f32[4]{0:T(128)S(1)}, f32[4]{0:T(128)S(1)}, u32[]{:S(2)}, u32[]{:S(2)}) %collective-permute-start.7) | collective-permute-done | bytes 48 | tf_op jit(solution)/shard_map/ppermute | solution.py:46
  59.5 5.0 %collective-permute-done.8 = f32[4]{0:T(128)S(1)} collective-permute-done((f32[4]{0:T(128)S(1)}, f32[4]{0:T(128)S(1)}, u32[]{:S(2)}, u32[]{:S(2)}) %collective-permute-start.8) | collective-permute-done | bytes 48 | tf_op jit(solution)/shard_map/ppermute | solution.py:46
  64.5 1.1 %collective-permute-start.9 = (f32[4]{0:T(128)S(1)}, f32[4]{0:T(128)S(1)}, u32[]{:S(2)}, u32[]{:S(2)}) collective-permute-start(f32[4]{0:T(128)S(1)} %add.38), channel_id=1, source_target_pairs={{0,4},{4,0},{8,12},{12,8},{1,5},{5,1},{9,13},{13,9},{2,6},{6,2},{1... | collective-permute-start | bytes 56 | tf_op jit(solution)/shard_map/ppermute | solution.py:46
  65.7 2.4 %collective-permute-done.9 = f32[4]{0:T(128)S(1)} collective-permute-done((f32[4]{0:T(128)S(1)}, f32[4]{0:T(128)S(1)}, u32[]{:S(2)}, u32[]{:S(2)}) %collective-permute-start.9) | collective-permute-done | bytes 48 | tf_op jit(solution)/shard_map/ppermute | solution.py:46
  68.1 2.7 %collective-permute-start.10 = (f32[4]{0:T(128)S(1)}, f32[4]{0:T(128)S(1)}, u32[]{:S(2)}, u32[]{:S(2)}) collective-permute-start(f32[4]{0:T(128)S(1)} %add.39), channel_id=1, source_target_pairs={{0,8},{4,12},{8,0},{12,4},{1,9},{5,13},{9,1},{13,5},{2,10},{6,14},... | collective-permute-start | bytes 56 | tf_op jit(solution)/shard_map/ppermute | solution.py:46
  70.7 2.4 %collective-permute-done.10 = f32[4]{0:T(128)S(1)} collective-permute-done((f32[4]{0:T(128)S(1)}, f32[4]{0:T(128)S(1)}, u32[]{:S(2)}, u32[]{:S(2)}) %collective-permute-start.10) | collective-permute-done | bytes 48 | tf_op jit(solution)/shard_map/ppermute | solution.py:46
  73.1 2.4 %collective-permute-start.11 = (f32[4]{0:T(128)S(1)}, f32[4]{0:T(128)S(1)}, u32[]{:S(2)}, u32[]{:S(2)}) collective-permute-start(f32[4]{0:T(128)S(1)} %add.40), channel_id=1, source_target_pairs={{0,2},{2,0},{1,3},{3,1},{4,6},{6,4},{5,7},{7,5},{8,10},{10,8},{9,1... | collective-permute-start | bytes 56 | tf_op jit(solution)/shard_map/ppermute | solution.py:46
  75.5 5.1 %collective-permute-done.11 = f32[4]{0:T(128)S(1)} collective-permute-done((f32[4]{0:T(128)S(1)}, f32[4]{0:T(128)S(1)}, u32[]{:S(2)}, u32[]{:S(2)}) %collective-permute-start.11) | collective-permute-done | bytes 48 | tf_op jit(solution)/shard_map/ppermute | solution.py:46
  81.1 2.6 %shard_map.131 = (f32[64,2048]{1,0:T(8,128)}, f32[64,2048]{1,0:T(8,128)}, f32[64,2048]{1,0:T(8,128)}) custom-call(f32[1,4]{1,0:T(1,128)} %add_bitcast_fusion.sums_ref, f32[64,2048]{1,0:T(8,128)} %iterate_ref.1, f32[64,2048]{1,0:T(8,128)} %residual_ref.1, f32[64,2048]{1,0:T(8,128)} %direction_ref.1, f32[64,2048]{1,0:T(8,128)} %copy-done.1), custom_call_target="tpu_custom_call" | custom-call | tf_op jit(solution)/shard_map/pallas_call | solution.py:275
  (50 shorter events, 8.9 us)
Async XLA Ops:
  0.6 22.6 %copy-start.7 = (f32[32,32]{1,0:T(8,128)S(1)}, f32[32,32]{1,0:T(8,128)}, u32[]{:S(2)}) copy-start(f32[32,32]{1,0:T(8,128)} %param.15) | copy-start | bytes 12292
  2.6 12.6 %collective-permute-start = (f32[68,16]{1,0:T(8,128)S(1)}, f32[68,16]{1,0:T(8,128)S(1)}, u32[]{:S(2)}, u32[]{:S(2)}) collective-permute-start(f32[68,16]{1,0:T(8,128)S(1)} %copy.16), channel_id=1, source_target_pairs={{0,1},{1,2},{2,3},{3,4},{4,5},{5,6},{6,7},{7,8},{8,9},{9,10},{10,1... | collective-permute-start | bytes 13064 | tf_op jit(solution)/shard_map/ppermute | solution.py:30
  4.5 12.2 %collective-permute-start.1 = (f32[64,16]{1,0:T(8,128)S(1)}, f32[64,16]{1,0:T(8,128)S(1)}, u32[]{:S(2)}, u32[]{:S(2)}) collective-permute-start(f32[64,16]{1,0:T(8,128)S(1)} %get-tuple-element.10), channel_id=1, source_target_pairs={{1,0},{2,1},{3,2},{4,3},{5,4},{6,5},{7,6},{8,7},{9,8},{10,9},{11,1... | collective-permute-start | bytes 12296 | tf_op jit(solution)/shard_map/ppermute | solution.py:30
  18.1 6.5 %copy-start.2 = (f32[64,2304]{1,0:T(8,128)}, f32[64,2304]{1,0:T(8,128)S(1)}, u32[]{:S(2)}) copy-start(f32[64,2304]{1,0:T(8,128)S(1)} %concatenate.16.middle_ref) | copy-start | bytes 1769476
  18.2 7.2 %collective-permute-start.2 = (f32[17,2304]{1,0:T(8,128)S(1)}, f32[17,2304]{1,0:T(8,128)S(1)}, u32[]{:S(2)}, u32[]{:S(2)}) collective-permute-start(f32[17,2304]{1,0:T(8,128)S(1)} %pad_maximum_fusion), channel_id=1, source_target_pairs={{0,64},{64,128},{128,192},{1,65},{65,129},{129,193},{2,66},{66,130... | collective-permute-start | bytes 470024 | tf_op jit(solution)/shard_map/ppermute | solution.py:30
  22.0 3.4 %copy-start.6 = (f32[4,128]{1,0:T(4,128)S(1)}, f32[4,128]{1,0:T(4,128)}, u32[]{:S(2)}) copy-start(f32[4,128]{1,0:T(4,128)} %param.14) | copy-start | bytes 6148
  22.0 7.0 %collective-permute-start.3 = (f32[16,2304]{1,0:T(8,128)S(1)}, f32[16,2304]{1,0:T(8,128)S(1)}, u32[]{:S(2)}, u32[]{:S(2)}) collective-permute-start(f32[16,2304]{1,0:T(8,128)S(1)} %get-tuple-element.5), channel_id=1, source_target_pairs={{64,0},{128,64},{192,128},{65,1},{129,65},{193,129},{66,2},{130,66... | collective-permute-start | bytes 442376 | tf_op jit(solution)/shard_map/ppermute | solution.py:30
  25.4 3.6 %copy-start.4 = (f32[17,2304]{1,0:T(8,128)}, f32[17,2304]{1,0:T(8,128)S(1)}, u32[]{:S(2)}) copy-start(f32[17,2304]{1,0:T(8,128)S(1)} %collective-permute-done.2.above_ref) | copy-start | bytes 470020
  26.7 15.6 %copy-start = (f32[64,2048]{1,0:T(8,128)S(1)}, f32[64,2048]{1,0:T(8,128)}, u32[]{:S(2)}) copy-start(f32[64,2048]{1,0:T(8,128)} %direction_ref.1) | copy-start | bytes 1572868
  29.0 0.7 copy-start.5
  42.3 1.3 %copy-start.3 = (f32[64,2048]{1,0:T(8,128)S(1)}, f32[64,2048]{1,0:T(8,128)}, u32[]{:S(2)}) copy-start(f32[64,2048]{1,0:T(8,128)} %residual_ref.1) | copy-start | bytes 1572868
  43.6 0.8 copy-start.1
  44.7 3.0 %collective-permute-start.4 = (f32[4]{0:T(128)S(1)}, f32[4]{0:T(128)S(1)}, u32[]{:S(2)}, u32[]{:S(2)}) collective-permute-start(f32[4]{0:T(128)S(1)} %reduce_sum.19), channel_id=1, source_target_pairs={{0,1},{1,0},{2,3},{3,2},{4,5},{5,4},{6,7},{7,6},{8,9},{9,8},{10,11... | collective-permute-start | bytes 56 | tf_op jit(solution)/shard_map/ppermute | solution.py:46
  47.7 3.5 %collective-permute-start.5 = (f32[4]{0:T(128)S(1)}, f32[4]{0:T(128)S(1)}, u32[]{:S(2)}, u32[]{:S(2)}) collective-permute-start(f32[4]{0:T(128)S(1)} %add.34), channel_id=1, source_target_pairs={{0,64},{64,0},{128,192},{192,128},{1,65},{65,1},{129,193},{193,129... | collective-permute-start | bytes 56 | tf_op jit(solution)/shard_map/ppermute | solution.py:46
  51.2 4.7 %collective-permute-start.6 = (f32[4]{0:T(128)S(1)}, f32[4]{0:T(128)S(1)}, u32[]{:S(2)}, u32[]{:S(2)}) collective-permute-start(f32[4]{0:T(128)S(1)} %add.35), channel_id=1, source_target_pairs={{0,128},{64,192},{128,0},{192,64},{1,129},{65,193},{129,1},{193,65... | collective-permute-start | bytes 56 | tf_op jit(solution)/shard_map/ppermute | solution.py:46
  55.9 3.5 %collective-permute-start.7 = (f32[4]{0:T(128)S(1)}, f32[4]{0:T(128)S(1)}, u32[]{:S(2)}, u32[]{:S(2)}) collective-permute-start(f32[4]{0:T(128)S(1)} %add.36), channel_id=1, source_target_pairs={{0,16},{16,0},{32,48},{48,32},{1,17},{17,1},{33,49},{49,33},{2,18}... | collective-permute-start | bytes 56 | tf_op jit(solution)/shard_map/ppermute | solution.py:46
  59.5 5.0 %collective-permute-start.8 = (f32[4]{0:T(128)S(1)}, f32[4]{0:T(128)S(1)}, u32[]{:S(2)}, u32[]{:S(2)}) collective-permute-start(f32[4]{0:T(128)S(1)} %add.37), channel_id=1, source_target_pairs={{0,32},{16,48},{32,0},{48,16},{1,33},{17,49},{33,1},{49,17},{2,34}... | collective-permute-start | bytes 56 | tf_op jit(solution)/shard_map/ppermute | solution.py:46
  64.5 3.5 %collective-permute-start.9 = (f32[4]{0:T(128)S(1)}, f32[4]{0:T(128)S(1)}, u32[]{:S(2)}, u32[]{:S(2)}) collective-permute-start(f32[4]{0:T(128)S(1)} %add.38), channel_id=1, source_target_pairs={{0,4},{4,0},{8,12},{12,8},{1,5},{5,1},{9,13},{13,9},{2,6},{6,2},{1... | collective-permute-start | bytes 56 | tf_op jit(solution)/shard_map/ppermute | solution.py:46
  68.1 5.0 %collective-permute-start.10 = (f32[4]{0:T(128)S(1)}, f32[4]{0:T(128)S(1)}, u32[]{:S(2)}, u32[]{:S(2)}) collective-permute-start(f32[4]{0:T(128)S(1)} %add.39), channel_id=1, source_target_pairs={{0,8},{4,12},{8,0},{12,4},{1,9},{5,13},{9,1},{13,5},{2,10},{6,14},... | collective-permute-start | bytes 56 | tf_op jit(solution)/shard_map/ppermute | solution.py:46
  73.1 7.4 %collective-permute-start.11 = (f32[4]{0:T(128)S(1)}, f32[4]{0:T(128)S(1)}, u32[]{:S(2)}, u32[]{:S(2)}) collective-permute-start(f32[4]{0:T(128)S(1)} %add.40), channel_id=1, source_target_pairs={{0,2},{2,0},{1,3},{3,1},{4,6},{6,4},{5,7},{7,5},{8,10},{10,8},{9,1... | collective-permute-start | bytes 56 | tf_op jit(solution)/shard_map/ppermute | solution.py:46

commit v17 on v15

--- a/solution.py
+++ b/solution.py
@@ -10,13 +10,13 @@
 COL = ("col_0", "col_1", "col_2", "col_3")
 DOUBLING = (
     ("col_3", 1),
+    ("col_2", 1),
     ("row", 1),
     ("row", 2),
     ("col_0", 1),
     ("col_0", 2),
     ("col_1", 1),
     ("col_1", 2),
-    ("col_2", 1),
 )
 
 

time: 84 us -> 84 us (level)
  no operation moved by 1% of the time
where the time goes in v17:
time: 84 us; the launch traced here: 83.6 us
  starting transfers between devices  32 us (38%)
  waiting for transfers between devices  25.3 us (30%)
  Pallas kernels  15.2 us (18%)
  local copies, waits for them, and re-layouts  7.12 us (8%)
  other arithmetic  3.21 us (4%)
    ppermute x8, waiting for transfers between devices, summed_everywhere(): x = x + lax.ppermute(x, axis, [(i, i ^ mask) for i in range(count)])  21.4 us
    ppermute x4, starting transfers between devices, passed_along(): lax.ppermute(value, axis, [(source, source + steps) for source in range(l...  17.6 us
    ppermute x8, starting transfers between devices, summed_everywhere(): x = x + lax.ppermute(x, axis, [(i, i ^ mask) for i in range(count)])  14.4 us
    pallas_call x1, Pallas kernels, analyze_weigh_synthesize(): pl.pallas_call(transform_kernel, out_shape=jax.ShapeDtypeStruct((rows - 3...  12.6 us
    ppermute x4, waiting for transfers between devices, passed_along(): lax.ppermute(value, axis, [(source, source + steps) for source in range(l...  3.87 us
    pallas_call x1, Pallas kernels, updated(): pl.pallas_call(update_kernel, grid=(height // rows,), out_shape=(shape, s...  2.57 us
  transfers between devices with their start and end apart: 12, of which 11 were waited for; matrix products, arithmetic and copies ran while one was open for 4% of the time, Pallas kernels for 0%

profile of v17, /device:TPU:16, one launch (start us, length us, event | category | flops | bytes accessed | tf_op | source)
XLA Modules:
  0.0 83.6 jit_solution(6313077878899923146)
XLA Ops:
  2.6 1.9 %collective-permute-start = (f32[68,16]{1,0:T(8,128)S(1)}, f32[68,16]{1,0:T(8,128)S(1)}, u32[]{:S(2)}, u32[]{:S(2)}) collective-permute-start(f32[68,16]{1,0:T(8,128)S(1)} %copy.16), channel_id=1, source_target_pairs={{0,1},{1,2},{2,3},{3,4},{4,5},{5,6},{6,7},{7,8},{8,9},{9,10},{10,1... | collective-permute-start | bytes 13064 | tf_op jit(solution)/shard_map/ppermute | solution.py:30
  4.5 10.6 %collective-permute-start.1 = (f32[64,16]{1,0:T(8,128)S(1)}, f32[64,16]{1,0:T(8,128)S(1)}, u32[]{:S(2)}, u32[]{:S(2)}) collective-permute-start(f32[64,16]{1,0:T(8,128)S(1)} %get-tuple-element.10), channel_id=1, source_target_pairs={{1,0},{2,1},{3,2},{4,3},{5,4},{6,5},{7,6},{8,7},{9,8},{10,9},{11,1... | collective-permute-start | bytes 12296 | tf_op jit(solution)/shard_map/ppermute | solution.py:30
  16.7 1.4 %concatenate.16.middle_ref = f32[64,2304]{1,0:T(8,128)S(1)} concatenate(f32[64,16]{1,0:T(8,128)S(1)} %slice.42, f32[64,2048]{1,0:T(8,128)} %direction_ref.1, f32[64,16]{1,0:T(8,128)S(1)} %collective-permute-done.1, f32[64,224]{1,0:T(8,128)S(1)} %broadcast_in_dim.15), dimensions={1} | concatenate | bytes 1179648 | tf_op jit(solution)/shard_map/concatenate | solution.py:293
  18.2 3.8 %collective-permute-start.2 = (f32[17,2304]{1,0:T(8,128)S(1)}, f32[17,2304]{1,0:T(8,128)S(1)}, u32[]{:S(2)}, u32[]{:S(2)}) collective-permute-start(f32[17,2304]{1,0:T(8,128)S(1)} %pad_maximum_fusion), channel_id=1, source_target_pairs={{0,64},{64,128},{128,192},{1,65},{65,129},{129,193},{2,66},{66,130... | collective-permute-start | bytes 470024 | tf_op jit(solution)/shard_map/ppermute | solution.py:30
  22.0 1.3 %collective-permute-start.3 = (f32[16,2304]{1,0:T(8,128)S(1)}, f32[16,2304]{1,0:T(8,128)S(1)}, u32[]{:S(2)}, u32[]{:S(2)}) collective-permute-start(f32[16,2304]{1,0:T(8,128)S(1)} %get-tuple-element.5), channel_id=1, source_target_pairs={{64,0},{128,64},{192,128},{65,1},{129,65},{193,129},{66,2},{130,66... | collective-permute-start | bytes 442376 | tf_op jit(solution)/shard_map/ppermute | solution.py:30
  23.4 1.2 %reshape.19.fw_ref = f32[160,512]{1,0:T(8,128)} reshape(f32[5,32,2,8,32]{4,3,2,1,0:T(8,128)S(1)} %broadcast_in_dim.16) | data formatting | bytes 655360 | tf_op jit(solution)/shard_map/reshape | solution.py:237
  26.7 2.3 %collective-permute-done.3.below_ref = f32[16,2304]{1,0:T(8,128)S(1)} collective-permute-done((f32[16,2304]{1,0:T(8,128)S(1)}, f32[16,2304]{1,0:T(8,128)S(1)}, u32[]{:S(2)}, u32[]{:S(2)}) %collective-permute-start.3) | collective-permute-done | bytes 147488 | tf_op jit(solution)/shard_map/ppermute | solution.py:30
  29.7 12.6 %shard_map.130 = f32[64,2304]{1,0:T(8,128)} custom-call(f32[17,2304]{1,0:T(8,128)} %copy-done.4, f32[64,2304]{1,0:T(8,128)} %copy-done.2, f32[16,2304]{1,0:T(8,128)} %copy-done.5, bf16[256,512]{1,0:T(8,128)(2,1)} %constant.7.clone.mh_ref, bf16[256,512]{1,0:T(8,128)(2,1)} %constant.20.clone.ml_ref, bf16[160,192]{1,0:T(8,128)(2,1)} %constant.21.clone.fh_ref, ...), custom_call_target="tpu_custom_call" | custom-call | tf_op jit(solution)/shard_map/pallas_call | solution.py:243
  42.3 1.3 %multiply_bitcast_fusion.2 = (f32[1,64,2048]{2,1,0:T(8,128)S(1)}, f32[64,2048]{1,0:T(8,128)S(1)}) fusion(f32[64,2048]{1,0:T(8,128)S(1)} %copy-done, f32[64,2304]{1,0:T(8,128)} %shard_map.130), kind=kLoop, calls=%fused_computation.4 | loop fusion | flops 393216 | bytes 2097152 | tf_op jit(solution)/shard_map/stack | solution.py:311
  44.7 2.1 %collective-permute-start.4 = (f32[4]{0:T(128)S(1)}, f32[4]{0:T(128)S(1)}, u32[]{:S(2)}, u32[]{:S(2)}) collective-permute-start(f32[4]{0:T(128)S(1)} %maximum_reduce_fusion), channel_id=1, source_target_pairs={{0,1},{1,0},{2,3},{3,2},{4,5},{5,4},{6,7},{7,6},{8,9},{9,8},{10,11... | collective-permute-start | bytes 56 | tf_op jit(solution)/shard_map/ppermute | solution.py:46
  47.6 2.6 %collective-permute-start.5 = (f32[4]{0:T(128)S(1)}, f32[4]{0:T(128)S(1)}, u32[]{:S(2)}, u32[]{:S(2)}) collective-permute-start(f32[4]{0:T(128)S(1)} %add.34), channel_id=1, source_target_pairs={{0,2},{2,0},{1,3},{3,1},{4,6},{6,4},{5,7},{7,5},{8,10},{10,8},{9,1... | collective-permute-start | bytes 56 | tf_op jit(solution)/shard_map/ppermute | solution.py:46
  50.2 4.8 %collective-permute-done.5 = f32[4]{0:T(128)S(1)} collective-permute-done((f32[4]{0:T(128)S(1)}, f32[4]{0:T(128)S(1)}, u32[]{:S(2)}, u32[]{:S(2)}) %collective-permute-start.5) | collective-permute-done | bytes 48 | tf_op jit(solution)/shard_map/ppermute | solution.py:46
  55.1 1.4 %collective-permute-start.6 = (f32[4]{0:T(128)S(1)}, f32[4]{0:T(128)S(1)}, u32[]{:S(2)}, u32[]{:S(2)}) collective-permute-start(f32[4]{0:T(128)S(1)} %add.35), channel_id=1, source_target_pairs={{0,64},{64,0},{128,192},{192,128},{1,65},{65,1},{129,193},{193,129... | collective-permute-start | bytes 56 | tf_op jit(solution)/shard_map/ppermute | solution.py:46
  56.4 2.2 %collective-permute-done.6 = f32[4]{0:T(128)S(1)} collective-permute-done((f32[4]{0:T(128)S(1)}, f32[4]{0:T(128)S(1)}, u32[]{:S(2)}, u32[]{:S(2)}) %collective-permute-start.6) | collective-permute-done | bytes 48 | tf_op jit(solution)/shard_map/ppermute | solution.py:46
  58.6 3.2 %collective-permute-start.7 = (f32[4]{0:T(128)S(1)}, f32[4]{0:T(128)S(1)}, u32[]{:S(2)}, u32[]{:S(2)}) collective-permute-start(f32[4]{0:T(128)S(1)} %add.36), channel_id=1, source_target_pairs={{0,128},{64,192},{128,0},{192,64},{1,129},{65,193},{129,1},{193,65... | collective-permute-start | bytes 56 | tf_op jit(solution)/shard_map/ppermute | solution.py:46
  61.8 1.5 %collective-permute-done.7 = f32[4]{0:T(128)S(1)} collective-permute-done((f32[4]{0:T(128)S(1)}, f32[4]{0:T(128)S(1)}, u32[]{:S(2)}, u32[]{:S(2)}) %collective-permute-start.7) | collective-permute-done | bytes 48 | tf_op jit(solution)/shard_map/ppermute | solution.py:46
  63.3 1.3 %collective-permute-start.8 = (f32[4]{0:T(128)S(1)}, f32[4]{0:T(128)S(1)}, u32[]{:S(2)}, u32[]{:S(2)}) collective-permute-start(f32[4]{0:T(128)S(1)} %add.37), channel_id=1, source_target_pairs={{0,16},{16,0},{32,48},{48,32},{1,17},{17,1},{33,49},{49,33},{2,18}... | collective-permute-start | bytes 56 | tf_op jit(solution)/shard_map/ppermute | solution.py:46
  64.6 2.3 %collective-permute-done.8 = f32[4]{0:T(128)S(1)} collective-permute-done((f32[4]{0:T(128)S(1)}, f32[4]{0:T(128)S(1)}, u32[]{:S(2)}, u32[]{:S(2)}) %collective-permute-start.8) | collective-permute-done | bytes 48 | tf_op jit(solution)/shard_map/ppermute | solution.py:46
  66.9 5.0 %collective-permute-done.9 = f32[4]{0:T(128)S(1)} collective-permute-done((f32[4]{0:T(128)S(1)}, f32[4]{0:T(128)S(1)}, u32[]{:S(2)}, u32[]{:S(2)}) %collective-permute-start.9) | collective-permute-done | bytes 48 | tf_op jit(solution)/shard_map/ppermute | solution.py:46
  71.9 1.1 %collective-permute-start.10 = (f32[4]{0:T(128)S(1)}, f32[4]{0:T(128)S(1)}, u32[]{:S(2)}, u32[]{:S(2)}) collective-permute-start(f32[4]{0:T(128)S(1)} %add.39), channel_id=1, source_target_pairs={{0,4},{4,0},{8,12},{12,8},{1,5},{5,1},{9,13},{13,9},{2,6},{6,2},{1... | collective-permute-start | bytes 56 | tf_op jit(solution)/shard_map/ppermute | solution.py:46
  73.0 2.4 %collective-permute-done.10 = f32[4]{0:T(128)S(1)} collective-permute-done((f32[4]{0:T(128)S(1)}, f32[4]{0:T(128)S(1)}, u32[]{:S(2)}, u32[]{:S(2)}) %collective-permute-start.10) | collective-permute-done | bytes 48 | tf_op jit(solution)/shard_map/ppermute | solution.py:46
  75.4 2.7 %collective-permute-start.11 = (f32[4]{0:T(128)S(1)}, f32[4]{0:T(128)S(1)}, u32[]{:S(2)}, u32[]{:S(2)}) collective-permute-start(f32[4]{0:T(128)S(1)} %add.40), channel_id=1, source_target_pairs={{0,8},{4,12},{8,0},{12,4},{1,9},{5,13},{9,1},{13,5},{2,10},{6,14},... | collective-permute-start | bytes 56 | tf_op jit(solution)/shard_map/ppermute | solution.py:46
  78.1 2.4 %collective-permute-done.11 = f32[4]{0:T(128)S(1)} collective-permute-done((f32[4]{0:T(128)S(1)}, f32[4]{0:T(128)S(1)}, u32[]{:S(2)}, u32[]{:S(2)}) %collective-permute-start.11) | collective-permute-done | bytes 48 | tf_op jit(solution)/shard_map/ppermute | solution.py:46
  81.0 2.6 %shard_map.131 = (f32[64,2048]{1,0:T(8,128)}, f32[64,2048]{1,0:T(8,128)}, f32[64,2048]{1,0:T(8,128)}) custom-call(f32[1,4]{1,0:T(1,128)} %add_bitcast_fusion.sums_ref, f32[64,2048]{1,0:T(8,128)} %iterate_ref.1, f32[64,2048]{1,0:T(8,128)} %residual_ref.1, f32[64,2048]{1,0:T(8,128)} %direction_ref.1, f32[64,2048]{1,0:T(8,128)} %copy-done.1), custom_call_target="tpu_custom_call" | custom-call | tf_op jit(solution)/shard_map/pallas_call | solution.py:275
  (49 shorter events, 8.8 us)
Async XLA Ops:
  0.6 22.6 %copy-start.7 = (f32[32,32]{1,0:T(8,128)S(1)}, f32[32,32]{1,0:T(8,128)}, u32[]{:S(2)}) copy-start(f32[32,32]{1,0:T(8,128)} %param.15) | copy-start | bytes 12292
  2.6 12.6 %collective-permute-start = (f32[68,16]{1,0:T(8,128)S(1)}, f32[68,16]{1,0:T(8,128)S(1)}, u32[]{:S(2)}, u32[]{:S(2)}) collective-permute-start(f32[68,16]{1,0:T(8,128)S(1)} %copy.16), channel_id=1, source_target_pairs={{0,1},{1,2},{2,3},{3,4},{4,5},{5,6},{6,7},{7,8},{8,9},{9,10},{10,1... | collective-permute-start | bytes 13064 | tf_op jit(solution)/shard_map/ppermute | solution.py:30
  4.5 12.2 %collective-permute-start.1 = (f32[64,16]{1,0:T(8,128)S(1)}, f32[64,16]{1,0:T(8,128)S(1)}, u32[]{:S(2)}, u32[]{:S(2)}) collective-permute-start(f32[64,16]{1,0:T(8,128)S(1)} %get-tuple-element.10), channel_id=1, source_target_pairs={{1,0},{2,1},{3,2},{4,3},{5,4},{6,5},{7,6},{8,7},{9,8},{10,9},{11,1... | collective-permute-start | bytes 12296 | tf_op jit(solution)/shard_map/ppermute | solution.py:30
  18.1 6.5 %copy-start.2 = (f32[64,2304]{1,0:T(8,128)}, f32[64,2304]{1,0:T(8,128)S(1)}, u32[]{:S(2)}) copy-start(f32[64,2304]{1,0:T(8,128)S(1)} %concatenate.16.middle_ref) | copy-start | bytes 1769476
  18.2 7.2 %collective-permute-start.2 = (f32[17,2304]{1,0:T(8,128)S(1)}, f32[17,2304]{1,0:T(8,128)S(1)}, u32[]{:S(2)}, u32[]{:S(2)}) collective-permute-start(f32[17,2304]{1,0:T(8,128)S(1)} %pad_maximum_fusion), channel_id=1, source_target_pairs={{0,64},{64,128},{128,192},{1,65},{65,129},{129,193},{2,66},{66,130... | collective-permute-start | bytes 470024 | tf_op jit(solution)/shard_map/ppermute | solution.py:30
  22.0 3.4 %copy-start.6 = (f32[4,128]{1,0:T(4,128)S(1)}, f32[4,128]{1,0:T(4,128)}, u32[]{:S(2)}) copy-start(f32[4,128]{1,0:T(4,128)} %param.14) | copy-start | bytes 6148
  22.0 7.0 %collective-permute-start.3 = (f32[16,2304]{1,0:T(8,128)S(1)}, f32[16,2304]{1,0:T(8,128)S(1)}, u32[]{:S(2)}, u32[]{:S(2)}) collective-permute-start(f32[16,2304]{1,0:T(8,128)S(1)} %get-tuple-element.5), channel_id=1, source_target_pairs={{64,0},{128,64},{192,128},{65,1},{129,65},{193,129},{66,2},{130,66... | collective-permute-start | bytes 442376 | tf_op jit(solution)/shard_map/ppermute | solution.py:30
  25.4 3.6 %copy-start.4 = (f32[17,2304]{1,0:T(8,128)}, f32[17,2304]{1,0:T(8,128)S(1)}, u32[]{:S(2)}) copy-start(f32[17,2304]{1,0:T(8,128)S(1)} %collective-permute-done.2.above_ref) | copy-start | bytes 470020
  26.7 15.6 %copy-start = (f32[64,2048]{1,0:T(8,128)S(1)}, f32[64,2048]{1,0:T(8,128)}, u32[]{:S(2)}) copy-start(f32[64,2048]{1,0:T(8,128)} %direction_ref.1) | copy-start | bytes 1572868
  29.0 0.7 copy-start.5
  42.3 1.3 %copy-start.3 = (f32[64,2048]{1,0:T(8,128)S(1)}, f32[64,2048]{1,0:T(8,128)}, u32[]{:S(2)}) copy-start(f32[64,2048]{1,0:T(8,128)} %residual_ref.1) | copy-start | bytes 1572868
  43.6 0.8 copy-start.1
  44.7 2.9 %collective-permute-start.4 = (f32[4]{0:T(128)S(1)}, f32[4]{0:T(128)S(1)}, u32[]{:S(2)}, u32[]{:S(2)}) collective-permute-start(f32[4]{0:T(128)S(1)} %maximum_reduce_fusion), channel_id=1, source_target_pairs={{0,1},{1,0},{2,3},{3,2},{4,5},{5,4},{6,7},{7,6},{8,9},{9,8},{10,11... | collective-permute-start | bytes 56 | tf_op jit(solution)/shard_map/ppermute | solution.py:46
  47.6 7.4 %collective-permute-start.5 = (f32[4]{0:T(128)S(1)}, f32[4]{0:T(128)S(1)}, u32[]{:S(2)}, u32[]{:S(2)}) collective-permute-start(f32[4]{0:T(128)S(1)} %add.34), channel_id=1, source_target_pairs={{0,2},{2,0},{1,3},{3,1},{4,6},{6,4},{5,7},{7,5},{8,10},{10,8},{9,1... | collective-permute-start | bytes 56 | tf_op jit(solution)/shard_map/ppermute | solution.py:46
  55.1 3.5 %collective-permute-start.6 = (f32[4]{0:T(128)S(1)}, f32[4]{0:T(128)S(1)}, u32[]{:S(2)}, u32[]{:S(2)}) collective-permute-start(f32[4]{0:T(128)S(1)} %add.35), channel_id=1, source_target_pairs={{0,64},{64,0},{128,192},{192,128},{1,65},{65,1},{129,193},{193,129... | collective-permute-start | bytes 56 | tf_op jit(solution)/shard_map/ppermute | solution.py:46
  58.6 4.7 %collective-permute-start.7 = (f32[4]{0:T(128)S(1)}, f32[4]{0:T(128)S(1)}, u32[]{:S(2)}, u32[]{:S(2)}) collective-permute-start(f32[4]{0:T(128)S(1)} %add.36), channel_id=1, source_target_pairs={{0,128},{64,192},{128,0},{192,64},{1,129},{65,193},{129,1},{193,65... | collective-permute-start | bytes 56 | tf_op jit(solution)/shard_map/ppermute | solution.py:46
  63.3 3.5 %collective-permute-start.8 = (f32[4]{0:T(128)S(1)}, f32[4]{0:T(128)S(1)}, u32[]{:S(2)}, u32[]{:S(2)}) collective-permute-start(f32[4]{0:T(128)S(1)} %add.37), channel_id=1, source_target_pairs={{0,16},{16,0},{32,48},{48,32},{1,17},{17,1},{33,49},{49,33},{2,18}... | collective-permute-start | bytes 56 | tf_op jit(solution)/shard_map/ppermute | solution.py:46
  66.9 5.0 %collective-permute-start.9 = (f32[4]{0:T(128)S(1)}, f32[4]{0:T(128)S(1)}, u32[]{:S(2)}, u32[]{:S(2)}) collective-permute-start(f32[4]{0:T(128)S(1)} %add.38), channel_id=1, source_target_pairs={{0,32},{16,48},{32,0},{48,16},{1,33},{17,49},{33,1},{49,17},{2,34}... | collective-permute-start | bytes 56 | tf_op jit(solution)/shard_map/ppermute | solution.py:46
  71.9 3.5 %collective-permute-start.10 = (f32[4]{0:T(128)S(1)}, f32[4]{0:T(128)S(1)}, u32[]{:S(2)}, u32[]{:S(2)}) collective-permute-start(f32[4]{0:T(128)S(1)} %add.39), channel_id=1, source_target_pairs={{0,4},{4,0},{8,12},{12,8},{1,5},{5,1},{9,13},{13,9},{2,6},{6,2},{1... | collective-permute-start | bytes 56 | tf_op jit(solution)/shard_map/ppermute | solution.py:46
  75.4 5.0 %collective-permute-start.11 = (f32[4]{0:T(128)S(1)}, f32[4]{0:T(128)S(1)}, u32[]{:S(2)}, u32[]{:S(2)}) collective-permute-start(f32[4]{0:T(128)S(1)} %add.40), channel_id=1, source_target_pairs={{0,8},{4,12},{8,0},{12,4},{1,9},{5,13},{9,1},{13,5},{2,10},{6,14},... | collective-permute-start | bytes 56 | tf_op jit(solution)/shard_map/ppermute | solution.py:46

commit v18 on v17

--- a/solution.py
+++ b/solution.py
@@ -9,8 +9,8 @@
 
 COL = ("col_0", "col_1", "col_2", "col_3")
 DOUBLING = (
+    ("col_2", 1),
     ("col_3", 1),
-    ("col_2", 1),
     ("row", 1),
     ("row", 2),
     ("col_0", 1),

time: 84 us -> 84 us (level)
  no operation moved by 1% of the time
where the time goes in v18:
time: 84 us; the launch traced here: 83.6 us
  starting transfers between devices  31.9 us (38%)
  waiting for transfers between devices  25.3 us (30%)
  Pallas kernels  15.2 us (18%)
  local copies, waits for them, and re-layouts  7.12 us (8%)
  other arithmetic  3.21 us (4%)
    ppermute x8, waiting for transfers between devices, summed_everywhere(): x = x + lax.ppermute(x, axis, [(i, i ^ mask) for i in range(count)])  21.4 us
    ppermute x4, starting transfers between devices, passed_along(): lax.ppermute(value, axis, [(source, source + steps) for source in range(l...  17.6 us
    ppermute x8, starting transfers between devices, summed_everywhere(): x = x + lax.ppermute(x, axis, [(i, i ^ mask) for i in range(count)])  14.3 us
    pallas_call x1, Pallas kernels, analyze_weigh_synthesize(): pl.pallas_call(transform_kernel, out_shape=jax.ShapeDtypeStruct((rows - 3...  12.6 us
    ppermute x4, waiting for transfers between devices, passed_along(): lax.ppermute(value, axis, [(source, source + steps) for source in range(l...  3.87 us
    pallas_call x1, Pallas kernels, updated(): pl.pallas_call(update_kernel, grid=(height // rows,), out_shape=(shape, s...  2.57 us
  transfers between devices with their start and end apart: 12, of which 11 were waited for; matrix products, arithmetic and copies ran while one was open for 4% of the time, Pallas kernels for 0%

profile of v18, /device:TPU:16, one launch (start us, length us, event | category | flops | bytes accessed | tf_op | source)
XLA Modules:
  0.0 83.6 jit_solution(10078996928628348219)
XLA Ops:
  2.6 1.9 %collective-permute-start = (f32[68,16]{1,0:T(8,128)S(1)}, f32[68,16]{1,0:T(8,128)S(1)}, u32[]{:S(2)}, u32[]{:S(2)}) collective-permute-start(f32[68,16]{1,0:T(8,128)S(1)} %copy.16), channel_id=1, source_target_pairs={{0,1},{1,2},{2,3},{3,4},{4,5},{5,6},{6,7},{7,8},{8,9},{9,10},{10,1... | collective-permute-start | bytes 13064 | tf_op jit(solution)/shard_map/ppermute | solution.py:30
  4.5 10.6 %collective-permute-start.1 = (f32[64,16]{1,0:T(8,128)S(1)}, f32[64,16]{1,0:T(8,128)S(1)}, u32[]{:S(2)}, u32[]{:S(2)}) collective-permute-start(f32[64,16]{1,0:T(8,128)S(1)} %get-tuple-element.10), channel_id=1, source_target_pairs={{1,0},{2,1},{3,2},{4,3},{5,4},{6,5},{7,6},{8,7},{9,8},{10,9},{11,1... | collective-permute-start | bytes 12296 | tf_op jit(solution)/shard_map/ppermute | solution.py:30
  16.7 1.4 %concatenate.16.middle_ref = f32[64,2304]{1,0:T(8,128)S(1)} concatenate(f32[64,16]{1,0:T(8,128)S(1)} %slice.42, f32[64,2048]{1,0:T(8,128)} %direction_ref.1, f32[64,16]{1,0:T(8,128)S(1)} %collective-permute-done.1, f32[64,224]{1,0:T(8,128)S(1)} %broadcast_in_dim.15), dimensions={1} | concatenate | bytes 1179648 | tf_op jit(solution)/shard_map/concatenate | solution.py:293
  18.2 3.8 %collective-permute-start.2 = (f32[17,2304]{1,0:T(8,128)S(1)}, f32[17,2304]{1,0:T(8,128)S(1)}, u32[]{:S(2)}, u32[]{:S(2)}) collective-permute-start(f32[17,2304]{1,0:T(8,128)S(1)} %pad_maximum_fusion), channel_id=1, source_target_pairs={{0,64},{64,128},{128,192},{1,65},{65,129},{129,193},{2,66},{66,130... | collective-permute-start | bytes 470024 | tf_op jit(solution)/shard_map/ppermute | solution.py:30
  22.0 1.3 %collective-permute-start.3 = (f32[16,2304]{1,0:T(8,128)S(1)}, f32[16,2304]{1,0:T(8,128)S(1)}, u32[]{:S(2)}, u32[]{:S(2)}) collective-permute-start(f32[16,2304]{1,0:T(8,128)S(1)} %get-tuple-element.5), channel_id=1, source_target_pairs={{64,0},{128,64},{192,128},{65,1},{129,65},{193,129},{66,2},{130,66... | collective-permute-start | bytes 442376 | tf_op jit(solution)/shard_map/ppermute | solution.py:30
  23.4 1.2 %reshape.19.fw_ref = f32[160,512]{1,0:T(8,128)} reshape(f32[5,32,2,8,32]{4,3,2,1,0:T(8,128)S(1)} %broadcast_in_dim.16) | data formatting | bytes 655360 | tf_op jit(solution)/shard_map/reshape | solution.py:237
  25.7 1.0 %reshape.20.ww_ref = f32[5,8704]{1,0:T(8,128)} reshape(f32[5,17,2,8,32]{4,3,2,1,0:T(8,128)S(1)} %broadcast_in_dim.18) | data formatting | bytes 348160 | tf_op jit(solution)/shard_map/reshape | solution.py:241
  26.7 2.3 %collective-permute-done.3.below_ref = f32[16,2304]{1,0:T(8,128)S(1)} collective-permute-done((f32[16,2304]{1,0:T(8,128)S(1)}, f32[16,2304]{1,0:T(8,128)S(1)}, u32[]{:S(2)}, u32[]{:S(2)}) %collective-permute-start.3) | collective-permute-done | bytes 147488 | tf_op jit(solution)/shard_map/ppermute | solution.py:30
  29.7 12.6 %shard_map.130 = f32[64,2304]{1,0:T(8,128)} custom-call(f32[17,2304]{1,0:T(8,128)} %copy-done.4, f32[64,2304]{1,0:T(8,128)} %copy-done.2, f32[16,2304]{1,0:T(8,128)} %copy-done.5, bf16[256,512]{1,0:T(8,128)(2,1)} %constant.7.clone.mh_ref, bf16[256,512]{1,0:T(8,128)(2,1)} %constant.20.clone.ml_ref, bf16[160,192]{1,0:T(8,128)(2,1)} %constant.21.clone.fh_ref, ...), custom_call_target="tpu_custom_call" | custom-call | tf_op jit(solution)/shard_map/pallas_call | solution.py:243
  42.3 1.3 %multiply_bitcast_fusion.2 = (f32[1,64,2048]{2,1,0:T(8,128)S(1)}, f32[64,2048]{1,0:T(8,128)S(1)}) fusion(f32[64,2048]{1,0:T(8,128)S(1)} %copy-done, f32[64,2304]{1,0:T(8,128)} %shard_map.130), kind=kLoop, calls=%fused_computation.4 | loop fusion | flops 393216 | bytes 2097152 | tf_op jit(solution)/shard_map/stack | solution.py:311
  44.7 4.4 %collective-permute-start.4 = (f32[4]{0:T(128)S(1)}, f32[4]{0:T(128)S(1)}, u32[]{:S(2)}, u32[]{:S(2)}) collective-permute-start(f32[4]{0:T(128)S(1)} %maximum_reduce_fusion), channel_id=1, source_target_pairs={{0,2},{2,0},{1,3},{3,1},{4,6},{6,4},{5,7},{7,5},{8,10},{10,8},{9,1... | collective-permute-start | bytes 56 | tf_op jit(solution)/shard_map/ppermute | solution.py:46
  49.1 3.1 %collective-permute-done.4 = f32[4]{0:T(128)S(1)} collective-permute-done((f32[4]{0:T(128)S(1)}, f32[4]{0:T(128)S(1)}, u32[]{:S(2)}, u32[]{:S(2)}) %collective-permute-start.4) | collective-permute-done | bytes 48 | tf_op jit(solution)/shard_map/ppermute | solution.py:46
  52.2 0.9 %collective-permute-start.5 = (f32[4]{0:T(128)S(1)}, f32[4]{0:T(128)S(1)}, u32[]{:S(2)}, u32[]{:S(2)}) collective-permute-start(f32[4]{0:T(128)S(1)} %add.34), channel_id=1, source_target_pairs={{0,1},{1,0},{2,3},{3,2},{4,5},{5,4},{6,7},{7,6},{8,9},{9,8},{10,11... | collective-permute-start | bytes 56 | tf_op jit(solution)/shard_map/ppermute | solution.py:46
  53.9 1.9 %collective-permute-start.6 = (f32[4]{0:T(128)S(1)}, f32[4]{0:T(128)S(1)}, u32[]{:S(2)}, u32[]{:S(2)}) collective-permute-start(f32[4]{0:T(128)S(1)} %add.35), channel_id=1, source_target_pairs={{0,64},{64,0},{128,192},{192,128},{1,65},{65,1},{129,193},{193,129... | collective-permute-start | bytes 56 | tf_op jit(solution)/shard_map/ppermute | solution.py:46
  55.8 1.7 %collective-permute-done.6 = f32[4]{0:T(128)S(1)} collective-permute-done((f32[4]{0:T(128)S(1)}, f32[4]{0:T(128)S(1)}, u32[]{:S(2)}, u32[]{:S(2)}) %collective-permute-start.6) | collective-permute-done | bytes 48 | tf_op jit(solution)/shard_map/ppermute | solution.py:46
  57.5 4.3 %collective-permute-start.7 = (f32[4]{0:T(128)S(1)}, f32[4]{0:T(128)S(1)}, u32[]{:S(2)}, u32[]{:S(2)}) collective-permute-start(f32[4]{0:T(128)S(1)} %add.36), channel_id=1, source_target_pairs={{0,128},{64,192},{128,0},{192,64},{1,129},{65,193},{129,1},{193,65... | collective-permute-start | bytes 56 | tf_op jit(solution)/shard_map/ppermute | solution.py:46
  61.8 1.5 %collective-permute-done.7 = f32[4]{0:T(128)S(1)} collective-permute-done((f32[4]{0:T(128)S(1)}, f32[4]{0:T(128)S(1)}, u32[]{:S(2)}, u32[]{:S(2)}) %collective-permute-start.7) | collective-permute-done | bytes 48 | tf_op jit(solution)/shard_map/ppermute | solution.py:46
  63.3 1.3 %collective-permute-start.8 = (f32[4]{0:T(128)S(1)}, f32[4]{0:T(128)S(1)}, u32[]{:S(2)}, u32[]{:S(2)}) collective-permute-start(f32[4]{0:T(128)S(1)} %add.37), channel_id=1, source_target_pairs={{0,16},{16,0},{32,48},{48,32},{1,17},{17,1},{33,49},{49,33},{2,18}... | collective-permute-start | bytes 56 | tf_op jit(solution)/shard_map/ppermute | solution.py:46
  64.6 2.3 %collective-permute-done.8 = f32[4]{0:T(128)S(1)} collective-permute-done((f32[4]{0:T(128)S(1)}, f32[4]{0:T(128)S(1)}, u32[]{:S(2)}, u32[]{:S(2)}) %collective-permute-start.8) | collective-permute-done | bytes 48 | tf_op jit(solution)/shard_map/ppermute | solution.py:46
  66.9 5.0 %collective-permute-done.9 = f32[4]{0:T(128)S(1)} collective-permute-done((f32[4]{0:T(128)S(1)}, f32[4]{0:T(128)S(1)}, u32[]{:S(2)}, u32[]{:S(2)}) %collective-permute-start.9) | collective-permute-done | bytes 48 | tf_op jit(solution)/shard_map/ppermute | solution.py:46
  71.9 3.5 %collective-permute-done.10 = f32[4]{0:T(128)S(1)} collective-permute-done((f32[4]{0:T(128)S(1)}, f32[4]{0:T(128)S(1)}, u32[]{:S(2)}, u32[]{:S(2)}) %collective-permute-start.10) | collective-permute-done | bytes 48 | tf_op jit(solution)/shard_map/ppermute | solution.py:46
  75.4 1.5 %collective-permute-start.11 = (f32[4]{0:T(128)S(1)}, f32[4]{0:T(128)S(1)}, u32[]{:S(2)}, u32[]{:S(2)}) collective-permute-start(f32[4]{0:T(128)S(1)} %add.40), channel_id=1, source_target_pairs={{0,8},{4,12},{8,0},{12,4},{1,9},{5,13},{9,1},{13,5},{2,10},{6,14},... | collective-permute-start | bytes 56 | tf_op jit(solution)/shard_map/ppermute | solution.py:46
  77.0 3.5 %collective-permute-done.11 = f32[4]{0:T(128)S(1)} collective-permute-done((f32[4]{0:T(128)S(1)}, f32[4]{0:T(128)S(1)}, u32[]{:S(2)}, u32[]{:S(2)}) %collective-permute-start.11) | collective-permute-done | bytes 48 | tf_op jit(solution)/shard_map/ppermute | solution.py:46
  81.0 2.6 %shard_map.131 = (f32[64,2048]{1,0:T(8,128)}, f32[64,2048]{1,0:T(8,128)}, f32[64,2048]{1,0:T(8,128)}) custom-call(f32[1,4]{1,0:T(1,128)} %add_bitcast_fusion.sums_ref, f32[64,2048]{1,0:T(8,128)} %iterate_ref.1, f32[64,2048]{1,0:T(8,128)} %residual_ref.1, f32[64,2048]{1,0:T(8,128)} %direction_ref.1, f32[64,2048]{1,0:T(8,128)} %copy-done.1), custom_call_target="tpu_custom_call" | custom-call | tf_op jit(solution)/shard_map/pallas_call | solution.py:275
  (49 shorter events, 7.8 us)
Async XLA Ops:
  0.6 22.6 %copy-start.7 = (f32[32,32]{1,0:T(8,128)S(1)}, f32[32,32]{1,0:T(8,128)}, u32[]{:S(2)}) copy-start(f32[32,32]{1,0:T(8,128)} %param.15) | copy-start | bytes 12292
  2.6 12.6 %collective-permute-start = (f32[68,16]{1,0:T(8,128)S(1)}, f32[68,16]{1,0:T(8,128)S(1)}, u32[]{:S(2)}, u32[]{:S(2)}) collective-permute-start(f32[68,16]{1,0:T(8,128)S(1)} %copy.16), channel_id=1, source_target_pairs={{0,1},{1,2},{2,3},{3,4},{4,5},{5,6},{6,7},{7,8},{8,9},{9,10},{10,1... | collective-permute-start | bytes 13064 | tf_op jit(solution)/shard_map/ppermute | solution.py:30
  4.5 12.2 %collective-permute-start.1 = (f32[64,16]{1,0:T(8,128)S(1)}, f32[64,16]{1,0:T(8,128)S(1)}, u32[]{:S(2)}, u32[]{:S(2)}) collective-permute-start(f32[64,16]{1,0:T(8,128)S(1)} %get-tuple-element.10), channel_id=1, source_target_pairs={{1,0},{2,1},{3,2},{4,3},{5,4},{6,5},{7,6},{8,7},{9,8},{10,9},{11,1... | collective-permute-start | bytes 12296 | tf_op jit(solution)/shard_map/ppermute | solution.py:30
  18.1 6.5 %copy-start.2 = (f32[64,2304]{1,0:T(8,128)}, f32[64,2304]{1,0:T(8,128)S(1)}, u32[]{:S(2)}) copy-start(f32[64,2304]{1,0:T(8,128)S(1)} %concatenate.16.middle_ref) | copy-start | bytes 1769476
  18.2 7.2 %collective-permute-start.2 = (f32[17,2304]{1,0:T(8,128)S(1)}, f32[17,2304]{1,0:T(8,128)S(1)}, u32[]{:S(2)}, u32[]{:S(2)}) collective-permute-start(f32[17,2304]{1,0:T(8,128)S(1)} %pad_maximum_fusion), channel_id=1, source_target_pairs={{0,64},{64,128},{128,192},{1,65},{65,129},{129,193},{2,66},{66,130... | collective-permute-start | bytes 470024 | tf_op jit(solution)/shard_map/ppermute | solution.py:30
  22.0 3.4 %copy-start.6 = (f32[4,128]{1,0:T(4,128)S(1)}, f32[4,128]{1,0:T(4,128)}, u32[]{:S(2)}) copy-start(f32[4,128]{1,0:T(4,128)} %param.14) | copy-start | bytes 6148
  22.0 7.0 %collective-permute-start.3 = (f32[16,2304]{1,0:T(8,128)S(1)}, f32[16,2304]{1,0:T(8,128)S(1)}, u32[]{:S(2)}, u32[]{:S(2)}) collective-permute-start(f32[16,2304]{1,0:T(8,128)S(1)} %get-tuple-element.5), channel_id=1, source_target_pairs={{64,0},{128,64},{192,128},{65,1},{129,65},{193,129},{66,2},{130,66... | collective-permute-start | bytes 442376 | tf_op jit(solution)/shard_map/ppermute | solution.py:30
  25.4 3.6 %copy-start.4 = (f32[17,2304]{1,0:T(8,128)}, f32[17,2304]{1,0:T(8,128)S(1)}, u32[]{:S(2)}) copy-start(f32[17,2304]{1,0:T(8,128)S(1)} %collective-permute-done.2.above_ref) | copy-start | bytes 470020
  26.7 15.6 %copy-start = (f32[64,2048]{1,0:T(8,128)S(1)}, f32[64,2048]{1,0:T(8,128)}, u32[]{:S(2)}) copy-start(f32[64,2048]{1,0:T(8,128)} %direction_ref.1) | copy-start | bytes 1572868
  29.0 0.7 copy-start.5
  42.3 1.3 %copy-start.3 = (f32[64,2048]{1,0:T(8,128)S(1)}, f32[64,2048]{1,0:T(8,128)}, u32[]{:S(2)}) copy-start(f32[64,2048]{1,0:T(8,128)} %residual_ref.1) | copy-start | bytes 1572868
  43.6 0.8 copy-start.1
  44.7 7.5 %collective-permute-start.4 = (f32[4]{0:T(128)S(1)}, f32[4]{0:T(128)S(1)}, u32[]{:S(2)}, u32[]{:S(2)}) collective-permute-start(f32[4]{0:T(128)S(1)} %maximum_reduce_fusion), channel_id=1, source_target_pairs={{0,2},{2,0},{1,3},{3,1},{4,6},{6,4},{5,7},{7,5},{8,10},{10,8},{9,1... | collective-permute-start | bytes 56 | tf_op jit(solution)/shard_map/ppermute | solution.py:46
  52.2 1.7 %collective-permute-start.5 = (f32[4]{0:T(128)S(1)}, f32[4]{0:T(128)S(1)}, u32[]{:S(2)}, u32[]{:S(2)}) collective-permute-start(f32[4]{0:T(128)S(1)} %add.34), channel_id=1, source_target_pairs={{0,1},{1,0},{2,3},{3,2},{4,5},{5,4},{6,7},{7,6},{8,9},{9,8},{10,11... | collective-permute-start | bytes 56 | tf_op jit(solution)/shard_map/ppermute | solution.py:46
  53.9 3.5 %collective-permute-start.6 = (f32[4]{0:T(128)S(1)}, f32[4]{0:T(128)S(1)}, u32[]{:S(2)}, u32[]{:S(2)}) collective-permute-start(f32[4]{0:T(128)S(1)} %add.35), channel_id=1, source_target_pairs={{0,64},{64,0},{128,192},{192,128},{1,65},{65,1},{129,193},{193,129... | collective-permute-start | bytes 56 | tf_op jit(solution)/shard_map/ppermute | solution.py:46
  57.5 5.8 %collective-permute-start.7 = (f32[4]{0:T(128)S(1)}, f32[4]{0:T(128)S(1)}, u32[]{:S(2)}, u32[]{:S(2)}) collective-permute-start(f32[4]{0:T(128)S(1)} %add.36), channel_id=1, source_target_pairs={{0,128},{64,192},{128,0},{192,64},{1,129},{65,193},{129,1},{193,65... | collective-permute-start | bytes 56 | tf_op jit(solution)/shard_map/ppermute | solution.py:46
  63.3 3.5 %collective-permute-start.8 = (f32[4]{0:T(128)S(1)}, f32[4]{0:T(128)S(1)}, u32[]{:S(2)}, u32[]{:S(2)}) collective-permute-start(f32[4]{0:T(128)S(1)} %add.37), channel_id=1, source_target_pairs={{0,16},{16,0},{32,48},{48,32},{1,17},{17,1},{33,49},{49,33},{2,18}... | collective-permute-start | bytes 56 | tf_op jit(solution)/shard_map/ppermute | solution.py:46
  66.9 5.0 %collective-permute-start.9 = (f32[4]{0:T(128)S(1)}, f32[4]{0:T(128)S(1)}, u32[]{:S(2)}, u32[]{:S(2)}) collective-permute-start(f32[4]{0:T(128)S(1)} %add.38), channel_id=1, source_target_pairs={{0,32},{16,48},{32,0},{48,16},{1,33},{17,49},{33,1},{49,17},{2,34}... | collective-permute-start | bytes 56 | tf_op jit(solution)/shard_map/ppermute | solution.py:46
  71.9 3.5 %collective-permute-start.10 = (f32[4]{0:T(128)S(1)}, f32[4]{0:T(128)S(1)}, u32[]{:S(2)}, u32[]{:S(2)}) collective-permute-start(f32[4]{0:T(128)S(1)} %add.39), channel_id=1, source_target_pairs={{0,4},{4,0},{8,12},{12,8},{1,5},{5,1},{9,13},{13,9},{2,6},{6,2},{1... | collective-permute-start | bytes 56 | tf_op jit(solution)/shard_map/ppermute | solution.py:46
  75.4 5.0 %collective-permute-start.11 = (f32[4]{0:T(128)S(1)}, f32[4]{0:T(128)S(1)}, u32[]{:S(2)}, u32[]{:S(2)}) collective-permute-start(f32[4]{0:T(128)S(1)} %add.40), channel_id=1, source_target_pairs={{0,8},{4,12},{8,0},{12,4},{1,9},{5,13},{9,1},{13,5},{2,10},{6,14},... | collective-permute-start | bytes 56 | tf_op jit(solution)/shard_map/ppermute | solution.py:46

commit v19 on v17

--- a/solution.py
+++ b/solution.py
@@ -138,10 +138,11 @@
     return [columns, forward, backward]
 
 
-def split_constant(table):
+def split_constant(table, stacked=False):
     high = table.astype(jnp.bfloat16)
     low = (table - high.astype(np.float32)).astype(jnp.bfloat16)
-    return [jnp.asarray(high), jnp.asarray(low)]
+    parts = [high, low] + ([np.concatenate([high, low], axis=0)] if stacked else [])
+    return [jnp.asarray(part) for part in parts]
 
 
 def split_value(value):
@@ -165,16 +166,14 @@
 
 def constant_first_dot(a, b):
     rows = a[0].shape[0]
-    both = jnp.dot(
-        jnp.concatenate([a[0], a[1]], axis=0), b[0], preferred_element_type=jnp.float32
-    )
+    both = jnp.dot(a[2], b[0], preferred_element_type=jnp.float32)
     total = jnp.dot(a[0], b[1], preferred_element_type=jnp.float32)
     total += both[rows:]
     return total + both[:rows]
 
 
 def transform_kernel(
-    above_ref, middle_ref, below_ref, mh_ref, ml_ref, fh_ref, fl_ref, gh_ref, gl_ref, fw_ref,
+    above_ref, middle_ref, below_ref, mh_ref, ml_ref, fh_ref, fl_ref, fs_ref, gh_ref, gl_ref, gs_ref, fw_ref,
     ww_ref, out_ref, y_ref, e_ref,
 ):
     x = jnp.concatenate([above_ref[:16], middle_ref[...], below_ref[...]], axis=0)
@@ -185,8 +184,8 @@
         [x[:, t * LANES : (t + 2) * LANES] for t in range(tiles)], axis=0
     )
     y_ref[...] = three_pass_dot(split_value(stacked_x), (mh_ref[...], ml_ref[...]))
-    forward = (fh_ref[...], fl_ref[...])
-    backward = (gh_ref[...], gl_ref[...])
+    forward = (fh_ref[...], fl_ref[...], fs_ref[...])
+    backward = (gh_ref[...], gl_ref[...], gs_ref[...])
     freq = fw_ref[...]
 
     def turn(value, sign):
@@ -230,8 +229,8 @@
     window_weight = jnp.pad(window_weight, ((0, 0), (0, tiles * WINDOWS_PER_TILE - windows)))
     win_rows = rows // 16 - 1
     constants = []
-    for table in transform_tables(win_rows):
-        constants += split_constant(table)
+    for i, table in enumerate(transform_tables(win_rows)):
+        constants += split_constant(table, stacked=i > 0)
     freq = jnp.broadcast_to(
         freq_weight.reshape(1, 32, 1, 1, 32), (win_rows, 32, 2, WINDOWS_PER_TILE, 32)
     ).reshape(win_rows * 32, 2 * HALF)
@@ -243,7 +242,7 @@
     out = pl.pallas_call(
         transform_kernel,
         out_shape=jax.ShapeDtypeStruct((rows - 32, wide), jnp.float32),
-        in_specs=[vmem] * 11,
+        in_specs=[vmem] * 13,
         out_specs=vmem,
         scratch_shapes=[
             pltpu.VMEM((tiles * rows, 2 * HALF), jnp.float32),

time: 84 us -> 84.1 us (level)
  no operation moved by 1% of the time
where the time goes in v19:
time: 84.1 us; the launch traced here: 83.7 us
  starting transfers between devices  32 us (38%)
  waiting for transfers between devices  25.3 us (30%)
  Pallas kernels  15.3 us (18%)
  local copies, waits for them, and re-layouts  7.12 us (8%)
  other arithmetic  3.21 us (4%)
    ppermute x8, waiting for transfers between devices, summed_everywhere(): x = x + lax.ppermute(x, axis, [(i, i ^ mask) for i in range(count)])  21.4 us
    ppermute x4, starting transfers between devices, passed_along(): lax.ppermute(value, axis, [(source, source + steps) for source in range(l...  17.6 us
    ppermute x8, starting transfers between devices, summed_everywhere(): x = x + lax.ppermute(x, axis, [(i, i ^ mask) for i in range(count)])  14.4 us
    pallas_call x1, Pallas kernels, analyze_weigh_synthesize(): pl.pallas_call(transform_kernel, out_shape=jax.ShapeDtypeStruct((rows - 3...  12.7 us
    ppermute x4, waiting for transfers between devices, passed_along(): lax.ppermute(value, axis, [(source, source + steps) for source in range(l...  3.87 us
    pallas_call x1, Pallas kernels, updated(): pl.pallas_call(update_kernel, grid=(height // rows,), out_shape=(shape, s...  2.57 us
  transfers between devices with their start and end apart: 12, of which 11 were waited for; matrix products, arithmetic and copies ran while one was open for 4% of the time, Pallas kernels for 0%

profile of v19, /device:TPU:16, one launch (start us, length us, event | category | flops | bytes accessed | tf_op | source)
XLA Modules:
  0.0 83.7 jit_solution(8932363282478499205)
XLA Ops:
  2.6 1.9 %collective-permute-start = (f32[68,16]{1,0:T(8,128)S(1)}, f32[68,16]{1,0:T(8,128)S(1)}, u32[]{:S(2)}, u32[]{:S(2)}) collective-permute-start(f32[68,16]{1,0:T(8,128)S(1)} %copy.18), channel_id=1, source_target_pairs={{0,1},{1,2},{2,3},{3,4},{4,5},{5,6},{6,7},{7,8},{8,9},{9,10},{10,1... | collective-permute-start | bytes 13064 | tf_op jit(solution)/shard_map/ppermute | solution.py:30
  4.5 10.6 %collective-permute-start.1 = (f32[64,16]{1,0:T(8,128)S(1)}, f32[64,16]{1,0:T(8,128)S(1)}, u32[]{:S(2)}, u32[]{:S(2)}) collective-permute-start(f32[64,16]{1,0:T(8,128)S(1)} %get-tuple-element.10), channel_id=1, source_target_pairs={{1,0},{2,1},{3,2},{4,3},{5,4},{6,5},{7,6},{8,7},{9,8},{10,9},{11,1... | collective-permute-start | bytes 12296 | tf_op jit(solution)/shard_map/ppermute | solution.py:30
  16.7 1.4 %concatenate.16.middle_ref = f32[64,2304]{1,0:T(8,128)S(1)} concatenate(f32[64,16]{1,0:T(8,128)S(1)} %slice.42, f32[64,2048]{1,0:T(8,128)} %direction_ref.1, f32[64,16]{1,0:T(8,128)S(1)} %collective-permute-done.1, f32[64,224]{1,0:T(8,128)S(1)} %broadcast_in_dim.15), dimensions={1} | concatenate | bytes 1179648 | tf_op jit(solution)/shard_map/concatenate | solution.py:292
  18.2 3.8 %collective-permute-start.2 = (f32[17,2304]{1,0:T(8,128)S(1)}, f32[17,2304]{1,0:T(8,128)S(1)}, u32[]{:S(2)}, u32[]{:S(2)}) collective-permute-start(f32[17,2304]{1,0:T(8,128)S(1)} %pad_maximum_fusion), channel_id=1, source_target_pairs={{0,64},{64,128},{128,192},{1,65},{65,129},{129,193},{2,66},{66,130... | collective-permute-start | bytes 470024 | tf_op jit(solution)/shard_map/ppermute | solution.py:30
  22.0 1.3 %collective-permute-start.3 = (f32[16,2304]{1,0:T(8,128)S(1)}, f32[16,2304]{1,0:T(8,128)S(1)}, u32[]{:S(2)}, u32[]{:S(2)}) collective-permute-start(f32[16,2304]{1,0:T(8,128)S(1)} %get-tuple-element.5), channel_id=1, source_target_pairs={{64,0},{128,64},{192,128},{65,1},{129,65},{193,129},{66,2},{130,66... | collective-permute-start | bytes 442376 | tf_op jit(solution)/shard_map/ppermute | solution.py:30
  23.4 1.2 %reshape.19.fw_ref = f32[160,512]{1,0:T(8,128)} reshape(f32[5,32,2,8,32]{4,3,2,1,0:T(8,128)S(1)} %broadcast_in_dim.16) | data formatting | bytes 655360 | tf_op jit(solution)/shard_map/reshape | solution.py:236
  26.7 2.3 %collective-permute-done.3.below_ref = f32[16,2304]{1,0:T(8,128)S(1)} collective-permute-done((f32[16,2304]{1,0:T(8,128)S(1)}, f32[16,2304]{1,0:T(8,128)S(1)}, u32[]{:S(2)}, u32[]{:S(2)}) %collective-permute-start.3) | collective-permute-done | bytes 147488 | tf_op jit(solution)/shard_map/ppermute | solution.py:30
  29.7 12.7 %shard_map.148 = f32[64,2304]{1,0:T(8,128)} custom-call(f32[17,2304]{1,0:T(8,128)} %copy-done.4, f32[64,2304]{1,0:T(8,128)} %copy-done.2, f32[16,2304]{1,0:T(8,128)} %copy-done.5, bf16[256,512]{1,0:T(8,128)(2,1)} %constant.9.clone.mh_ref, bf16[256,512]{1,0:T(8,128)(2,1)} %constant.24.clone.ml_ref, bf16[160,192]{1,0:T(8,128)(2,1)} %constant.25.clone.fh_ref, ...), custom_call_target="tpu_custom_call" | custom-call | tf_op jit(solution)/shard_map/pallas_call | solution.py:242
  42.4 1.3 %multiply_bitcast_fusion.2 = (f32[1,64,2048]{2,1,0:T(8,128)S(1)}, f32[64,2048]{1,0:T(8,128)S(1)}) fusion(f32[64,2048]{1,0:T(8,128)S(1)} %copy-done, f32[64,2304]{1,0:T(8,128)} %shard_map.148), kind=kLoop, calls=%fused_computation.4 | loop fusion | flops 393216 | bytes 2097152 | tf_op jit(solution)/shard_map/stack | solution.py:310
  44.8 2.1 %collective-permute-start.4 = (f32[4]{0:T(128)S(1)}, f32[4]{0:T(128)S(1)}, u32[]{:S(2)}, u32[]{:S(2)}) collective-permute-start(f32[4]{0:T(128)S(1)} %maximum_reduce_fusion), channel_id=1, source_target_pairs={{0,1},{1,0},{2,3},{3,2},{4,5},{5,4},{6,7},{7,6},{8,9},{9,8},{10,11... | collective-permute-start | bytes 56 | tf_op jit(solution)/shard_map/ppermute | solution.py:46
  47.7 2.6 %collective-permute-start.5 = (f32[4]{0:T(128)S(1)}, f32[4]{0:T(128)S(1)}, u32[]{:S(2)}, u32[]{:S(2)}) collective-permute-start(f32[4]{0:T(128)S(1)} %add.34), channel_id=1, source_target_pairs={{0,2},{2,0},{1,3},{3,1},{4,6},{6,4},{5,7},{7,5},{8,10},{10,8},{9,1... | collective-permute-start | bytes 56 | tf_op jit(solution)/shard_map/ppermute | solution.py:46
  50.3 4.8 %collective-permute-done.5 = f32[4]{0:T(128)S(1)} collective-permute-done((f32[4]{0:T(128)S(1)}, f32[4]{0:T(128)S(1)}, u32[]{:S(2)}, u32[]{:S(2)}) %collective-permute-start.5) | collective-permute-done | bytes 48 | tf_op jit(solution)/shard_map/ppermute | solution.py:46
  55.2 1.4 %collective-permute-start.6 = (f32[4]{0:T(128)S(1)}, f32[4]{0:T(128)S(1)}, u32[]{:S(2)}, u32[]{:S(2)}) collective-permute-start(f32[4]{0:T(128)S(1)} %add.35), channel_id=1, source_target_pairs={{0,64},{64,0},{128,192},{192,128},{1,65},{65,1},{129,193},{193,129... | collective-permute-start | bytes 56 | tf_op jit(solution)/shard_map/ppermute | solution.py:46
  56.5 2.2 %collective-permute-done.6 = f32[4]{0:T(128)S(1)} collective-permute-done((f32[4]{0:T(128)S(1)}, f32[4]{0:T(128)S(1)}, u32[]{:S(2)}, u32[]{:S(2)}) %collective-permute-start.6) | collective-permute-done | bytes 48 | tf_op jit(solution)/shard_map/ppermute | solution.py:46
  58.7 3.2 %collective-permute-start.7 = (f32[4]{0:T(128)S(1)}, f32[4]{0:T(128)S(1)}, u32[]{:S(2)}, u32[]{:S(2)}) collective-permute-start(f32[4]{0:T(128)S(1)} %add.36), channel_id=1, source_target_pairs={{0,128},{64,192},{128,0},{192,64},{1,129},{65,193},{129,1},{193,65... | collective-permute-start | bytes 56 | tf_op jit(solution)/shard_map/ppermute | solution.py:46
  61.9 1.5 %collective-permute-done.7 = f32[4]{0:T(128)S(1)} collective-permute-done((f32[4]{0:T(128)S(1)}, f32[4]{0:T(128)S(1)}, u32[]{:S(2)}, u32[]{:S(2)}) %collective-permute-start.7) | collective-permute-done | bytes 48 | tf_op jit(solution)/shard_map/ppermute | solution.py:46
  63.4 1.3 %collective-permute-start.8 = (f32[4]{0:T(128)S(1)}, f32[4]{0:T(128)S(1)}, u32[]{:S(2)}, u32[]{:S(2)}) collective-permute-start(f32[4]{0:T(128)S(1)} %add.37), channel_id=1, source_target_pairs={{0,16},{16,0},{32,48},{48,32},{1,17},{17,1},{33,49},{49,33},{2,18}... | collective-permute-start | bytes 56 | tf_op jit(solution)/shard_map/ppermute | solution.py:46
  64.7 2.3 %collective-permute-done.8 = f32[4]{0:T(128)S(1)} collective-permute-done((f32[4]{0:T(128)S(1)}, f32[4]{0:T(128)S(1)}, u32[]{:S(2)}, u32[]{:S(2)}) %collective-permute-start.8) | collective-permute-done | bytes 48 | tf_op jit(solution)/shard_map/ppermute | solution.py:46
  67.0 5.0 %collective-permute-done.9 = f32[4]{0:T(128)S(1)} collective-permute-done((f32[4]{0:T(128)S(1)}, f32[4]{0:T(128)S(1)}, u32[]{:S(2)}, u32[]{:S(2)}) %collective-permute-start.9) | collective-permute-done | bytes 48 | tf_op jit(solution)/shard_map/ppermute | solution.py:46
  72.0 1.1 %collective-permute-start.10 = (f32[4]{0:T(128)S(1)}, f32[4]{0:T(128)S(1)}, u32[]{:S(2)}, u32[]{:S(2)}) collective-permute-start(f32[4]{0:T(128)S(1)} %add.39), channel_id=1, source_target_pairs={{0,4},{4,0},{8,12},{12,8},{1,5},{5,1},{9,13},{13,9},{2,6},{6,2},{1... | collective-permute-start | bytes 56 | tf_op jit(solution)/shard_map/ppermute | solution.py:46
  73.1 2.4 %collective-permute-done.10 = f32[4]{0:T(128)S(1)} collective-permute-done((f32[4]{0:T(128)S(1)}, f32[4]{0:T(128)S(1)}, u32[]{:S(2)}, u32[]{:S(2)}) %collective-permute-start.10) | collective-permute-done | bytes 48 | tf_op jit(solution)/shard_map/ppermute | solution.py:46
  75.5 2.7 %collective-permute-start.11 = (f32[4]{0:T(128)S(1)}, f32[4]{0:T(128)S(1)}, u32[]{:S(2)}, u32[]{:S(2)}) collective-permute-start(f32[4]{0:T(128)S(1)} %add.40), channel_id=1, source_target_pairs={{0,8},{4,12},{8,0},{12,4},{1,9},{5,13},{9,1},{13,5},{2,10},{6,14},... | collective-permute-start | bytes 56 | tf_op jit(solution)/shard_map/ppermute | solution.py:46
  78.2 2.4 %collective-permute-done.11 = f32[4]{0:T(128)S(1)} collective-permute-done((f32[4]{0:T(128)S(1)}, f32[4]{0:T(128)S(1)}, u32[]{:S(2)}, u32[]{:S(2)}) %collective-permute-start.11) | collective-permute-done | bytes 48 | tf_op jit(solution)/shard_map/ppermute | solution.py:46
  81.1 2.6 %shard_map.149 = (f32[64,2048]{1,0:T(8,128)}, f32[64,2048]{1,0:T(8,128)}, f32[64,2048]{1,0:T(8,128)}) custom-call(f32[1,4]{1,0:T(1,128)} %add_bitcast_fusion.sums_ref, f32[64,2048]{1,0:T(8,128)} %iterate_ref.1, f32[64,2048]{1,0:T(8,128)} %residual_ref.1, f32[64,2048]{1,0:T(8,128)} %direction_ref.1, f32[64,2048]{1,0:T(8,128)} %copy-done.1), custom_call_target="tpu_custom_call" | custom-call | tf_op jit(solution)/shard_map/pallas_call | solution.py:274
  (49 shorter events, 8.8 us)
Async XLA Ops:
  0.6 22.6 %copy-start.7 = (f32[32,32]{1,0:T(8,128)S(1)}, f32[32,32]{1,0:T(8,128)}, u32[]{:S(2)}) copy-start(f32[32,32]{1,0:T(8,128)} %param.17) | copy-start | bytes 12292
  2.6 12.6 %collective-permute-start = (f32[68,16]{1,0:T(8,128)S(1)}, f32[68,16]{1,0:T(8,128)S(1)}, u32[]{:S(2)}, u32[]{:S(2)}) collective-permute-start(f32[68,16]{1,0:T(8,128)S(1)} %copy.18), channel_id=1, source_target_pairs={{0,1},{1,2},{2,3},{3,4},{4,5},{5,6},{6,7},{7,8},{8,9},{9,10},{10,1... | collective-permute-start | bytes 13064 | tf_op jit(solution)/shard_map/ppermute | solution.py:30
  4.5 12.2 %collective-permute-start.1 = (f32[64,16]{1,0:T(8,128)S(1)}, f32[64,16]{1,0:T(8,128)S(1)}, u32[]{:S(2)}, u32[]{:S(2)}) collective-permute-start(f32[64,16]{1,0:T(8,128)S(1)} %get-tuple-element.10), channel_id=1, source_target_pairs={{1,0},{2,1},{3,2},{4,3},{5,4},{6,5},{7,6},{8,7},{9,8},{10,9},{11,1... | collective-permute-start | bytes 12296 | tf_op jit(solution)/shard_map/ppermute | solution.py:30
  18.1 6.5 %copy-start.2 = (f32[64,2304]{1,0:T(8,128)}, f32[64,2304]{1,0:T(8,128)S(1)}, u32[]{:S(2)}) copy-start(f32[64,2304]{1,0:T(8,128)S(1)} %concatenate.16.middle_ref) | copy-start | bytes 1769476
  18.2 7.2 %collective-permute-start.2 = (f32[17,2304]{1,0:T(8,128)S(1)}, f32[17,2304]{1,0:T(8,128)S(1)}, u32[]{:S(2)}, u32[]{:S(2)}) collective-permute-start(f32[17,2304]{1,0:T(8,128)S(1)} %pad_maximum_fusion), channel_id=1, source_target_pairs={{0,64},{64,128},{128,192},{1,65},{65,129},{129,193},{2,66},{66,130... | collective-permute-start | bytes 470024 | tf_op jit(solution)/shard_map/ppermute | solution.py:30
  22.0 3.4 %copy-start.6 = (f32[4,128]{1,0:T(4,128)S(1)}, f32[4,128]{1,0:T(4,128)}, u32[]{:S(2)}) copy-start(f32[4,128]{1,0:T(4,128)} %param.16) | copy-start | bytes 6148
  22.0 7.0 %collective-permute-start.3 = (f32[16,2304]{1,0:T(8,128)S(1)}, f32[16,2304]{1,0:T(8,128)S(1)}, u32[]{:S(2)}, u32[]{:S(2)}) collective-permute-start(f32[16,2304]{1,0:T(8,128)S(1)} %get-tuple-element.5), channel_id=1, source_target_pairs={{64,0},{128,64},{192,128},{65,1},{129,65},{193,129},{66,2},{130,66... | collective-permute-start | bytes 442376 | tf_op jit(solution)/shard_map/ppermute | solution.py:30
  25.4 3.6 %copy-start.4 = (f32[17,2304]{1,0:T(8,128)}, f32[17,2304]{1,0:T(8,128)S(1)}, u32[]{:S(2)}) copy-start(f32[17,2304]{1,0:T(8,128)S(1)} %collective-permute-done.2.above_ref) | copy-start | bytes 470020
  26.7 15.7 %copy-start = (f32[64,2048]{1,0:T(8,128)S(1)}, f32[64,2048]{1,0:T(8,128)}, u32[]{:S(2)}) copy-start(f32[64,2048]{1,0:T(8,128)} %direction_ref.1) | copy-start | bytes 1572868
  29.0 0.7 copy-start.5
  42.4 1.3 %copy-start.3 = (f32[64,2048]{1,0:T(8,128)S(1)}, f32[64,2048]{1,0:T(8,128)}, u32[]{:S(2)}) copy-start(f32[64,2048]{1,0:T(8,128)} %residual_ref.1) | copy-start | bytes 1572868
  43.7 0.8 copy-start.1
  44.8 2.9 %collective-permute-start.4 = (f32[4]{0:T(128)S(1)}, f32[4]{0:T(128)S(1)}, u32[]{:S(2)}, u32[]{:S(2)}) collective-permute-start(f32[4]{0:T(128)S(1)} %maximum_reduce_fusion), channel_id=1, source_target_pairs={{0,1},{1,0},{2,3},{3,2},{4,5},{5,4},{6,7},{7,6},{8,9},{9,8},{10,11... | collective-permute-start | bytes 56 | tf_op jit(solution)/shard_map/ppermute | solution.py:46
  47.7 7.4 %collective-permute-start.5 = (f32[4]{0:T(128)S(1)}, f32[4]{0:T(128)S(1)}, u32[]{:S(2)}, u32[]{:S(2)}) collective-permute-start(f32[4]{0:T(128)S(1)} %add.34), channel_id=1, source_target_pairs={{0,2},{2,0},{1,3},{3,1},{4,6},{6,4},{5,7},{7,5},{8,10},{10,8},{9,1... | collective-permute-start | bytes 56 | tf_op jit(solution)/shard_map/ppermute | solution.py:46
  55.2 3.5 %collective-permute-start.6 = (f32[4]{0:T(128)S(1)}, f32[4]{0:T(128)S(1)}, u32[]{:S(2)}, u32[]{:S(2)}) collective-permute-start(f32[4]{0:T(128)S(1)} %add.35), channel_id=1, source_target_pairs={{0,64},{64,0},{128,192},{192,128},{1,65},{65,1},{129,193},{193,129... | collective-permute-start | bytes 56 | tf_op jit(solution)/shard_map/ppermute | solution.py:46
  58.7 4.7 %collective-permute-start.7 = (f32[4]{0:T(128)S(1)}, f32[4]{0:T(128)S(1)}, u32[]{:S(2)}, u32[]{:S(2)}) collective-permute-start(f32[4]{0:T(128)S(1)} %add.36), channel_id=1, source_target_pairs={{0,128},{64,192},{128,0},{192,64},{1,129},{65,193},{129,1},{193,65... | collective-permute-start | bytes 56 | tf_op jit(solution)/shard_map/ppermute | solution.py:46
  63.4 3.5 %collective-permute-start.8 = (f32[4]{0:T(128)S(1)}, f32[4]{0:T(128)S(1)}, u32[]{:S(2)}, u32[]{:S(2)}) collective-permute-start(f32[4]{0:T(128)S(1)} %add.37), channel_id=1, source_target_pairs={{0,16},{16,0},{32,48},{48,32},{1,17},{17,1},{33,49},{49,33},{2,18}... | collective-permute-start | bytes 56 | tf_op jit(solution)/shard_map/ppermute | solution.py:46
  67.0 5.0 %collective-permute-start.9 = (f32[4]{0:T(128)S(1)}, f32[4]{0:T(128)S(1)}, u32[]{:S(2)}, u32[]{:S(2)}) collective-permute-start(f32[4]{0:T(128)S(1)} %add.38), channel_id=1, source_target_pairs={{0,32},{16,48},{32,0},{48,16},{1,33},{17,49},{33,1},{49,17},{2,34}... | collective-permute-start | bytes 56 | tf_op jit(solution)/shard_map/ppermute | solution.py:46
  72.0 3.5 %collective-permute-start.10 = (f32[4]{0:T(128)S(1)}, f32[4]{0:T(128)S(1)}, u32[]{:S(2)}, u32[]{:S(2)}) collective-permute-start(f32[4]{0:T(128)S(1)} %add.39), channel_id=1, source_target_pairs={{0,4},{4,0},{8,12},{12,8},{1,5},{5,1},{9,13},{13,9},{2,6},{6,2},{1... | collective-permute-start | bytes 56 | tf_op jit(solution)/shard_map/ppermute | solution.py:46
  75.5 5.0 %collective-permute-start.11 = (f32[4]{0:T(128)S(1)}, f32[4]{0:T(128)S(1)}, u32[]{:S(2)}, u32[]{:S(2)}) collective-permute-start(f32[4]{0:T(128)S(1)} %add.40), channel_id=1, source_target_pairs={{0,8},{4,12},{8,0},{12,4},{1,9},{5,13},{9,1},{13,5},{2,10},{6,14},... | collective-permute-start | bytes 56 | tf_op jit(solution)/shard_map/ppermute | solution.py:46
